TPU v7x, 32 devices: a whole 2x2x4 slice. The times are simulated.
32 devices in a mesh: groups: 2 (over x), seq: 16 (over z, y, core).
Axes of the slice: x: 2, y: 2, z: 4, core: 2. Of those that a mesh axis runs over, the one named last changes fastest.
Arguments:
- layer_input: bfloat16 [4096, 768], P(('groups', 'seq')), parts along dimension 0, may hold values from -60 to 60
- norm_gain: bfloat16 [768], replicated, may hold values from 0.099609375 to 1.8984375
- projection: bfloat16 [768, 2304], replicated, may hold values from -8 to 8
- output_weight: bfloat16 [768, 768], replicated, may hold values from -0.21875 to 0.21875
- deep_weight: bfloat16 [768, 512], replicated, may hold values from -0.21875 to 0.21875
- skip_weight: bfloat16 [768, 512], replicated, may hold values from -0.21875 to 0.21875
- conv_kernel: bfloat16 [3, 3, 3, 128, 64], replicated, may hold values from -0.109375 to 0.109375
Outputs:
- encoded: bfloat16 [4096, 768], P(('groups', 'seq')), parts along dimension 0
- decoded: bfloat16 [32, 2, 32, 16, 64], P(('groups', 'seq')), parts along dimension 0
There are 2 independent parts, one for each index of `groups`. A program takes and returns all parts, laid end to end along the dimension named above; an argument that names none is the same for every part. Nothing has to cross between parts.
All inputs are finite; a program needn't handle non-finite values.
Results may differ from a plain program's by a relative error of at most 0.0078.
Values may be sent and summed in bfloat16 or wider, within the bound.
No kernel may reach another device: no remote copies, remote signals or barrier semaphores. Data moves between devices by JAX's collectives and lax.ppermute only.
A program may use at most 128 MiB of HBM per device.

v0:
```python
import math

import jax
import jax.numpy as jnp
from jax import lax
from jax.sharding import PartitionSpec as P

HEADS = 12
GZ = 8


epsilon = 1e-06
leak_slope = 0.01


def shifted(block, axis, distance):
    devices = range(lax.axis_size(axis))
    route = [(i - distance, i) for i in devices if i - distance in devices]
    return lax.ppermute(block, axis, route)


def swapped(x, axis, distance):
    return lax.ppermute(x, axis, [(i, i ^ 1 << distance) for i in range(lax.axis_size(axis))])


def layer_norm(inputs, gain):
    values32 = inputs.astype(jnp.float32)
    row_mean = jnp.mean(values32, axis=-1, keepdims=True)
    centered = values32 - row_mean
    row_var = jnp.mean(centered * centered, axis=-1, keepdims=True)
    return centered * lax.rsqrt(row_var + epsilon) * gain.astype(jnp.float32)


def to_voxels(flat_out, channels):
    extent_x, extent_y, extent_z = (flat_out.shape[0], flat_out.shape[1], flat_out.shape[2])
    shaped = flat_out.reshape(extent_x, extent_y, extent_z, 2, 2, 2, channels)
    shaped = shaped.transpose(0, 3, 1, 4, 2, 5, 6)
    return shaped.reshape(2 * extent_x, 2 * extent_y, 2 * extent_z, channels)


def upsample(token_grid, weight):
    model_width = token_grid.shape[-1]
    product = jnp.dot(
        token_grid.reshape(-1, model_width), weight, preferred_element_type=jnp.float32
    )
    flat_out = product.astype(jnp.bfloat16).reshape(token_grid.shape[:3] + (weight.shape[1],))
    return to_voxels(flat_out, weight.shape[1] // 8)


def convolve(full_xy, conv_kernel):
    full_field = jnp.pad(full_xy, ((0, 0), (0, 0), (1, 1), (0, 0)))
    extent = (full_field.shape[0] - 2, full_field.shape[1] - 2, full_field.shape[2] - 2)
    columns = []
    for tap_x in range(3):
        for tap_y in range(3):
            for tap_z in range(3):
                columns.append(
                    full_field[
                        tap_x : tap_x + extent[0],
                        tap_y : tap_y + extent[1],
                        tap_z : tap_z + extent[2],
                        :,
                    ]
                )
    stacked = jnp.concatenate(columns, axis=-1)
    channels = conv_kernel.shape[-1]
    accumulated = jnp.dot(
        stacked.reshape(-1, stacked.shape[-1]),
        conv_kernel.reshape(-1, channels),
        preferred_element_type=jnp.float32,
    )
    activated = jnp.where(accumulated > 0, accumulated, leak_slope * accumulated)
    return activated.astype(jnp.bfloat16).reshape(extent + (channels,))


def plane_send(plane, offset):
    return shifted(plane, "seq", offset)


def body(layer_input, norm_gain, projection, output_weight, deep_weight, skip_weight, conv_kernel):
    token_count, model_width = layer_input.shape
    head_size = model_width // HEADS
    score_scale = 1.0 / math.sqrt(head_size)
    normed = layer_norm(layer_input, norm_gain).astype(jnp.bfloat16)
    projected = jnp.dot(normed, projection, preferred_element_type=jnp.float32)
    queries = projected[:, :model_width].astype(jnp.bfloat16).reshape(token_count, HEADS, head_size)
    key_value = projected[:, model_width:].astype(jnp.bfloat16)

    def update(running, key_block, value_block):
        row_max, denominator, numerator = running
        key_heads = key_block.reshape(-1, HEADS, head_size)
        value_heads = value_block.reshape(-1, HEADS, head_size)
        scores = (
            jnp.einsum("qhd,khd->hqk", queries, key_heads, preferred_element_type=jnp.float32)
            * score_scale
        )
        new_max = jnp.maximum(row_max, jnp.max(scores, axis=-1))
        rescale = jnp.exp(row_max - new_max)
        exp_scores = jnp.exp(scores - new_max[:, :, None])
        denominator = denominator * rescale + jnp.sum(exp_scores, axis=-1)
        softmax_weights = exp_scores.astype(jnp.bfloat16)
        numerator = numerator * rescale.T[:, :, None] + jnp.einsum(
            "hqk,khd->qhd", softmax_weights, value_heads, preferred_element_type=jnp.float32
        )
        return (new_max, denominator, numerator)

    def attend(running, pair_rows):
        rows_in = pair_rows.shape[0]
        if rows_in > 2048 and rows_in % 2048 == 0:

            def step_body(block_index, inner_state):
                row_slab = lax.dynamic_slice_in_dim(pair_rows, block_index * 2048, 2048, 0)
                return update(inner_state, row_slab[:, :model_width], row_slab[:, model_width:])

            return lax.fori_loop(0, rows_in // 2048, step_body, running)
        return update(running, pair_rows[:, :model_width], pair_rows[:, model_width:])

    initial = (
        jnp.full((HEADS, token_count), -1e30, jnp.float32),
        jnp.zeros((HEADS, token_count), jnp.float32),
        jnp.zeros((token_count, HEADS, head_size), jnp.float32),
    )
    final_state = attend(initial, lax.all_gather(key_value, "seq", axis=0, tiled=True))
    denominator = final_state[1]
    numerator = final_state[2]
    attended = (
        (numerator / denominator.T[:, :, None])
        .astype(jnp.bfloat16)
        .reshape(token_count, model_width)
    )
    encoded = (
        layer_input.astype(jnp.float32)
        + jnp.dot(attended, output_weight, preferred_element_type=jnp.float32)
    ).astype(jnp.bfloat16)
    position = lax.axis_index("seq")
    half_rows = token_count // GZ
    input_grid = layer_input.reshape(1, half_rows, GZ, model_width)
    encoded_grid = encoded.reshape(1, half_rows, GZ, model_width)
    joined = jnp.concatenate(
        [upsample(encoded_grid, deep_weight), upsample(input_grid, skip_weight)], axis=-1
    )
    lower_half = position % 2 == 0
    boundary = jnp.where(lower_half, joined[:, -1:], joined[:, :1])
    partner = swapped(boundary, "seq", 0)
    zero_plane = jnp.zeros_like(partner)
    low_rim = jnp.where(lower_half, zero_plane, partner)
    high_rim = jnp.where(lower_half, partner, zero_plane)
    extended = jnp.concatenate([low_rim, joined, high_rim], axis=1)
    full_xy = jnp.concatenate(
        [plane_send(extended[-1:], 2), extended, plane_send(extended[:1], -2)], axis=0
    )
    decoded = convolve(full_xy, conv_kernel)[None]
    return (encoded, decoded)


def solution(mesh):
    return jax.shard_map(
        body,
        mesh=mesh,
        in_specs=(P(("groups", "seq"), None), P(), P(), P(), P(), P(), P()),
        out_specs=(P(("groups", "seq"), None), P(("groups", "seq"), None, None, None, None)),
        check_vma=False,
    )
```

profile of v0, /device:TPU:0, one launch (start us, length us, event | category | flops | bytes accessed | tf_op | source)
XLA Modules:
  0.0 156.4 jit_solution(16506574645892172306)
XLA Ops:
  7.2 0.0 copy-start
  7.2 0.0 all-gather.2.cloned.1.call-start
  7.2 0.8 convert_element_type.33
  8.1 1.2 convert_reduce_fusion
  9.3 1.1 fusion.29
  10.4 0.0 copy-done
  10.4 1.6 %convolution_convert_fusion = bf16[128,2304]{1,0:T(8,128)(2,1)S(1)} fusion(bf16[768,2304]{1,0:T(8,128)(2,1)S(1)} %copy-done, bf16[128,768]{1,0:T(8,128)(2,1)} %param.7, f32[768]{0:T(1024)S(1)} %convert_element_type.33, f32[128]{0:T(128)S(1)} %add_rsqrt_fusion, f32[128]{0:T(128)S(1)} %broadcast_multiply_fusion), kind=kOutput, calls=%fused_computation.7 | convolution fusion | flops 453771264 | bytes 4329472 | tf_op jit(solution)/shard_map/dot_general | solution.py:85
  12.1 0.0 copy-start.6
  12.1 0.8 copy-done.6
  12.9 0.8 slice.160
  13.7 0.0 all-gather.2.cloned.1.call-update
  13.7 1.6 %slice.159 = bf16[128,768]{1,0:T(8,128)(2,1)} slice(bf16[128,2304]{1,0:T(8,128)(2,1)} %copy-done.6), slice={[0:128], [0:768]} | slice | bytes 393216 | tf_op jit(solution)/shard_map/slice | solution.py:86
  15.3 1.7 %copy.13 = bf16[128,768]{0,1:T(8,128)(2,1)} copy(bf16[128,768]{1,0:T(8,128)(2,1)} %slice.159) | data formatting | bytes 393216 | tf_op jit(solution)/shard_map/slice | solution.py:86
  17.0 2.2 %convolution_convert_fusion.1 = bf16[128,512]{1,0:T(8,128)(2,1)} fusion(bf16[128,768]{1,0:T(8,128)(2,1)} %param.7, bf16[768,512]{1,0:T(8,128)(2,1)} %param.12), kind=kOutput, calls=%fused_computation.15 | convolution fusion | flops 100728832 | bytes 1114112 | tf_op jit(solution)/shard_map/dot_general | solution.py:43
  19.2 1.8 %reshape_reshape.7 = bf16[1,16,8,2,2,2,64]{6,5,4,3,2,1,0:T(2,128)(2,1)} reshape(bf16[128,512]{1,0:T(8,128)(2,1)} %convolution_convert_fusion.1) | data formatting | bytes 262144 | tf_op jit(solution)/shard_map/reshape;reshape | solution.py:36
  21.0 1.8 %copy.17 = bf16[1,16,8,2,2,2,64]{6,5,2,4,1,3,0:T(2,128)(2,1)} copy(bf16[1,16,8,2,2,2,64]{6,5,4,3,2,1,0:T(2,128)(2,1)} %reshape_reshape.7) | data formatting | bytes 262144 | tf_op jit(solution)/shard_map/reshape;reshape | solution.py:36
  22.9 55.1 %all-gather.2.cloned.1.call-done = bf16[2048,1536]{1,0:T(8,128)(2,1)} async-done(((bf16[128,1536]{1,0:T(8,128)(2,1)}), bf16[2048,1536]{1,0:T(8,128)(2,1)}) %all-gather.2.cloned.1.call-update) | async-done | bytes 6291472 | tf_op jit(solution)/shard_map/all_gather | solution.py:123
  78.0 5.9 %fusion.39 = (bf16[2048,768]{1,0:T(8,128)(2,1)}, bf16[2048,768]{1,0:T(8,128)(2,1)}) fusion(bf16[2048,1536]{1,0:T(8,128)(2,1)} %all-gather.2.cloned.1.call-done), kind=kLoop, calls=%fused_computation.57 | loop fusion | bytes 12582912 | tf_op jit(solution)/shard_map/slice | solution.py:116
  83.9 4.7 %copy.15 = bf16[2048,768]{0,1:T(8,128)(2,1)} copy(bf16[2048,768]{1,0:T(8,128)(2,1)} %get-tuple-element.5) | data formatting | bytes 6291456 | tf_op jit(solution)/shard_map/slice | solution.py:116
  88.6 4.7 %copy.14 = bf16[2048,768]{0,1:T(8,128)(2,1)} copy(bf16[2048,768]{1,0:T(8,128)(2,1)} %get-tuple-element.4) | data formatting | bytes 6291456 | tf_op jit(solution)/shard_map/slice | solution.py:116
  93.3 3.9 %multiply_reduce_fusion = (f32[12,128]{1,0:T(8,128)S(1)}, f32[12,128,2048]{2,1,0:T(8,128)S(1)}) fusion(bf16[128,12,64]{0,2,1:T(8,128)(2,1)} %bitcast.110, bf16[2048,12,64]{0,2,1:T(8,128)(2,1)} %bitcast.81), kind=kOutput, calls=%fused_computation.1 | convolution fusion | flops 408943104 | bytes 15931392 | tf_op jit(solution)/shard_map/qhd,khd->hqk/dot_general | solution.py:94
  97.2 0.0 copy-start.4
  97.2 2.5 %fusion = f32[12,128]{1,0:T(8,128)S(1)} fusion(f32[12,128,2048]{2,1,0:T(8,128)S(1)} %get-tuple-element.41, f32[12,128]{1,0:T(8,128)S(1)} %get-tuple-element.39), kind=kLoop, calls=%fused_computation.2 | loop fusion | flops 9435648 | bytes 12595200 | tf_op jit(solution)/shard_map/reduce_sum | solution.py:100
  99.7 0.0 copy-done.4
  99.7 0.0 copy-start.5
  99.7 0.0 copy-start.7
  99.8 0.0 copy-start.8
  99.8 3.0 %fusion.17 = bf16[128,12,64]{0,2,1:T(8,128)(2,1)S(1)} fusion(bf16[2048,12,64]{0,2,1:T(8,128)(2,1)S(1)} %bitcast.82, f32[12,128,2048]{2,1,0:T(8,128)S(1)} %get-tuple-element.41, f32[12,128]{1,0:T(8,128)S(1)} %get-tuple-element.39, f32[128,12]{0,1:T(8,128)S(1)} %bitcast_add_fusion, f32[128,12]{0,1:T(8,128)S(1)} %get-tuple-element.38), kind=kOutput, calls=%fused_computation.18 | convolution fusion | flops 412385280 | bytes 15943680 | tf_op jit(solution)/shard_map/hqk,khd->qhd/dot_general | solution.py:102
  102.8 0.0 copy-done.5
  102.8 0.0 copy-done.7
  102.8 0.4 fusion.13
  103.1 0.0 copy-start.9
  103.2 0.7 copy-done.9
  103.8 0.0 copy-done.8
  103.8 0.9 convolution_convert_fusion.2
  104.8 1.8 %reshape_reshape.6 = bf16[1,16,8,2,2,2,64]{6,5,4,3,2,1,0:T(2,128)(2,1)} reshape(bf16[128,512]{1,0:T(8,128)(2,1)} %convolution_convert_fusion.2) | data formatting | bytes 262144 | tf_op jit(solution)/shard_map/reshape;reshape | solution.py:36
  106.6 1.1 copy.16
  107.7 0.0 copy-start.2
  107.7 0.9 fusion.37
  108.6 0.3 collective-permute-start
  108.9 0.9 collective-permute-done
  109.8 0.0 copy-done.2
  109.8 1.1 pad_maximum_fusion.1
  110.9 0.7 fusion.43
  111.6 1.3 collective-permute-start.2
  112.9 5.2 %collective-permute-start.1 = (bf16[1,34,16,128]{3,2,1,0:T(8,128)(2,1)}, bf16[1,34,16,128]{3,2,1,0:T(8,128)(2,1)}, u32[]{:S(2)}, u32[]{:S(2)}) collective-permute-start(bf16[1,34,16,128]{3,2,1,0:T(8,128)(2,1)} %get-tuple-element.34), channel_id=1, source_target_pairs={{0,2},{1,3},{2,4},{3,5},{4,6},{5,7},{6,8},{7,9},{8,10},{9,11},{10,... | collective-permute-start | bytes 417800 | tf_op jit(solution)/shard_map/ppermute | solution.py:19
  118.1 2.2 %copy.18 = bf16[3,3,3,128,64]{3,2,1,0,4:T(4,128)(2,1)} copy(bf16[3,3,3,128,64]{3,4,2,1,0:T(8,128)(2,1)} %param.13) | data formatting | bytes 884736 | tf_op args[6]
  120.4 2.1 %reshape.80 = bf16[3456,64]{0,1:T(8,128)(2,1)} reshape(bf16[3,3,3,128,64]{3,2,1,0,4:T(4,128)(2,1)} %copy.18) | data formatting | bytes 884736 | tf_op jit(solution)/shard_map/reshape | solution.py:69
  122.5 2.4 %pad_maximum_fusion.2 = (bf16[2,32,16,128]{3,2,1,0:T(8,128)(2,1)}, bf16[2,32,16,128]{3,2,1,0:T(8,128)(2,1)}) fusion(bf16[2,1,16,128]{3,2,1,0:T(8,128)(2,1)S(1)} %get-tuple-element.37, bf16[2,32,16,64]{3,2,1,0:T(8,128)(2,1)} %bitcast.71, bf16[2,32,16,64]{3,2,1,0:T(8,128)(2,1)} %bitcast.77, bf16[2,1,16,128]{3,2,1,0:T(8,128)(2,1)S(1)} %get-tuple-element.36), kind=kLoop, calls=%fused_computation.40 | loop fusion | flops 1572864 | bytes 802816 | tf_op jit(solution)/shard_map/concatenate | solution.py:148
  124.9 0.0 collective-permute-done.2
  124.9 0.0 collective-permute-done.1
  124.9 1.8 %select_maximum_fusion = bf16[4,34,18,128]{3,2,1,0:T(8,128)(2,1)S(1)} fusion(bf16[1,34,16,128]{3,2,1,0:T(8,128)(2,1)} %collective-permute-done.2, bf16[1,34,16,128]{3,2,1,0:T(8,128)(2,1)} %collective-permute-done.1, bf16[2,1,16,128]{3,2,1,0:T(8,128)(2,1)S(1)} %get-tuple-element.37, bf16[2,1,16,128]{3,2,1,0:T(8,128)(2,1)S(1)} %get-tuple-element.36, ...), kind=kLoop, calls=%fused_computation.19 | loop fusion | flops 6580224 | bytes 1183744 | tf_op jit(solution)/shard_map/concatenate | solution.py:149
  126.7 0.0 copy-start.1
  126.7 0.0 copy-start.3
  126.7 2.2 %fusion.40 = (bf16[2,32,16,128]{3,2,1,0:T(8,128)(2,1)}, bf16[2,32,16,128]{3,2,1,0:T(8,128)(2,1)}, bf16[2,32,16,128]{3,2,1,0:T(8,128)(2,1)}, bf16[2,32,16,128]{3,...) fusion(bf16[4,34,18,128]{3,2,1,0:T(8,128)(2,1)S(1)} %select_max, ...), kind=kLoop, calls=%fused_computation.58 | loop fusion | bytes 9437184 | tf_op jit(solution)/shard_map/slice | solution.py:58
  128.9 0.0 copy-done.1
  128.9 0.0 copy-done.3
  128.9 1.2 pad_maximum_fusion
  130.1 1.2 fusion.41
  131.3 10.6 %concatenate.121 = bf16[1024,3456]{1,0:T(8,128)(2,1)} concatenate(bf16[1024,128]{1,0:T(8,128)(2,1)} %bitcast.100, bf16[1024,128]{1,0:T(8,128)(2,1)} %bitcast.104, bf16[1024,128]{1,0:T(8,128)(2,1)} %bitcast.99, bf16[1024,128]{1,0:T(8,128)(2,1)} %bitcast.98, bf16[1024,128]{1,0:T(8,128)(2,1)} %bitcast.105, bf16[1024,128]{1,0:T(8,128)(2,1)} %bitcast.97, bf16[1024,128]{1,0:T(8,128)(2,1)} %bitcast.96, ...), dimensions={1} | concatenate | bytes 14155776 | tf_op jit(solution)/shard_map/concatenate | solution.py:65
  141.9 5.9 %fusion.32 = bf16[1024,64]{0,1:T(8,128)(2,1)} fusion(bf16[1024,3456]{1,0:T(8,128)(2,1)} %concatenate.121, bf16[3456,64]{0,1:T(8,128)(2,1)} %reshape.80), kind=kOutput, calls=%fused_computation.39 | convolution fusion | flops 453246976 | bytes 7651328 | tf_op jit(solution)/shard_map/dot_general | solution.py:67
  147.9 1.7 %copy.19 = bf16[1024,64]{1,0:T(8,128)(2,1)} copy(bf16[1024,64]{0,1:T(8,128)(2,1)} %fusion.32) | data formatting | bytes 262144 | tf_op jit(solution)/shard_map/convert_element_type | solution.py:73
  (5 shorter events, 0.0 us)
Async XLA Ops:
  7.2 3.3 %copy-start = (bf16[768,2304]{1,0:T(8,128)(2,1)S(1)}, bf16[768,2304]{1,0:T(8,128)(2,1)}, u32[]{:S(2)}) copy-start(bf16[768,2304]{1,0:T(8,128)(2,1)} %param.9) | copy-start | bytes 10616836
  7.2 70.8 %all-gather.2.cloned.1.call-start = ((), (), s32[]{:S(2)}) async-start(), calls=%async_computation | async-start | bytes 6684672 | tf_op jit(solution)/shard_map/all_gather | solution.py:123
  12.1 0.8 copy-start.6
  97.2 2.5 %copy-start.4 = (bf16[2048,768]{0,1:T(8,128)(2,1)S(1)}, bf16[2048,768]{0,1:T(8,128)(2,1)}, u32[]{:S(2)}) copy-start(bf16[2048,768]{0,1:T(8,128)(2,1)} %copy.15) | copy-start | bytes 9437188
  99.7 3.0 %copy-start.5 = (bf16[128,768]{1,0:T(8,128)(2,1)S(1)}, bf16[128,768]{1,0:T(8,128)(2,1)}, u32[]{:S(2)}) copy-start(bf16[128,768]{1,0:T(8,128)(2,1)} %param.7) | copy-start | bytes 589828
  99.7 3.0 %copy-start.7 = (bf16[768,768]{1,0:T(8,128)(2,1)S(1)}, bf16[768,768]{1,0:T(8,128)(2,1)}, u32[]{:S(2)}) copy-start(bf16[768,768]{1,0:T(8,128)(2,1)} %param.10) | copy-start | bytes 3538948
  99.8 4.1 %copy-start.8 = (bf16[768,512]{1,0:T(8,128)(2,1)S(1)}, bf16[768,512]{1,0:T(8,128)(2,1)}, u32[]{:S(2)}) copy-start(bf16[768,512]{1,0:T(8,128)(2,1)} %param.11) | copy-start | bytes 2359300
  103.1 0.7 copy-start.9
  107.7 2.1 %copy-start.2 = (bf16[1,16,8,2,2,2,64]{6,5,2,4,1,3,0:T(2,128)(2,1)}, bf16[1,16,8,2,2,2,64]{6,5,2,4,1,3,0:T(2,128)(2,1)S(1)}, u32[]{:S(2)}) copy-start(bf16[1,16,8,2,2,2,64]{6,5,2,4,1,3,0:T(2,128)(2,1)S(1)} %copy.16) | copy-start | bytes 393220
  108.6 1.2 collective-permute-start
  111.6 13.3 %collective-permute-start.2 = (bf16[1,34,16,128]{3,2,1,0:T(8,128)(2,1)}, bf16[1,34,16,128]{3,2,1,0:T(8,128)(2,1)}, u32[]{:S(2)}, u32[]{:S(2)}) collective-permute-start(bf16[1,34,16,128]{3,2,1,0:T(8,128)(2,1)} %get-tuple-element.35), channel_id=1, source_target_pairs={{2,0},{3,1},{4,2},{5,3},{6,4},{7,5},{8,6},{9,7},{10,8},{11,9},{12,... | collective-permute-start | bytes 417800 | tf_op jit(solution)/shard_map/ppermute | solution.py:19
  112.9 12.0 %collective-permute-start.1 = (bf16[1,34,16,128]{3,2,1,0:T(8,128)(2,1)}, bf16[1,34,16,128]{3,2,1,0:T(8,128)(2,1)}, u32[]{:S(2)}, u32[]{:S(2)}) collective-permute-start(bf16[1,34,16,128]{3,2,1,0:T(8,128)(2,1)} %get-tuple-element.34), channel_id=1, source_target_pairs={{0,2},{1,3},{2,4},{3,5},{4,6},{5,7},{6,8},{7,9},{8,10},{9,11},{10,... | collective-permute-start | bytes 417800 | tf_op jit(solution)/shard_map/ppermute | solution.py:19
  126.7 2.2 %copy-start.1 = (bf16[1,16,8,2,2,2,64]{6,5,2,4,1,3,0:T(2,128)(2,1)S(1)}, bf16[1,16,8,2,2,2,64]{6,5,2,4,1,3,0:T(2,128)(2,1)}, u32[]{:S(2)}) copy-start(bf16[1,16,8,2,2,2,64]{6,5,2,4,1,3,0:T(2,128)(2,1)} %copy.17) | copy-start | bytes 393220
  126.7 2.2 %copy-start.3 = (bf16[1,16,8,2,2,2,64]{6,5,2,4,1,3,0:T(2,128)(2,1)S(1)}, bf16[1,16,8,2,2,2,64]{6,5,2,4,1,3,0:T(2,128)(2,1)}, u32[]{:S(2)}) copy-start(bf16[1,16,8,2,2,2,64]{6,5,2,4,1,3,0:T(2,128)(2,1)} %copy-done.2) | copy-start | bytes 393220
Sparse Core Ops, SparseCore 0:
  13.8 64.1 all-gather.1
where the time goes:
time: 158 us; the launch traced here: 156 us
  waiting for transfers between devices  56 us (35%)
  local copies, waits for them, and re-layouts  48.4 us (31%)
  matrix products  17.9 us (11%)
  between operations  14.3 us (9%)
  other arithmetic  13 us (8%)
  starting transfers between devices  6.8 us (4%)
    all_gather x1, waiting for transfers between devices, body(): lax.all_gather(key_value, 'seq', axis=0, tiled=True)  55.1 us
    slice x2, local copies, waits for them, and re-layouts, attend(): pair_rows[:, :model_width]  10.6 us
    concatenate x1, local copies, waits for them, and re-layouts, convolve(): stacked = jnp.concatenate(columns, axis=-1)  10.6 us
    another operation x4, local copies, waits for them, and re-layouts, to_voxels(): shaped = flat_out.reshape(extent_x, extent_y, extent_z, 2, 2, 2, channels)  6.58 us
    ppermute x2, starting transfers between devices, shifted(): return lax.ppermute(block, axis, route)  6.49 us
    dot_general x1, matrix products, convolve(): jnp.dot(stacked.reshape(-1, stacked.shape[-1]), conv_kernel.reshape(-1, c...  5.93 us
    slice x1, local copies, waits for them, and re-layouts, attend(): pair_rows[:, model_width:]  4.69 us
    dot_general x1, matrix products, update(): jnp.einsum('qhd,khd->hqk', queries, key_heads, preferred_element_type=jnp...  3.92 us
  transfers between devices with their start and end apart: 4, of which 2 were waited for; matrix products, arithmetic and copies ran while one was open for 10% of the time, Pallas kernels for 0%

commit v1 on v0

v1 whole, which is shorter than its diff:
```python
import math

import jax
import jax.numpy as jnp
from jax import lax
from jax.experimental import pallas as pl
from jax.sharding import PartitionSpec as P

HEADS = 12
GZ = 8


epsilon = 1e-06
leak_slope = 0.01


def shifted(block, axis, distance):
    devices = range(lax.axis_size(axis))
    route = [(i - distance, i) for i in devices if i - distance in devices]
    return lax.ppermute(block, axis, route)


def swapped(x, axis, distance):
    return lax.ppermute(x, axis, [(i, i ^ 1 << distance) for i in range(lax.axis_size(axis))])


def layer_norm(inputs, gain):
    values32 = inputs.astype(jnp.float32)
    row_mean = jnp.mean(values32, axis=-1, keepdims=True)
    centered = values32 - row_mean
    row_var = jnp.mean(centered * centered, axis=-1, keepdims=True)
    return centered * lax.rsqrt(row_var + epsilon) * gain.astype(jnp.float32)


def to_voxels(flat_out, channels):
    extent_x, extent_y, extent_z = (flat_out.shape[0], flat_out.shape[1], flat_out.shape[2])
    shaped = flat_out.reshape(extent_x, extent_y, extent_z, 2, 2, 2, channels)
    shaped = shaped.transpose(0, 3, 1, 4, 2, 5, 6)
    return shaped.reshape(2 * extent_x, 2 * extent_y, 2 * extent_z, channels)


def upsample(token_grid, weight):
    model_width = token_grid.shape[-1]
    product = jnp.dot(
        token_grid.reshape(-1, model_width), weight, preferred_element_type=jnp.float32
    )
    flat_out = product.astype(jnp.bfloat16).reshape(token_grid.shape[:3] + (weight.shape[1],))
    return to_voxels(flat_out, weight.shape[1] // 8)


def convolve(full_xy, conv_kernel):
    accumulated = lax.conv_general_dilated(
        full_xy[None],
        conv_kernel,
        window_strides=(1, 1, 1),
        padding=((0, 0), (0, 0), (1, 1)),
        dimension_numbers=("NDHWC", "DHWIO", "NDHWC"),
        preferred_element_type=jnp.float32,
    )[0]
    activated = jnp.where(accumulated > 0, accumulated, leak_slope * accumulated)
    return activated.astype(jnp.bfloat16)


def plane_send(plane, offset):
    return shifted(plane, "seq", offset)


def attention_kernel(q_ref, k_ref, v_ref, o_ref, *, head_size, score_scale):
    pair = q_ref.shape[-1]
    lane = lax.broadcasted_iota(jnp.int32, (1, pair), 1)
    q = q_ref[...]
    k = k_ref[...]
    v = v_ref[...]
    result = None
    for h in range(pair // head_size):
        in_head = (lane >= h * head_size) & (lane < (h + 1) * head_size)
        q_h = jnp.where(in_head, q, jnp.zeros_like(q))
        scores = (
            lax.dot_general(q_h, k, (((1,), (1,)), ((), ())), preferred_element_type=jnp.float32)
            * score_scale
        )
        row_max = jnp.max(scores, axis=-1, keepdims=True)
        exp_scores = jnp.exp(scores - row_max)
        denominator = jnp.sum(exp_scores, axis=-1, keepdims=True)
        numerator = jnp.dot(
            exp_scores.astype(jnp.bfloat16), v, preferred_element_type=jnp.float32
        )
        head_out = numerator / denominator
        result = head_out if result is None else jnp.where(in_head, head_out, result)
    o_ref[...] = result.astype(o_ref.dtype)


def attention(queries, key_value, head_size, score_scale):
    token_count, model_width = queries.shape
    total = key_value.shape[0]
    pair = 2 * head_size
    pairs = model_width // pair
    kernel = lambda *refs: attention_kernel(*refs, head_size=head_size, score_scale=score_scale)
    return pl.pallas_call(
        kernel,
        grid=(pairs,),
        in_specs=[
            pl.BlockSpec((token_count, pair), lambda j: (0, j)),
            pl.BlockSpec((total, pair), lambda j: (0, j)),
            pl.BlockSpec((total, pair), lambda j: (0, j + pairs)),
        ],
        out_specs=pl.BlockSpec((token_count, pair), lambda j: (0, j)),
        out_shape=jax.ShapeDtypeStruct((token_count, model_width), jnp.bfloat16),
    )(queries, key_value, key_value)


def body(layer_input, norm_gain, projection, output_weight, deep_weight, skip_weight, conv_kernel):
    token_count, model_width = layer_input.shape
    head_size = model_width // HEADS
    score_scale = 1.0 / math.sqrt(head_size)
    all_input = lax.all_gather(layer_input, "seq", axis=0, tiled=True)
    normed = layer_norm(layer_input, norm_gain).astype(jnp.bfloat16)
    queries = jnp.dot(
        normed, projection[:, :model_width], preferred_element_type=jnp.float32
    ).astype(jnp.bfloat16)
    all_normed = layer_norm(all_input, norm_gain).astype(jnp.bfloat16)
    key_value = jnp.dot(
        all_normed, projection[:, model_width:], preferred_element_type=jnp.float32
    ).astype(jnp.bfloat16)
    attended = attention(queries, key_value, head_size, score_scale)
    encoded = (
        layer_input.astype(jnp.float32)
        + jnp.dot(attended, output_weight, preferred_element_type=jnp.float32)
    ).astype(jnp.bfloat16)
    position = lax.axis_index("seq")
    half_rows = token_count // GZ
    input_grid = layer_input.reshape(1, half_rows, GZ, model_width)
    encoded_grid = encoded.reshape(1, half_rows, GZ, model_width)
    joined = jnp.concatenate(
        [upsample(encoded_grid, deep_weight), upsample(input_grid, skip_weight)], axis=-1
    )
    lower_half = position % 2 == 0
    boundary = jnp.where(lower_half, joined[:, -1:], joined[:, :1])
    partner = swapped(boundary, "seq", 0)
    zero_plane = jnp.zeros_like(partner)
    low_rim = jnp.where(lower_half, zero_plane, partner)
    high_rim = jnp.where(lower_half, partner, zero_plane)
    extended = jnp.concatenate([low_rim, joined, high_rim], axis=1)
    full_xy = jnp.concatenate(
        [plane_send(extended[-1:], 2), extended, plane_send(extended[:1], -2)], axis=0
    )
    decoded = convolve(full_xy, conv_kernel)[None]
    return (encoded, decoded)


def solution(mesh):
    return jax.shard_map(
        body,
        mesh=mesh,
        in_specs=(P(("groups", "seq"), None), P(), P(), P(), P(), P(), P()),
        out_specs=(P(("groups", "seq"), None), P(("groups", "seq"), None, None, None, None)),
        check_vma=False,
    )
```

time: 158 us -> 107 us (0.68)
  local copies, waits for them, and re-layouts: 48.4 us -> 2.92 us
  Pallas kernels: 0 us -> 9.7 us
  other arithmetic: 13 us -> 6.87 us
  waiting for transfers between devices: 56 us -> 51.7 us
  starting transfers between devices: 6.8 us -> 4.01 us
    slice x8 -> x0, local copies, waits for them, and re-layouts: 22.9 us -> none  [the longest x2 10.6 us: attend(): pair_rows[:, :model_width]]
    all_gather x1, waiting for transfers between devices: 55.1 us -> 43.3 us  [body(): all_input = lax.all_gather(layer_input, 'seq', axis=0, tiled=True)]
    concatenate x1 -> x0, local copies, waits for them, and re-layouts: 10.6 us -> none  [convolve(): stacked = jnp.concatenate(columns, axis=-1)]
    pallas_call x0 -> x1, Pallas kernels: none -> 9.7 us  [attention(): pl.pallas_call(kernel, grid=(pairs,), in_specs=[pl.BlockSpec((token_count...]
    ppermute x2, waiting for transfers between devices: 0.01 us -> 6.74 us  [shifted(): return lax.ppermute(block, axis, route)]
    another operation x4, local copies, waits for them, and re-layouts: 6.58 us -> 0.73 us  [to_voxels(): shaped = flat_out.reshape(extent_x, extent_y, extent_z, 2, 2, 2, channels)]
    concatenate x2 -> x1, other arithmetic: 3.53 us -> 0.15 us  [body(): extended = jnp.concatenate([low_rim, joined, high_rim], axis=1)]
    dot_general x4 -> x2, matrix products: 14.5 us -> 11.4 us  [the longest x1 8.91 us: body(): jnp.dot(all_normed, projection[:, model_width:], preferred_element_type=j...]
  transfers between devices with their start and end apart: 4 -> 4, of which waited for: 2 -> 4; matrix products, arithmetic and copies ran while one was open for 10% -> 7% of each run, Pallas kernels for 0% -> 0%
where the time goes in v1:
time: 107 us
  waiting for transfers between devices  51.7 us (48%)
  matrix products  17.3 us (16%)
  between operations  14.3 us (13%)
  Pallas kernels  9.7 us (9%)
  other arithmetic  6.87 us (6%)
  starting transfers between devices  4.01 us (4%)
  local copies, waits for them, and re-layouts  2.92 us (3%)
    all_gather x1, waiting for transfers between devices, body(): all_input = lax.all_gather(layer_input, 'seq', axis=0, tiled=True)  43.3 us
    pallas_call x1, Pallas kernels, attention(): pl.pallas_call(kernel, grid=(pairs,), in_specs=[pl.BlockSpec((token_count...  9.7 us
    dot_general x1, matrix products, body(): jnp.dot(all_normed, projection[:, model_width:], preferred_element_type=j...  8.91 us
    ppermute x2, waiting for transfers between devices, shifted(): return lax.ppermute(block, axis, route)  6.74 us
    ppermute x2, starting transfers between devices, shifted(): return lax.ppermute(block, axis, route)  3.75 us
    reduce_sum x2, other arithmetic, layer_norm(): row_mean = jnp.mean(values32, axis=-1, keepdims=True)  3.56 us
    conv_general_dilated x1, matrix products, convolve(): lax.conv_general_dilated(full_xy[None], conv_kernel, window_strides=(1, 1...  2.91 us
    dot_general x1, matrix products, body(): jnp.dot(normed, projection[:, :model_width], preferred_element_type=jnp.f...  2.44 us
  transfers between devices with their start and end apart: 4, of which 4 were waited for; matrix products, arithmetic and copies ran while one was open for 7% of the time, Pallas kernels for 0%

profile of v1, /device:TPU:0, one launch (start us, length us, event | category | flops | bytes accessed | tf_op | source)
XLA Modules:
  0.0 106.8 jit_solution(4011522263760218131)
XLA Ops:
  7.2 0.0 copy-start
  7.2 0.0 all-gather.2.cloned.1.call-start
  7.2 0.7 all-gather.2.cloned.1.call-update
  7.9 0.7 convert_element_type.37
  8.6 1.5 %convolution_convert_fusion.1 = bf16[128,512]{1,0:T(8,128)(2,1)S(1)} fusion(bf16[128,768]{1,0:T(8,128)(2,1)} %param.7, bf16[768,512]{1,0:T(8,128)(2,1)} %param.12), kind=kOutput, calls=%fused_computation.28 | convolution fusion | flops 100728832 | bytes 1114112 | tf_op jit(solution)/shard_map/dot_general | solution.py:44
  10.1 0.2 reshape_reshape.7
  10.3 0.2 copy.10
  10.5 1.0 convert_reduce_fusion.1
  11.6 1.1 %fusion.35 = f32[128]{0:T(128)S(1)} fusion(bf16[128,768]{1,0:T(8,128)(2,1)} %param.7, f32[128]{0:T(128)S(1)} %broadcast_multiply_fusion.1), kind=kLoop, calls=%fused_computation.36 | loop fusion | flops 393088 | bytes 197632 | tf_op jit(solution)/shard_map/reduce_sum | solution.py:31
  12.7 2.4 %fusion.28.refs_0_ = bf16[128,768]{1,0:T(8,128)(2,1)} fusion(bf16[768,2304]{1,0:T(8,128)(2,1)} %param.9, bf16[128,768]{1,0:T(8,128)(2,1)} %param.7, f32[768]{0:T(1024)S(1)} %convert_element_type.37, f32[128]{0:T(128)S(1)} %add_rsqrt_fusion.1, f32[128]{0:T(128)S(1)} %broadcast_multiply_fusion.1), kind=kOutput, calls=%fused_computation.26 | convolution fusion | flops 151584768 | bytes 1576960 | tf_op jit(solution)/shard_map/dot_general | solution.py:118
  15.1 43.3 %all-gather.2.cloned.1.call-done = bf16[2048,768]{1,0:T(8,128)(2,1)} async-done(((bf16[128,768]{1,0:T(8,128)(2,1)}), bf16[2048,768]{1,0:T(8,128)(2,1)}) %all-gather.2.cloned.1.call-update) | async-done | bytes 3145744 | tf_op jit(solution)/shard_map/all_gather | solution.py:116
  58.5 0.0 copy-start.1
  58.5 2.5 %convert_reduce_fusion = f32[2048]{0:T(1024)S(1)} fusion(bf16[2048,768]{1,0:T(8,128)(2,1)} %all-gather.2.cloned.1.call-done), kind=kLoop, calls=%fused_computation.1 | loop fusion | flops 3143680 | bytes 3153920 | tf_op jit(solution)/shard_map/reduce_sum | solution.py:29
  61.0 0.3 copy-done.1
  61.3 1.1 %fusion.2 = f32[2048]{0:T(1024)S(1)} fusion(bf16[2048,768]{1,0:T(8,128)(2,1)S(1)} %copy-done.1, f32[2048]{0:T(1024)S(1)} %broadcast_multiply_fusion), kind=kLoop, calls=%fused_computation.5 | loop fusion | flops 6289408 | bytes 3162112 | tf_op jit(solution)/shard_map/reduce_sum | solution.py:31
  62.4 8.9 %convolution_convert_fusion.refs_1_.refs_2_ = bf16[2048,1536]{1,0:T(8,128)(2,1)} fusion(bf16[2048,768]{1,0:T(8,128)(2,1)S(1)} %copy-done.1, f32[768]{0:T(1024)S(1)} %convert_element_type.37, f32[2048]{0:T(1024)S(1)} %add_rsqrt_fusion, f32[2048]{0:T(1024)S(1)} %broadcast_multiply_fusion, bf16[768,2304]{1,0:T(8,128)(2,1)} %param.9), kind=kOutput, calls=%fused_computation.2 | convolution fusion | flops 4842848256 | bytes 11815936 | tf_op jit(solution)/shard_map/dot_general | solution.py:122
  71.3 0.0 copy-start.2
  71.3 0.0 copy-start.3
  71.3 9.7 %shard_map.86 = bf16[128,768]{1,0:T(8,128)(2,1)} custom-call(bf16[128,768]{1,0:T(8,128)(2,1)} %fusion.28.refs_0_, bf16[2048,1536]{1,0:T(8,128)(2,1)} %convolution_convert_fusion.refs_1_.refs_2_, bf16[2048,1536]{1,0:T(8,128)(2,1)} %convolution_convert_fusion.refs_1_.refs_2_), custom_call_target="tpu_custom_call" | custom-call | tf_op jit(solution)/shard_map/pallas_call | solution.py:99
  81.0 0.0 copy-done
  81.0 0.0 copy-done.2
  81.0 1.3 %fusion.31 = bf16[128,768]{1,0:T(8,128)(2,1)S(1)} fusion(bf16[128,768]{1,0:T(8,128)(2,1)} %shard_map.86, bf16[768,768]{1,0:T(8,128)(2,1)S(1)} %copy-done, bf16[128,768]{1,0:T(8,128)(2,1)S(1)} %copy-done.2), kind=kOutput, calls=%fused_computation.27 | convolution fusion | flops 151289856 | bytes 1769472 | tf_op jit(solution)/shard_map/dot_general | solution.py:128
  82.3 0.0 copy-done.3
  82.3 0.0 copy-start.4
  82.3 0.3 convolution_convert_fusion.2
  82.6 0.2 reshape_reshape.6
  82.8 0.2 copy.9
  83.0 0.1 fusion.42
  83.1 0.2 collective-permute-start
  83.3 1.0 collective-permute-done
  84.2 0.1 pad_maximum_fusion
  84.4 2.5 %collective-permute-start.1 = (bf16[1,34,16,128]{3,2,1,0:T(8,128)(2,1)S(1)}, bf16[1,34,16,128]{3,2,1,0:T(8,128)(2,1)S(1)}, u32[]{:S(2)}, u32[]{:S(2)}) collective-permute-start(bf16[1,34,16,128]{3,2,1,0:T(8,128)(2,1)S(1)} %get-tuple-element.4), channel_id=1, source_target_pairs={{0,2},{1,3},{2,4},{3,5},{4,6},{5,7},{6,8},{7,9},{8,10},{9,11},{10,... | collective-permute-start | bytes 417800 | tf_op jit(solution)/shard_map/ppermute | solution.py:20
  86.9 1.3 %collective-permute-start.2 = (bf16[1,34,16,128]{3,2,1,0:T(8,128)(2,1)S(1)}, bf16[1,34,16,128]{3,2,1,0:T(8,128)(2,1)S(1)}, u32[]{:S(2)}, u32[]{:S(2)}) collective-permute-start(bf16[1,34,16,128]{3,2,1,0:T(8,128)(2,1)S(1)} %get-tuple-element.5), channel_id=1, source_target_pairs={{2,0},{3,1},{4,2},{5,3},{6,4},{7,5},{8,6},{9,7},{10,8},{11,9},{12,... | collective-permute-start | bytes 417800 | tf_op jit(solution)/shard_map/ppermute | solution.py:20
  88.2 2.0 %collective-permute-done.1 = bf16[1,34,16,128]{3,2,1,0:T(8,128)(2,1)S(1)} collective-permute-done((bf16[1,34,16,128]{3,2,1,0:T(8,128)(2,1)S(1)}, bf16[1,34,16,128]{3,2,1,0:T(8,128)(2,1)S(1)}, u32[]{:S(2)}, u32[]{:S(2)}) %collective-permute-start.1) | collective-permute-done | bytes 139296 | tf_op jit(solution)/shard_map/ppermute | solution.py:20
  90.2 4.7 %collective-permute-done.2 = bf16[1,34,16,128]{3,2,1,0:T(8,128)(2,1)S(1)} collective-permute-done((bf16[1,34,16,128]{3,2,1,0:T(8,128)(2,1)S(1)}, bf16[1,34,16,128]{3,2,1,0:T(8,128)(2,1)S(1)}, u32[]{:S(2)}, u32[]{:S(2)}) %collective-permute-start.2) | collective-permute-done | bytes 139296 | tf_op jit(solution)/shard_map/ppermute | solution.py:20
  94.9 0.2 maximum_bitcast_fusion
  95.1 0.0 copy-start.5
  95.1 0.0 copy-start.6
  95.1 0.3 copy.16
  95.4 0.0 copy-done.4
  95.4 0.3 pad.clone
  95.7 0.1 copy.13
  95.8 0.1 slice.28
  96.0 0.1 copy-done.5
  96.1 0.0 copy-done.6
  96.1 2.9 %fusion.23 = bf16[2,32,8,3,64]{4,2,3,1,0:T(8,128)(2,1)S(1)} fusion(bf16[3,3,3,128,64]{3,4,2,1,0:T(8,128)(2,1)S(1)} %copy-done.5, bf16[4,34,1,7,2,128]{5,3,4,1,0,2:T(8,128)(2,1)S(1)} %slice.28, bf16[4,34,1,8,3,128]{5,3,4,1,0,2:T(8,128)(2,1)S(1)} %copy.13, pred[8,3]{0,1:T(4,128)(4,1)S(1)} %copy-done.6), kind=kOutput, calls=%fused_computation.23 | convolution fusion | flops 684146688 | bytes 1962008 | tf_op jit(solution)/shard_map/conv_general_dilated | solution.py:52
  99.0 0.1 copy.14
  99.1 0.8 copy.15
  (7 shorter events, 0.1 us)
Async XLA Ops:
  7.2 73.9 %copy-start = (bf16[768,768]{1,0:T(8,128)(2,1)S(1)}, bf16[768,768]{1,0:T(8,128)(2,1)}, u32[]{:S(2)}) copy-start(bf16[768,768]{1,0:T(8,128)(2,1)} %param.10) | copy-start | bytes 3538948
  7.2 51.3 %all-gather.2.cloned.1.call-start = ((), (), s32[]{:S(2)}) async-start(), calls=%async_computation | async-start | bytes 3342336 | tf_op jit(solution)/shard_map/all_gather | solution.py:116
  58.5 2.8 %copy-start.1 = (bf16[2048,768]{1,0:T(8,128)(2,1)S(1)}, bf16[2048,768]{1,0:T(8,128)(2,1)}, u32[]{:S(2)}) copy-start(bf16[2048,768]{1,0:T(8,128)(2,1)} %all-gather.2.cloned.1.call-done) | copy-start | bytes 9437188
  71.3 9.7 %copy-start.2 = (bf16[128,768]{1,0:T(8,128)(2,1)S(1)}, bf16[128,768]{1,0:T(8,128)(2,1)}, u32[]{:S(2)}) copy-start(bf16[128,768]{1,0:T(8,128)(2,1)} %param.7) | copy-start | bytes 589828
  71.3 11.0 %copy-start.3 = (bf16[768,512]{1,0:T(8,128)(2,1)S(1)}, bf16[768,512]{1,0:T(8,128)(2,1)}, u32[]{:S(2)}) copy-start(bf16[768,512]{1,0:T(8,128)(2,1)} %param.11) | copy-start | bytes 2359300
  82.3 13.1 %copy-start.4 = (bf16[128,768]{1,0:T(8,128)(2,1)}, bf16[128,768]{1,0:T(8,128)(2,1)S(1)}, u32[]{:S(2)}) copy-start(bf16[128,768]{1,0:T(8,128)(2,1)S(1)} %fusion.31) | copy-start | bytes 589828
  83.1 1.2 %collective-permute-start = (bf16[2,1,16,128]{3,2,1,0:T(8,128)(2,1)S(1)}, bf16[2,1,16,128]{3,2,1,0:T(8,128)(2,1)S(1)}, u32[]{:S(2)}, u32[]{:S(2)}) collective-permute-start(bf16[2,1,16,128]{3,2,1,0:T(8,128)(2,1)S(1)} %fusion.42), channel_id=1, source_target_pairs={{0,1},{1,0},{2,3},{3,2},{4,5},{5,4},{6,7},{7,6},{8,9},{9,8},{10,11... | collective-permute-start | bytes 24584 | tf_op jit(solution)/shard_map/ppermute | solution.py:24
  84.4 5.8 %collective-permute-start.1 = (bf16[1,34,16,128]{3,2,1,0:T(8,128)(2,1)S(1)}, bf16[1,34,16,128]{3,2,1,0:T(8,128)(2,1)S(1)}, u32[]{:S(2)}, u32[]{:S(2)}) collective-permute-start(bf16[1,34,16,128]{3,2,1,0:T(8,128)(2,1)S(1)} %get-tuple-element.4), channel_id=1, source_target_pairs={{0,2},{1,3},{2,4},{3,5},{4,6},{5,7},{6,8},{7,9},{8,10},{9,11},{10,... | collective-permute-start | bytes 417800 | tf_op jit(solution)/shard_map/ppermute | solution.py:20
  86.9 8.0 %collective-permute-start.2 = (bf16[1,34,16,128]{3,2,1,0:T(8,128)(2,1)S(1)}, bf16[1,34,16,128]{3,2,1,0:T(8,128)(2,1)S(1)}, u32[]{:S(2)}, u32[]{:S(2)}) collective-permute-start(bf16[1,34,16,128]{3,2,1,0:T(8,128)(2,1)S(1)} %get-tuple-element.5), channel_id=1, source_target_pairs={{2,0},{3,1},{4,2},{5,3},{6,4},{7,5},{8,6},{9,7},{10,8},{11,9},{12,... | collective-permute-start | bytes 417800 | tf_op jit(solution)/shard_map/ppermute | solution.py:20
  95.1 1.0 copy-start.5
  95.1 1.0 copy-start.6
Sparse Core Ops, SparseCore 0:
  10.3 48.1 all-gather.1

commit v2 on v1

--- a/solution.py
+++ b/solution.py
@@ -65,64 +65,88 @@
     return shifted(plane, "seq", offset)
 
 
-def attention_kernel(q_ref, k_ref, v_ref, o_ref, *, head_size, score_scale):
+def attention_kernel(*refs, head_size, score_scale, chunks):
+    q_ref = refs[0]
+    k_refs = refs[1 : 1 + chunks]
+    v_refs = refs[1 + chunks : 1 + 2 * chunks]
+    o_ref = refs[-1]
     pair = q_ref.shape[-1]
     lane = lax.broadcasted_iota(jnp.int32, (1, pair), 1)
     q = q_ref[...]
-    k = k_ref[...]
-    v = v_ref[...]
     result = None
     for h in range(pair // head_size):
         in_head = (lane >= h * head_size) & (lane < (h + 1) * head_size)
         q_h = jnp.where(in_head, q, jnp.zeros_like(q))
-        scores = (
-            lax.dot_general(q_h, k, (((1,), (1,)), ((), ())), preferred_element_type=jnp.float32)
+        scores = [
+            lax.dot_general(
+                q_h, k_ref[...], (((1,), (1,)), ((), ())), preferred_element_type=jnp.float32
+            )
             * score_scale
-        )
-        row_max = jnp.max(scores, axis=-1, keepdims=True)
-        exp_scores = jnp.exp(scores - row_max)
-        denominator = jnp.sum(exp_scores, axis=-1, keepdims=True)
-        numerator = jnp.dot(
-            exp_scores.astype(jnp.bfloat16), v, preferred_element_type=jnp.float32
-        )
+            for k_ref in k_refs
+        ]
+        row_max = scores[0].max(axis=-1, keepdims=True)
+        for block in scores[1:]:
+            row_max = jnp.maximum(row_max, block.max(axis=-1, keepdims=True))
+        denominator = None
+        numerator = None
+        for block, v_ref in zip(scores, v_refs):
+            exp_scores = jnp.exp(block - row_max)
+            part_sum = jnp.sum(exp_scores, axis=-1, keepdims=True)
+            part = jnp.dot(
+                exp_scores.astype(jnp.bfloat16), v_ref[...], preferred_element_type=jnp.float32
+            )
+            denominator = part_sum if denominator is None else denominator + part_sum
+            numerator = part if numerator is None else numerator + part
         head_out = numerator / denominator
         result = head_out if result is None else jnp.where(in_head, head_out, result)
     o_ref[...] = result.astype(o_ref.dtype)
 
 
-def attention(queries, key_value, head_size, score_scale):
+def attention(queries, kv_chunks, head_size, score_scale):
     token_count, model_width = queries.shape
-    total = key_value.shape[0]
     pair = 2 * head_size
     pairs = model_width // pair
-    kernel = lambda *refs: attention_kernel(*refs, head_size=head_size, score_scale=score_scale)
+    chunks = len(kv_chunks)
+    kernel = lambda *refs: attention_kernel(
+        *refs, head_size=head_size, score_scale=score_scale, chunks=chunks
+    )
+    key_specs = [pl.BlockSpec((c.shape[0], pair), lambda j: (0, j)) for c in kv_chunks]
+    value_specs = [pl.BlockSpec((c.shape[0], pair), lambda j: (0, j + pairs)) for c in kv_chunks]
     return pl.pallas_call(
         kernel,
         grid=(pairs,),
-        in_specs=[
-            pl.BlockSpec((token_count, pair), lambda j: (0, j)),
-            pl.BlockSpec((total, pair), lambda j: (0, j)),
-            pl.BlockSpec((total, pair), lambda j: (0, j + pairs)),
-        ],
+        in_specs=[pl.BlockSpec((token_count, pair), lambda j: (0, j))] + key_specs + value_specs,
         out_specs=pl.BlockSpec((token_count, pair), lambda j: (0, j)),
         out_shape=jax.ShapeDtypeStruct((token_count, model_width), jnp.bfloat16),
-    )(queries, key_value, key_value)
+    )(queries, *kv_chunks, *kv_chunks)
+
+
+def gathered_rows(rows):
+    devices = lax.axis_size("seq")
+    local = [rows]
+    for distance in range(2, devices, 2):
+        local.append(lax.ppermute(rows, "seq", [(i, (i + distance) % devices) for i in range(devices)]))
+    partner = [lax.ppermute(c, "seq", [(i, i ^ 1) for i in range(devices)]) for c in local]
+    return local + partner
 
 
 def body(layer_input, norm_gain, projection, output_weight, deep_weight, skip_weight, conv_kernel):
     token_count, model_width = layer_input.shape
     head_size = model_width // HEADS
     score_scale = 1.0 / math.sqrt(head_size)
-    all_input = lax.all_gather(layer_input, "seq", axis=0, tiled=True)
+    chunks = gathered_rows(layer_input)
     normed = layer_norm(layer_input, norm_gain).astype(jnp.bfloat16)
     queries = jnp.dot(
         normed, projection[:, :model_width], preferred_element_type=jnp.float32
     ).astype(jnp.bfloat16)
-    all_normed = layer_norm(all_input, norm_gain).astype(jnp.bfloat16)
-    key_value = jnp.dot(
-        all_normed, projection[:, model_width:], preferred_element_type=jnp.float32
-    ).astype(jnp.bfloat16)
-    attended = attention(queries, key_value, head_size, score_scale)
+    kv_weight = projection[:, model_width:]
+    kv_chunks = [jnp.dot(normed, kv_weight, preferred_element_type=jnp.float32).astype(jnp.bfloat16)]
+    for chunk in chunks[1:]:
+        chunk_normed = layer_norm(chunk, norm_gain).astype(jnp.bfloat16)
+        kv_chunks.append(
+            jnp.dot(chunk_normed, kv_weight, preferred_element_type=jnp.float32).astype(jnp.bfloat16)
+        )
+    attended = attention(queries, kv_chunks, head_size, score_scale)
     encoded = (
         layer_input.astype(jnp.float32)
         + jnp.dot(attended, output_weight, preferred_element_type=jnp.float32)

time: 107 us -> 106 us (level)
  waiting for transfers between devices: 51.7 us -> 27.2 us
  starting transfers between devices: 4.01 us -> 23.2 us
  between operations: 14.3 us -> 1.23 us
  matrix products: 17.3 us -> 29.5 us
  Pallas kernels: 9.7 us -> 13.2 us
  other arithmetic: 6.87 us -> 8.16 us
    all_gather x1 -> x0, waiting for transfers between devices: 43.3 us -> none  [body(): all_input = lax.all_gather(layer_input, 'seq', axis=0, tiled=True)]
    ppermute x0 -> x15, starting transfers between devices: none -> 20.1 us  [the longest x7 18.3 us: gathered_rows(): lax.ppermute(rows, 'seq', [(i, (i + distance) % devices) for i in range(d...]
    ppermute x0 -> x15, waiting for transfers between devices: none -> 19.9 us  [the longest x7 19.9 us: gathered_rows(): lax.ppermute(rows, 'seq', [(i, (i + distance) % devices) for i in range(d...]
    dot_general x1 -> x16, matrix products: 8.91 us -> 22.5 us  [the longest x15 19.4 us: body(): jnp.dot(chunk_normed, kv_weight, preferred_element_type=jnp.float32)]
    pallas_call x1, Pallas kernels: 9.7 us -> 13.2 us  [attention(): pl.pallas_call(kernel, grid=(pairs,), in_specs=[pl.BlockSpec((token_count...]
    reduce_sum x2 -> x16, other arithmetic: 2.21 us -> 4.14 us  [layer_norm(): row_var = jnp.mean(centered * centered, axis=-1, keepdims=True)]
    dot_general x1, matrix products: 2.44 us -> 1.04 us  [body(): jnp.dot(normed, projection[:, :model_width], preferred_element_type=jnp.f...]
    ppermute x2, starting transfers between devices: 3.75 us -> 2.59 us  [shifted(): return lax.ppermute(block, axis, route)]
  transfers between devices with their start and end apart: 4 -> 18, of which waited for: 4 -> 6; matrix products, arithmetic and copies ran while one was open for 7% -> 22% of each run, Pallas kernels for 0% -> 0%
where the time goes in v2:
time: 106 us; the launch traced here: 105 us
  matrix products  29.5 us (28%)
  waiting for transfers between devices  27.2 us (26%)
  starting transfers between devices  23.2 us (22%)
  Pallas kernels  13.2 us (12%)
  other arithmetic  8.16 us (8%)
  local copies, waits for them, and re-layouts  2.93 us (3%)
  between operations  1.23 us (1%)
    ppermute x7, waiting for transfers between devices, gathered_rows(): lax.ppermute(rows, 'seq', [(i, (i + distance) % devices) for i in range(d...  19.9 us
    dot_general x15, matrix products, body(): jnp.dot(chunk_normed, kv_weight, preferred_element_type=jnp.float32)  19.4 us
    ppermute x7, starting transfers between devices, gathered_rows(): lax.ppermute(rows, 'seq', [(i, (i + distance) % devices) for i in range(d...  18.3 us
    pallas_call x1, Pallas kernels, attention(): pl.pallas_call(kernel, grid=(pairs,), in_specs=[pl.BlockSpec((token_count...  13.2 us
    ppermute x2, waiting for transfers between devices, shifted(): return lax.ppermute(block, axis, route)  6.52 us
    reduce_sum x16, other arithmetic, layer_norm(): row_var = jnp.mean(centered * centered, axis=-1, keepdims=True)  4.14 us
    dot_general x1, matrix products, body(): jnp.dot(normed, kv_weight, preferred_element_type=jnp.float32)  3.1 us
    conv_general_dilated x1, matrix products, convolve(): lax.conv_general_dilated(full_xy[None], conv_kernel, window_strides=(1, 1...  2.9 us
  transfers between devices with their start and end apart: 18, of which 6 were waited for; matrix products, arithmetic and copies ran while one was open for 22% of the time, Pallas kernels for 0%

profile of v2, /device:TPU:0, one launch (start us, length us, event | category | flops | bytes accessed | tf_op | source)
XLA Modules:
  0.0 105.4 jit_solution(8421356636386023001)
XLA Ops:
  0.7 6.1 %collective-permute-start.6 = (bf16[128,768]{1,0:T(8,128)(2,1)}, bf16[128,768]{1,0:T(8,128)(2,1)S(1)}, u32[]{:S(2)}, u32[]{:S(2)}) collective-permute-start(bf16[128,768]{1,0:T(8,128)(2,1)} %param.7), channel_id=1, source_target_pairs={{0,14},{1,15},{2,0},{3,1},{4,2},{5,3},{6,4},{7,5},{8,6},{9,7},{10,... | collective-permute-start | bytes 589832 | tf_op jit(solution)/shard_map/ppermute | solution.py:128
  6.7 0.4 collective-permute-start.5
  7.2 3.0 %collective-permute-start.3 = (bf16[128,768]{1,0:T(8,128)(2,1)}, bf16[128,768]{1,0:T(8,128)(2,1)S(1)}, u32[]{:S(2)}, u32[]{:S(2)}) collective-permute-start(bf16[128,768]{1,0:T(8,128)(2,1)} %param.7), channel_id=1, source_target_pairs={{0,8},{1,9},{2,10},{3,11},{4,12},{5,13},{6,14},{7,15},{8,0},{9,1},... | collective-permute-start | bytes 589832 | tf_op jit(solution)/shard_map/ppermute | solution.py:128
  10.2 1.1 %convert_reduce_fusion = f32[128]{0:T(128)S(1)} fusion(bf16[128,768]{1,0:T(8,128)(2,1)} %param.7), kind=kLoop, calls=%fused_computation.36 | loop fusion | flops 196480 | bytes 197120 | tf_op jit(solution)/shard_map/reduce_sum | solution.py:29
  11.3 0.7 convert_element_type.180
  12.0 1.1 %fusion.55 = f32[128]{0:T(128)S(1)} fusion(bf16[128,768]{1,0:T(8,128)(2,1)} %param.7, f32[128]{0:T(128)S(1)} %broadcast_multiply_fusion.15), kind=kLoop, calls=%fused_computation.100 | loop fusion | flops 393088 | bytes 197632 | tf_op jit(solution)/shard_map/reduce_sum | solution.py:31
  13.1 1.5 %convolution_convert_fusion.16 = bf16[128,512]{1,0:T(8,128)(2,1)S(1)} fusion(bf16[128,768]{1,0:T(8,128)(2,1)} %param.7, bf16[768,512]{1,0:T(8,128)(2,1)} %param.12), kind=kOutput, calls=%fused_computation.32 | convolution fusion | flops 100728832 | bytes 1114112 | tf_op jit(solution)/shard_map/dot_general | solution.py:44
  14.6 0.2 reshape_reshape.7
  14.8 0.2 copy.10
  15.0 3.1 %convolution_convert_fusion.15.refs_1_.refs_17_ = bf16[128,1536]{1,0:T(8,128)(2,1)} fusion(bf16[128,768]{1,0:T(8,128)(2,1)S(1)} %copy-done.1, f32[768]{0:T(1024)S(1)} %convert_element_type.180, f32[128]{0:T(128)S(1)} %add_rsqrt_fusion.15, f32[128]{0:T(128)S(1)} %broadcast_multiply_fusion.15, bf16[768,2304]{1,0:T(8,128)(2,1)} %param.9), kind=kOutput, calls=%fused_computation.17 | convolution fusion | flops 302678016 | bytes 2953216 | tf_op jit(solution)/shard_map/dot_general | solution.py:143
  18.1 1.0 fusion.18.refs_0_
  19.2 1.7 %collective-permute-done.4 = bf16[128,768]{1,0:T(8,128)(2,1)S(1)} collective-permute-done((bf16[128,768]{1,0:T(8,128)(2,1)}, bf16[128,768]{1,0:T(8,128)(2,1)S(1)}, u32[]{:S(2)}, u32[]{:S(2)}) %collective-permute-start.4) | collective-permute-done | bytes 196640 | tf_op jit(solution)/shard_map/ppermute | solution.py:128
  20.9 8.8 %collective-permute-start.1 = (bf16[128,768]{1,0:T(8,128)(2,1)S(1)}, bf16[128,768]{1,0:T(8,128)(2,1)S(1)}, u32[]{:S(2)}, u32[]{:S(2)}) collective-permute-start(bf16[128,768]{1,0:T(8,128)(2,1)S(1)} %copy-done.1), channel_id=1, source_target_pairs={{0,4},{1,5},{2,6},{3,7},{4,8},{5,9},{6,10},{7,11},{8,12},{9,13},{1... | collective-permute-start | bytes 589832 | tf_op jit(solution)/shard_map/ppermute | solution.py:128
  29.8 0.2 fusion.88
  30.0 10.5 %collective-permute-done.3 = bf16[128,768]{1,0:T(8,128)(2,1)S(1)} collective-permute-done((bf16[128,768]{1,0:T(8,128)(2,1)}, bf16[128,768]{1,0:T(8,128)(2,1)S(1)}, u32[]{:S(2)}, u32[]{:S(2)}) %collective-permute-start.3) | collective-permute-done | bytes 196640 | tf_op jit(solution)/shard_map/ppermute | solution.py:128
  40.6 0.2 fusion.91
  41.1 0.2 fusion.94
  41.4 0.2 fusion.97
  41.8 0.2 fusion.82
  42.1 0.2 fusion.85
  42.3 7.7 %collective-permute-done = bf16[128,768]{1,0:T(8,128)(2,1)S(1)} collective-permute-done((bf16[128,768]{1,0:T(8,128)(2,1)S(1)}, bf16[128,768]{1,0:T(8,128)(2,1)S(1)}, u32[]{:S(2)}, u32[]{:S(2)}) %collective-permute-start) | collective-permute-done | bytes 196640 | tf_op jit(solution)/shard_map/ppermute | solution.py:128
  50.1 0.2 fusion.100
  50.5 0.2 fusion.79
  50.8 0.5 collective-permute-start.13
  51.3 0.4 collective-permute-start.11
  51.8 1.3 %convolution_convert_fusion.10.refs_6_.refs_22_ = bf16[128,1536]{1,0:T(8,128)(2,1)} fusion(bf16[128,768]{1,0:T(8,128)(2,1)S(1)} %collective-permute-done.4, f32[128]{0:T(128)S(1)} %add_rsqrt_fusion.10, f32[128]{0:T(128)S(1)} %broadcast_multiply_fusion.10, f32[768]{0:T(1024)S(1)} %convert_element_type.180, bf16[768,2304]{1,0:T(8,128)(2,1)S(1)} %copy-done.4), kind=kOutput, calls=%fused_computation.12 | convolution fusion | flops 302678016 | bytes 2954240 | tf_op jit(solution)/shard_map/dot_general | solution.py:147
  53.2 1.3 %convolution_convert_fusion.11.refs_5_.refs_21_ = bf16[128,1536]{1,0:T(8,128)(2,1)} fusion(bf16[128,768]{1,0:T(8,128)(2,1)S(1)} %collective-permute-done.3, f32[128]{0:T(128)S(1)} %add_rsqrt_fusion.11, f32[128]{0:T(128)S(1)} %broadcast_multiply_fusion.11, f32[768]{0:T(1024)S(1)} %convert_element_type.180, bf16[768,2304]{1,0:T(8,128)(2,1)S(1)} %copy-done.4), kind=kOutput, calls=%fused_computation.13 | convolution fusion | flops 302678016 | bytes 2954240 | tf_op jit(solution)/shard_map/dot_general | solution.py:147
  54.4 1.3 %convolution_convert_fusion.12.refs_4_.refs_20_ = bf16[128,1536]{1,0:T(8,128)(2,1)} fusion(bf16[128,768]{1,0:T(8,128)(2,1)S(1)} %collective-permute-done.2, f32[128]{0:T(128)S(1)} %add_rsqrt_fusion.12, f32[128]{0:T(128)S(1)} %broadcast_multiply_fusion.12, f32[768]{0:T(1024)S(1)} %convert_element_type.180, bf16[768,2304]{1,0:T(8,128)(2,1)S(1)} %copy-done.4), kind=kOutput, calls=%fused_computation.14 | convolution fusion | flops 302678016 | bytes 2954240 | tf_op jit(solution)/shard_map/dot_general | solution.py:147
  55.8 1.3 %convolution_convert_fusion.13.refs_3_.refs_19_ = bf16[128,1536]{1,0:T(8,128)(2,1)} fusion(bf16[128,768]{1,0:T(8,128)(2,1)S(1)} %collective-permute-done.1, f32[128]{0:T(128)S(1)} %add_rsqrt_fusion.13, f32[128]{0:T(128)S(1)} %broadcast_multiply_fusion.13, f32[768]{0:T(1024)S(1)} %convert_element_type.180, bf16[768,2304]{1,0:T(8,128)(2,1)S(1)} %copy-done.4), kind=kOutput, calls=%fused_computation.15 | convolution fusion | flops 302678016 | bytes 2954240 | tf_op jit(solution)/shard_map/dot_general | solution.py:147
  57.0 1.3 %convolution_convert_fusion.8.refs_8_.refs_24_ = bf16[128,1536]{1,0:T(8,128)(2,1)} fusion(bf16[128,768]{1,0:T(8,128)(2,1)S(1)} %collective-permute-done.6, f32[128]{0:T(128)S(1)} %add_rsqrt_fusion.8, f32[128]{0:T(128)S(1)} %broadcast_multiply_fusion.8, f32[768]{0:T(1024)S(1)} %convert_element_type.180, bf16[768,2304]{1,0:T(8,128)(2,1)S(1)} %copy-done.4), kind=kOutput, calls=%fused_computation.10 | convolution fusion | flops 302678016 | bytes 2954240 | tf_op jit(solution)/shard_map/dot_general | solution.py:147
  58.3 1.3 %convolution_convert_fusion.9.refs_7_.refs_23_ = bf16[128,1536]{1,0:T(8,128)(2,1)} fusion(bf16[128,768]{1,0:T(8,128)(2,1)S(1)} %collective-permute-done.5, f32[128]{0:T(128)S(1)} %add_rsqrt_fusion.9, f32[128]{0:T(128)S(1)} %broadcast_multiply_fusion.9, f32[768]{0:T(1024)S(1)} %convert_element_type.180, bf16[768,2304]{1,0:T(8,128)(2,1)S(1)} %copy-done.4), kind=kOutput, calls=%fused_computation.11 | convolution fusion | flops 302678016 | bytes 2954240 | tf_op jit(solution)/shard_map/dot_general | solution.py:147
  59.6 1.3 %convolution_convert_fusion.14.refs_2_.refs_18_ = bf16[128,1536]{1,0:T(8,128)(2,1)} fusion(bf16[128,768]{1,0:T(8,128)(2,1)S(1)} %collective-permute-done, f32[128]{0:T(128)S(1)} %add_rsqrt_fusion.14, f32[128]{0:T(128)S(1)} %broadcast_multiply_fusion.14, f32[768]{0:T(1024)S(1)} %convert_element_type.180, bf16[768,2304]{1,0:T(8,128)(2,1)S(1)} %copy-done.4), kind=kOutput, calls=%fused_computation.16 | convolution fusion | flops 302678016 | bytes 2954240 | tf_op jit(solution)/shard_map/dot_general | solution.py:147
  60.9 1.3 %convolution_convert_fusion.7.refs_9_.refs_25_ = bf16[128,1536]{1,0:T(8,128)(2,1)} fusion(bf16[128,768]{1,0:T(8,128)(2,1)S(1)} %collective-permute-done.7, f32[128]{0:T(128)S(1)} %add_rsqrt_fusion.7, f32[128]{0:T(128)S(1)} %broadcast_multiply_fusion.7, f32[768]{0:T(1024)S(1)} %convert_element_type.180, bf16[768,2304]{1,0:T(8,128)(2,1)S(1)} %copy-done.4), kind=kOutput, calls=%fused_computation.9 | convolution fusion | flops 302678016 | bytes 2954240 | tf_op jit(solution)/shard_map/dot_general | solution.py:147
  62.2 0.4 collective-permute-start.9
  62.8 0.2 fusion.58
  63.2 0.2 fusion.61
  63.6 0.2 fusion.64
  64.0 0.2 fusion.67
  64.3 0.2 fusion.70
  64.7 0.2 fusion.73
  65.0 0.2 fusion.76
  65.2 1.3 %convolution_convert_fusion.refs_16_.refs_32_ = bf16[128,1536]{1,0:T(8,128)(2,1)} fusion(bf16[128,768]{1,0:T(8,128)(2,1)S(1)} %collective-permute-done.14, f32[128]{0:T(128)S(1)} %add_rsqrt_fusion, f32[128]{0:T(128)S(1)} %broadcast_multiply_fusion, f32[768]{0:T(1024)S(1)} %convert_element_type.180, bf16[768,2304]{1,0:T(8,128)(2,1)S(1)} %copy-done.4), kind=kOutput, calls=%fused_computation.2 | convolution fusion | flops 302678016 | bytes 2954240 | tf_op jit(solution)/shard_map/dot_general | solution.py:147
  66.5 1.3 %convolution_convert_fusion.1.refs_15_.refs_31_ = bf16[128,1536]{1,0:T(8,128)(2,1)} fusion(bf16[128,768]{1,0:T(8,128)(2,1)S(1)} %collective-permute-done.13, f32[128]{0:T(128)S(1)} %add_rsqrt_fusion.1, f32[128]{0:T(128)S(1)} %broadcast_multiply_fusion.1, f32[768]{0:T(1024)S(1)} %convert_element_type.180, bf16[768,2304]{1,0:T(8,128)(2,1)S(1)} %copy-done.4), kind=kOutput, calls=%fused_computation.3 | convolution fusion | flops 302678016 | bytes 2954240 | tf_op jit(solution)/shard_map/dot_general | solution.py:147
  67.8 1.3 %convolution_convert_fusion.2.refs_14_.refs_30_ = bf16[128,1536]{1,0:T(8,128)(2,1)} fusion(bf16[128,768]{1,0:T(8,128)(2,1)S(1)} %collective-permute-done.12, f32[128]{0:T(128)S(1)} %add_rsqrt_fusion.2, f32[128]{0:T(128)S(1)} %broadcast_multiply_fusion.2, f32[768]{0:T(1024)S(1)} %convert_element_type.180, bf16[768,2304]{1,0:T(8,128)(2,1)S(1)} %copy-done.4), kind=kOutput, calls=%fused_computation.4 | convolution fusion | flops 302678016 | bytes 2954240 | tf_op jit(solution)/shard_map/dot_general | solution.py:147
  69.1 1.3 %convolution_convert_fusion.3.refs_13_.refs_29_ = bf16[128,1536]{1,0:T(8,128)(2,1)} fusion(bf16[128,768]{1,0:T(8,128)(2,1)S(1)} %collective-permute-done.11, f32[128]{0:T(128)S(1)} %add_rsqrt_fusion.3, f32[128]{0:T(128)S(1)} %broadcast_multiply_fusion.3, f32[768]{0:T(1024)S(1)} %convert_element_type.180, bf16[768,2304]{1,0:T(8,128)(2,1)S(1)} %copy-done.4), kind=kOutput, calls=%fused_computation.5 | convolution fusion | flops 302678016 | bytes 2954240 | tf_op jit(solution)/shard_map/dot_general | solution.py:147
  70.4 1.3 %convolution_convert_fusion.4.refs_12_.refs_28_ = bf16[128,1536]{1,0:T(8,128)(2,1)} fusion(bf16[128,768]{1,0:T(8,128)(2,1)S(1)} %collective-permute-done.10, f32[128]{0:T(128)S(1)} %add_rsqrt_fusion.4, f32[128]{0:T(128)S(1)} %broadcast_multiply_fusion.4, f32[768]{0:T(1024)S(1)} %convert_element_type.180, bf16[768,2304]{1,0:T(8,128)(2,1)S(1)} %copy-done.4), kind=kOutput, calls=%fused_computation.6 | convolution fusion | flops 302678016 | bytes 2954240 | tf_op jit(solution)/shard_map/dot_general | solution.py:147
  71.7 1.3 %convolution_convert_fusion.5.refs_11_.refs_27_ = bf16[128,1536]{1,0:T(8,128)(2,1)} fusion(bf16[128,768]{1,0:T(8,128)(2,1)S(1)} %collective-permute-done.9, f32[128]{0:T(128)S(1)} %add_rsqrt_fusion.5, f32[128]{0:T(128)S(1)} %broadcast_multiply_fusion.5, f32[768]{0:T(1024)S(1)} %convert_element_type.180, bf16[768,2304]{1,0:T(8,128)(2,1)S(1)} %copy-done.4), kind=kOutput, calls=%fused_computation.7 | convolution fusion | flops 302678016 | bytes 2954240 | tf_op jit(solution)/shard_map/dot_general | solution.py:147
  73.0 1.3 %convolution_convert_fusion.6.refs_10_.refs_26_ = bf16[128,1536]{1,0:T(8,128)(2,1)} fusion(bf16[128,768]{1,0:T(8,128)(2,1)S(1)} %collective-permute-done.8, f32[128]{0:T(128)S(1)} %add_rsqrt_fusion.6, f32[128]{0:T(128)S(1)} %broadcast_multiply_fusion.6, f32[768]{0:T(1024)S(1)} %convert_element_type.180, bf16[768,2304]{1,0:T(8,128)(2,1)S(1)} %copy-done.4), kind=kOutput, calls=%fused_computation.8 | convolution fusion | flops 302678016 | bytes 2954240 | tf_op jit(solution)/shard_map/dot_general | solution.py:147
  74.3 13.2 %shard_map.86 = bf16[128,768]{1,0:T(8,128)(2,1)} custom-call(bf16[128,768]{1,0:T(8,128)(2,1)} %fusion.18.refs_0_, bf16[128,1536]{1,0:T(8,128)(2,1)} %convolution_convert_fusion.15.refs_1_.refs_17_, bf16[128,1536]{1,0:T(8,128)(2,1)} %convolution_convert_fusion.14.refs_2_.refs_18_, bf16[128,1536]{1,0:T(8,128)(2,1)} %convolution_convert_fusion.13.refs_3_.refs_19_, ...), custom_call_target="tpu_custom_call" | custom-call | tf_op jit(solution)/shard_map/pallas_call | solution.py:115
  87.5 1.3 %fusion.21 = bf16[128,768]{1,0:T(8,128)(2,1)S(1)} fusion(bf16[128,768]{1,0:T(8,128)(2,1)} %shard_map.86, bf16[768,768]{1,0:T(8,128)(2,1)S(1)} %copy-done, bf16[128,768]{1,0:T(8,128)(2,1)S(1)} %copy-done.1), kind=kOutput, calls=%fused_computation.31 | convolution fusion | flops 151289856 | bytes 1769472 | tf_op jit(solution)/shard_map/dot_general | solution.py:152
  88.7 0.3 convolution_convert_fusion.17
  89.0 0.2 reshape_reshape.6
  89.2 0.2 copy.9
  89.5 0.4 collective-permute-start.15
  89.9 0.8 collective-permute-done.15
  90.9 1.3 %collective-permute-start.16 = (bf16[1,34,16,128]{3,2,1,0:T(8,128)(2,1)S(1)}, bf16[1,34,16,128]{3,2,1,0:T(8,128)(2,1)S(1)}, u32[]{:S(2)}, u32[]{:S(2)}) collective-permute-start(bf16[1,34,16,128]{3,2,1,0:T(8,128)(2,1)S(1)} %get-tuple-element.4), channel_id=1, source_target_pairs={{0,2},{1,3},{2,4},{3,5},{4,6},{5,7},{6,8},{7,9},{8,10},{9,11},{10,... | collective-permute-start | bytes 417800 | tf_op jit(solution)/shard_map/ppermute | solution.py:20
  92.3 1.3 %collective-permute-start.17 = (bf16[1,34,16,128]{3,2,1,0:T(8,128)(2,1)S(1)}, bf16[1,34,16,128]{3,2,1,0:T(8,128)(2,1)S(1)}, u32[]{:S(2)}, u32[]{:S(2)}) collective-permute-start(bf16[1,34,16,128]{3,2,1,0:T(8,128)(2,1)S(1)} %get-tuple-element.5), channel_id=1, source_target_pairs={{2,0},{3,1},{4,2},{5,3},{6,4},{7,5},{8,6},{9,7},{10,8},{11,9},{12,... | collective-permute-start | bytes 417800 | tf_op jit(solution)/shard_map/ppermute | solution.py:20
  93.6 5.4 %collective-permute-done.16 = bf16[1,34,16,128]{3,2,1,0:T(8,128)(2,1)S(1)} collective-permute-done((bf16[1,34,16,128]{3,2,1,0:T(8,128)(2,1)S(1)}, bf16[1,34,16,128]{3,2,1,0:T(8,128)(2,1)S(1)}, u32[]{:S(2)}, u32[]{:S(2)}) %collective-permute-start.16) | collective-permute-done | bytes 139296 | tf_op jit(solution)/shard_map/ppermute | solution.py:20
  98.9 1.1 %collective-permute-done.17 = bf16[1,34,16,128]{3,2,1,0:T(8,128)(2,1)S(1)} collective-permute-done((bf16[1,34,16,128]{3,2,1,0:T(8,128)(2,1)S(1)}, bf16[1,34,16,128]{3,2,1,0:T(8,128)(2,1)S(1)}, u32[]{:S(2)}, u32[]{:S(2)}) %collective-permute-start.17) | collective-permute-done | bytes 139296 | tf_op jit(solution)/shard_map/ppermute | solution.py:20
  100.2 0.3 copy.16
  100.6 0.3 pad.clone
  101.1 0.4 copy-done.5
  101.6 2.9 %fusion.13 = bf16[2,32,8,3,64]{4,2,3,1,0:T(8,128)(2,1)S(1)} fusion(bf16[3,3,3,128,64]{3,4,2,1,0:T(8,128)(2,1)S(1)} %copy-done.5, bf16[4,34,1,7,2,128]{5,3,4,1,0,2:T(8,128)(2,1)S(1)} %slice.28, bf16[4,34,1,8,3,128]{5,3,4,1,0,2:T(8,128)(2,1)S(1)} %copy.13, pred[8,3]{0,1:T(4,128)(4,1)S(1)} %copy-done.6), kind=kOutput, calls=%fused_computation.27 | convolution fusion | flops 684146688 | bytes 1962008 | tf_op jit(solution)/shard_map/conv_general_dilated | solution.py:52
  104.5 0.8 copy.15
  (89 shorter events, 3.1 us)
Async XLA Ops:
  0.6 86.8 %copy-start = (bf16[768,768]{1,0:T(8,128)(2,1)S(1)}, bf16[768,768]{1,0:T(8,128)(2,1)}, u32[]{:S(2)}) copy-start(bf16[768,768]{1,0:T(8,128)(2,1)} %param.10) | copy-start | bytes 3538948
  0.6 14.4 %copy-start.1 = (bf16[128,768]{1,0:T(8,128)(2,1)S(1)}, bf16[128,768]{1,0:T(8,128)(2,1)}, u32[]{:S(2)}) copy-start(bf16[128,768]{1,0:T(8,128)(2,1)} %param.7) | copy-start | bytes 589828
  0.7 41.0 %collective-permute-start.6 = (bf16[128,768]{1,0:T(8,128)(2,1)}, bf16[128,768]{1,0:T(8,128)(2,1)S(1)}, u32[]{:S(2)}, u32[]{:S(2)}) collective-permute-start(bf16[128,768]{1,0:T(8,128)(2,1)} %param.7), channel_id=1, source_target_pairs={{0,14},{1,15},{2,0},{3,1},{4,2},{5,3},{6,4},{7,5},{8,6},{9,7},{10,... | collective-permute-start | bytes 589832 | tf_op jit(solution)/shard_map/ppermute | solution.py:128
  6.7 35.2 %collective-permute-start.5 = (bf16[128,768]{1,0:T(8,128)(2,1)}, bf16[128,768]{1,0:T(8,128)(2,1)S(1)}, u32[]{:S(2)}, u32[]{:S(2)}) collective-permute-start(bf16[128,768]{1,0:T(8,128)(2,1)} %param.7), channel_id=1, source_target_pairs={{0,12},{1,13},{2,14},{3,15},{4,0},{5,1},{6,2},{7,3},{8,4},{9,5},{1... | collective-permute-start | bytes 589832 | tf_op jit(solution)/shard_map/ppermute | solution.py:128
  7.2 13.7 %collective-permute-start.4 = (bf16[128,768]{1,0:T(8,128)(2,1)}, bf16[128,768]{1,0:T(8,128)(2,1)S(1)}, u32[]{:S(2)}, u32[]{:S(2)}) collective-permute-start(bf16[128,768]{1,0:T(8,128)(2,1)} %param.7), channel_id=1, source_target_pairs={{0,10},{1,11},{2,12},{3,13},{4,14},{5,15},{6,0},{7,1},{8,2},{9,3},... | collective-permute-start | bytes 589832 | tf_op jit(solution)/shard_map/ppermute | solution.py:128
  7.2 33.3 %collective-permute-start.3 = (bf16[128,768]{1,0:T(8,128)(2,1)}, bf16[128,768]{1,0:T(8,128)(2,1)S(1)}, u32[]{:S(2)}, u32[]{:S(2)}) collective-permute-start(bf16[128,768]{1,0:T(8,128)(2,1)} %param.7), channel_id=1, source_target_pairs={{0,8},{1,9},{2,10},{3,11},{4,12},{5,13},{6,14},{7,15},{8,0},{9,1},... | collective-permute-start | bytes 589832 | tf_op jit(solution)/shard_map/ppermute | solution.py:128
  10.2 30.7 %collective-permute-start.2 = (bf16[128,768]{1,0:T(8,128)(2,1)}, bf16[128,768]{1,0:T(8,128)(2,1)S(1)}, u32[]{:S(2)}, u32[]{:S(2)}) collective-permute-start(bf16[128,768]{1,0:T(8,128)(2,1)} %param.7), channel_id=1, source_target_pairs={{0,6},{1,7},{2,8},{3,9},{4,10},{5,11},{6,12},{7,13},{8,14},{9,15},... | collective-permute-start | bytes 589832 | tf_op jit(solution)/shard_map/ppermute | solution.py:128
  14.8 3.3 %copy-start.4 = (bf16[768,2304]{1,0:T(8,128)(2,1)S(1)}, bf16[768,2304]{1,0:T(8,128)(2,1)}, u32[]{:S(2)}) copy-start(bf16[768,2304]{1,0:T(8,128)(2,1)} %param.9) | copy-start | bytes 10616836
  20.9 20.4 %collective-permute-start.1 = (bf16[128,768]{1,0:T(8,128)(2,1)S(1)}, bf16[128,768]{1,0:T(8,128)(2,1)S(1)}, u32[]{:S(2)}, u32[]{:S(2)}) collective-permute-start(bf16[128,768]{1,0:T(8,128)(2,1)S(1)} %copy-done.1), channel_id=1, source_target_pairs={{0,4},{1,5},{2,6},{3,7},{4,8},{5,9},{6,10},{7,11},{8,12},{9,13},{1... | collective-permute-start | bytes 589832 | tf_op jit(solution)/shard_map/ppermute | solution.py:128
  40.5 9.5 %collective-permute-start = (bf16[128,768]{1,0:T(8,128)(2,1)S(1)}, bf16[128,768]{1,0:T(8,128)(2,1)S(1)}, u32[]{:S(2)}, u32[]{:S(2)}) collective-permute-start(bf16[128,768]{1,0:T(8,128)(2,1)S(1)} %copy-done.1), channel_id=1, source_target_pairs={{0,2},{1,3},{2,4},{3,5},{4,6},{5,7},{6,8},{7,9},{8,10},{9,11},{10,... | collective-permute-start | bytes 589832 | tf_op jit(solution)/shard_map/ppermute | solution.py:128
  40.8 9.5 %collective-permute-start.7 = (bf16[128,768]{1,0:T(8,128)(2,1)S(1)}, bf16[128,768]{1,0:T(8,128)(2,1)S(1)}, u32[]{:S(2)}, u32[]{:S(2)}) collective-permute-start(bf16[128,768]{1,0:T(8,128)(2,1)S(1)} %copy-done.1), channel_id=1, source_target_pairs={{0,1},{1,0},{2,3},{3,2},{4,5},{5,4},{6,7},{7,6},{8,9},{9,8},{10,11... | collective-permute-start | bytes 589832 | tf_op jit(solution)/shard_map/ppermute | solution.py:129
  50.7 11.5 %collective-permute-start.14 = (bf16[128,768]{1,0:T(8,128)(2,1)S(1)}, bf16[128,768]{1,0:T(8,128)(2,1)S(1)}, u32[]{:S(2)}, u32[]{:S(2)}) collective-permute-start(bf16[128,768]{1,0:T(8,128)(2,1)S(1)} %collective-permute-done.6), channel_id=1, source_target_pairs={{0,1},{1,0},{2,3},{3,2},{4,5},{5,4},{6,7},{7,6},{8,9},{9,8},{10,11... | collective-permute-start | bytes 589832 | tf_op jit(solution)/shard_map/ppermute | solution.py:129
  50.8 12.2 %collective-permute-start.13 = (bf16[128,768]{1,0:T(8,128)(2,1)S(1)}, bf16[128,768]{1,0:T(8,128)(2,1)S(1)}, u32[]{:S(2)}, u32[]{:S(2)}) collective-permute-start(bf16[128,768]{1,0:T(8,128)(2,1)S(1)} %collective-permute-done.5), channel_id=1, source_target_pairs={{0,1},{1,0},{2,3},{3,2},{4,5},{5,4},{6,7},{7,6},{8,9},{9,8},{10,11... | collective-permute-start | bytes 589832 | tf_op jit(solution)/shard_map/ppermute | solution.py:129
  51.3 12.2 %collective-permute-start.12 = (bf16[128,768]{1,0:T(8,128)(2,1)S(1)}, bf16[128,768]{1,0:T(8,128)(2,1)S(1)}, u32[]{:S(2)}, u32[]{:S(2)}) collective-permute-start(bf16[128,768]{1,0:T(8,128)(2,1)S(1)} %collective-permute-done.4), channel_id=1, source_target_pairs={{0,1},{1,0},{2,3},{3,2},{4,5},{5,4},{6,7},{7,6},{8,9},{9,8},{10,11... | collective-permute-start | bytes 589832 | tf_op jit(solution)/shard_map/ppermute | solution.py:129
  51.3 12.5 %collective-permute-start.11 = (bf16[128,768]{1,0:T(8,128)(2,1)S(1)}, bf16[128,768]{1,0:T(8,128)(2,1)S(1)}, u32[]{:S(2)}, u32[]{:S(2)}) collective-permute-start(bf16[128,768]{1,0:T(8,128)(2,1)S(1)} %collective-permute-done.3), channel_id=1, source_target_pairs={{0,1},{1,0},{2,3},{3,2},{4,5},{5,4},{6,7},{7,6},{8,9},{9,8},{10,11... | collective-permute-start | bytes 589832 | tf_op jit(solution)/shard_map/ppermute | solution.py:129
  51.8 12.4 %collective-permute-start.10 = (bf16[128,768]{1,0:T(8,128)(2,1)S(1)}, bf16[128,768]{1,0:T(8,128)(2,1)S(1)}, u32[]{:S(2)}, u32[]{:S(2)}) collective-permute-start(bf16[128,768]{1,0:T(8,128)(2,1)S(1)} %collective-permute-done.2), channel_id=1, source_target_pairs={{0,1},{1,0},{2,3},{3,2},{4,5},{5,4},{6,7},{7,6},{8,9},{9,8},{10,11... | collective-permute-start | bytes 589832 | tf_op jit(solution)/shard_map/ppermute | solution.py:129
  62.2 2.3 %collective-permute-start.9 = (bf16[128,768]{1,0:T(8,128)(2,1)S(1)}, bf16[128,768]{1,0:T(8,128)(2,1)S(1)}, u32[]{:S(2)}, u32[]{:S(2)}) collective-permute-start(bf16[128,768]{1,0:T(8,128)(2,1)S(1)} %collective-permute-done.1), channel_id=1, source_target_pairs={{0,1},{1,0},{2,3},{3,2},{4,5},{5,4},{6,7},{7,6},{8,9},{9,8},{10,11... | collective-permute-start | bytes 589832 | tf_op jit(solution)/shard_map/ppermute | solution.py:129
  63.0 1.9 %collective-permute-start.8 = (bf16[128,768]{1,0:T(8,128)(2,1)S(1)}, bf16[128,768]{1,0:T(8,128)(2,1)S(1)}, u32[]{:S(2)}, u32[]{:S(2)}) collective-permute-start(bf16[128,768]{1,0:T(8,128)(2,1)S(1)} %collective-permute-done), channel_id=1, source_target_pairs={{0,1},{1,0},{2,3},{3,2},{4,5},{5,4},{6,7},{7,6},{8,9},{9,8},{10,11... | collective-permute-start | bytes 589832 | tf_op jit(solution)/shard_map/ppermute | solution.py:129
  74.3 14.5 %copy-start.2 = (bf16[768,512]{1,0:T(8,128)(2,1)S(1)}, bf16[768,512]{1,0:T(8,128)(2,1)}, u32[]{:S(2)}) copy-start(bf16[768,512]{1,0:T(8,128)(2,1)} %param.11) | copy-start | bytes 2359300
  88.7 11.5 %copy-start.3 = (bf16[128,768]{1,0:T(8,128)(2,1)}, bf16[128,768]{1,0:T(8,128)(2,1)S(1)}, u32[]{:S(2)}) copy-start(bf16[128,768]{1,0:T(8,128)(2,1)S(1)} %fusion.21) | copy-start | bytes 589828
  89.5 1.3 %collective-permute-start.15 = (bf16[2,1,16,128]{3,2,1,0:T(8,128)(2,1)S(1)}, bf16[2,1,16,128]{3,2,1,0:T(8,128)(2,1)S(1)}, u32[]{:S(2)}, u32[]{:S(2)}) collective-permute-start(bf16[2,1,16,128]{3,2,1,0:T(8,128)(2,1)S(1)} %fusion.163), channel_id=1, source_target_pairs={{0,1},{1,0},{2,3},{3,2},{4,5},{5,4},{6,7},{7,6},{8,9},{9,8},{10,11... | collective-permute-start | bytes 24584 | tf_op jit(solution)/shard_map/ppermute | solution.py:24
  90.9 8.0 %collective-permute-start.16 = (bf16[1,34,16,128]{3,2,1,0:T(8,128)(2,1)S(1)}, bf16[1,34,16,128]{3,2,1,0:T(8,128)(2,1)S(1)}, u32[]{:S(2)}, u32[]{:S(2)}) collective-permute-start(bf16[1,34,16,128]{3,2,1,0:T(8,128)(2,1)S(1)} %get-tuple-element.4), channel_id=1, source_target_pairs={{0,2},{1,3},{2,4},{3,5},{4,6},{5,7},{6,8},{7,9},{8,10},{9,11},{10,... | collective-permute-start | bytes 417800 | tf_op jit(solution)/shard_map/ppermute | solution.py:20
  92.3 7.8 %collective-permute-start.17 = (bf16[1,34,16,128]{3,2,1,0:T(8,128)(2,1)S(1)}, bf16[1,34,16,128]{3,2,1,0:T(8,128)(2,1)S(1)}, u32[]{:S(2)}, u32[]{:S(2)}) collective-permute-start(bf16[1,34,16,128]{3,2,1,0:T(8,128)(2,1)S(1)} %get-tuple-element.5), channel_id=1, source_target_pairs={{2,0},{3,1},{4,2},{5,3},{6,4},{7,5},{8,6},{9,7},{10,8},{11,9},{12,... | collective-permute-start | bytes 417800 | tf_op jit(solution)/shard_map/ppermute | solution.py:20
  100.5 1.0 copy-start.5
  100.5 1.0 copy-start.6

commit v3 on v2

--- a/solution.py
+++ b/solution.py
@@ -69,11 +69,12 @@
     q_ref = refs[0]
     k_refs = refs[1 : 1 + chunks]
     v_refs = refs[1 + chunks : 1 + 2 * chunks]
-    o_ref = refs[-1]
+    o_ref, lse_ref = refs[-2:]
     pair = q_ref.shape[-1]
     lane = lax.broadcasted_iota(jnp.int32, (1, pair), 1)
     q = q_ref[...]
     result = None
+    log_sum = None
     for h in range(pair // head_size):
         in_head = (lane >= h * head_size) & (lane < (h + 1) * head_size)
         q_h = jnp.where(in_head, q, jnp.zeros_like(q))
@@ -98,11 +99,18 @@
             denominator = part_sum if denominator is None else denominator + part_sum
             numerator = part if numerator is None else numerator + part
         head_out = numerator / denominator
+        head_lse = row_max + jnp.log(denominator)
         result = head_out if result is None else jnp.where(in_head, head_out, result)
+        log_sum = (
+            jnp.broadcast_to(head_lse, result.shape)
+            if log_sum is None
+            else jnp.where(in_head, head_lse, log_sum)
+        )
     o_ref[...] = result.astype(o_ref.dtype)
-
-
-def attention(queries, kv_chunks, head_size, score_scale):
+    lse_ref[...] = log_sum
+
+
+def attention(queries, kv_chunks, head_size, score_scale, out_dtype):
     token_count, model_width = queries.shape
     pair = 2 * head_size
     pairs = model_width // pair
@@ -112,41 +120,55 @@
     )
     key_specs = [pl.BlockSpec((c.shape[0], pair), lambda j: (0, j)) for c in kv_chunks]
     value_specs = [pl.BlockSpec((c.shape[0], pair), lambda j: (0, j + pairs)) for c in kv_chunks]
-    return pl.pallas_call(
+    row_spec = pl.BlockSpec((token_count, pair), lambda j: (0, j))
+    output, log_sum = pl.pallas_call(
         kernel,
         grid=(pairs,),
-        in_specs=[pl.BlockSpec((token_count, pair), lambda j: (0, j))] + key_specs + value_specs,
-        out_specs=pl.BlockSpec((token_count, pair), lambda j: (0, j)),
-        out_shape=jax.ShapeDtypeStruct((token_count, model_width), jnp.bfloat16),
+        in_specs=[row_spec] + key_specs + value_specs,
+        out_specs=[row_spec, row_spec],
+        out_shape=[
+            jax.ShapeDtypeStruct((token_count, model_width), out_dtype),
+            jax.ShapeDtypeStruct((token_count, model_width), jnp.float32),
+        ],
     )(queries, *kv_chunks, *kv_chunks)
-
-
-def gathered_rows(rows):
+    return output, log_sum[:, ::head_size]
+
+
+def exchanged(x, mask):
     devices = lax.axis_size("seq")
-    local = [rows]
-    for distance in range(2, devices, 2):
-        local.append(lax.ppermute(rows, "seq", [(i, (i + distance) % devices) for i in range(devices)]))
-    partner = [lax.ppermute(c, "seq", [(i, i ^ 1) for i in range(devices)]) for c in local]
-    return local + partner
+    return lax.ppermute(x, "seq", [(i, i ^ mask) for i in range(devices)])
+
+
+def projected(rows, norm_gain, weight):
+    normed = layer_norm(rows, norm_gain).astype(jnp.bfloat16)
+    return jnp.dot(normed, weight, preferred_element_type=jnp.float32).astype(jnp.bfloat16)
 
 
 def body(layer_input, norm_gain, projection, output_weight, deep_weight, skip_weight, conv_kernel):
     token_count, model_width = layer_input.shape
     head_size = model_width // HEADS
     score_scale = 1.0 / math.sqrt(head_size)
-    chunks = gathered_rows(layer_input)
-    normed = layer_norm(layer_input, norm_gain).astype(jnp.bfloat16)
-    queries = jnp.dot(
-        normed, projection[:, :model_width], preferred_element_type=jnp.float32
+    half = lax.axis_size("seq") // 2
+    queries = projected(layer_input, norm_gain, projection[:, :model_width])
+    mirrored_queries = exchanged(queries, half)
+    same_core = [layer_input] + [exchanged(layer_input, mask) for mask in range(2, half, 2)]
+    mine = jnp.concatenate(same_core, axis=0)
+    theirs = exchanged(mine, 1)
+    kv_weight = projection[:, model_width:]
+    kv_chunks = [projected(mine, norm_gain, kv_weight), projected(theirs, norm_gain, kv_weight)]
+    remote_out, remote_lse = attention(
+        mirrored_queries, kv_chunks, head_size, score_scale, jnp.bfloat16
+    )
+    other_out = exchanged(remote_out, half)
+    other_lse = exchanged(remote_lse, half)
+    own_out, own_lse = attention(queries, kv_chunks, head_size, score_scale, jnp.float32)
+    top = jnp.maximum(own_lse, other_lse)
+    own_weight = jnp.repeat(jnp.exp(own_lse - top), head_size, axis=1)
+    other_weight = jnp.repeat(jnp.exp(other_lse - top), head_size, axis=1)
+    attended = (
+        (own_weight * own_out + other_weight * other_out.astype(jnp.float32))
+        / (own_weight + other_weight)
     ).astype(jnp.bfloat16)
-    kv_weight = projection[:, model_width:]
-    kv_chunks = [jnp.dot(normed, kv_weight, preferred_element_type=jnp.float32).astype(jnp.bfloat16)]
-    for chunk in chunks[1:]:
-        chunk_normed = layer_norm(chunk, norm_gain).astype(jnp.bfloat16)
-        kv_chunks.append(
-            jnp.dot(chunk_normed, kv_weight, preferred_element_type=jnp.float32).astype(jnp.bfloat16)
-        )
-    attended = attention(queries, kv_chunks, head_size, score_scale)
     encoded = (
         layer_input.astype(jnp.float32)
         + jnp.dot(attended, output_weight, preferred_element_type=jnp.float32)

time: 106 us -> 77 us (0.73)
  matrix products: 29.5 us -> 11.9 us
  starting transfers between devices: 23.2 us -> 15.8 us
  waiting for transfers between devices: 27.2 us -> 20.9 us
  local copies, waits for them, and re-layouts: 2.93 us -> 7.09 us
  other arithmetic: 8.16 us -> 4.44 us
  Pallas kernels: 13.2 us -> 15.3 us
    dot_general x17 -> x3, matrix products: 23.5 us -> 7.2 us  [projected(): jnp.dot(normed, weight, preferred_element_type=jnp.float32)]
    ppermute x15 -> x7, starting transfers between devices: 20.1 us -> 10.8 us  [exchanged(): return lax.ppermute(x, 'seq', [(i, i ^ mask) for i in range(devices)])]
    ppermute x15 -> x7, waiting for transfers between devices: 19.9 us -> 13.9 us  [exchanged(): return lax.ppermute(x, 'seq', [(i, i ^ mask) for i in range(devices)])]
    slice x0 -> x2, local copies, waits for them, and re-layouts: none -> 2.56 us  [attention(): return (output, log_sum[:, ::head_size])]
    ppermute x2, starting transfers between devices: 2.59 us -> 4.93 us  [shifted(): return lax.ppermute(block, axis, route)]
    reduce_sum x16 -> x3, other arithmetic: 4.14 us -> 1.84 us  [layer_norm(): row_var = jnp.mean(centered * centered, axis=-1, keepdims=True)]
    pallas_call x1 -> x2, Pallas kernels: 13.2 us -> 15.3 us  [attention(): pl.pallas_call(kernel, grid=(pairs,), in_specs=[row_spec] + key_specs + v...]
    reduce_sum x16 -> x3, other arithmetic: 2.75 us -> 1.45 us  [layer_norm(): row_mean = jnp.mean(values32, axis=-1, keepdims=True)]
  transfers between devices with their start and end apart: 18 -> 10, of which waited for: 6 -> 5; matrix products, arithmetic and copies ran while one was open for 22% -> 18% of each run, Pallas kernels for 0% -> 10%
where the time goes in v3:
time: 77 us; the launch traced here: 76.4 us
  waiting for transfers between devices  20.9 us (27%)
  starting transfers between devices  15.8 us (21%)
  Pallas kernels  15.3 us (20%)
  matrix products  11.9 us (15%)
  local copies, waits for them, and re-layouts  7.09 us (9%)
  other arithmetic  4.44 us (6%)
  between operations  1.03 us (1%)
    pallas_call x2, Pallas kernels, attention(): pl.pallas_call(kernel, grid=(pairs,), in_specs=[row_spec] + key_specs + v...  15.3 us
    ppermute x7, waiting for transfers between devices, exchanged(): return lax.ppermute(x, 'seq', [(i, i ^ mask) for i in range(devices)])  13.9 us
    ppermute x7, starting transfers between devices, exchanged(): return lax.ppermute(x, 'seq', [(i, i ^ mask) for i in range(devices)])  10.8 us
    dot_general x3, matrix products, projected(): jnp.dot(normed, weight, preferred_element_type=jnp.float32)  7.2 us
    ppermute x2, waiting for transfers between devices, shifted(): return lax.ppermute(block, axis, route)  5.88 us
    ppermute x2, starting transfers between devices, shifted(): return lax.ppermute(block, axis, route)  4.93 us
    conv_general_dilated x1, matrix products, convolve(): lax.conv_general_dilated(full_xy[None], conv_kernel, window_strides=(1, 1...  2.91 us
    unnamed x29, local copies, waits for them, and re-layouts  2.6 us
  transfers between devices with their start and end apart: 10, of which 5 were waited for; matrix products, arithmetic and copies ran while one was open for 18% of the time, Pallas kernels for 10%

profile of v3, /device:TPU:0, one launch (start us, length us, event | category | flops | bytes accessed | tf_op | source)
XLA Modules:
  0.0 76.4 jit_solution(17142881257645378928)
XLA Ops:
  0.6 0.0 copy-start
  0.6 0.0 copy-start.1
  0.7 3.1 %collective-permute-start = (bf16[128,768]{1,0:T(8,128)(2,1)}, bf16[128,768]{1,0:T(8,128)(2,1)S(1)}, u32[]{:S(2)}, u32[]{:S(2)}) collective-permute-start(bf16[128,768]{1,0:T(8,128)(2,1)} %param.7), channel_id=1, source_target_pairs={{0,2},{1,3},{2,0},{3,1},{4,6},{5,7},{6,4},{7,5},{8,10},{9,11},{10,... | collective-permute-start | bytes 589832 | tf_op jit(solution)/shard_map/ppermute | solution.py:139
  3.7 1.6 %collective-permute-start.1 = (bf16[128,768]{1,0:T(8,128)(2,1)}, bf16[128,768]{1,0:T(8,128)(2,1)S(1)}, u32[]{:S(2)}, u32[]{:S(2)}) collective-permute-start(bf16[128,768]{1,0:T(8,128)(2,1)} %param.7), channel_id=1, source_target_pairs={{0,4},{1,5},{2,6},{3,7},{4,0},{5,1},{6,2},{7,3},{8,12},{9,13},{10,... | collective-permute-start | bytes 589832 | tf_op jit(solution)/shard_map/ppermute | solution.py:139
  5.3 0.0 collective-permute-start.2
  5.3 1.1 %convert_reduce_fusion.2 = f32[128]{0:T(128)S(1)} fusion(bf16[128,768]{1,0:T(8,128)(2,1)} %param.7), kind=kLoop, calls=%fused_computation.44 | loop fusion | flops 196480 | bytes 197120 | tf_op jit(solution)/shard_map/reduce_sum | solution.py:29
  6.4 0.7 convert_element_type.53
  7.1 1.1 %fusion.45 = f32[128]{0:T(128)S(1)} fusion(bf16[128,768]{1,0:T(8,128)(2,1)} %param.7, f32[128]{0:T(128)S(1)} %broadcast_multiply_fusion.2), kind=kLoop, calls=%fused_computation.48 | loop fusion | flops 393088 | bytes 197632 | tf_op jit(solution)/shard_map/reduce_sum | solution.py:31
  8.2 0.0 copy-start.7
  8.2 1.9 %fusion.30.refs_0_ = bf16[128,768]{1,0:T(8,128)(2,1)S(1)} fusion(bf16[768,2304]{1,0:T(8,128)(2,1)} %param.9, bf16[128,768]{1,0:T(8,128)(2,1)} %param.7, f32[768]{0:T(1024)S(1)} %convert_element_type.53, f32[128]{0:T(128)S(1)} %add_rsqrt_fusion.2, f32[128]{0:T(128)S(1)} %broadcast_multiply_fusion.2), kind=kOutput, calls=%fused_computation.32 | convolution fusion | flops 151584768 | bytes 1576960 | tf_op jit(solution)/shard_map/dot_general | solution.py:144
  10.1 3.0 %collective-permute-start.4 = (bf16[128,768]{1,0:T(8,128)(2,1)S(1)}, bf16[128,768]{1,0:T(8,128)(2,1)S(1)}, u32[]{:S(2)}, u32[]{:S(2)}) collective-permute-start(bf16[128,768]{1,0:T(8,128)(2,1)S(1)} %fusion.30.refs_0_), channel_id=1, source_target_pairs={{0,8},{1,9},{2,10},{3,11},{4,12},{5,13},{6,14},{7,15},{8,0},{9,1},... | collective-permute-start | bytes 589832 | tf_op jit(solution)/shard_map/ppermute | solution.py:139
  13.2 0.0 collective-permute-done
  13.2 0.0 collective-permute-done.1
  13.2 2.3 %collective-permute-done.2 = bf16[128,768]{1,0:T(8,128)(2,1)S(1)} collective-permute-done((bf16[128,768]{1,0:T(8,128)(2,1)}, bf16[128,768]{1,0:T(8,128)(2,1)S(1)}, u32[]{:S(2)}, u32[]{:S(2)}) %collective-permute-start.2) | collective-permute-done | bytes 196640 | tf_op jit(solution)/shard_map/ppermute | solution.py:139
  15.6 0.1 collective-permute-start.3
  15.7 0.2 convert_reduce_fusion.1
  15.9 0.4 fusion.10
  16.2 2.6 %convolution_convert_fusion.1.refs_1_.refs_3_ = bf16[512,1536]{1,0:T(8,128)(2,1)} fusion(bf16[768,2304]{1,0:T(8,128)(2,1)S(1)} %copy-done.7, bf16[512,768]{1,0:T(8,128)(2,1)S(1)} %constant_dynamic-update-slice_fusion, f32[768]{0:T(1024)S(1)} %convert_element_type.53, f32[512]{0:T(512)S(1)} %add_rsqrt_fusion.1, f32[512]{0:T(512)S(1)} %broadcast_multiply_fusion.1), kind=kOutput, calls=%fused_computation.1 | convolution fusion | flops 1210712064 | bytes 4726784 | tf_op jit(solution)/shard_map/dot_general | solution.py:144
  18.9 0.0 collective-permute-done.3
  18.9 0.2 convert_reduce_fusion
  19.1 0.4 fusion.7
  19.5 2.7 %convolution_convert_fusion.refs_2_.refs_4_ = bf16[512,1536]{1,0:T(8,128)(2,1)} fusion(bf16[768,2304]{1,0:T(8,128)(2,1)S(1)} %copy-done.7, bf16[512,768]{1,0:T(8,128)(2,1)S(1)} %collective-permute-done.3, f32[512]{0:T(512)S(1)} %add_rsqrt_fusion, f32[512]{0:T(512)S(1)} %broadcast_multiply_fusion, f32[768]{0:T(1024)S(1)} %convert_element_type.53), kind=kOutput, calls=%fused_computation | convolution fusion | flops 1210712064 | bytes 4726784 | tf_op jit(solution)/shard_map/dot_general | solution.py:144
  22.1 0.0 collective-permute-done.4.refs_0_
  22.1 0.7 copy-done.5
  22.8 7.6 %shard_map.87 = (bf16[128,768]{1,0:T(8,128)(2,1)}, f32[128,768]{1,0:T(8,128)}) custom-call(bf16[128,768]{1,0:T(8,128)(2,1)} %copy-done.5, bf16[512,1536]{1,0:T(8,128)(2,1)} %convolution_convert_fusion.1.refs_1_.refs_3_, bf16[512,1536]{1,0:T(8,128)(2,1)} %convolution_convert_fusion.refs_2_.refs_4_, ...), custom_call_target="tpu_custom_call" | custom-call | tf_op jit(solution)/shard_map/pallas_call | solution.py:124
  30.4 1.3 %slice.27 = f32[128,12]{1,0:T(8,128)S(1)} slice(f32[128,768]{1,0:T(8,128)} %get-tuple-element.7), slice={[0:128:1], [0:768:64]} | slice | bytes 12288 | tf_op jit(solution)/shard_map/slice | solution.py:134
  31.6 2.9 %collective-permute-start.5 = (f32[128,12]{1,0:T(8,128)S(1)}, f32[128,12]{1,0:T(8,128)S(1)}, u32[]{:S(2)}, u32[]{:S(2)}) collective-permute-start(f32[128,12]{1,0:T(8,128)S(1)} %slice.27), channel_id=1, source_target_pairs={{0,8},{1,9},{2,10},{3,11},{4,12},{5,13},{6,14},{7,15},{8,0},{9,1},... | collective-permute-start | bytes 18440 | tf_op jit(solution)/shard_map/ppermute | solution.py:139
  34.6 0.3 convolution_convert_fusion.2
  34.9 0.2 reshape_reshape.7
  35.1 0.2 copy.29
  35.3 0.0 copy-start.10
  35.3 7.7 %shard_map.86 = (f32[128,768]{1,0:T(8,128)}, f32[128,768]{1,0:T(8,128)}) custom-call(bf16[128,768]{1,0:T(8,128)(2,1)} %copy-done.4, bf16[512,1536]{1,0:T(8,128)(2,1)} %convolution_convert_fusion.1.refs_1_.refs_3_, bf16[512,1536]{1,0:T(8,128)(2,1)} %convolution_convert_fusion.refs_2_.refs_4_, bf16[512,1536]{1,0:T(8,128)(2,1)} %convolution_convert_fusion.1.refs_1_.refs_3_, ...), custom_call_target="tpu_custom_call" | custom-call | tf_op jit(solution)/shard_map/pallas_call | solution.py:124
  43.0 1.3 %slice.26 = f32[128,12]{1,0:T(8,128)S(1)} slice(f32[128,768]{1,0:T(8,128)} %get-tuple-element.6), slice={[0:128:1], [0:768:64]} | slice | bytes 12288 | tf_op jit(solution)/shard_map/slice | solution.py:134
  44.3 0.1 collective-permute-start.6
  44.4 0.1 copy.22
  44.6 0.2 copy.23
  44.7 0.1 copy.24
  44.8 0.2 copy.25
  45.0 0.0 copy-start.3
  45.0 11.5 %collective-permute-done.6 = bf16[128,768]{1,0:T(8,128)(2,1)} collective-permute-done((bf16[128,768]{1,0:T(8,128)(2,1)S(1)}, bf16[128,768]{1,0:T(8,128)(2,1)}, u32[]{:S(2)}, u32[]{:S(2)}) %collective-permute-start.6) | collective-permute-done | bytes 196640 | tf_op jit(solution)/shard_map/ppermute | solution.py:139
  56.6 1.3 %fusion.33 = bf16[128,768]{1,0:T(8,128)(2,1)S(1)} fusion(bf16[768,768]{1,0:T(8,128)(2,1)S(1)} %copy-done, bf16[128,768]{1,0:T(8,128)(2,1)S(1)} %copy-done.1, f32[128,768]{1,0:T(8,128)S(1)} %copy.23, f32[128,768]{1,0:T(8,128)S(1)} %copy.25, bf16[128,768]{1,0:T(8,128)(2,1)} %collective-permute-done.6, f32[128,768]{1,0:T(8,128)S(1)} %copy-done.9), kind=kOutput, calls=%fused_computation.33 | convolution fusion | flops 151977984 | bytes 2949120 | tf_op jit(solution)/shard_map/dot_general | solution.py:174
  57.9 0.0 copy-start.6
  57.9 0.3 convolution_convert_fusion.3
  58.2 0.2 reshape_reshape.6
  58.3 0.2 copy.28
  58.5 0.1 fusion.54
  58.6 0.1 collective-permute-start.7
  58.7 1.1 %collective-permute-done.7 = bf16[2,1,16,128]{3,2,1,0:T(8,128)(2,1)S(1)} collective-permute-done((bf16[2,1,16,128]{3,2,1,0:T(8,128)(2,1)S(1)}, bf16[2,1,16,128]{3,2,1,0:T(8,128)(2,1)S(1)}, u32[]{:S(2)}, u32[]{:S(2)}) %collective-permute-start.7) | collective-permute-done | bytes 8224 | tf_op jit(solution)/shard_map/ppermute | solution.py:24
  59.8 0.1 pad_maximum_fusion
  60.0 3.5 %collective-permute-start.8 = (bf16[1,34,16,128]{3,2,1,0:T(8,128)(2,1)S(1)}, bf16[1,34,16,128]{3,2,1,0:T(8,128)(2,1)S(1)}, u32[]{:S(2)}, u32[]{:S(2)}) collective-permute-start(bf16[1,34,16,128]{3,2,1,0:T(8,128)(2,1)S(1)} %get-tuple-element.14), channel_id=1, source_target_pairs={{0,2},{1,3},{2,4},{3,5},{4,6},{5,7},{6,8},{7,9},{8,10},{9,11},{10,... | collective-permute-start | bytes 417800 | tf_op jit(solution)/shard_map/ppermute | solution.py:20
  63.5 1.5 %collective-permute-start.9 = (bf16[1,34,16,128]{3,2,1,0:T(8,128)(2,1)S(1)}, bf16[1,34,16,128]{3,2,1,0:T(8,128)(2,1)S(1)}, u32[]{:S(2)}, u32[]{:S(2)}) collective-permute-start(bf16[1,34,16,128]{3,2,1,0:T(8,128)(2,1)S(1)} %get-tuple-element.15), channel_id=1, source_target_pairs={{2,0},{3,1},{4,2},{5,3},{6,4},{7,5},{8,6},{9,7},{10,8},{11,9},{12,... | collective-permute-start | bytes 417800 | tf_op jit(solution)/shard_map/ppermute | solution.py:20
  64.9 1.8 %collective-permute-done.8 = bf16[1,34,16,128]{3,2,1,0:T(8,128)(2,1)S(1)} collective-permute-done((bf16[1,34,16,128]{3,2,1,0:T(8,128)(2,1)S(1)}, bf16[1,34,16,128]{3,2,1,0:T(8,128)(2,1)S(1)}, u32[]{:S(2)}, u32[]{:S(2)}) %collective-permute-start.8) | collective-permute-done | bytes 139296 | tf_op jit(solution)/shard_map/ppermute | solution.py:20
  66.8 4.1 %collective-permute-done.9 = bf16[1,34,16,128]{3,2,1,0:T(8,128)(2,1)S(1)} collective-permute-done((bf16[1,34,16,128]{3,2,1,0:T(8,128)(2,1)S(1)}, bf16[1,34,16,128]{3,2,1,0:T(8,128)(2,1)S(1)}, u32[]{:S(2)}, u32[]{:S(2)}) %collective-permute-start.9) | collective-permute-done | bytes 139296 | tf_op jit(solution)/shard_map/ppermute | solution.py:20
  70.8 0.2 maximum_bitcast_fusion
  71.0 0.3 copy.35
  71.3 0.3 pad.clone
  71.6 0.0 copy-start.8
  71.6 0.0 copy-start.11
  71.6 0.1 copy.32
  71.7 0.1 slice.36
  71.9 0.7 copy-done.8
  72.6 2.9 %fusion.25 = bf16[2,32,8,3,64]{4,2,3,1,0:T(8,128)(2,1)S(1)} fusion(bf16[3,3,3,128,64]{3,4,2,1,0:T(8,128)(2,1)S(1)} %copy-done.8, bf16[4,34,1,7,2,128]{5,3,4,1,0,2:T(8,128)(2,1)S(1)} %slice.36, bf16[4,34,1,8,3,128]{5,3,4,1,0,2:T(8,128)(2,1)S(1)} %copy.32, pred[8,3]{0,1:T(4,128)(4,1)S(1)} %copy-done.11), kind=kOutput, calls=%fused_computation.29 | convolution fusion | flops 684146688 | bytes 1962008 | tf_op jit(solution)/shard_map/conv_general_dilated | solution.py:52
  75.5 0.1 copy.33
  75.6 0.8 %copy.34 = bf16[1,2,32,16,64]{4,3,2,1,0:T(8,128)(2,1)} copy(bf16[1,2,32,16,64]{4,2,3,1,0:T(8,128)(2,1)S(1)} %slice_bitcast_fusion) | data formatting | bytes 262144
  (31 shorter events, 0.3 us)
Async XLA Ops:
  0.6 55.9 %copy-start = (bf16[768,768]{1,0:T(8,128)(2,1)S(1)}, bf16[768,768]{1,0:T(8,128)(2,1)}, u32[]{:S(2)}) copy-start(bf16[768,768]{1,0:T(8,128)(2,1)} %param.10) | copy-start | bytes 3538948
  0.6 12.5 %copy-start.1 = (bf16[128,768]{1,0:T(8,128)(2,1)S(1)}, bf16[128,768]{1,0:T(8,128)(2,1)}, u32[]{:S(2)}) copy-start(bf16[128,768]{1,0:T(8,128)(2,1)} %param.7) | copy-start | bytes 589828
  0.7 12.5 %collective-permute-start = (bf16[128,768]{1,0:T(8,128)(2,1)}, bf16[128,768]{1,0:T(8,128)(2,1)S(1)}, u32[]{:S(2)}, u32[]{:S(2)}) collective-permute-start(bf16[128,768]{1,0:T(8,128)(2,1)} %param.7), channel_id=1, source_target_pairs={{0,2},{1,3},{2,0},{3,1},{4,6},{5,7},{6,4},{7,5},{8,10},{9,11},{10,... | collective-permute-start | bytes 589832 | tf_op jit(solution)/shard_map/ppermute | solution.py:139
  3.7 9.5 %collective-permute-start.1 = (bf16[128,768]{1,0:T(8,128)(2,1)}, bf16[128,768]{1,0:T(8,128)(2,1)S(1)}, u32[]{:S(2)}, u32[]{:S(2)}) collective-permute-start(bf16[128,768]{1,0:T(8,128)(2,1)} %param.7), channel_id=1, source_target_pairs={{0,4},{1,5},{2,6},{3,7},{4,0},{5,1},{6,2},{7,3},{8,12},{9,13},{10,... | collective-permute-start | bytes 589832 | tf_op jit(solution)/shard_map/ppermute | solution.py:139
  5.3 10.3 %collective-permute-start.2 = (bf16[128,768]{1,0:T(8,128)(2,1)}, bf16[128,768]{1,0:T(8,128)(2,1)S(1)}, u32[]{:S(2)}, u32[]{:S(2)}) collective-permute-start(bf16[128,768]{1,0:T(8,128)(2,1)} %param.7), channel_id=1, source_target_pairs={{0,6},{1,7},{2,4},{3,5},{4,2},{5,3},{6,0},{7,1},{8,14},{9,15},{10,... | collective-permute-start | bytes 589832 | tf_op jit(solution)/shard_map/ppermute | solution.py:139
  8.2 8.0 %copy-start.7 = (bf16[768,2304]{1,0:T(8,128)(2,1)S(1)}, bf16[768,2304]{1,0:T(8,128)(2,1)}, u32[]{:S(2)}) copy-start(bf16[768,2304]{1,0:T(8,128)(2,1)} %param.9) | copy-start | bytes 10616836
  10.1 6.1 %copy-start.4 = (bf16[128,768]{1,0:T(8,128)(2,1)}, bf16[128,768]{1,0:T(8,128)(2,1)S(1)}, u32[]{:S(2)}) copy-start(bf16[128,768]{1,0:T(8,128)(2,1)S(1)} %fusion.30.refs_0_) | copy-start | bytes 589828
  10.1 12.0 %collective-permute-start.4 = (bf16[128,768]{1,0:T(8,128)(2,1)S(1)}, bf16[128,768]{1,0:T(8,128)(2,1)S(1)}, u32[]{:S(2)}, u32[]{:S(2)}) collective-permute-start(bf16[128,768]{1,0:T(8,128)(2,1)S(1)} %fusion.30.refs_0_), channel_id=1, source_target_pairs={{0,8},{1,9},{2,10},{3,11},{4,12},{5,13},{6,14},{7,15},{8,0},{9,1},... | collective-permute-start | bytes 589832 | tf_op jit(solution)/shard_map/ppermute | solution.py:139
  15.6 3.3 %collective-permute-start.3 = (bf16[512,768]{1,0:T(8,128)(2,1)S(1)}, bf16[512,768]{1,0:T(8,128)(2,1)S(1)}, u32[]{:S(2)}, u32[]{:S(2)}) collective-permute-start(bf16[512,768]{1,0:T(8,128)(2,1)S(1)} %constant_dynamic-update-slice_fusion), channel_id=1, source_target_pairs={{0,1},{1,0},{2,3},{3,2},{4,5},{5,4},{6,7},{7,6},{8,9},{9,8},{10,11... | collective-permute-start | bytes 2359304 | tf_op jit(solution)/shard_map/ppermute | solution.py:139
  22.1 12.5 %copy-start.2 = (bf16[768,512]{1,0:T(8,128)(2,1)S(1)}, bf16[768,512]{1,0:T(8,128)(2,1)}, u32[]{:S(2)}) copy-start(bf16[768,512]{1,0:T(8,128)(2,1)} %param.12) | copy-start | bytes 2359300
  22.1 0.7 copy-start.5
  31.6 12.8 %collective-permute-start.5 = (f32[128,12]{1,0:T(8,128)S(1)}, f32[128,12]{1,0:T(8,128)S(1)}, u32[]{:S(2)}, u32[]{:S(2)}) collective-permute-start(f32[128,12]{1,0:T(8,128)S(1)} %slice.27), channel_id=1, source_target_pairs={{0,8},{1,9},{2,10},{3,11},{4,12},{5,13},{6,14},{7,15},{8,0},{9,1},... | collective-permute-start | bytes 18440 | tf_op jit(solution)/shard_map/ppermute | solution.py:139
  35.3 9.0 %copy-start.10 = (bf16[128,768]{1,0:T(8,128)(2,1)S(1)}, bf16[128,768]{1,0:T(8,128)(2,1)}, u32[]{:S(2)}) copy-start(bf16[128,768]{1,0:T(8,128)(2,1)} %get-tuple-element.9) | copy-start | bytes 589828
  43.0 13.6 %copy-start.9 = (f32[128,768]{1,0:T(8,128)S(1)}, f32[128,768]{1,0:T(8,128)}, u32[]{:S(2)}) copy-start(f32[128,768]{1,0:T(8,128)} %get-tuple-element.8) | copy-start | bytes 1179652
  44.3 12.3 %collective-permute-start.6 = (bf16[128,768]{1,0:T(8,128)(2,1)S(1)}, bf16[128,768]{1,0:T(8,128)(2,1)}, u32[]{:S(2)}, u32[]{:S(2)}) collective-permute-start(bf16[128,768]{1,0:T(8,128)(2,1)S(1)} %copy-done.10), channel_id=1, source_target_pairs={{0,8},{1,9},{2,10},{3,11},{4,12},{5,13},{6,14},{7,15},{8,0},{9,1},... | collective-permute-start | bytes 589832 | tf_op jit(solution)/shard_map/ppermute | solution.py:139
  45.0 12.8 %copy-start.3 = (bf16[768,512]{1,0:T(8,128)(2,1)S(1)}, bf16[768,512]{1,0:T(8,128)(2,1)}, u32[]{:S(2)}) copy-start(bf16[768,512]{1,0:T(8,128)(2,1)} %param.11) | copy-start | bytes 2359300
  57.9 2.1 %copy-start.6 = (bf16[128,768]{1,0:T(8,128)(2,1)}, bf16[128,768]{1,0:T(8,128)(2,1)S(1)}, u32[]{:S(2)}) copy-start(bf16[128,768]{1,0:T(8,128)(2,1)S(1)} %fusion.33) | copy-start | bytes 589828
  58.6 1.2 %collective-permute-start.7 = (bf16[2,1,16,128]{3,2,1,0:T(8,128)(2,1)S(1)}, bf16[2,1,16,128]{3,2,1,0:T(8,128)(2,1)S(1)}, u32[]{:S(2)}, u32[]{:S(2)}) collective-permute-start(bf16[2,1,16,128]{3,2,1,0:T(8,128)(2,1)S(1)} %fusion.54), channel_id=1, source_target_pairs={{0,1},{1,0},{2,3},{3,2},{4,5},{5,4},{6,7},{7,6},{8,9},{9,8},{10,11... | collective-permute-start | bytes 24584 | tf_op jit(solution)/shard_map/ppermute | solution.py:24
  60.0 6.8 %collective-permute-start.8 = (bf16[1,34,16,128]{3,2,1,0:T(8,128)(2,1)S(1)}, bf16[1,34,16,128]{3,2,1,0:T(8,128)(2,1)S(1)}, u32[]{:S(2)}, u32[]{:S(2)}) collective-permute-start(bf16[1,34,16,128]{3,2,1,0:T(8,128)(2,1)S(1)} %get-tuple-element.14), channel_id=1, source_target_pairs={{0,2},{1,3},{2,4},{3,5},{4,6},{5,7},{6,8},{7,9},{8,10},{9,11},{10,... | collective-permute-start | bytes 417800 | tf_op jit(solution)/shard_map/ppermute | solution.py:20
  63.5 7.4 %collective-permute-start.9 = (bf16[1,34,16,128]{3,2,1,0:T(8,128)(2,1)S(1)}, bf16[1,34,16,128]{3,2,1,0:T(8,128)(2,1)S(1)}, u32[]{:S(2)}, u32[]{:S(2)}) collective-permute-start(bf16[1,34,16,128]{3,2,1,0:T(8,128)(2,1)S(1)} %get-tuple-element.15), channel_id=1, source_target_pairs={{2,0},{3,1},{4,2},{5,3},{6,4},{7,5},{8,6},{9,7},{10,8},{11,9},{12,... | collective-permute-start | bytes 417800 | tf_op jit(solution)/shard_map/ppermute | solution.py:20
  71.6 1.0 %copy-start.8 = (bf16[3,3,3,128,64]{3,4,2,1,0:T(8,128)(2,1)S(1)}, bf16[3,3,3,128,64]{3,4,2,1,0:T(8,128)(2,1)}, u32[]{:S(2)}) copy-start(bf16[3,3,3,128,64]{3,4,2,1,0:T(8,128)(2,1)} %param.13) | copy-start | bytes 1327108
  71.6 1.0 %copy-start.11 = (pred[8,3]{0,1:T(4,128)(4,1)S(1)}, pred[8,3]{0,1:T(4,128)(4,1)}, u32[]{:S(2)}) copy-start(pred[8,3]{0,1:T(4,128)(4,1)} %constant.41) | copy-start | bytes 76

commit v4 on v3

--- a/solution.py
+++ b/solution.py
@@ -4,6 +4,7 @@
 import jax.numpy as jnp
 from jax import lax
 from jax.experimental import pallas as pl
+from jax.experimental.pallas import tpu as pltpu
 from jax.sharding import PartitionSpec as P
 
 HEADS = 12
@@ -65,17 +66,27 @@
     return shifted(plane, "seq", offset)
 
 
-def attention_kernel(*refs, head_size, score_scale, chunks):
+def attention_kernel(*refs, head_size, score_scale, chunks, whole_output, ordered):
+    if ordered:
+        refs = refs[:-3] + refs[-2:]
     q_ref = refs[0]
     k_refs = refs[1 : 1 + chunks]
     v_refs = refs[1 + chunks : 1 + 2 * chunks]
     o_ref, lse_ref = refs[-2:]
+    step = pl.program_id(0)
     pair = q_ref.shape[-1]
     lane = lax.broadcasted_iota(jnp.int32, (1, pair), 1)
+    stat_lane = lax.broadcasted_iota(jnp.int32, (1, lse_ref.shape[-1]), 1)
+
+    @pl.when(step == 0)
+    def _():
+        lse_ref[...] = jnp.zeros_like(lse_ref)
+
     q = q_ref[...]
     result = None
-    log_sum = None
-    for h in range(pair // head_size):
+    log_sum = lse_ref[...]
+    heads = pair // head_size
+    for h in range(heads):
         in_head = (lane >= h * head_size) & (lane < (h + 1) * head_size)
         q_h = jnp.where(in_head, q, jnp.zeros_like(q))
         scores = [
@@ -101,37 +112,58 @@
         head_out = numerator / denominator
         head_lse = row_max + jnp.log(denominator)
         result = head_out if result is None else jnp.where(in_head, head_out, result)
-        log_sum = (
-            jnp.broadcast_to(head_lse, result.shape)
-            if log_sum is None
-            else jnp.where(in_head, head_lse, log_sum)
-        )
-    o_ref[...] = result.astype(o_ref.dtype)
+        log_sum = jnp.where(stat_lane == step * heads + h, head_lse, log_sum)
+    if whole_output:
+        o_ref[:, pl.ds(pl.multiple_of(step * pair, pair), pair)] = result.astype(o_ref.dtype)
+    else:
+        o_ref[...] = result.astype(o_ref.dtype)
     lse_ref[...] = log_sum
 
 
-def attention(queries, kv_chunks, head_size, score_scale, out_dtype):
+def attention(queries, kv_chunks, head_size, score_scale, out_dtype, whole_output, after=None):
     token_count, model_width = queries.shape
     pair = 2 * head_size
     pairs = model_width // pair
     chunks = len(kv_chunks)
     kernel = lambda *refs: attention_kernel(
-        *refs, head_size=head_size, score_scale=score_scale, chunks=chunks
+        *refs,
+        head_size=head_size,
+        score_scale=score_scale,
+        chunks=chunks,
+        whole_output=whole_output,
+        ordered=after is not None,
     )
     key_specs = [pl.BlockSpec((c.shape[0], pair), lambda j: (0, j)) for c in kv_chunks]
     value_specs = [pl.BlockSpec((c.shape[0], pair), lambda j: (0, j + pairs)) for c in kv_chunks]
     row_spec = pl.BlockSpec((token_count, pair), lambda j: (0, j))
+    stat_width = 128
+    if whole_output:
+        out_specs = [
+            pl.BlockSpec(memory_space=pltpu.VMEM),
+            pl.BlockSpec(memory_space=pltpu.VMEM),
+        ]
+    else:
+        out_specs = [row_spec, pl.BlockSpec((token_count, stat_width), lambda j: (0, 0))]
+    extra = [] if after is None else [after]
+    extra_specs = [pl.BlockSpec(memory_space=pl.ANY) for _ in extra]
+    keys = sum(c.shape[0] for c in kv_chunks)
+    cost = pl.CostEstimate(
+        flops=8 * token_count * keys * model_width,
+        transcendentals=token_count * keys * (model_width // head_size),
+        bytes_accessed=2 * keys * 2 * model_width + 8 * token_count * model_width,
+    )
     output, log_sum = pl.pallas_call(
         kernel,
         grid=(pairs,),
-        in_specs=[row_spec] + key_specs + value_specs,
-        out_specs=[row_spec, row_spec],
+        cost_estimate=cost,
+        in_specs=[row_spec] + key_specs + value_specs + extra_specs,
+        out_specs=out_specs,
         out_shape=[
             jax.ShapeDtypeStruct((token_count, model_width), out_dtype),
-            jax.ShapeDtypeStruct((token_count, model_width), jnp.float32),
+            jax.ShapeDtypeStruct((token_count, stat_width), jnp.float32),
         ],
-    )(queries, *kv_chunks, *kv_chunks)
-    return output, log_sum[:, ::head_size]
+    )(queries, *kv_chunks, *kv_chunks, *extra)
+    return output, log_sum
 
 
 def exchanged(x, mask):
@@ -157,14 +189,18 @@
     kv_weight = projection[:, model_width:]
     kv_chunks = [projected(mine, norm_gain, kv_weight), projected(theirs, norm_gain, kv_weight)]
     remote_out, remote_lse = attention(
-        mirrored_queries, kv_chunks, head_size, score_scale, jnp.bfloat16
-    )
+        mirrored_queries, kv_chunks, head_size, score_scale, jnp.float32, False
+    )
+    remote_out = remote_out.astype(jnp.bfloat16)
     other_out = exchanged(remote_out, half)
     other_lse = exchanged(remote_lse, half)
-    own_out, own_lse = attention(queries, kv_chunks, head_size, score_scale, jnp.float32)
+    own_out, own_lse = attention(
+        queries, kv_chunks, head_size, score_scale, jnp.float32, False, after=remote_out
+    )
+    heads = model_width // head_size
     top = jnp.maximum(own_lse, other_lse)
-    own_weight = jnp.repeat(jnp.exp(own_lse - top), head_size, axis=1)
-    other_weight = jnp.repeat(jnp.exp(other_lse - top), head_size, axis=1)
+    own_weight = jnp.repeat(jnp.exp(own_lse - top)[:, :heads], head_size, axis=1)
+    other_weight = jnp.repeat(jnp.exp(other_lse - top)[:, :heads], head_size, axis=1)
     attended = (
         (own_weight * own_out + other_weight * other_out.astype(jnp.float32))
         / (own_weight + other_weight)

time: 77 us -> 68.8 us (0.89)
  waiting for transfers between devices: 20.9 us -> 11.7 us
  other arithmetic: 4.44 us -> 7.2 us
  local copies, waits for them, and re-layouts: 7.09 us -> 4.53 us
  starting transfers between devices: 15.8 us -> 16.7 us
    ppermute x7, waiting for transfers between devices: 13.9 us -> 4.65 us  [exchanged(): return lax.ppermute(x, 'seq', [(i, i ^ mask) for i in range(devices)])]
    slice x2, local copies, waits for them, and re-layouts: 2.56 us -> 0.12 us  [the longest x1 0.06 us: body(): jnp.exp(own_lse - top)[:, :heads]]
    ppermute x2, starting transfers between devices: 4.93 us -> 5.96 us  [shifted(): return lax.ppermute(block, axis, route)]
    convert_element_type x0 -> x1, other arithmetic: none -> 1.02 us  [body(): remote_out = remote_out.astype(jnp.bfloat16)]
    max x0 -> x1, other arithmetic: none -> 0.9 us  [body(): top = jnp.maximum(own_lse, other_lse)]
    exp x1, other arithmetic: 0.03 us -> 0.86 us  [body(): jnp.exp(other_lse - top)[:, :heads]]
  transfers between devices with their start and end apart: 10 -> 10, of which waited for: 5 -> 5; matrix products, arithmetic and copies ran while one was open for 18% -> 21% of each run, Pallas kernels for 10% -> 11%
where the time goes in v4:
time: 68.8 us; the launch traced here: 68.2 us
  starting transfers between devices  16.7 us (24%)
  Pallas kernels  15.3 us (22%)
  matrix products  11.8 us (17%)
  waiting for transfers between devices  11.7 us (17%)
  other arithmetic  7.2 us (10%)
  local copies, waits for them, and re-layouts  4.53 us (7%)
  between operations  1.03 us (1%)
    pallas_call x2, Pallas kernels, attention(): pl.pallas_call(kernel, grid=(pairs,), cost_estimate=cost, in_specs=[row_s...  15.3 us
    ppermute x7, starting transfers between devices, exchanged(): return lax.ppermute(x, 'seq', [(i, i ^ mask) for i in range(devices)])  10.7 us
    dot_general x3, matrix products, projected(): jnp.dot(normed, weight, preferred_element_type=jnp.float32)  7.07 us
    ppermute x2, starting transfers between devices, shifted(): return lax.ppermute(block, axis, route)  5.96 us
    ppermute x2, waiting for transfers between devices, shifted(): return lax.ppermute(block, axis, route)  5.88 us
    ppermute x7, waiting for transfers between devices, exchanged(): return lax.ppermute(x, 'seq', [(i, i ^ mask) for i in range(devices)])  4.65 us
    conv_general_dilated x1, matrix products, convolve(): lax.conv_general_dilated(full_xy[None], conv_kernel, window_strides=(1, 1...  2.9 us
    unnamed x29, local copies, waits for them, and re-layouts  2.6 us
  transfers between devices with their start and end apart: 10, of which 5 were waited for; matrix products, arithmetic and copies ran while one was open for 21% of the time, Pallas kernels for 11%

profile of v4, /device:TPU:0, one launch (start us, length us, event | category | flops | bytes accessed | tf_op | source)
XLA Modules:
  0.0 68.2 jit_solution(3765319817258632082)
XLA Ops:
  0.6 0.0 copy-start
  0.6 0.0 copy-start.1
  0.7 3.1 %collective-permute-start = (bf16[128,768]{1,0:T(8,128)(2,1)}, bf16[128,768]{1,0:T(8,128)(2,1)S(1)}, u32[]{:S(2)}, u32[]{:S(2)}) collective-permute-start(bf16[128,768]{1,0:T(8,128)(2,1)} %param.7), channel_id=1, source_target_pairs={{0,2},{1,3},{2,0},{3,1},{4,6},{5,7},{6,4},{7,5},{8,10},{9,11},{10,... | collective-permute-start | bytes 589832 | tf_op jit(solution)/shard_map/ppermute | solution.py:171
  3.7 1.6 %collective-permute-start.1 = (bf16[128,768]{1,0:T(8,128)(2,1)}, bf16[128,768]{1,0:T(8,128)(2,1)S(1)}, u32[]{:S(2)}, u32[]{:S(2)}) collective-permute-start(bf16[128,768]{1,0:T(8,128)(2,1)} %param.7), channel_id=1, source_target_pairs={{0,4},{1,5},{2,6},{3,7},{4,0},{5,1},{6,2},{7,3},{8,12},{9,13},{10,... | collective-permute-start | bytes 589832 | tf_op jit(solution)/shard_map/ppermute | solution.py:171
  5.3 0.0 collective-permute-start.2
  5.3 1.1 %convert_reduce_fusion.2 = f32[128]{0:T(128)S(1)} fusion(bf16[128,768]{1,0:T(8,128)(2,1)} %param.7), kind=kLoop, calls=%fused_computation.44 | loop fusion | flops 196480 | bytes 197120 | tf_op jit(solution)/shard_map/reduce_sum | solution.py:30
  6.4 0.7 %convert_element_type.56 = f32[768]{0:T(1024)S(1)} convert(bf16[768]{0:T(1024)(128)(2,1)} %param.8) | non-fusion elementwise | flops 768 | bytes 4608 | tf_op jit(solution)/shard_map/convert_element_type | solution.py:33
  7.1 1.1 %fusion.45 = f32[128]{0:T(128)S(1)} fusion(bf16[128,768]{1,0:T(8,128)(2,1)} %param.7, f32[128]{0:T(128)S(1)} %broadcast_multiply_fusion.2), kind=kLoop, calls=%fused_computation.48 | loop fusion | flops 393088 | bytes 197632 | tf_op jit(solution)/shard_map/reduce_sum | solution.py:32
  8.2 1.8 %fusion.30.refs_0_ = bf16[128,768]{1,0:T(8,128)(2,1)S(1)} fusion(bf16[768,2304]{1,0:T(8,128)(2,1)} %param.9, bf16[128,768]{1,0:T(8,128)(2,1)} %param.7, f32[768]{0:T(1024)S(1)} %convert_element_type.56, f32[128]{0:T(128)S(1)} %add_rsqrt_fusion.2, f32[128]{0:T(128)S(1)} %broadcast_multiply_fusion.2), kind=kOutput, calls=%fused_computation.32 | convolution fusion | flops 151584768 | bytes 1576960 | tf_op jit(solution)/shard_map/dot_general | solution.py:176
  10.0 0.0 copy-start.5
  10.0 3.0 %collective-permute-start.4 = (bf16[128,768]{1,0:T(8,128)(2,1)S(1)}, bf16[128,768]{1,0:T(8,128)(2,1)S(1)}, u32[]{:S(2)}, u32[]{:S(2)}) collective-permute-start(bf16[128,768]{1,0:T(8,128)(2,1)S(1)} %fusion.30.refs_0_), channel_id=1, source_target_pairs={{0,8},{1,9},{2,10},{3,11},{4,12},{5,13},{6,14},{7,15},{8,0},{9,1},... | collective-permute-start | bytes 589832 | tf_op jit(solution)/shard_map/ppermute | solution.py:171
  13.0 0.3 convolution_convert_fusion.2
  13.3 0.2 reshape_reshape.7
  13.5 0.0 copy-start.8
  13.5 0.2 copy.16
  13.7 0.0 collective-permute-done
  13.8 0.0 collective-permute-done.1
  13.8 2.0 %collective-permute-done.2 = bf16[128,768]{1,0:T(8,128)(2,1)S(1)} collective-permute-done((bf16[128,768]{1,0:T(8,128)(2,1)}, bf16[128,768]{1,0:T(8,128)(2,1)S(1)}, u32[]{:S(2)}, u32[]{:S(2)}) %collective-permute-start.2) | collective-permute-done | bytes 196640 | tf_op jit(solution)/shard_map/ppermute | solution.py:171
  15.9 0.1 collective-permute-start.3
  15.9 0.2 convert_reduce_fusion.1
  16.1 0.4 fusion.10
  16.5 2.7 %convolution_convert_fusion.1.refs_1_.refs_3_ = bf16[512,1536]{1,0:T(8,128)(2,1)} fusion(bf16[768,2304]{1,0:T(8,128)(2,1)S(1)} %copy-done.8, bf16[512,768]{1,0:T(8,128)(2,1)S(1)} %constant_dynamic-update-slice_fusion, f32[768]{0:T(1024)S(1)} %convert_element_type.56, f32[512]{0:T(512)S(1)} %add_rsqrt_fusion.1, f32[512]{0:T(512)S(1)} %broadcast_multiply_fusion.1), kind=kOutput, calls=%fused_computation.1 | convolution fusion | flops 1210712064 | bytes 4726784 | tf_op jit(solution)/shard_map/dot_general | solution.py:176
  19.2 0.2 convert_reduce_fusion
  19.4 0.4 fusion.7
  19.7 2.7 %convolution_convert_fusion.refs_2_.refs_4_ = bf16[512,1536]{1,0:T(8,128)(2,1)} fusion(bf16[768,2304]{1,0:T(8,128)(2,1)S(1)} %copy-done.8, bf16[512,768]{1,0:T(8,128)(2,1)S(1)} %collective-permute-done.3, f32[512]{0:T(512)S(1)} %add_rsqrt_fusion, f32[512]{0:T(512)S(1)} %broadcast_multiply_fusion, f32[768]{0:T(1024)S(1)} %convert_element_type.56), kind=kOutput, calls=%fused_computation | convolution fusion | flops 1210712064 | bytes 4726784 | tf_op jit(solution)/shard_map/dot_general | solution.py:176
  22.4 0.7 copy-done.6
  23.1 7.6 %shard_map.86 = (f32[128,768]{1,0:T(8,128)}, f32[128,128]{1,0:T(8,128)}) custom-call(bf16[128,768]{1,0:T(8,128)(2,1)} %copy-done.6, bf16[512,1536]{1,0:T(8,128)(2,1)} %convolution_convert_fusion.1.refs_1_.refs_3_, bf16[512,1536]{1,0:T(8,128)(2,1)} %convolution_convert_fusion.refs_2_.refs_4_, bf16[512,1536]{1,0:T(8,128)(2,1)} %convolution_convert_fusion.1.refs_1_.refs_3_, ...), custom_call_target="tpu_custom_call" | custom-call | flops 805306368 | bytes 3932160 | tf_op jit(solution)/shard_map/pallas_call | solution.py:155
  30.7 1.0 %convert_element_type.65.refs_5_ = bf16[128,768]{1,0:T(8,128)(2,1)S(1)} convert(f32[128,768]{1,0:T(8,128)} %get-tuple-element.6) | non-fusion elementwise | flops 98304 | bytes 589824 | tf_op jit(solution)/shard_map/convert_element_type | solution.py:194
  31.7 0.0 copy-start.2
  31.7 2.7 %collective-permute-start.5 = (f32[128,128]{1,0:T(8,128)}, f32[128,128]{1,0:T(8,128)S(1)}, u32[]{:S(2)}, u32[]{:S(2)}) collective-permute-start(f32[128,128]{1,0:T(8,128)} %get-tuple-element.8), channel_id=1, source_target_pairs={{0,8},{1,9},{2,10},{3,11},{4,12},{5,13},{6,14},{7,15},{8,0},{9,1},... | collective-permute-start | bytes 196616 | tf_op jit(solution)/shard_map/ppermute | solution.py:171
  34.4 0.3 collective-permute-start.6
  34.7 7.6 %shard_map.87 = (f32[128,768]{1,0:T(8,128)}, f32[128,128]{1,0:T(8,128)}) custom-call(bf16[128,768]{1,0:T(8,128)(2,1)} %copy-done.5, bf16[512,1536]{1,0:T(8,128)(2,1)} %convolution_convert_fusion.1.refs_1_.refs_3_, bf16[512,1536]{1,0:T(8,128)(2,1)} %convolution_convert_fusion.refs_2_.refs_4_, bf16[512,1536]{1,0:T(8,128)(2,1)} %convolution_convert_fusion.1.refs_1_.refs_3_, ...), custom_call_target="tpu_custom_call" | custom-call | flops 805306368 | bytes 3932160 | tf_op jit(solution)/shard_map/pallas_call | solution.py:155
  42.4 0.9 %max.3 = f32[128,128]{1,0:T(8,128)S(1)} maximum(f32[128,128]{1,0:T(8,128)} %get-tuple-element.7, f32[128,128]{1,0:T(8,128)S(1)} %collective-permute-done.5) | non-fusion elementwise | flops 16384 | bytes 196608 | tf_op jit(solution)/shard_map/max | solution.py:201
  43.3 0.9 %fusion.52 = (f32[128,12]{1,0:T(8,128)S(1)}, f32[128,12]{1,0:T(8,128)S(1)}) fusion(f32[128,128]{1,0:T(8,128)S(1)} %collective-permute-done.5, f32[128,128]{1,0:T(8,128)S(1)} %max.3, f32[128,128]{1,0:T(8,128)} %get-tuple-element.7), kind=kLoop, calls=%fused_computation.58 | loop fusion | flops 3072 | bytes 30720 | tf_op jit(solution)/shard_map/exp | solution.py:203
  44.1 0.1 copy.9
  44.3 0.2 copy.10
  44.4 0.1 copy.11
  44.5 0.2 copy.12
  44.7 0.0 copy-start.4
  44.7 2.6 %collective-permute-done.6 = bf16[128,768]{1,0:T(8,128)(2,1)} collective-permute-done((bf16[128,768]{1,0:T(8,128)(2,1)S(1)}, bf16[128,768]{1,0:T(8,128)(2,1)}, u32[]{:S(2)}, u32[]{:S(2)}) %collective-permute-start.6) | collective-permute-done | bytes 196640 | tf_op jit(solution)/shard_map/ppermute | solution.py:171
  47.4 1.3 %fusion.33 = bf16[128,768]{1,0:T(8,128)(2,1)S(1)} fusion(bf16[768,768]{1,0:T(8,128)(2,1)S(1)} %copy-done, bf16[128,768]{1,0:T(8,128)(2,1)S(1)} %copy-done.1, f32[128,768]{1,0:T(8,128)S(1)} %copy.10, f32[128,768]{1,0:T(8,128)S(1)} %copy.12, bf16[128,768]{1,0:T(8,128)(2,1)} %collective-permute-done.6, f32[128,768]{1,0:T(8,128)S(1)} %copy-done.10), kind=kOutput, calls=%fused_computation.33 | convolution fusion | flops 151977984 | bytes 2949120 | tf_op jit(solution)/shard_map/dot_general | solution.py:210
  48.6 0.0 copy-start.7
  48.7 0.3 convolution_convert_fusion.3
  48.9 0.2 reshape_reshape.6
  49.1 0.2 copy.15
  49.3 0.1 fusion.54
  49.4 0.0 collective-permute-start.7
  49.4 1.1 %collective-permute-done.7 = bf16[2,1,16,128]{3,2,1,0:T(8,128)(2,1)S(1)} collective-permute-done((bf16[2,1,16,128]{3,2,1,0:T(8,128)(2,1)S(1)}, bf16[2,1,16,128]{3,2,1,0:T(8,128)(2,1)S(1)}, u32[]{:S(2)}, u32[]{:S(2)}) %collective-permute-start.7) | collective-permute-done | bytes 8224 | tf_op jit(solution)/shard_map/ppermute | solution.py:25
  50.6 0.1 pad_maximum_fusion
  50.8 4.5 %collective-permute-start.8 = (bf16[1,34,16,128]{3,2,1,0:T(8,128)(2,1)S(1)}, bf16[1,34,16,128]{3,2,1,0:T(8,128)(2,1)S(1)}, u32[]{:S(2)}, u32[]{:S(2)}) collective-permute-start(bf16[1,34,16,128]{3,2,1,0:T(8,128)(2,1)S(1)} %get-tuple-element.12), channel_id=1, source_target_pairs={{0,2},{1,3},{2,4},{3,5},{4,6},{5,7},{6,8},{7,9},{8,10},{9,11},{10,... | collective-permute-start | bytes 417800 | tf_op jit(solution)/shard_map/ppermute | solution.py:21
  55.3 1.5 %collective-permute-start.9 = (bf16[1,34,16,128]{3,2,1,0:T(8,128)(2,1)S(1)}, bf16[1,34,16,128]{3,2,1,0:T(8,128)(2,1)S(1)}, u32[]{:S(2)}, u32[]{:S(2)}) collective-permute-start(bf16[1,34,16,128]{3,2,1,0:T(8,128)(2,1)S(1)} %get-tuple-element.13), channel_id=1, source_target_pairs={{2,0},{3,1},{4,2},{5,3},{6,4},{7,5},{8,6},{9,7},{10,8},{11,9},{12,... | collective-permute-start | bytes 417800 | tf_op jit(solution)/shard_map/ppermute | solution.py:21
  56.7 1.8 %collective-permute-done.8 = bf16[1,34,16,128]{3,2,1,0:T(8,128)(2,1)S(1)} collective-permute-done((bf16[1,34,16,128]{3,2,1,0:T(8,128)(2,1)S(1)}, bf16[1,34,16,128]{3,2,1,0:T(8,128)(2,1)S(1)}, u32[]{:S(2)}, u32[]{:S(2)}) %collective-permute-start.8) | collective-permute-done | bytes 139296 | tf_op jit(solution)/shard_map/ppermute | solution.py:21
  58.6 4.1 %collective-permute-done.9 = bf16[1,34,16,128]{3,2,1,0:T(8,128)(2,1)S(1)} collective-permute-done((bf16[1,34,16,128]{3,2,1,0:T(8,128)(2,1)S(1)}, bf16[1,34,16,128]{3,2,1,0:T(8,128)(2,1)S(1)}, u32[]{:S(2)}, u32[]{:S(2)}) %collective-permute-start.9) | collective-permute-done | bytes 139296 | tf_op jit(solution)/shard_map/ppermute | solution.py:21
  62.6 0.2 maximum_bitcast_fusion
  62.8 0.3 copy.22
  63.1 0.3 pad.clone
  63.4 0.0 copy-start.9
  63.4 0.0 copy-start.11
  63.4 0.1 copy.19
  63.5 0.1 slice.40
  63.7 0.7 %copy-done.9 = bf16[3,3,3,128,64]{3,4,2,1,0:T(8,128)(2,1)S(1)} copy-done((bf16[3,3,3,128,64]{3,4,2,1,0:T(8,128)(2,1)S(1)}, bf16[3,3,3,128,64]{3,4,2,1,0:T(8,128)(2,1)}, u32[]{:S(2)}) %copy-start.9) | copy-done | bytes 442392
  64.4 2.9 %fusion.25 = bf16[2,32,8,3,64]{4,2,3,1,0:T(8,128)(2,1)S(1)} fusion(bf16[3,3,3,128,64]{3,4,2,1,0:T(8,128)(2,1)S(1)} %copy-done.9, bf16[4,34,1,7,2,128]{5,3,4,1,0,2:T(8,128)(2,1)S(1)} %slice.40, bf16[4,34,1,8,3,128]{5,3,4,1,0,2:T(8,128)(2,1)S(1)} %copy.19, pred[8,3]{0,1:T(4,128)(4,1)S(1)} %copy-done.11), kind=kOutput, calls=%fused_computation.29 | convolution fusion | flops 684146688 | bytes 1962008 | tf_op jit(solution)/shard_map/conv_general_dilated | solution.py:53
  67.3 0.1 copy.20
  67.4 0.8 %copy.21 = bf16[1,2,32,16,64]{4,3,2,1,0:T(8,128)(2,1)} copy(bf16[1,2,32,16,64]{4,2,3,1,0:T(8,128)(2,1)S(1)} %slice_bitcast_fusion) | data formatting | bytes 262144
  (31 shorter events, 0.3 us)
Async XLA Ops:
  0.6 46.7 %copy-start = (bf16[768,768]{1,0:T(8,128)(2,1)S(1)}, bf16[768,768]{1,0:T(8,128)(2,1)}, u32[]{:S(2)}) copy-start(bf16[768,768]{1,0:T(8,128)(2,1)} %param.10) | copy-start | bytes 3538948
  0.6 12.4 %copy-start.1 = (bf16[128,768]{1,0:T(8,128)(2,1)S(1)}, bf16[128,768]{1,0:T(8,128)(2,1)}, u32[]{:S(2)}) copy-start(bf16[128,768]{1,0:T(8,128)(2,1)} %param.7) | copy-start | bytes 589828
  0.7 12.4 %copy-start.3 = (bf16[768,512]{1,0:T(8,128)(2,1)S(1)}, bf16[768,512]{1,0:T(8,128)(2,1)}, u32[]{:S(2)}) copy-start(bf16[768,512]{1,0:T(8,128)(2,1)} %param.12) | copy-start | bytes 2359300
  0.7 13.1 %collective-permute-start = (bf16[128,768]{1,0:T(8,128)(2,1)}, bf16[128,768]{1,0:T(8,128)(2,1)S(1)}, u32[]{:S(2)}, u32[]{:S(2)}) collective-permute-start(bf16[128,768]{1,0:T(8,128)(2,1)} %param.7), channel_id=1, source_target_pairs={{0,2},{1,3},{2,0},{3,1},{4,6},{5,7},{6,4},{7,5},{8,10},{9,11},{10,... | collective-permute-start | bytes 589832 | tf_op jit(solution)/shard_map/ppermute | solution.py:171
  3.7 10.1 %collective-permute-start.1 = (bf16[128,768]{1,0:T(8,128)(2,1)}, bf16[128,768]{1,0:T(8,128)(2,1)S(1)}, u32[]{:S(2)}, u32[]{:S(2)}) collective-permute-start(bf16[128,768]{1,0:T(8,128)(2,1)} %param.7), channel_id=1, source_target_pairs={{0,4},{1,5},{2,6},{3,7},{4,0},{5,1},{6,2},{7,3},{8,12},{9,13},{10,... | collective-permute-start | bytes 589832 | tf_op jit(solution)/shard_map/ppermute | solution.py:171
  5.3 10.5 %collective-permute-start.2 = (bf16[128,768]{1,0:T(8,128)(2,1)}, bf16[128,768]{1,0:T(8,128)(2,1)S(1)}, u32[]{:S(2)}, u32[]{:S(2)}) collective-permute-start(bf16[128,768]{1,0:T(8,128)(2,1)} %param.7), channel_id=1, source_target_pairs={{0,6},{1,7},{2,4},{3,5},{4,2},{5,3},{6,0},{7,1},{8,14},{9,15},{10,... | collective-permute-start | bytes 589832 | tf_op jit(solution)/shard_map/ppermute | solution.py:171
  10.0 3.8 %copy-start.5 = (bf16[128,768]{1,0:T(8,128)(2,1)}, bf16[128,768]{1,0:T(8,128)(2,1)S(1)}, u32[]{:S(2)}) copy-start(bf16[128,768]{1,0:T(8,128)(2,1)S(1)} %fusion.30.refs_0_) | copy-start | bytes 589828
  10.0 12.4 %collective-permute-start.4 = (bf16[128,768]{1,0:T(8,128)(2,1)S(1)}, bf16[128,768]{1,0:T(8,128)(2,1)S(1)}, u32[]{:S(2)}, u32[]{:S(2)}) collective-permute-start(bf16[128,768]{1,0:T(8,128)(2,1)S(1)} %fusion.30.refs_0_), channel_id=1, source_target_pairs={{0,8},{1,9},{2,10},{3,11},{4,12},{5,13},{6,14},{7,15},{8,0},{9,1},... | collective-permute-start | bytes 589832 | tf_op jit(solution)/shard_map/ppermute | solution.py:171
  13.5 3.0 %copy-start.8 = (bf16[768,2304]{1,0:T(8,128)(2,1)S(1)}, bf16[768,2304]{1,0:T(8,128)(2,1)}, u32[]{:S(2)}) copy-start(bf16[768,2304]{1,0:T(8,128)(2,1)} %param.9) | copy-start | bytes 10616836
  15.9 3.3 %collective-permute-start.3 = (bf16[512,768]{1,0:T(8,128)(2,1)S(1)}, bf16[512,768]{1,0:T(8,128)(2,1)S(1)}, u32[]{:S(2)}, u32[]{:S(2)}) collective-permute-start(bf16[512,768]{1,0:T(8,128)(2,1)S(1)} %constant_dynamic-update-slice_fusion), channel_id=1, source_target_pairs={{0,1},{1,0},{2,3},{3,2},{4,5},{5,4},{6,7},{7,6},{8,9},{9,8},{10,11... | collective-permute-start | bytes 2359304 | tf_op jit(solution)/shard_map/ppermute | solution.py:171
  22.4 0.7 copy-start.6
  31.7 3.0 %copy-start.2 = (bf16[128,768]{1,0:T(8,128)(2,1)}, bf16[128,768]{1,0:T(8,128)(2,1)S(1)}, u32[]{:S(2)}) copy-start(bf16[128,768]{1,0:T(8,128)(2,1)S(1)} %convert_element_type.65.refs_5_) | copy-start | bytes 589828
  31.7 10.6 %collective-permute-start.5 = (f32[128,128]{1,0:T(8,128)}, f32[128,128]{1,0:T(8,128)S(1)}, u32[]{:S(2)}, u32[]{:S(2)}) collective-permute-start(f32[128,128]{1,0:T(8,128)} %get-tuple-element.8), channel_id=1, source_target_pairs={{0,8},{1,9},{2,10},{3,11},{4,12},{5,13},{6,14},{7,15},{8,0},{9,1},... | collective-permute-start | bytes 196616 | tf_op jit(solution)/shard_map/ppermute | solution.py:171
  34.4 12.9 %collective-permute-start.6 = (bf16[128,768]{1,0:T(8,128)(2,1)S(1)}, bf16[128,768]{1,0:T(8,128)(2,1)}, u32[]{:S(2)}, u32[]{:S(2)}) collective-permute-start(bf16[128,768]{1,0:T(8,128)(2,1)S(1)} %convert_element_type.65.refs_5_), channel_id=1, source_target_pairs={{0,8},{1,9},{2,10},{3,11},{4,12},{5,13},{6,14},{7,15},{8,0},{9,1},... | collective-permute-start | bytes 589832 | tf_op jit(solution)/shard_map/ppermute | solution.py:171
  42.4 5.0 %copy-start.10 = (f32[128,768]{1,0:T(8,128)S(1)}, f32[128,768]{1,0:T(8,128)}, u32[]{:S(2)}) copy-start(f32[128,768]{1,0:T(8,128)} %get-tuple-element.9) | copy-start | bytes 1179652
  44.7 3.9 %copy-start.4 = (bf16[768,512]{1,0:T(8,128)(2,1)S(1)}, bf16[768,512]{1,0:T(8,128)(2,1)}, u32[]{:S(2)}) copy-start(bf16[768,512]{1,0:T(8,128)(2,1)} %param.11) | copy-start | bytes 2359300
  48.6 2.1 %copy-start.7 = (bf16[128,768]{1,0:T(8,128)(2,1)}, bf16[128,768]{1,0:T(8,128)(2,1)S(1)}, u32[]{:S(2)}) copy-start(bf16[128,768]{1,0:T(8,128)(2,1)S(1)} %fusion.33) | copy-start | bytes 589828
  49.4 1.2 %collective-permute-start.7 = (bf16[2,1,16,128]{3,2,1,0:T(8,128)(2,1)S(1)}, bf16[2,1,16,128]{3,2,1,0:T(8,128)(2,1)S(1)}, u32[]{:S(2)}, u32[]{:S(2)}) collective-permute-start(bf16[2,1,16,128]{3,2,1,0:T(8,128)(2,1)S(1)} %fusion.54), channel_id=1, source_target_pairs={{0,1},{1,0},{2,3},{3,2},{4,5},{5,4},{6,7},{7,6},{8,9},{9,8},{10,11... | collective-permute-start | bytes 24584 | tf_op jit(solution)/shard_map/ppermute | solution.py:25
  50.8 7.8 %collective-permute-start.8 = (bf16[1,34,16,128]{3,2,1,0:T(8,128)(2,1)S(1)}, bf16[1,34,16,128]{3,2,1,0:T(8,128)(2,1)S(1)}, u32[]{:S(2)}, u32[]{:S(2)}) collective-permute-start(bf16[1,34,16,128]{3,2,1,0:T(8,128)(2,1)S(1)} %get-tuple-element.12), channel_id=1, source_target_pairs={{0,2},{1,3},{2,4},{3,5},{4,6},{5,7},{6,8},{7,9},{8,10},{9,11},{10,... | collective-permute-start | bytes 417800 | tf_op jit(solution)/shard_map/ppermute | solution.py:21
  55.3 7.4 %collective-permute-start.9 = (bf16[1,34,16,128]{3,2,1,0:T(8,128)(2,1)S(1)}, bf16[1,34,16,128]{3,2,1,0:T(8,128)(2,1)S(1)}, u32[]{:S(2)}, u32[]{:S(2)}) collective-permute-start(bf16[1,34,16,128]{3,2,1,0:T(8,128)(2,1)S(1)} %get-tuple-element.13), channel_id=1, source_target_pairs={{2,0},{3,1},{4,2},{5,3},{6,4},{7,5},{8,6},{9,7},{10,8},{11,9},{12,... | collective-permute-start | bytes 417800 | tf_op jit(solution)/shard_map/ppermute | solution.py:21
  63.4 1.0 %copy-start.9 = (bf16[3,3,3,128,64]{3,4,2,1,0:T(8,128)(2,1)S(1)}, bf16[3,3,3,128,64]{3,4,2,1,0:T(8,128)(2,1)}, u32[]{:S(2)}) copy-start(bf16[3,3,3,128,64]{3,4,2,1,0:T(8,128)(2,1)} %param.13) | copy-start | bytes 1327108
  63.4 1.0 %copy-start.11 = (pred[8,3]{0,1:T(4,128)(4,1)S(1)}, pred[8,3]{0,1:T(4,128)(4,1)}, u32[]{:S(2)}) copy-start(pred[8,3]{0,1:T(4,128)(4,1)} %constant.41) | copy-start | bytes 76

commit v5 on v4

--- a/solution.py
+++ b/solution.py
@@ -49,15 +49,22 @@
     return to_voxels(flat_out, weight.shape[1] // 8)
 
 
-def convolve(full_xy, conv_kernel):
-    accumulated = lax.conv_general_dilated(
-        full_xy[None],
-        conv_kernel,
-        window_strides=(1, 1, 1),
-        padding=((0, 0), (0, 0), (1, 1)),
-        dimension_numbers=("NDHWC", "DHWIO", "NDHWC"),
-        preferred_element_type=jnp.float32,
-    )[0]
+def convolve(extended, low_plane, high_plane, conv_kernel):
+    def conv(field, kernel, x_pad):
+        return lax.conv_general_dilated(
+            field[None],
+            kernel,
+            window_strides=(1, 1, 1),
+            padding=((x_pad, x_pad), (0, 0), (1, 1)),
+            dimension_numbers=("NDHWC", "DHWIO", "NDHWC"),
+            preferred_element_type=jnp.float32,
+        )[0]
+
+    interior = conv(extended, conv_kernel, 1)
+    rims = jnp.concatenate(
+        [conv(low_plane, conv_kernel[:1], 0), conv(high_plane, conv_kernel[2:], 0)], axis=0
+    )
+    accumulated = interior + rims
     activated = jnp.where(accumulated > 0, accumulated, leak_slope * accumulated)
     return activated.astype(jnp.bfloat16)
 
@@ -189,9 +196,8 @@
     kv_weight = projection[:, model_width:]
     kv_chunks = [projected(mine, norm_gain, kv_weight), projected(theirs, norm_gain, kv_weight)]
     remote_out, remote_lse = attention(
-        mirrored_queries, kv_chunks, head_size, score_scale, jnp.float32, False
-    )
-    remote_out = remote_out.astype(jnp.bfloat16)
+        mirrored_queries, kv_chunks, head_size, score_scale, jnp.bfloat16, False
+    )
     other_out = exchanged(remote_out, half)
     other_lse = exchanged(remote_lse, half)
     own_out, own_lse = attention(
@@ -223,10 +229,9 @@
     low_rim = jnp.where(lower_half, zero_plane, partner)
     high_rim = jnp.where(lower_half, partner, zero_plane)
     extended = jnp.concatenate([low_rim, joined, high_rim], axis=1)
-    full_xy = jnp.concatenate(
-        [plane_send(extended[-1:], 2), extended, plane_send(extended[:1], -2)], axis=0
-    )
-    decoded = convolve(full_xy, conv_kernel)[None]
+    low_plane = plane_send(extended[-1:], 2)
+    high_plane = plane_send(extended[:1], -2)
+    decoded = convolve(extended, low_plane, high_plane, conv_kernel)[None]
     return (encoded, decoded)
 
 

time: 68.8 us -> 66.3 us (0.964)
  waiting for transfers between devices: 11.7 us -> 10.6 us
  other arithmetic: 7.2 us -> 6.17 us
    conv_general_dilated x1 -> x3, matrix products: 2.9 us -> 4.14 us  [conv(): lax.conv_general_dilated(field[None], kernel, window_strides=(1, 1, 1), p...]
    convert_element_type x1 -> x0, other arithmetic: 1.02 us -> none  [body(): remote_out = remote_out.astype(jnp.bfloat16)]
    ppermute x2, waiting for transfers between devices: 5.88 us -> 4.87 us  [shifted(): return lax.ppermute(block, axis, route)]
    dot_general x1, matrix products: 1.27 us -> 0.35 us  [body(): jnp.dot(attended, output_weight, preferred_element_type=jnp.float32)]
    unnamed x29, local copies, waits for them, and re-layouts: 2.6 us -> 1.89 us
  transfers between devices with their start and end apart: 10 -> 10, of which waited for: 5 -> 5; matrix products, arithmetic and copies ran while one was open for 21% -> 23% of each run, Pallas kernels for 11% -> 12%
where the time goes in v5:
time: 66.3 us; the launch traced here: 65.7 us
  starting transfers between devices  16.6 us (25%)
  Pallas kernels  15.2 us (23%)
  matrix products  12.1 us (18%)
  waiting for transfers between devices  10.6 us (16%)
  other arithmetic  6.17 us (9%)
  local copies, waits for them, and re-layouts  3.88 us (6%)
  between operations  1.11 us (2%)
    pallas_call x2, Pallas kernels, attention(): pl.pallas_call(kernel, grid=(pairs,), cost_estimate=cost, in_specs=[row_s...  15.2 us
    ppermute x7, starting transfers between devices, exchanged(): return lax.ppermute(x, 'seq', [(i, i ^ mask) for i in range(devices)])  10.6 us
    dot_general x3, matrix products, projected(): jnp.dot(normed, weight, preferred_element_type=jnp.float32)  7.08 us
    ppermute x2, starting transfers between devices, shifted(): return lax.ppermute(block, axis, route)  5.95 us
    ppermute x2, waiting for transfers between devices, shifted(): return lax.ppermute(block, axis, route)  4.87 us
    ppermute x7, waiting for transfers between devices, exchanged(): return lax.ppermute(x, 'seq', [(i, i ^ mask) for i in range(devices)])  4.56 us
    conv_general_dilated x3, matrix products, conv(): lax.conv_general_dilated(field[None], kernel, window_strides=(1, 1, 1), p...  4.14 us
    unnamed x29, local copies, waits for them, and re-layouts  1.89 us
  transfers between devices with their start and end apart: 10, of which 5 were waited for; matrix products, arithmetic and copies ran while one was open for 23% of the time, Pallas kernels for 12%

profile of v5, /device:TPU:0, one launch (start us, length us, event | category | flops | bytes accessed | tf_op | source)
XLA Modules:
  0.0 65.7 jit_solution(14013938399916245343)
XLA Ops:
  0.6 0.0 copy-start
  0.6 0.0 copy-start.1
  0.7 3.1 %collective-permute-start = (bf16[128,768]{1,0:T(8,128)(2,1)}, bf16[128,768]{1,0:T(8,128)(2,1)S(1)}, u32[]{:S(2)}, u32[]{:S(2)}) collective-permute-start(bf16[128,768]{1,0:T(8,128)(2,1)} %param.7), channel_id=1, source_target_pairs={{0,2},{1,3},{2,0},{3,1},{4,6},{5,7},{6,4},{7,5},{8,10},{9,11},{10,... | collective-permute-start | bytes 589832 | tf_op jit(solution)/shard_map/ppermute | solution.py:178
  3.7 1.6 %collective-permute-start.1 = (bf16[128,768]{1,0:T(8,128)(2,1)}, bf16[128,768]{1,0:T(8,128)(2,1)S(1)}, u32[]{:S(2)}, u32[]{:S(2)}) collective-permute-start(bf16[128,768]{1,0:T(8,128)(2,1)} %param.7), channel_id=1, source_target_pairs={{0,4},{1,5},{2,6},{3,7},{4,0},{5,1},{6,2},{7,3},{8,12},{9,13},{10,... | collective-permute-start | bytes 589832 | tf_op jit(solution)/shard_map/ppermute | solution.py:178
  5.3 0.0 collective-permute-start.2
  5.3 1.1 %convert_reduce_fusion.2 = f32[128]{0:T(128)S(1)} fusion(bf16[128,768]{1,0:T(8,128)(2,1)} %param.7), kind=kLoop, calls=%fused_computation.48 | loop fusion | flops 196480 | bytes 197120 | tf_op jit(solution)/shard_map/reduce_sum | solution.py:30
  6.4 0.7 %convert_element_type.53 = f32[768]{0:T(1024)S(1)} convert(bf16[768]{0:T(1024)(128)(2,1)} %param.8) | non-fusion elementwise | flops 768 | bytes 4608 | tf_op jit(solution)/shard_map/convert_element_type | solution.py:33
  7.1 1.1 %fusion.39 = f32[128]{0:T(128)S(1)} fusion(bf16[128,768]{1,0:T(8,128)(2,1)} %param.7, f32[128]{0:T(128)S(1)} %broadcast_multiply_fusion.2), kind=kLoop, calls=%fused_computation.51 | loop fusion | flops 393088 | bytes 197632 | tf_op jit(solution)/shard_map/reduce_sum | solution.py:32
  8.2 1.8 %fusion.17.refs_0_ = bf16[128,768]{1,0:T(8,128)(2,1)S(1)} fusion(bf16[768,2304]{1,0:T(8,128)(2,1)} %param.9, bf16[128,768]{1,0:T(8,128)(2,1)} %param.7, f32[768]{0:T(1024)S(1)} %convert_element_type.53, f32[128]{0:T(128)S(1)} %add_rsqrt_fusion.2, f32[128]{0:T(128)S(1)} %broadcast_multiply_fusion.2), kind=kOutput, calls=%fused_computation.29 | convolution fusion | flops 151584768 | bytes 1576960 | tf_op jit(solution)/shard_map/dot_general | solution.py:183
  10.0 3.0 %collective-permute-start.4 = (bf16[128,768]{1,0:T(8,128)(2,1)S(1)}, bf16[128,768]{1,0:T(8,128)(2,1)S(1)}, u32[]{:S(2)}, u32[]{:S(2)}) collective-permute-start(bf16[128,768]{1,0:T(8,128)(2,1)S(1)} %fusion.17.refs_0_), channel_id=1, source_target_pairs={{0,8},{1,9},{2,10},{3,11},{4,12},{5,13},{6,14},{7,15},{8,0},{9,1},... | collective-permute-start | bytes 589832 | tf_op jit(solution)/shard_map/ppermute | solution.py:178
  13.0 0.3 convolution_convert_fusion.2
  13.3 0.2 reshape_reshape.7
  13.5 0.0 copy-start.7
  13.5 0.2 copy.16
  13.7 0.0 collective-permute-done
  13.8 2.0 %collective-permute-done.2 = bf16[128,768]{1,0:T(8,128)(2,1)S(1)} collective-permute-done((bf16[128,768]{1,0:T(8,128)(2,1)}, bf16[128,768]{1,0:T(8,128)(2,1)S(1)}, u32[]{:S(2)}, u32[]{:S(2)}) %collective-permute-start.2) | collective-permute-done | bytes 196640 | tf_op jit(solution)/shard_map/ppermute | solution.py:178
  15.9 0.1 collective-permute-start.3
  16.0 0.2 convert_reduce_fusion.1
  16.1 0.4 fusion.9
  16.5 2.7 %convolution_convert_fusion.1.refs_1_.refs_3_ = bf16[512,1536]{1,0:T(8,128)(2,1)} fusion(bf16[768,2304]{1,0:T(8,128)(2,1)S(1)} %copy-done.7, bf16[512,768]{1,0:T(8,128)(2,1)S(1)} %constant_dynamic-update-slice_fusion, f32[768]{0:T(1024)S(1)} %convert_element_type.53, f32[512]{0:T(512)S(1)} %add_rsqrt_fusion.1, f32[512]{0:T(512)S(1)} %broadcast_multiply_fusion.1), kind=kOutput, calls=%fused_computation.1 | convolution fusion | flops 1210712064 | bytes 4726784 | tf_op jit(solution)/shard_map/dot_general | solution.py:183
  19.2 0.0 collective-permute-done.3
  19.2 0.2 convert_reduce_fusion
  19.4 0.4 fusion.6
  19.7 2.7 %convolution_convert_fusion.refs_2_.refs_4_ = bf16[512,1536]{1,0:T(8,128)(2,1)} fusion(bf16[768,2304]{1,0:T(8,128)(2,1)S(1)} %copy-done.7, bf16[512,768]{1,0:T(8,128)(2,1)S(1)} %collective-permute-done.3, f32[512]{0:T(512)S(1)} %add_rsqrt_fusion, f32[512]{0:T(512)S(1)} %broadcast_multiply_fusion, f32[768]{0:T(1024)S(1)} %convert_element_type.53), kind=kOutput, calls=%fused_computation | convolution fusion | flops 1210712064 | bytes 4726784 | tf_op jit(solution)/shard_map/dot_general | solution.py:183
  22.4 0.0 collective-permute-done.4.refs_0_
  22.4 0.7 %copy-done.5 = bf16[128,768]{1,0:T(8,128)(2,1)} copy-done((bf16[128,768]{1,0:T(8,128)(2,1)}, bf16[128,768]{1,0:T(8,128)(2,1)S(1)}, u32[]{:S(2)}) %copy-start.5) | copy-done | bytes 196632
  23.1 7.6 %shard_map.86 = (bf16[128,768]{1,0:T(8,128)(2,1)}, f32[128,128]{1,0:T(8,128)}) custom-call(bf16[128,768]{1,0:T(8,128)(2,1)} %copy-done.5, bf16[512,1536]{1,0:T(8,128)(2,1)} %convolution_convert_fusion.1.refs_1_.refs_3_, bf16[512,1536]{1,0:T(8,128)(2,1)} %convolution_convert_fusion.refs_2_.refs_4_, ...), custom_call_target="tpu_custom_call" | custom-call | flops 805306368 | bytes 3932160 | tf_op jit(solution)/shard_map/pallas_call | solution.py:162
  30.7 2.6 %collective-permute-start.5 = (f32[128,128]{1,0:T(8,128)}, f32[128,128]{1,0:T(8,128)S(1)}, u32[]{:S(2)}, u32[]{:S(2)}) collective-permute-start(f32[128,128]{1,0:T(8,128)} %get-tuple-element.8), channel_id=1, source_target_pairs={{0,8},{1,9},{2,10},{3,11},{4,12},{5,13},{6,14},{7,15},{8,0},{9,1},... | collective-permute-start | bytes 196616 | tf_op jit(solution)/shard_map/ppermute | solution.py:178
  33.3 0.3 collective-permute-start.6
  33.6 7.6 %shard_map.87 = (f32[128,768]{1,0:T(8,128)}, f32[128,128]{1,0:T(8,128)}) custom-call(bf16[128,768]{1,0:T(8,128)(2,1)} %copy-done.4, bf16[512,1536]{1,0:T(8,128)(2,1)} %convolution_convert_fusion.1.refs_1_.refs_3_, bf16[512,1536]{1,0:T(8,128)(2,1)} %convolution_convert_fusion.refs_2_.refs_4_, bf16[512,1536]{1,0:T(8,128)(2,1)} %convolution_convert_fusion.1.refs_1_.refs_3_, ...), custom_call_target="tpu_custom_call" | custom-call | flops 805306368 | bytes 3932160 | tf_op jit(solution)/shard_map/pallas_call | solution.py:162
  41.2 0.0 collective-permute-done.5
  41.2 0.9 %max.3 = f32[128,128]{1,0:T(8,128)S(1)} maximum(f32[128,128]{1,0:T(8,128)} %get-tuple-element.7, f32[128,128]{1,0:T(8,128)S(1)} %collective-permute-done.5) | non-fusion elementwise | flops 16384 | bytes 196608 | tf_op jit(solution)/shard_map/max | solution.py:207
  42.1 0.9 %fusion.63 = (f32[128,12]{1,0:T(8,128)S(1)}, f32[128,12]{1,0:T(8,128)S(1)}) fusion(f32[128,128]{1,0:T(8,128)S(1)} %collective-permute-done.5, f32[128,128]{1,0:T(8,128)S(1)} %max.3, f32[128,128]{1,0:T(8,128)} %get-tuple-element.7), kind=kLoop, calls=%fused_computation.76 | loop fusion | flops 3072 | bytes 30720 | tf_op jit(solution)/shard_map/exp | solution.py:209
  43.0 0.1 copy.9
  43.1 0.2 copy.10
  43.3 0.1 copy.11
  43.4 0.2 copy.12
  43.6 0.0 copy-start.3
  43.6 2.5 %collective-permute-done.6 = bf16[128,768]{1,0:T(8,128)(2,1)S(1)} collective-permute-done((bf16[128,768]{1,0:T(8,128)(2,1)}, bf16[128,768]{1,0:T(8,128)(2,1)S(1)}, u32[]{:S(2)}, u32[]{:S(2)}) %collective-permute-start.6) | collective-permute-done | bytes 196640 | tf_op jit(solution)/shard_map/ppermute | solution.py:178
  46.1 0.3 fusion.20
  46.5 0.0 copy-start.6
  46.5 0.3 convolution_convert_fusion.3
  46.8 0.2 reshape_reshape.6
  47.0 0.2 copy.15
  47.1 0.1 fusion.65
  47.2 0.0 collective-permute-start.7
  47.3 1.1 %collective-permute-done.7 = bf16[2,1,16,128]{3,2,1,0:T(8,128)(2,1)S(1)} collective-permute-done((bf16[2,1,16,128]{3,2,1,0:T(8,128)(2,1)S(1)}, bf16[2,1,16,128]{3,2,1,0:T(8,128)(2,1)S(1)}, u32[]{:S(2)}, u32[]{:S(2)}) %collective-permute-start.7) | collective-permute-done | bytes 8224 | tf_op jit(solution)/shard_map/ppermute | solution.py:25
  48.4 0.1 pad_maximum_fusion
  48.6 4.5 %collective-permute-start.8 = (bf16[1,34,16,128]{3,2,1,0:T(8,128)(2,1)S(1)}, bf16[1,34,16,128]{3,2,1,0:T(8,128)(2,1)S(1)}, u32[]{:S(2)}, u32[]{:S(2)}) collective-permute-start(bf16[1,34,16,128]{3,2,1,0:T(8,128)(2,1)S(1)} %get-tuple-element.12), channel_id=1, source_target_pairs={{0,2},{1,3},{2,4},{3,5},{4,6},{5,7},{6,8},{7,9},{8,10},{9,11},{10,... | collective-permute-start | bytes 417800 | tf_op jit(solution)/shard_map/ppermute | solution.py:21
  53.1 1.5 %collective-permute-start.9 = (bf16[1,34,16,128]{3,2,1,0:T(8,128)(2,1)S(1)}, bf16[1,34,16,128]{3,2,1,0:T(8,128)(2,1)S(1)}, u32[]{:S(2)}, u32[]{:S(2)}) collective-permute-start(bf16[1,34,16,128]{3,2,1,0:T(8,128)(2,1)S(1)} %get-tuple-element.13), channel_id=1, source_target_pairs={{2,0},{3,1},{4,2},{5,3},{6,4},{7,5},{8,6},{9,7},{10,8},{11,9},{12,... | collective-permute-start | bytes 417800 | tf_op jit(solution)/shard_map/ppermute | solution.py:21
  54.6 0.1 fusion.82
  54.7 0.2 copy.28
  55.0 0.3 pad.clone
  55.2 0.1 copy.19
  55.3 0.1 slice.48
  55.4 0.0 copy-start.8
  55.4 0.0 copy-start.10
  55.4 1.0 %collective-permute-done.8 = bf16[1,34,16,128]{3,2,1,0:T(8,128)(2,1)S(1)} collective-permute-done((bf16[1,34,16,128]{3,2,1,0:T(8,128)(2,1)S(1)}, bf16[1,34,16,128]{3,2,1,0:T(8,128)(2,1)S(1)}, u32[]{:S(2)}, u32[]{:S(2)}) %collective-permute-start.8) | collective-permute-done | bytes 139296 | tf_op jit(solution)/shard_map/ppermute | solution.py:21
  56.5 3.9 %collective-permute-done.9 = bf16[1,34,16,128]{3,2,1,0:T(8,128)(2,1)S(1)} collective-permute-done((bf16[1,34,16,128]{3,2,1,0:T(8,128)(2,1)S(1)}, bf16[1,34,16,128]{3,2,1,0:T(8,128)(2,1)S(1)}, u32[]{:S(2)}, u32[]{:S(2)}) %collective-permute-start.9) | collective-permute-done | bytes 139296 | tf_op jit(solution)/shard_map/ppermute | solution.py:21
  60.6 0.6 convolution_select_fusion.2
  61.2 0.6 convolution_select_fusion.1
  61.9 2.9 %fusion.14 = bf16[2,32,8,3,64]{4,2,3,1,0:T(8,128)(2,1)S(1)} fusion(bf16[3,3,3,128,64]{3,4,2,1,0:T(8,128)(2,1)S(1)} %copy-done.8, f32[1,32,8,3,64]{4,2,3,1,0:T(8,128)S(1)} %convolution_select_fusion.1, f32[1,32,8,3,64]{4,2,3,1,0:T(8,128)S(1)} %convolution_select_fusion.2, bf16[2,34,1,7,2,128]{5,3,4,1,0,2:T(8,128)(2,1)S(1)} %slice.48, ...), kind=kOutput, calls=%fused_computation.26 | convolution fusion | flops 455761920 | bytes 1693720 | tf_op jit(solution)/shard_map/conv_general_dilated | solution.py:54
  64.8 0.1 copy.26
  64.9 0.8 %copy.27 = bf16[1,2,32,16,64]{4,3,2,1,0:T(8,128)(2,1)} copy(bf16[1,2,32,16,64]{4,2,3,1,0:T(8,128)(2,1)S(1)} %slice_bitcast_fusion) | data formatting | bytes 262144
  (38 shorter events, 0.5 us)
Async XLA Ops:
  0.6 45.5 %copy-start = (bf16[768,768]{1,0:T(8,128)(2,1)S(1)}, bf16[768,768]{1,0:T(8,128)(2,1)}, u32[]{:S(2)}) copy-start(bf16[768,768]{1,0:T(8,128)(2,1)} %param.10) | copy-start | bytes 3538948
  0.6 12.4 %copy-start.1 = (bf16[128,768]{1,0:T(8,128)(2,1)S(1)}, bf16[128,768]{1,0:T(8,128)(2,1)}, u32[]{:S(2)}) copy-start(bf16[128,768]{1,0:T(8,128)(2,1)} %param.7) | copy-start | bytes 589828
  0.7 12.4 %copy-start.2 = (bf16[768,512]{1,0:T(8,128)(2,1)S(1)}, bf16[768,512]{1,0:T(8,128)(2,1)}, u32[]{:S(2)}) copy-start(bf16[768,512]{1,0:T(8,128)(2,1)} %param.12) | copy-start | bytes 2359300
  0.7 13.1 %collective-permute-start = (bf16[128,768]{1,0:T(8,128)(2,1)}, bf16[128,768]{1,0:T(8,128)(2,1)S(1)}, u32[]{:S(2)}, u32[]{:S(2)}) collective-permute-start(bf16[128,768]{1,0:T(8,128)(2,1)} %param.7), channel_id=1, source_target_pairs={{0,2},{1,3},{2,0},{3,1},{4,6},{5,7},{6,4},{7,5},{8,10},{9,11},{10,... | collective-permute-start | bytes 589832 | tf_op jit(solution)/shard_map/ppermute | solution.py:178
  3.7 10.0 %collective-permute-start.1 = (bf16[128,768]{1,0:T(8,128)(2,1)}, bf16[128,768]{1,0:T(8,128)(2,1)S(1)}, u32[]{:S(2)}, u32[]{:S(2)}) collective-permute-start(bf16[128,768]{1,0:T(8,128)(2,1)} %param.7), channel_id=1, source_target_pairs={{0,4},{1,5},{2,6},{3,7},{4,0},{5,1},{6,2},{7,3},{8,12},{9,13},{10,... | collective-permute-start | bytes 589832 | tf_op jit(solution)/shard_map/ppermute | solution.py:178
  5.3 10.6 %collective-permute-start.2 = (bf16[128,768]{1,0:T(8,128)(2,1)}, bf16[128,768]{1,0:T(8,128)(2,1)S(1)}, u32[]{:S(2)}, u32[]{:S(2)}) collective-permute-start(bf16[128,768]{1,0:T(8,128)(2,1)} %param.7), channel_id=1, source_target_pairs={{0,6},{1,7},{2,4},{3,5},{4,2},{5,3},{6,0},{7,1},{8,14},{9,15},{10,... | collective-permute-start | bytes 589832 | tf_op jit(solution)/shard_map/ppermute | solution.py:178
  10.0 3.8 %copy-start.4 = (bf16[128,768]{1,0:T(8,128)(2,1)}, bf16[128,768]{1,0:T(8,128)(2,1)S(1)}, u32[]{:S(2)}) copy-start(bf16[128,768]{1,0:T(8,128)(2,1)S(1)} %fusion.17.refs_0_) | copy-start | bytes 589828
  10.0 12.4 %collective-permute-start.4 = (bf16[128,768]{1,0:T(8,128)(2,1)S(1)}, bf16[128,768]{1,0:T(8,128)(2,1)S(1)}, u32[]{:S(2)}, u32[]{:S(2)}) collective-permute-start(bf16[128,768]{1,0:T(8,128)(2,1)S(1)} %fusion.17.refs_0_), channel_id=1, source_target_pairs={{0,8},{1,9},{2,10},{3,11},{4,12},{5,13},{6,14},{7,15},{8,0},{9,1},... | collective-permute-start | bytes 589832 | tf_op jit(solution)/shard_map/ppermute | solution.py:178
  13.5 3.0 %copy-start.7 = (bf16[768,2304]{1,0:T(8,128)(2,1)S(1)}, bf16[768,2304]{1,0:T(8,128)(2,1)}, u32[]{:S(2)}) copy-start(bf16[768,2304]{1,0:T(8,128)(2,1)} %param.9) | copy-start | bytes 10616836
  15.9 3.3 %collective-permute-start.3 = (bf16[512,768]{1,0:T(8,128)(2,1)S(1)}, bf16[512,768]{1,0:T(8,128)(2,1)S(1)}, u32[]{:S(2)}, u32[]{:S(2)}) collective-permute-start(bf16[512,768]{1,0:T(8,128)(2,1)S(1)} %constant_dynamic-update-slice_fusion), channel_id=1, source_target_pairs={{0,1},{1,0},{2,3},{3,2},{4,5},{5,4},{6,7},{7,6},{8,9},{9,8},{10,11... | collective-permute-start | bytes 2359304 | tf_op jit(solution)/shard_map/ppermute | solution.py:178
  22.4 0.7 %copy-start.5 = (bf16[128,768]{1,0:T(8,128)(2,1)}, bf16[128,768]{1,0:T(8,128)(2,1)S(1)}, u32[]{:S(2)}) copy-start(bf16[128,768]{1,0:T(8,128)(2,1)S(1)} %collective-permute-done.4.refs_0_) | copy-start | bytes 589828
  30.7 10.6 %collective-permute-start.5 = (f32[128,128]{1,0:T(8,128)}, f32[128,128]{1,0:T(8,128)S(1)}, u32[]{:S(2)}, u32[]{:S(2)}) collective-permute-start(f32[128,128]{1,0:T(8,128)} %get-tuple-element.8), channel_id=1, source_target_pairs={{0,8},{1,9},{2,10},{3,11},{4,12},{5,13},{6,14},{7,15},{8,0},{9,1},... | collective-permute-start | bytes 196616 | tf_op jit(solution)/shard_map/ppermute | solution.py:178
  33.3 12.8 %collective-permute-start.6 = (bf16[128,768]{1,0:T(8,128)(2,1)}, bf16[128,768]{1,0:T(8,128)(2,1)S(1)}, u32[]{:S(2)}, u32[]{:S(2)}) collective-permute-start(bf16[128,768]{1,0:T(8,128)(2,1)} %get-tuple-element.6.refs_5_), channel_id=1, source_target_pairs={{0,8},{1,9},{2,10},{3,11},{4,12},{5,13},{6,14},{7,15},{8,0},{9,1},... | collective-permute-start | bytes 589832 | tf_op jit(solution)/shard_map/ppermute | solution.py:178
  41.2 4.9 %copy-start.9 = (f32[128,768]{1,0:T(8,128)S(1)}, f32[128,768]{1,0:T(8,128)}, u32[]{:S(2)}) copy-start(f32[128,768]{1,0:T(8,128)} %get-tuple-element.9) | copy-start | bytes 1179652
  43.6 2.9 %copy-start.3 = (bf16[768,512]{1,0:T(8,128)(2,1)S(1)}, bf16[768,512]{1,0:T(8,128)(2,1)}, u32[]{:S(2)}) copy-start(bf16[768,512]{1,0:T(8,128)(2,1)} %param.11) | copy-start | bytes 2359300
  46.5 2.1 %copy-start.6 = (bf16[128,768]{1,0:T(8,128)(2,1)}, bf16[128,768]{1,0:T(8,128)(2,1)S(1)}, u32[]{:S(2)}) copy-start(bf16[128,768]{1,0:T(8,128)(2,1)S(1)} %fusion.20) | copy-start | bytes 589828
  47.2 1.2 %collective-permute-start.7 = (bf16[2,1,16,128]{3,2,1,0:T(8,128)(2,1)S(1)}, bf16[2,1,16,128]{3,2,1,0:T(8,128)(2,1)S(1)}, u32[]{:S(2)}, u32[]{:S(2)}) collective-permute-start(bf16[2,1,16,128]{3,2,1,0:T(8,128)(2,1)S(1)} %fusion.65), channel_id=1, source_target_pairs={{0,1},{1,0},{2,3},{3,2},{4,5},{5,4},{6,7},{7,6},{8,9},{9,8},{10,11... | collective-permute-start | bytes 24584 | tf_op jit(solution)/shard_map/ppermute | solution.py:25
  48.6 7.8 %collective-permute-start.8 = (bf16[1,34,16,128]{3,2,1,0:T(8,128)(2,1)S(1)}, bf16[1,34,16,128]{3,2,1,0:T(8,128)(2,1)S(1)}, u32[]{:S(2)}, u32[]{:S(2)}) collective-permute-start(bf16[1,34,16,128]{3,2,1,0:T(8,128)(2,1)S(1)} %get-tuple-element.12), channel_id=1, source_target_pairs={{0,2},{1,3},{2,4},{3,5},{4,6},{5,7},{6,8},{7,9},{8,10},{9,11},{10,... | collective-permute-start | bytes 417800 | tf_op jit(solution)/shard_map/ppermute | solution.py:21
  53.1 7.4 %collective-permute-start.9 = (bf16[1,34,16,128]{3,2,1,0:T(8,128)(2,1)S(1)}, bf16[1,34,16,128]{3,2,1,0:T(8,128)(2,1)S(1)}, u32[]{:S(2)}, u32[]{:S(2)}) collective-permute-start(bf16[1,34,16,128]{3,2,1,0:T(8,128)(2,1)S(1)} %get-tuple-element.13), channel_id=1, source_target_pairs={{2,0},{3,1},{4,2},{5,3},{6,4},{7,5},{8,6},{9,7},{10,8},{11,9},{12,... | collective-permute-start | bytes 417800 | tf_op jit(solution)/shard_map/ppermute | solution.py:21
  55.4 5.2 %copy-start.8 = (bf16[3,3,3,128,64]{3,4,2,1,0:T(8,128)(2,1)S(1)}, bf16[3,3,3,128,64]{3,4,2,1,0:T(8,128)(2,1)}, u32[]{:S(2)}) copy-start(bf16[3,3,3,128,64]{3,4,2,1,0:T(8,128)(2,1)} %param.13) | copy-start | bytes 1327108
  55.4 5.2 %copy-start.10 = (pred[8,3]{0,1:T(4,128)(4,1)S(1)}, pred[8,3]{0,1:T(4,128)(4,1)}, u32[]{:S(2)}) copy-start(pred[8,3]{0,1:T(4,128)(4,1)} %constant.49) | copy-start | bytes 76

commit v6 on v5

--- a/solution.py
+++ b/solution.py
@@ -60,7 +60,7 @@
             preferred_element_type=jnp.float32,
         )[0]
 
-    interior = conv(extended, conv_kernel, 1)
+    interior = lax.optimization_barrier(conv(extended, conv_kernel, 1))
     rims = jnp.concatenate(
         [conv(low_plane, conv_kernel[:1], 0), conv(high_plane, conv_kernel[2:], 0)], axis=0
     )
@@ -100,16 +100,16 @@
             lax.dot_general(
                 q_h, k_ref[...], (((1,), (1,)), ((), ())), preferred_element_type=jnp.float32
             )
-            * score_scale
             for k_ref in k_refs
         ]
-        row_max = scores[0].max(axis=-1, keepdims=True)
+        raw_max = scores[0].max(axis=-1, keepdims=True)
         for block in scores[1:]:
-            row_max = jnp.maximum(row_max, block.max(axis=-1, keepdims=True))
+            raw_max = jnp.maximum(raw_max, block.max(axis=-1, keepdims=True))
+        row_max = raw_max * score_scale
         denominator = None
         numerator = None
         for block, v_ref in zip(scores, v_refs):
-            exp_scores = jnp.exp(block - row_max)
+            exp_scores = jnp.exp2((block - raw_max) * (score_scale * math.log2(math.e)))
             part_sum = jnp.sum(exp_scores, axis=-1, keepdims=True)
             part = jnp.dot(
                 exp_scores.astype(jnp.bfloat16), v_ref[...], preferred_element_type=jnp.float32

time: 66.3 us -> 63.1 us (0.952)
  waiting for transfers between devices: 10.6 us -> 6.89 us
    ppermute x2, waiting for transfers between devices: 4.87 us -> 1.1 us  [shifted(): return lax.ppermute(block, axis, route)]
  transfers between devices with their start and end apart: 10 -> 10, of which waited for: 5 -> 4; matrix products, arithmetic and copies ran while one was open for 23% -> 30% of each run, Pallas kernels for 12% -> 12%
where the time goes in v6:
time: 63.1 us; the launch traced here: 62.5 us
  starting transfers between devices  16.8 us (27%)
  Pallas kernels  15 us (24%)
  matrix products  12.2 us (19%)
  waiting for transfers between devices  6.89 us (11%)
  other arithmetic  6.3 us (10%)
  local copies, waits for them, and re-layouts  4.19 us (7%)
  between operations  1.15 us (2%)
    pallas_call x2, Pallas kernels, attention(): pl.pallas_call(kernel, grid=(pairs,), cost_estimate=cost, in_specs=[row_s...  15 us
    ppermute x7, starting transfers between devices, exchanged(): return lax.ppermute(x, 'seq', [(i, i ^ mask) for i in range(devices)])  10.6 us
    dot_general x3, matrix products, projected(): jnp.dot(normed, weight, preferred_element_type=jnp.float32)  7.07 us
    ppermute x2, starting transfers between devices, shifted(): return lax.ppermute(block, axis, route)  6.08 us
    ppermute x7, waiting for transfers between devices, exchanged(): return lax.ppermute(x, 'seq', [(i, i ^ mask) for i in range(devices)])  4.67 us
    conv_general_dilated x3, matrix products, conv(): lax.conv_general_dilated(field[None], kernel, window_strides=(1, 1, 1), p...  4.22 us
    unnamed x29, local copies, waits for them, and re-layouts  1.89 us
    reduce_sum x3, other arithmetic, layer_norm(): row_var = jnp.mean(centered * centered, axis=-1, keepdims=True)  1.84 us
  transfers between devices with their start and end apart: 10, of which 4 were waited for; matrix products, arithmetic and copies ran while one was open for 30% of the time, Pallas kernels for 12%

profile of v6, /device:TPU:0, one launch (start us, length us, event | category | flops | bytes accessed | tf_op | source)
XLA Modules:
  0.0 62.5 jit_solution(17158555154642739548)
XLA Ops:
  0.6 0.0 copy-start
  0.6 0.0 copy-start.1
  0.7 3.1 %collective-permute-start = (bf16[128,768]{1,0:T(8,128)(2,1)}, bf16[128,768]{1,0:T(8,128)(2,1)S(1)}, u32[]{:S(2)}, u32[]{:S(2)}) collective-permute-start(bf16[128,768]{1,0:T(8,128)(2,1)} %param.7), channel_id=1, source_target_pairs={{0,2},{1,3},{2,0},{3,1},{4,6},{5,7},{6,4},{7,5},{8,10},{9,11},{10,... | collective-permute-start | bytes 589832 | tf_op jit(solution)/shard_map/ppermute | solution.py:178
  3.7 1.6 %collective-permute-start.1 = (bf16[128,768]{1,0:T(8,128)(2,1)}, bf16[128,768]{1,0:T(8,128)(2,1)S(1)}, u32[]{:S(2)}, u32[]{:S(2)}) collective-permute-start(bf16[128,768]{1,0:T(8,128)(2,1)} %param.7), channel_id=1, source_target_pairs={{0,4},{1,5},{2,6},{3,7},{4,0},{5,1},{6,2},{7,3},{8,12},{9,13},{10,... | collective-permute-start | bytes 589832 | tf_op jit(solution)/shard_map/ppermute | solution.py:178
  5.3 0.0 collective-permute-start.2
  5.3 1.1 %convert_reduce_fusion.2 = f32[128]{0:T(128)S(1)} fusion(bf16[128,768]{1,0:T(8,128)(2,1)} %param.7), kind=kLoop, calls=%fused_computation.46 | loop fusion | flops 196480 | bytes 197120 | tf_op jit(solution)/shard_map/reduce_sum | solution.py:30
  6.4 0.7 %convert_element_type.52 = f32[768]{0:T(1024)S(1)} convert(bf16[768]{0:T(1024)(128)(2,1)} %param.8) | non-fusion elementwise | flops 768 | bytes 4608 | tf_op jit(solution)/shard_map/convert_element_type | solution.py:33
  7.1 1.1 %fusion.38 = f32[128]{0:T(128)S(1)} fusion(bf16[128,768]{1,0:T(8,128)(2,1)} %param.7, f32[128]{0:T(128)S(1)} %broadcast_multiply_fusion.2), kind=kLoop, calls=%fused_computation.52 | loop fusion | flops 393088 | bytes 197632 | tf_op jit(solution)/shard_map/reduce_sum | solution.py:32
  8.2 1.8 %fusion.15.refs_0_ = bf16[128,768]{1,0:T(8,128)(2,1)S(1)} fusion(bf16[768,2304]{1,0:T(8,128)(2,1)} %param.9, bf16[128,768]{1,0:T(8,128)(2,1)} %param.7, f32[768]{0:T(1024)S(1)} %convert_element_type.52, f32[128]{0:T(128)S(1)} %add_rsqrt_fusion.2, f32[128]{0:T(128)S(1)} %broadcast_multiply_fusion.2), kind=kOutput, calls=%fused_computation.27 | convolution fusion | flops 151584768 | bytes 1576960 | tf_op jit(solution)/shard_map/dot_general | solution.py:183
  10.0 3.0 %collective-permute-start.4 = (bf16[128,768]{1,0:T(8,128)(2,1)S(1)}, bf16[128,768]{1,0:T(8,128)(2,1)S(1)}, u32[]{:S(2)}, u32[]{:S(2)}) collective-permute-start(bf16[128,768]{1,0:T(8,128)(2,1)S(1)} %fusion.15.refs_0_), channel_id=1, source_target_pairs={{0,8},{1,9},{2,10},{3,11},{4,12},{5,13},{6,14},{7,15},{8,0},{9,1},... | collective-permute-start | bytes 589832 | tf_op jit(solution)/shard_map/ppermute | solution.py:178
  13.0 0.3 convolution_convert_fusion.2
  13.3 0.2 reshape_reshape.7
  13.5 0.0 copy-start.7
  13.5 0.2 copy.16
  13.7 0.0 collective-permute-done
  13.8 0.0 collective-permute-done.1
  13.8 2.0 %collective-permute-done.2 = bf16[128,768]{1,0:T(8,128)(2,1)S(1)} collective-permute-done((bf16[128,768]{1,0:T(8,128)(2,1)}, bf16[128,768]{1,0:T(8,128)(2,1)S(1)}, u32[]{:S(2)}, u32[]{:S(2)}) %collective-permute-start.2) | collective-permute-done | bytes 196640 | tf_op jit(solution)/shard_map/ppermute | solution.py:178
  15.9 0.1 collective-permute-start.3
  16.0 0.2 convert_reduce_fusion.1
  16.1 0.4 fusion.9
  16.5 2.6 %convolution_convert_fusion.1.refs_1_.refs_3_ = bf16[512,1536]{1,0:T(8,128)(2,1)} fusion(bf16[768,2304]{1,0:T(8,128)(2,1)S(1)} %copy-done.7, bf16[512,768]{1,0:T(8,128)(2,1)S(1)} %constant_dynamic-update-slice_fusion, f32[768]{0:T(1024)S(1)} %convert_element_type.52, f32[512]{0:T(512)S(1)} %add_rsqrt_fusion.1, f32[512]{0:T(512)S(1)} %broadcast_multiply_fusion.1), kind=kOutput, calls=%fused_computation.1 | convolution fusion | flops 1210712064 | bytes 4726784 | tf_op jit(solution)/shard_map/dot_general | solution.py:183
  19.2 0.2 convert_reduce_fusion
  19.4 0.4 fusion.6
  19.7 2.7 %convolution_convert_fusion.refs_2_.refs_4_ = bf16[512,1536]{1,0:T(8,128)(2,1)} fusion(bf16[768,2304]{1,0:T(8,128)(2,1)S(1)} %copy-done.7, bf16[512,768]{1,0:T(8,128)(2,1)S(1)} %collective-permute-done.3, f32[512]{0:T(512)S(1)} %add_rsqrt_fusion, f32[512]{0:T(512)S(1)} %broadcast_multiply_fusion, f32[768]{0:T(1024)S(1)} %convert_element_type.52), kind=kOutput, calls=%fused_computation | convolution fusion | flops 1210712064 | bytes 4726784 | tf_op jit(solution)/shard_map/dot_general | solution.py:183
  22.4 0.7 %copy-done.5 = bf16[128,768]{1,0:T(8,128)(2,1)} copy-done((bf16[128,768]{1,0:T(8,128)(2,1)}, bf16[128,768]{1,0:T(8,128)(2,1)S(1)}, u32[]{:S(2)}) %copy-start.5) | copy-done | bytes 196632
  23.1 7.5 %shard_map.86 = (bf16[128,768]{1,0:T(8,128)(2,1)}, f32[128,128]{1,0:T(8,128)}) custom-call(bf16[128,768]{1,0:T(8,128)(2,1)} %copy-done.5, bf16[512,1536]{1,0:T(8,128)(2,1)} %convolution_convert_fusion.1.refs_1_.refs_3_, bf16[512,1536]{1,0:T(8,128)(2,1)} %convolution_convert_fusion.refs_2_.refs_4_, ...), custom_call_target="tpu_custom_call" | custom-call | flops 805306368 | bytes 3932160 | tf_op jit(solution)/shard_map/pallas_call | solution.py:162
  30.6 2.6 %collective-permute-start.5 = (f32[128,128]{1,0:T(8,128)}, f32[128,128]{1,0:T(8,128)S(1)}, u32[]{:S(2)}, u32[]{:S(2)}) collective-permute-start(f32[128,128]{1,0:T(8,128)} %get-tuple-element.8), channel_id=1, source_target_pairs={{0,8},{1,9},{2,10},{3,11},{4,12},{5,13},{6,14},{7,15},{8,0},{9,1},... | collective-permute-start | bytes 196616 | tf_op jit(solution)/shard_map/ppermute | solution.py:178
  33.2 0.3 collective-permute-start.6
  33.5 7.5 %shard_map.87 = (f32[128,768]{1,0:T(8,128)}, f32[128,128]{1,0:T(8,128)}) custom-call(bf16[128,768]{1,0:T(8,128)(2,1)} %copy-done.4, bf16[512,1536]{1,0:T(8,128)(2,1)} %convolution_convert_fusion.1.refs_1_.refs_3_, bf16[512,1536]{1,0:T(8,128)(2,1)} %convolution_convert_fusion.refs_2_.refs_4_, bf16[512,1536]{1,0:T(8,128)(2,1)} %convolution_convert_fusion.1.refs_1_.refs_3_, ...), custom_call_target="tpu_custom_call" | custom-call | flops 805306368 | bytes 3932160 | tf_op jit(solution)/shard_map/pallas_call | solution.py:162
  41.0 0.9 %max.3 = f32[128,128]{1,0:T(8,128)S(1)} maximum(f32[128,128]{1,0:T(8,128)} %get-tuple-element.7, f32[128,128]{1,0:T(8,128)S(1)} %collective-permute-done.5) | non-fusion elementwise | flops 16384 | bytes 196608 | tf_op jit(solution)/shard_map/max | solution.py:207
  41.9 0.9 %fusion.63 = (f32[128,12]{1,0:T(8,128)S(1)}, f32[128,12]{1,0:T(8,128)S(1)}) fusion(f32[128,128]{1,0:T(8,128)S(1)} %collective-permute-done.5, f32[128,128]{1,0:T(8,128)S(1)} %max.3, f32[128,128]{1,0:T(8,128)} %get-tuple-element.7), kind=kLoop, calls=%fused_computation.79 | loop fusion | flops 3072 | bytes 30720 | tf_op jit(solution)/shard_map/exp | solution.py:209
  42.8 0.1 copy.9
  42.9 0.2 copy.10
  43.1 0.1 copy.11
  43.2 0.2 copy.12
  43.4 0.0 copy-start.3
  43.4 2.6 %collective-permute-done.6 = bf16[128,768]{1,0:T(8,128)(2,1)S(1)} collective-permute-done((bf16[128,768]{1,0:T(8,128)(2,1)}, bf16[128,768]{1,0:T(8,128)(2,1)S(1)}, u32[]{:S(2)}, u32[]{:S(2)}) %collective-permute-start.6) | collective-permute-done | bytes 196640 | tf_op jit(solution)/shard_map/ppermute | solution.py:178
  46.0 0.3 fusion.18
  46.4 0.0 copy-start.6
  46.4 0.3 convolution_convert_fusion.3
  46.7 0.2 reshape_reshape.6
  46.9 0.2 copy.15
  47.0 0.1 fusion.65
  47.1 0.1 collective-permute-start.7
  47.2 1.1 %collective-permute-done.7 = bf16[2,1,16,128]{3,2,1,0:T(8,128)(2,1)S(1)} collective-permute-done((bf16[2,1,16,128]{3,2,1,0:T(8,128)(2,1)S(1)}, bf16[2,1,16,128]{3,2,1,0:T(8,128)(2,1)S(1)}, u32[]{:S(2)}, u32[]{:S(2)}) %collective-permute-start.7) | collective-permute-done | bytes 8224 | tf_op jit(solution)/shard_map/ppermute | solution.py:25
  48.3 0.1 pad_maximum_fusion
  48.5 0.1 fusion.82
  48.6 0.0 copy-start.8
  48.6 0.0 copy-start.10
  48.7 4.6 %collective-permute-start.8 = (bf16[1,34,16,128]{3,2,1,0:T(8,128)(2,1)S(1)}, bf16[1,34,16,128]{3,2,1,0:T(8,128)(2,1)S(1)}, u32[]{:S(2)}, u32[]{:S(2)}) collective-permute-start(bf16[1,34,16,128]{3,2,1,0:T(8,128)(2,1)S(1)} %get-tuple-element.12), channel_id=1, source_target_pairs={{0,2},{1,3},{2,4},{3,5},{4,6},{5,7},{6,8},{7,9},{8,10},{9,11},{10,... | collective-permute-start | bytes 417800 | tf_op jit(solution)/shard_map/ppermute | solution.py:21
  53.3 1.5 %collective-permute-start.9 = (bf16[1,34,16,128]{3,2,1,0:T(8,128)(2,1)S(1)}, bf16[1,34,16,128]{3,2,1,0:T(8,128)(2,1)S(1)}, u32[]{:S(2)}, u32[]{:S(2)}) collective-permute-start(bf16[1,34,16,128]{3,2,1,0:T(8,128)(2,1)S(1)} %get-tuple-element.13), channel_id=1, source_target_pairs={{2,0},{3,1},{4,2},{5,3},{6,4},{7,5},{8,6},{9,7},{10,8},{11,9},{12,... | collective-permute-start | bytes 417800 | tf_op jit(solution)/shard_map/ppermute | solution.py:21
  54.8 0.2 copy.30
  55.0 0.3 pad.clone
  55.3 0.1 copy.19
  55.4 0.1 slice.50
  55.5 3.0 %convolution_select_fusion = f32[2,32,8,3,64]{4,2,3,1,0:T(8,128)S(1)} fusion(bf16[3,3,3,128,64]{3,4,2,1,0:T(8,128)(2,1)S(1)} %copy-done.8, bf16[2,34,1,7,2,128]{5,3,4,1,0,2:T(8,128)(2,1)S(1)} %slice.50, bf16[2,34,1,8,3,128]{5,3,4,1,0,2:T(8,128)(2,1)S(1)} %copy.19, pred[8,3]{0,1:T(4,128)(4,1)S(1)} %copy-done.10), kind=kOutput, calls=%fused_computation.21 | convolution fusion | flops 455172096 | bytes 1497112 | tf_op jit(solution)/shard_map/conv_general_dilated | solution.py:54
  58.5 0.2 copy.20
  58.9 0.6 convolution_select_fusion.2
  59.5 0.1 copy.24
  59.6 1.1 %collective-permute-done.9 = bf16[1,34,16,128]{3,2,1,0:T(8,128)(2,1)S(1)} collective-permute-done((bf16[1,34,16,128]{3,2,1,0:T(8,128)(2,1)S(1)}, bf16[1,34,16,128]{3,2,1,0:T(8,128)(2,1)S(1)}, u32[]{:S(2)}, u32[]{:S(2)}) %collective-permute-start.9) | collective-permute-done | bytes 139296 | tf_op jit(solution)/shard_map/ppermute | solution.py:21
  60.8 0.6 convolution_select_fusion.1
  61.4 0.1 copy.28
  61.6 0.1 fusion.54
  61.7 0.8 %copy.29 = bf16[1,2,32,16,64]{4,3,2,1,0:T(8,128)(2,1)} copy(bf16[1,2,32,16,64]{4,2,3,1,0:T(8,128)(2,1)S(1)} %fusion.54) | data formatting | bytes 262144
  (42 shorter events, 0.6 us)
Async XLA Ops:
  0.6 45.4 %copy-start = (bf16[768,768]{1,0:T(8,128)(2,1)S(1)}, bf16[768,768]{1,0:T(8,128)(2,1)}, u32[]{:S(2)}) copy-start(bf16[768,768]{1,0:T(8,128)(2,1)} %param.10) | copy-start | bytes 3538948
  0.6 12.4 %copy-start.1 = (bf16[128,768]{1,0:T(8,128)(2,1)S(1)}, bf16[128,768]{1,0:T(8,128)(2,1)}, u32[]{:S(2)}) copy-start(bf16[128,768]{1,0:T(8,128)(2,1)} %param.7) | copy-start | bytes 589828
  0.7 12.4 %copy-start.2 = (bf16[768,512]{1,0:T(8,128)(2,1)S(1)}, bf16[768,512]{1,0:T(8,128)(2,1)}, u32[]{:S(2)}) copy-start(bf16[768,512]{1,0:T(8,128)(2,1)} %param.12) | copy-start | bytes 2359300
  0.7 13.1 %collective-permute-start = (bf16[128,768]{1,0:T(8,128)(2,1)}, bf16[128,768]{1,0:T(8,128)(2,1)S(1)}, u32[]{:S(2)}, u32[]{:S(2)}) collective-permute-start(bf16[128,768]{1,0:T(8,128)(2,1)} %param.7), channel_id=1, source_target_pairs={{0,2},{1,3},{2,0},{3,1},{4,6},{5,7},{6,4},{7,5},{8,10},{9,11},{10,... | collective-permute-start | bytes 589832 | tf_op jit(solution)/shard_map/ppermute | solution.py:178
  3.7 10.0 %collective-permute-start.1 = (bf16[128,768]{1,0:T(8,128)(2,1)}, bf16[128,768]{1,0:T(8,128)(2,1)S(1)}, u32[]{:S(2)}, u32[]{:S(2)}) collective-permute-start(bf16[128,768]{1,0:T(8,128)(2,1)} %param.7), channel_id=1, source_target_pairs={{0,4},{1,5},{2,6},{3,7},{4,0},{5,1},{6,2},{7,3},{8,12},{9,13},{10,... | collective-permute-start | bytes 589832 | tf_op jit(solution)/shard_map/ppermute | solution.py:178
  5.3 10.6 %collective-permute-start.2 = (bf16[128,768]{1,0:T(8,128)(2,1)}, bf16[128,768]{1,0:T(8,128)(2,1)S(1)}, u32[]{:S(2)}, u32[]{:S(2)}) collective-permute-start(bf16[128,768]{1,0:T(8,128)(2,1)} %param.7), channel_id=1, source_target_pairs={{0,6},{1,7},{2,4},{3,5},{4,2},{5,3},{6,0},{7,1},{8,14},{9,15},{10,... | collective-permute-start | bytes 589832 | tf_op jit(solution)/shard_map/ppermute | solution.py:178
  10.0 3.8 %copy-start.4 = (bf16[128,768]{1,0:T(8,128)(2,1)}, bf16[128,768]{1,0:T(8,128)(2,1)S(1)}, u32[]{:S(2)}) copy-start(bf16[128,768]{1,0:T(8,128)(2,1)S(1)} %fusion.15.refs_0_) | copy-start | bytes 589828
  10.0 12.4 %collective-permute-start.4 = (bf16[128,768]{1,0:T(8,128)(2,1)S(1)}, bf16[128,768]{1,0:T(8,128)(2,1)S(1)}, u32[]{:S(2)}, u32[]{:S(2)}) collective-permute-start(bf16[128,768]{1,0:T(8,128)(2,1)S(1)} %fusion.15.refs_0_), channel_id=1, source_target_pairs={{0,8},{1,9},{2,10},{3,11},{4,12},{5,13},{6,14},{7,15},{8,0},{9,1},... | collective-permute-start | bytes 589832 | tf_op jit(solution)/shard_map/ppermute | solution.py:178
  13.5 3.0 %copy-start.7 = (bf16[768,2304]{1,0:T(8,128)(2,1)S(1)}, bf16[768,2304]{1,0:T(8,128)(2,1)}, u32[]{:S(2)}) copy-start(bf16[768,2304]{1,0:T(8,128)(2,1)} %param.9) | copy-start | bytes 10616836
  15.9 3.3 %collective-permute-start.3 = (bf16[512,768]{1,0:T(8,128)(2,1)S(1)}, bf16[512,768]{1,0:T(8,128)(2,1)S(1)}, u32[]{:S(2)}, u32[]{:S(2)}) collective-permute-start(bf16[512,768]{1,0:T(8,128)(2,1)S(1)} %constant_dynamic-update-slice_fusion), channel_id=1, source_target_pairs={{0,1},{1,0},{2,3},{3,2},{4,5},{5,4},{6,7},{7,6},{8,9},{9,8},{10,11... | collective-permute-start | bytes 2359304 | tf_op jit(solution)/shard_map/ppermute | solution.py:178
  22.4 0.7 %copy-start.5 = (bf16[128,768]{1,0:T(8,128)(2,1)}, bf16[128,768]{1,0:T(8,128)(2,1)S(1)}, u32[]{:S(2)}) copy-start(bf16[128,768]{1,0:T(8,128)(2,1)S(1)} %collective-permute-done.4.refs_0_) | copy-start | bytes 589828
  30.6 10.5 %collective-permute-start.5 = (f32[128,128]{1,0:T(8,128)}, f32[128,128]{1,0:T(8,128)S(1)}, u32[]{:S(2)}, u32[]{:S(2)}) collective-permute-start(f32[128,128]{1,0:T(8,128)} %get-tuple-element.8), channel_id=1, source_target_pairs={{0,8},{1,9},{2,10},{3,11},{4,12},{5,13},{6,14},{7,15},{8,0},{9,1},... | collective-permute-start | bytes 196616 | tf_op jit(solution)/shard_map/ppermute | solution.py:178
  33.2 12.8 %collective-permute-start.6 = (bf16[128,768]{1,0:T(8,128)(2,1)}, bf16[128,768]{1,0:T(8,128)(2,1)S(1)}, u32[]{:S(2)}, u32[]{:S(2)}) collective-permute-start(bf16[128,768]{1,0:T(8,128)(2,1)} %get-tuple-element.6.refs_5_), channel_id=1, source_target_pairs={{0,8},{1,9},{2,10},{3,11},{4,12},{5,13},{6,14},{7,15},{8,0},{9,1},... | collective-permute-start | bytes 589832 | tf_op jit(solution)/shard_map/ppermute | solution.py:178
  41.0 5.0 %copy-start.9 = (f32[128,768]{1,0:T(8,128)S(1)}, f32[128,768]{1,0:T(8,128)}, u32[]{:S(2)}) copy-start(f32[128,768]{1,0:T(8,128)} %get-tuple-element.9) | copy-start | bytes 1179652
  43.4 3.0 %copy-start.3 = (bf16[768,512]{1,0:T(8,128)(2,1)S(1)}, bf16[768,512]{1,0:T(8,128)(2,1)}, u32[]{:S(2)}) copy-start(bf16[768,512]{1,0:T(8,128)(2,1)} %param.11) | copy-start | bytes 2359300
  46.4 2.1 %copy-start.6 = (bf16[128,768]{1,0:T(8,128)(2,1)}, bf16[128,768]{1,0:T(8,128)(2,1)S(1)}, u32[]{:S(2)}) copy-start(bf16[128,768]{1,0:T(8,128)(2,1)S(1)} %fusion.18) | copy-start | bytes 589828
  47.1 1.2 %collective-permute-start.7 = (bf16[2,1,16,128]{3,2,1,0:T(8,128)(2,1)S(1)}, bf16[2,1,16,128]{3,2,1,0:T(8,128)(2,1)S(1)}, u32[]{:S(2)}, u32[]{:S(2)}) collective-permute-start(bf16[2,1,16,128]{3,2,1,0:T(8,128)(2,1)S(1)} %fusion.65), channel_id=1, source_target_pairs={{0,1},{1,0},{2,3},{3,2},{4,5},{5,4},{6,7},{7,6},{8,9},{9,8},{10,11... | collective-permute-start | bytes 24584 | tf_op jit(solution)/shard_map/ppermute | solution.py:25
  48.6 6.8 %copy-start.8 = (bf16[3,3,3,128,64]{3,4,2,1,0:T(8,128)(2,1)S(1)}, bf16[3,3,3,128,64]{3,4,2,1,0:T(8,128)(2,1)}, u32[]{:S(2)}) copy-start(bf16[3,3,3,128,64]{3,4,2,1,0:T(8,128)(2,1)} %param.13) | copy-start | bytes 1327108
  48.6 6.8 %copy-start.10 = (pred[8,3]{0,1:T(4,128)(4,1)S(1)}, pred[8,3]{0,1:T(4,128)(4,1)}, u32[]{:S(2)}) copy-start(pred[8,3]{0,1:T(4,128)(4,1)} %constant.49) | copy-start | bytes 76
  48.7 10.0 %collective-permute-start.8 = (bf16[1,34,16,128]{3,2,1,0:T(8,128)(2,1)S(1)}, bf16[1,34,16,128]{3,2,1,0:T(8,128)(2,1)S(1)}, u32[]{:S(2)}, u32[]{:S(2)}) collective-permute-start(bf16[1,34,16,128]{3,2,1,0:T(8,128)(2,1)S(1)} %get-tuple-element.12), channel_id=1, source_target_pairs={{0,2},{1,3},{2,4},{3,5},{4,6},{5,7},{6,8},{7,9},{8,10},{9,11},{10,... | collective-permute-start | bytes 417800 | tf_op jit(solution)/shard_map/ppermute | solution.py:21
  53.3 7.4 %collective-permute-start.9 = (bf16[1,34,16,128]{3,2,1,0:T(8,128)(2,1)S(1)}, bf16[1,34,16,128]{3,2,1,0:T(8,128)(2,1)S(1)}, u32[]{:S(2)}, u32[]{:S(2)}) collective-permute-start(bf16[1,34,16,128]{3,2,1,0:T(8,128)(2,1)S(1)} %get-tuple-element.13), channel_id=1, source_target_pairs={{2,0},{3,1},{4,2},{5,3},{6,4},{7,5},{8,6},{9,7},{10,8},{11,9},{12,... | collective-permute-start | bytes 417800 | tf_op jit(solution)/shard_map/ppermute | solution.py:21

commit v7 on v6

--- a/solution.py
+++ b/solution.py
@@ -5,6 +5,7 @@
 from jax import lax
 from jax.experimental import pallas as pl
 from jax.experimental.pallas import tpu as pltpu
+from jax.experimental.layout import Layout, with_layout_constraint
 from jax.sharding import PartitionSpec as P
 
 HEADS = 12
@@ -73,7 +74,11 @@
     return shifted(plane, "seq", offset)
 
 
-def attention_kernel(*refs, head_size, score_scale, chunks, whole_output, ordered):
+def attention_kernel(*refs, head_size, score_scale, chunks, whole_output, ordered, rows_out):
+    rows_ref = None
+    if rows_out:
+        rows_ref = refs[-1]
+        refs = refs[:-1]
     if ordered:
         refs = refs[:-3] + refs[-2:]
     q_ref = refs[0]
@@ -125,9 +130,16 @@
     else:
         o_ref[...] = result.astype(o_ref.dtype)
     lse_ref[...] = log_sum
-
-
-def attention(queries, kv_chunks, head_size, score_scale, out_dtype, whole_output, after=None):
+    if rows_out:
+
+        @pl.when(step == pl.num_programs(0) - 1)
+        def _():
+            rows_ref[...] = jnp.transpose(log_sum)[: rows_ref.shape[0]]
+
+
+def attention(
+    queries, kv_chunks, head_size, score_scale, out_dtype, whole_output, after=None, rows_out=False
+):
     token_count, model_width = queries.shape
     pair = 2 * head_size
     pairs = model_width // pair
@@ -139,6 +151,7 @@
         chunks=chunks,
         whole_output=whole_output,
         ordered=after is not None,
+        rows_out=rows_out,
     )
     key_specs = [pl.BlockSpec((c.shape[0], pair), lambda j: (0, j)) for c in kv_chunks]
     value_specs = [pl.BlockSpec((c.shape[0], pair), lambda j: (0, j + pairs)) for c in kv_chunks]
@@ -159,18 +172,27 @@
         transcendentals=token_count * keys * (model_width // head_size),
         bytes_accessed=2 * keys * 2 * model_width + 8 * token_count * model_width,
     )
-    output, log_sum = pl.pallas_call(
+    heads = model_width // head_size
+    stat_rows = -(-heads // 8) * 8
+    if rows_out:
+        out_specs = out_specs + [pl.BlockSpec((stat_rows, stat_width), lambda j: (0, 0))]
+    out_shape = [
+        jax.ShapeDtypeStruct((token_count, model_width), out_dtype),
+        jax.ShapeDtypeStruct((token_count, stat_width), jnp.float32),
+    ]
+    if rows_out:
+        out_shape.append(jax.ShapeDtypeStruct((stat_rows, stat_width), jnp.float32))
+    results = pl.pallas_call(
         kernel,
         grid=(pairs,),
         cost_estimate=cost,
         in_specs=[row_spec] + key_specs + value_specs + extra_specs,
         out_specs=out_specs,
-        out_shape=[
-            jax.ShapeDtypeStruct((token_count, model_width), out_dtype),
-            jax.ShapeDtypeStruct((token_count, stat_width), jnp.float32),
-        ],
+        out_shape=out_shape,
     )(queries, *kv_chunks, *kv_chunks, *extra)
-    return output, log_sum
+    if rows_out:
+        return results[0], results[2]
+    return results[0], results[1]
 
 
 def exchanged(x, mask):
@@ -196,17 +218,20 @@
     kv_weight = projection[:, model_width:]
     kv_chunks = [projected(mine, norm_gain, kv_weight), projected(theirs, norm_gain, kv_weight)]
     remote_out, remote_lse = attention(
-        mirrored_queries, kv_chunks, head_size, score_scale, jnp.bfloat16, False
-    )
+        mirrored_queries, kv_chunks, head_size, score_scale, jnp.bfloat16, False, rows_out=True
+    )
+    heads = model_width // head_size
     other_out = exchanged(remote_out, half)
-    other_lse = exchanged(remote_lse, half)
+    row_major = Layout(major_to_minor=(0, 1))
+    sent_lse = with_layout_constraint(remote_lse, row_major)
+    other_lse = with_layout_constraint(exchanged(sent_lse, half), row_major)[:heads].T
     own_out, own_lse = attention(
         queries, kv_chunks, head_size, score_scale, jnp.float32, False, after=remote_out
     )
-    heads = model_width // head_size
-    top = jnp.maximum(own_lse, other_lse)
-    own_weight = jnp.repeat(jnp.exp(own_lse - top)[:, :heads], head_size, axis=1)
-    other_weight = jnp.repeat(jnp.exp(other_lse - top)[:, :heads], head_size, axis=1)
+    own_lse = own_lse[:, :heads]
+    top = jnp.maximum(own_lse, other_lse) + 0 * other_out[:1, :1].astype(jnp.float32)
+    own_weight = jnp.repeat(jnp.exp(own_lse - top), head_size, axis=1)
+    other_weight = jnp.repeat(jnp.exp(other_lse - top), head_size, axis=1)
     attended = (
         (own_weight * own_out + other_weight * other_out.astype(jnp.float32))
         / (own_weight + other_weight)

time: 63.1 us -> 63.5 us (level)
  local copies, waits for them, and re-layouts: 4.19 us -> 6.26 us
  other arithmetic: 6.3 us -> 4.54 us
  waiting for transfers between devices: 6.89 us -> 5.51 us
  between operations: 1.15 us -> 1.83 us
    ppermute x7, waiting for transfers between devices: 4.67 us -> 3.26 us  [exchanged(): return lax.ppermute(x, 'seq', [(i, i ^ mask) for i in range(devices)])]
    pallas_call x0 -> x1, local copies, waits for them, and re-layouts: none -> 0.98 us  [attention(): pl.pallas_call(kernel, grid=(pairs,), cost_estimate=cost, in_specs=[row_s...]
    max x1 -> x0, other arithmetic: 0.9 us -> none  [body(): top = jnp.maximum(own_lse, other_lse)]
    exp x1, other arithmetic: 0.87 us -> 0.01 us  [body(): other_weight = jnp.repeat(jnp.exp(other_lse - top), head_size, axis=1)]
    unnamed x29 -> x31, local copies, waits for them, and re-layouts: 1.89 us -> 2.64 us
  transfers between devices with their start and end apart: 10 -> 10, of which waited for: 4 -> 4; matrix products, arithmetic and copies ran while one was open for 30% -> 29% of each run, Pallas kernels for 12% -> 12%
where the time goes in v7:
time: 63.5 us; the launch traced here: 63 us
  starting transfers between devices  17.4 us (27%)
  Pallas kernels  15.2 us (24%)
  matrix products  12.3 us (19%)
  local copies, waits for them, and re-layouts  6.26 us (10%)
  waiting for transfers between devices  5.51 us (9%)
  other arithmetic  4.54 us (7%)
  between operations  1.83 us (3%)
    pallas_call x2, Pallas kernels, attention(): pl.pallas_call(kernel, grid=(pairs,), cost_estimate=cost, in_specs=[row_s...  15.2 us
    ppermute x7, starting transfers between devices, exchanged(): return lax.ppermute(x, 'seq', [(i, i ^ mask) for i in range(devices)])  10.8 us
    dot_general x3, matrix products, projected(): jnp.dot(normed, weight, preferred_element_type=jnp.float32)  7.22 us
    ppermute x2, starting transfers between devices, shifted(): return lax.ppermute(block, axis, route)  6.57 us
    conv_general_dilated x3, matrix products, conv(): lax.conv_general_dilated(field[None], kernel, window_strides=(1, 1, 1), p...  4.23 us
    ppermute x7, waiting for transfers between devices, exchanged(): return lax.ppermute(x, 'seq', [(i, i ^ mask) for i in range(devices)])  3.26 us
    unnamed x31, local copies, waits for them, and re-layouts  2.64 us
    reduce_sum x3, other arithmetic, layer_norm(): row_var = jnp.mean(centered * centered, axis=-1, keepdims=True)  1.84 us
  transfers between devices with their start and end apart: 10, of which 4 were waited for; matrix products, arithmetic and copies ran while one was open for 29% of the time, Pallas kernels for 12%

profile of v7, /device:TPU:0, one launch (start us, length us, event | category | flops | bytes accessed | tf_op | source)
XLA Modules:
  0.0 63.0 jit_solution(17636260134163087848)
XLA Ops:
  0.6 0.0 copy-start
  0.6 0.0 copy-start.1
  0.7 3.1 %collective-permute-start = (bf16[128,768]{1,0:T(8,128)(2,1)}, bf16[128,768]{1,0:T(8,128)(2,1)S(1)}, u32[]{:S(2)}, u32[]{:S(2)}) collective-permute-start(bf16[128,768]{1,0:T(8,128)(2,1)} %param.7), channel_id=1, source_target_pairs={{0,2},{1,3},{2,0},{3,1},{4,6},{5,7},{6,4},{7,5},{8,10},{9,11},{10,... | collective-permute-start | bytes 589832 | tf_op jit(solution)/shard_map/ppermute | solution.py:200
  3.7 1.6 %collective-permute-start.1 = (bf16[128,768]{1,0:T(8,128)(2,1)}, bf16[128,768]{1,0:T(8,128)(2,1)S(1)}, u32[]{:S(2)}, u32[]{:S(2)}) collective-permute-start(bf16[128,768]{1,0:T(8,128)(2,1)} %param.7), channel_id=1, source_target_pairs={{0,4},{1,5},{2,6},{3,7},{4,0},{5,1},{6,2},{7,3},{8,12},{9,13},{10,... | collective-permute-start | bytes 589832 | tf_op jit(solution)/shard_map/ppermute | solution.py:200
  5.3 0.0 collective-permute-start.2
  5.3 1.1 %convert_reduce_fusion.2 = f32[128]{0:T(128)S(1)} fusion(bf16[128,768]{1,0:T(8,128)(2,1)} %param.7), kind=kLoop, calls=%fused_computation.46 | loop fusion | flops 196480 | bytes 197120 | tf_op jit(solution)/shard_map/reduce_sum | solution.py:31
  6.4 0.7 %convert_element_type.55 = f32[768]{0:T(1024)S(1)} convert(bf16[768]{0:T(1024)(128)(2,1)} %param.8) | non-fusion elementwise | flops 768 | bytes 4608 | tf_op jit(solution)/shard_map/convert_element_type | solution.py:34
  7.1 1.1 %fusion.38 = f32[128]{0:T(128)S(1)} fusion(bf16[128,768]{1,0:T(8,128)(2,1)} %param.7, f32[128]{0:T(128)S(1)} %broadcast_multiply_fusion.2), kind=kLoop, calls=%fused_computation.52 | loop fusion | flops 393088 | bytes 197632 | tf_op jit(solution)/shard_map/reduce_sum | solution.py:33
  8.2 0.0 copy-start.7
  8.2 1.9 %fusion.15.refs_0_ = bf16[128,768]{1,0:T(8,128)(2,1)S(1)} fusion(bf16[768,2304]{1,0:T(8,128)(2,1)} %param.9, bf16[128,768]{1,0:T(8,128)(2,1)} %param.7, f32[768]{0:T(1024)S(1)} %convert_element_type.55, f32[128]{0:T(128)S(1)} %add_rsqrt_fusion.2, f32[128]{0:T(128)S(1)} %broadcast_multiply_fusion.2), kind=kOutput, calls=%fused_computation.27 | convolution fusion | flops 151584768 | bytes 1576960 | tf_op jit(solution)/shard_map/dot_general | solution.py:205
  10.1 3.0 %collective-permute-start.4 = (bf16[128,768]{1,0:T(8,128)(2,1)S(1)}, bf16[128,768]{1,0:T(8,128)(2,1)S(1)}, u32[]{:S(2)}, u32[]{:S(2)}) collective-permute-start(bf16[128,768]{1,0:T(8,128)(2,1)S(1)} %fusion.15.refs_0_), channel_id=1, source_target_pairs={{0,8},{1,9},{2,10},{3,11},{4,12},{5,13},{6,14},{7,15},{8,0},{9,1},... | collective-permute-start | bytes 589832 | tf_op jit(solution)/shard_map/ppermute | solution.py:200
  13.2 0.0 collective-permute-done
  13.2 2.3 %collective-permute-done.2 = bf16[128,768]{1,0:T(8,128)(2,1)S(1)} collective-permute-done((bf16[128,768]{1,0:T(8,128)(2,1)}, bf16[128,768]{1,0:T(8,128)(2,1)S(1)}, u32[]{:S(2)}, u32[]{:S(2)}) %collective-permute-start.2) | collective-permute-done | bytes 196640 | tf_op jit(solution)/shard_map/ppermute | solution.py:200
  15.6 0.1 collective-permute-start.3
  15.7 0.2 convert_reduce_fusion.1
  15.9 0.4 fusion.9
  16.2 2.7 %convolution_convert_fusion.1.refs_1_.refs_3_ = bf16[512,1536]{1,0:T(8,128)(2,1)} fusion(bf16[768,2304]{1,0:T(8,128)(2,1)S(1)} %copy-done.7, bf16[512,768]{1,0:T(8,128)(2,1)S(1)} %constant_dynamic-update-slice_fusion, f32[768]{0:T(1024)S(1)} %convert_element_type.55, f32[512]{0:T(512)S(1)} %add_rsqrt_fusion.1, f32[512]{0:T(512)S(1)} %broadcast_multiply_fusion.1), kind=kOutput, calls=%fused_computation.1 | convolution fusion | flops 1210712064 | bytes 4726784 | tf_op jit(solution)/shard_map/dot_general | solution.py:205
  18.9 0.0 collective-permute-done.3
  18.9 0.2 convert_reduce_fusion
  19.1 0.4 fusion.6
  19.5 2.7 %convolution_convert_fusion.refs_2_.refs_4_ = bf16[512,1536]{1,0:T(8,128)(2,1)} fusion(bf16[768,2304]{1,0:T(8,128)(2,1)S(1)} %copy-done.7, bf16[512,768]{1,0:T(8,128)(2,1)S(1)} %collective-permute-done.3, f32[512]{0:T(512)S(1)} %add_rsqrt_fusion, f32[512]{0:T(512)S(1)} %broadcast_multiply_fusion, f32[768]{0:T(1024)S(1)} %convert_element_type.55), kind=kOutput, calls=%fused_computation | convolution fusion | flops 1210712064 | bytes 4726784 | tf_op jit(solution)/shard_map/dot_general | solution.py:205
  22.1 0.0 collective-permute-done.4.refs_0_
  22.1 0.7 %copy-done.5 = bf16[128,768]{1,0:T(8,128)(2,1)} copy-done((bf16[128,768]{1,0:T(8,128)(2,1)}, bf16[128,768]{1,0:T(8,128)(2,1)S(1)}, u32[]{:S(2)}) %copy-start.5) | copy-done | bytes 196632
  22.8 7.6 %shard_map.86 = (bf16[128,768]{1,0:T(8,128)(2,1)}, f32[128,128]{1,0:T(8,128)}, f32[16,128]{1,0:T(8,128)}) custom-call(bf16[128,768]{1,0:T(8,128)(2,1)} %copy-done.5, bf16[512,1536]{1,0:T(8,128)(2,1)} %convolution_convert_fusion.1.refs_1_.refs_3_, bf16[512,1536]{1,0:T(8,128)(2,1)} %convolution_convert_fusion.refs_2_.refs_4_, ...), custom_call_target="tpu_custom_call" | custom-call | flops 805306368 | bytes 3932160 | tf_op jit(solution)/shard_map/pallas_call | solution.py:185
  30.4 2.9 %collective-permute-start.6 = (bf16[128,768]{1,0:T(8,128)(2,1)}, bf16[128,768]{1,0:T(8,128)(2,1)S(1)}, u32[]{:S(2)}, u32[]{:S(2)}) collective-permute-start(bf16[128,768]{1,0:T(8,128)(2,1)} %get-tuple-element.6.refs_5_), channel_id=1, source_target_pairs={{0,8},{1,9},{2,10},{3,11},{4,12},{5,13},{6,14},{7,15},{8,0},{9,1},... | collective-permute-start | bytes 589832 | tf_op jit(solution)/shard_map/ppermute | solution.py:200
  33.4 0.3 convolution_convert_fusion.2
  33.7 0.2 reshape_reshape.7
  33.9 0.2 copy.18
  34.1 0.1 collective-permute-start.5
  34.2 7.5 %shard_map.87 = (f32[128,768]{1,0:T(8,128)}, f32[128,128]{1,0:T(8,128)}) custom-call(bf16[128,768]{1,0:T(8,128)(2,1)} %copy-done.4, bf16[512,1536]{1,0:T(8,128)(2,1)} %convolution_convert_fusion.1.refs_1_.refs_3_, bf16[512,1536]{1,0:T(8,128)(2,1)} %convolution_convert_fusion.refs_2_.refs_4_, bf16[512,1536]{1,0:T(8,128)(2,1)} %convolution_convert_fusion.1.refs_1_.refs_3_, ...), custom_call_target="tpu_custom_call" | custom-call | flops 805306368 | bytes 3932160 | tf_op jit(solution)/shard_map/pallas_call | solution.py:185
  41.7 1.0 %copy.12 = f32[128,128]{0,1:T(8,128)S(1)} copy(f32[128,128]{1,0:T(8,128)} %get-tuple-element.7) | data formatting | bytes 131072 | tf_op jit(solution)/shard_map/pallas_call | solution.py:185
  42.7 0.9 %collective-permute-done.6 = bf16[128,768]{1,0:T(8,128)(2,1)S(1)} collective-permute-done((bf16[128,768]{1,0:T(8,128)(2,1)}, bf16[128,768]{1,0:T(8,128)(2,1)S(1)}, u32[]{:S(2)}, u32[]{:S(2)}) %collective-permute-start.6) | collective-permute-done | bytes 196640 | tf_op jit(solution)/shard_map/ppermute | solution.py:200
  43.6 0.5 slice.52
  44.8 0.0 collective-permute-done.5
  44.9 0.2 copy.13
  45.1 0.2 copy.14
  45.2 0.0 copy-start.3
  45.3 0.3 fusion.18
  45.6 0.8 %copy-done.3 = bf16[768,512]{1,0:T(8,128)(2,1)S(1)} copy-done((bf16[768,512]{1,0:T(8,128)(2,1)S(1)}, bf16[768,512]{1,0:T(8,128)(2,1)}, u32[]{:S(2)}) %copy-start.3) | copy-done | bytes 786456
  46.4 0.3 convolution_convert_fusion.3
  46.6 0.2 reshape_reshape.6
  46.8 0.2 copy.17
  47.0 0.1 fusion.63
  47.1 0.0 collective-permute-start.7
  47.1 1.2 %collective-permute-done.7 = bf16[2,1,16,128]{3,2,1,0:T(8,128)(2,1)S(1)} collective-permute-done((bf16[2,1,16,128]{3,2,1,0:T(8,128)(2,1)S(1)}, bf16[2,1,16,128]{3,2,1,0:T(8,128)(2,1)S(1)}, u32[]{:S(2)}, u32[]{:S(2)}) %collective-permute-start.7) | collective-permute-done | bytes 8224 | tf_op jit(solution)/shard_map/ppermute | solution.py:26
  48.3 0.1 pad_maximum_fusion
  48.5 0.1 fusion.80
  48.6 0.0 copy-start.8
  48.6 0.0 copy-start.11
  48.7 5.1 %collective-permute-start.8 = (bf16[1,34,16,128]{3,2,1,0:T(8,128)(2,1)S(1)}, bf16[1,34,16,128]{3,2,1,0:T(8,128)(2,1)S(1)}, u32[]{:S(2)}, u32[]{:S(2)}) collective-permute-start(bf16[1,34,16,128]{3,2,1,0:T(8,128)(2,1)S(1)} %get-tuple-element.12), channel_id=1, source_target_pairs={{0,2},{1,3},{2,4},{3,5},{4,6},{5,7},{6,8},{7,9},{8,10},{9,11},{10,... | collective-permute-start | bytes 417800 | tf_op jit(solution)/shard_map/ppermute | solution.py:22
  53.8 1.5 %collective-permute-start.9 = (bf16[1,34,16,128]{3,2,1,0:T(8,128)(2,1)S(1)}, bf16[1,34,16,128]{3,2,1,0:T(8,128)(2,1)S(1)}, u32[]{:S(2)}, u32[]{:S(2)}) collective-permute-start(bf16[1,34,16,128]{3,2,1,0:T(8,128)(2,1)S(1)} %get-tuple-element.13), channel_id=1, source_target_pairs={{2,0},{3,1},{4,2},{5,3},{6,4},{7,5},{8,6},{9,7},{10,8},{11,9},{12,... | collective-permute-start | bytes 417800 | tf_op jit(solution)/shard_map/ppermute | solution.py:22
  55.3 0.2 copy.32
  55.5 0.3 pad.clone
  55.8 0.1 copy.21
  55.8 0.1 slice.53
  55.9 3.0 %convolution_select_fusion = f32[2,32,8,3,64]{4,2,3,1,0:T(8,128)S(1)} fusion(bf16[3,3,3,128,64]{3,4,2,1,0:T(8,128)(2,1)S(1)} %copy-done.8, bf16[2,34,1,7,2,128]{5,3,4,1,0,2:T(8,128)(2,1)S(1)} %slice.53, bf16[2,34,1,8,3,128]{5,3,4,1,0,2:T(8,128)(2,1)S(1)} %copy.21, pred[8,3]{0,1:T(4,128)(4,1)S(1)} %copy-done.11), kind=kOutput, calls=%fused_computation.21 | convolution fusion | flops 455172096 | bytes 1497112 | tf_op jit(solution)/shard_map/conv_general_dilated | solution.py:55
  59.0 0.2 copy.22
  59.3 0.6 convolution_select_fusion.2
  60.0 0.1 copy.26
  60.0 1.1 %collective-permute-done.9 = bf16[1,34,16,128]{3,2,1,0:T(8,128)(2,1)S(1)} collective-permute-done((bf16[1,34,16,128]{3,2,1,0:T(8,128)(2,1)S(1)}, bf16[1,34,16,128]{3,2,1,0:T(8,128)(2,1)S(1)}, u32[]{:S(2)}, u32[]{:S(2)}) %collective-permute-start.9) | collective-permute-done | bytes 139296 | tf_op jit(solution)/shard_map/ppermute | solution.py:22
  61.3 0.6 convolution_select_fusion.1
  61.9 0.1 copy.30
  62.0 0.1 fusion.54
  62.2 0.8 %copy.31 = bf16[1,2,32,16,64]{4,3,2,1,0:T(8,128)(2,1)} copy(bf16[1,2,32,16,64]{4,2,3,1,0:T(8,128)(2,1)S(1)} %fusion.54) | data formatting | bytes 262144
  (43 shorter events, 0.6 us)
Async XLA Ops:
  0.6 44.6 %copy-start = (bf16[768,768]{1,0:T(8,128)(2,1)S(1)}, bf16[768,768]{1,0:T(8,128)(2,1)}, u32[]{:S(2)}) copy-start(bf16[768,768]{1,0:T(8,128)(2,1)} %param.10) | copy-start | bytes 3538948
  0.6 12.5 %copy-start.1 = (bf16[128,768]{1,0:T(8,128)(2,1)S(1)}, bf16[128,768]{1,0:T(8,128)(2,1)}, u32[]{:S(2)}) copy-start(bf16[128,768]{1,0:T(8,128)(2,1)} %param.7) | copy-start | bytes 589828
  0.7 12.5 %collective-permute-start = (bf16[128,768]{1,0:T(8,128)(2,1)}, bf16[128,768]{1,0:T(8,128)(2,1)S(1)}, u32[]{:S(2)}, u32[]{:S(2)}) collective-permute-start(bf16[128,768]{1,0:T(8,128)(2,1)} %param.7), channel_id=1, source_target_pairs={{0,2},{1,3},{2,0},{3,1},{4,6},{5,7},{6,4},{7,5},{8,10},{9,11},{10,... | collective-permute-start | bytes 589832 | tf_op jit(solution)/shard_map/ppermute | solution.py:200
  3.7 9.5 %collective-permute-start.1 = (bf16[128,768]{1,0:T(8,128)(2,1)}, bf16[128,768]{1,0:T(8,128)(2,1)S(1)}, u32[]{:S(2)}, u32[]{:S(2)}) collective-permute-start(bf16[128,768]{1,0:T(8,128)(2,1)} %param.7), channel_id=1, source_target_pairs={{0,4},{1,5},{2,6},{3,7},{4,0},{5,1},{6,2},{7,3},{8,12},{9,13},{10,... | collective-permute-start | bytes 589832 | tf_op jit(solution)/shard_map/ppermute | solution.py:200
  5.3 10.3 %collective-permute-start.2 = (bf16[128,768]{1,0:T(8,128)(2,1)}, bf16[128,768]{1,0:T(8,128)(2,1)S(1)}, u32[]{:S(2)}, u32[]{:S(2)}) collective-permute-start(bf16[128,768]{1,0:T(8,128)(2,1)} %param.7), channel_id=1, source_target_pairs={{0,6},{1,7},{2,4},{3,5},{4,2},{5,3},{6,0},{7,1},{8,14},{9,15},{10,... | collective-permute-start | bytes 589832 | tf_op jit(solution)/shard_map/ppermute | solution.py:200
  8.2 8.0 %copy-start.7 = (bf16[768,2304]{1,0:T(8,128)(2,1)S(1)}, bf16[768,2304]{1,0:T(8,128)(2,1)}, u32[]{:S(2)}) copy-start(bf16[768,2304]{1,0:T(8,128)(2,1)} %param.9) | copy-start | bytes 10616836
  10.1 6.1 %copy-start.4 = (bf16[128,768]{1,0:T(8,128)(2,1)}, bf16[128,768]{1,0:T(8,128)(2,1)S(1)}, u32[]{:S(2)}) copy-start(bf16[128,768]{1,0:T(8,128)(2,1)S(1)} %fusion.15.refs_0_) | copy-start | bytes 589828
  10.1 12.0 %collective-permute-start.4 = (bf16[128,768]{1,0:T(8,128)(2,1)S(1)}, bf16[128,768]{1,0:T(8,128)(2,1)S(1)}, u32[]{:S(2)}, u32[]{:S(2)}) collective-permute-start(bf16[128,768]{1,0:T(8,128)(2,1)S(1)} %fusion.15.refs_0_), channel_id=1, source_target_pairs={{0,8},{1,9},{2,10},{3,11},{4,12},{5,13},{6,14},{7,15},{8,0},{9,1},... | collective-permute-start | bytes 589832 | tf_op jit(solution)/shard_map/ppermute | solution.py:200
  15.6 3.3 %collective-permute-start.3 = (bf16[512,768]{1,0:T(8,128)(2,1)S(1)}, bf16[512,768]{1,0:T(8,128)(2,1)S(1)}, u32[]{:S(2)}, u32[]{:S(2)}) collective-permute-start(bf16[512,768]{1,0:T(8,128)(2,1)S(1)} %constant_dynamic-update-slice_fusion), channel_id=1, source_target_pairs={{0,1},{1,0},{2,3},{3,2},{4,5},{5,4},{6,7},{7,6},{8,9},{9,8},{10,11... | collective-permute-start | bytes 2359304 | tf_op jit(solution)/shard_map/ppermute | solution.py:200
  22.1 11.2 %copy-start.2 = (bf16[768,512]{1,0:T(8,128)(2,1)S(1)}, bf16[768,512]{1,0:T(8,128)(2,1)}, u32[]{:S(2)}) copy-start(bf16[768,512]{1,0:T(8,128)(2,1)} %param.12) | copy-start | bytes 2359300
  22.1 0.7 %copy-start.5 = (bf16[128,768]{1,0:T(8,128)(2,1)}, bf16[128,768]{1,0:T(8,128)(2,1)S(1)}, u32[]{:S(2)}) copy-start(bf16[128,768]{1,0:T(8,128)(2,1)S(1)} %collective-permute-done.4.refs_0_) | copy-start | bytes 589828
  30.4 3.6 %copy-start.10 = (f32[16,128]{1,0:T(8,128)S(1)}, f32[16,128]{1,0:T(8,128)}, u32[]{:S(2)}) copy-start(f32[16,128]{1,0:T(8,128)} %get-tuple-element.8) | copy-start | bytes 24580
  30.4 13.2 %collective-permute-start.6 = (bf16[128,768]{1,0:T(8,128)(2,1)}, bf16[128,768]{1,0:T(8,128)(2,1)S(1)}, u32[]{:S(2)}, u32[]{:S(2)}) collective-permute-start(bf16[128,768]{1,0:T(8,128)(2,1)} %get-tuple-element.6.refs_5_), channel_id=1, source_target_pairs={{0,8},{1,9},{2,10},{3,11},{4,12},{5,13},{6,14},{7,15},{8,0},{9,1},... | collective-permute-start | bytes 589832 | tf_op jit(solution)/shard_map/ppermute | solution.py:200
  34.1 10.7 %collective-permute-start.5 = (f32[16,128]{1,0:T(8,128)S(1)}, f32[16,128]{1,0:T(8,128)S(1)}, u32[]{:S(2)}, u32[]{:S(2)}) collective-permute-start(f32[16,128]{1,0:T(8,128)S(1)} %copy-done.10), channel_id=1, source_target_pairs={{0,8},{1,9},{2,10},{3,11},{4,12},{5,13},{6,14},{7,15},{8,0},{9,1},... | collective-permute-start | bytes 24584 | tf_op jit(solution)/shard_map/ppermute | solution.py:200
  41.7 3.5 %copy-start.9 = (f32[128,768]{1,0:T(8,128)S(1)}, f32[128,768]{1,0:T(8,128)}, u32[]{:S(2)}) copy-start(f32[128,768]{1,0:T(8,128)} %get-tuple-element.9) | copy-start | bytes 1179652
  45.2 1.1 %copy-start.3 = (bf16[768,512]{1,0:T(8,128)(2,1)S(1)}, bf16[768,512]{1,0:T(8,128)(2,1)}, u32[]{:S(2)}) copy-start(bf16[768,512]{1,0:T(8,128)(2,1)} %param.11) | copy-start | bytes 2359300
  46.4 2.1 %copy-start.6 = (bf16[128,768]{1,0:T(8,128)(2,1)}, bf16[128,768]{1,0:T(8,128)(2,1)S(1)}, u32[]{:S(2)}) copy-start(bf16[128,768]{1,0:T(8,128)(2,1)S(1)} %fusion.18) | copy-start | bytes 589828
  47.1 1.2 %collective-permute-start.7 = (bf16[2,1,16,128]{3,2,1,0:T(8,128)(2,1)S(1)}, bf16[2,1,16,128]{3,2,1,0:T(8,128)(2,1)S(1)}, u32[]{:S(2)}, u32[]{:S(2)}) collective-permute-start(bf16[2,1,16,128]{3,2,1,0:T(8,128)(2,1)S(1)} %fusion.63), channel_id=1, source_target_pairs={{0,1},{1,0},{2,3},{3,2},{4,5},{5,4},{6,7},{7,6},{8,9},{9,8},{10,11... | collective-permute-start | bytes 24584 | tf_op jit(solution)/shard_map/ppermute | solution.py:26
  48.6 7.3 %copy-start.8 = (bf16[3,3,3,128,64]{3,4,2,1,0:T(8,128)(2,1)S(1)}, bf16[3,3,3,128,64]{3,4,2,1,0:T(8,128)(2,1)}, u32[]{:S(2)}) copy-start(bf16[3,3,3,128,64]{3,4,2,1,0:T(8,128)(2,1)} %param.13) | copy-start | bytes 1327108
  48.6 7.3 %copy-start.11 = (pred[8,3]{0,1:T(4,128)(4,1)S(1)}, pred[8,3]{0,1:T(4,128)(4,1)}, u32[]{:S(2)}) copy-start(pred[8,3]{0,1:T(4,128)(4,1)} %constant.51) | copy-start | bytes 76
  48.7 10.5 %collective-permute-start.8 = (bf16[1,34,16,128]{3,2,1,0:T(8,128)(2,1)S(1)}, bf16[1,34,16,128]{3,2,1,0:T(8,128)(2,1)S(1)}, u32[]{:S(2)}, u32[]{:S(2)}) collective-permute-start(bf16[1,34,16,128]{3,2,1,0:T(8,128)(2,1)S(1)} %get-tuple-element.12), channel_id=1, source_target_pairs={{0,2},{1,3},{2,4},{3,5},{4,6},{5,7},{6,8},{7,9},{8,10},{9,11},{10,... | collective-permute-start | bytes 417800 | tf_op jit(solution)/shard_map/ppermute | solution.py:22
  53.8 7.4 %collective-permute-start.9 = (bf16[1,34,16,128]{3,2,1,0:T(8,128)(2,1)S(1)}, bf16[1,34,16,128]{3,2,1,0:T(8,128)(2,1)S(1)}, u32[]{:S(2)}, u32[]{:S(2)}) collective-permute-start(bf16[1,34,16,128]{3,2,1,0:T(8,128)(2,1)S(1)} %get-tuple-element.13), channel_id=1, source_target_pairs={{2,0},{3,1},{4,2},{5,3},{6,4},{7,5},{8,6},{9,7},{10,8},{11,9},{12,... | collective-permute-start | bytes 417800 | tf_op jit(solution)/shard_map/ppermute | solution.py:22

commit v8 on v7

--- a/solution.py
+++ b/solution.py
@@ -80,7 +80,7 @@
         rows_ref = refs[-1]
         refs = refs[:-1]
     if ordered:
-        refs = refs[:-3] + refs[-2:]
+        refs = refs[: -2 - ordered] + refs[-2:]
     q_ref = refs[0]
     k_refs = refs[1 : 1 + chunks]
     v_refs = refs[1 + chunks : 1 + 2 * chunks]
@@ -150,7 +150,7 @@
         score_scale=score_scale,
         chunks=chunks,
         whole_output=whole_output,
-        ordered=after is not None,
+        ordered=0 if after is None else len(after),
         rows_out=rows_out,
     )
     key_specs = [pl.BlockSpec((c.shape[0], pair), lambda j: (0, j)) for c in kv_chunks]
@@ -164,7 +164,7 @@
         ]
     else:
         out_specs = [row_spec, pl.BlockSpec((token_count, stat_width), lambda j: (0, 0))]
-    extra = [] if after is None else [after]
+    extra = [] if after is None else list(after)
     extra_specs = [pl.BlockSpec(memory_space=pl.ANY) for _ in extra]
     keys = sum(c.shape[0] for c in kv_chunks)
     cost = pl.CostEstimate(
@@ -210,6 +210,20 @@
     head_size = model_width // HEADS
     score_scale = 1.0 / math.sqrt(head_size)
     half = lax.axis_size("seq") // 2
+    position = lax.axis_index("seq")
+    half_rows = token_count // GZ
+    input_grid = layer_input.reshape(1, half_rows, GZ, model_width)
+    lower_half = position % 2 == 0
+
+    def with_rims(voxels):
+        boundary = jnp.where(lower_half, voxels[:, -1:], voxels[:, :1])
+        partner = swapped(boundary, "seq", 0)
+        zero_plane = jnp.zeros_like(partner)
+        low_rim = jnp.where(lower_half, zero_plane, partner)
+        high_rim = jnp.where(lower_half, partner, zero_plane)
+        extended = jnp.concatenate([low_rim, voxels, high_rim], axis=1)
+        return extended, plane_send(extended[-1:], 2), plane_send(extended[:1], -2)
+
     queries = projected(layer_input, norm_gain, projection[:, :model_width])
     mirrored_queries = exchanged(queries, half)
     same_core = [layer_input] + [exchanged(layer_input, mask) for mask in range(2, half, 2)]
@@ -225,8 +239,15 @@
     row_major = Layout(major_to_minor=(0, 1))
     sent_lse = with_layout_constraint(remote_lse, row_major)
     other_lse = with_layout_constraint(exchanged(sent_lse, half), row_major)[:heads].T
+    skip_parts = with_rims(upsample(layer_input.reshape(1, half_rows, GZ, model_width), skip_weight))
     own_out, own_lse = attention(
-        queries, kv_chunks, head_size, score_scale, jnp.float32, False, after=remote_out
+        queries,
+        kv_chunks,
+        head_size,
+        score_scale,
+        jnp.float32,
+        False,
+        after=[remote_out, skip_parts[1], skip_parts[2]],
     )
     own_lse = own_lse[:, :heads]
     top = jnp.maximum(own_lse, other_lse) + 0 * other_out[:1, :1].astype(jnp.float32)
@@ -240,22 +261,11 @@
         layer_input.astype(jnp.float32)
         + jnp.dot(attended, output_weight, preferred_element_type=jnp.float32)
     ).astype(jnp.bfloat16)
-    position = lax.axis_index("seq")
-    half_rows = token_count // GZ
-    input_grid = layer_input.reshape(1, half_rows, GZ, model_width)
     encoded_grid = encoded.reshape(1, half_rows, GZ, model_width)
-    joined = jnp.concatenate(
-        [upsample(encoded_grid, deep_weight), upsample(input_grid, skip_weight)], axis=-1
-    )
-    lower_half = position % 2 == 0
-    boundary = jnp.where(lower_half, joined[:, -1:], joined[:, :1])
-    partner = swapped(boundary, "seq", 0)
-    zero_plane = jnp.zeros_like(partner)
-    low_rim = jnp.where(lower_half, zero_plane, partner)
-    high_rim = jnp.where(lower_half, partner, zero_plane)
-    extended = jnp.concatenate([low_rim, joined, high_rim], axis=1)
-    low_plane = plane_send(extended[-1:], 2)
-    high_plane = plane_send(extended[:1], -2)
+    deep_parts = with_rims(upsample(encoded_grid, deep_weight))
+    extended, low_plane, high_plane = [
+        jnp.concatenate([deep, skip], axis=-1) for deep, skip in zip(deep_parts, skip_parts)
+    ]
     decoded = convolve(extended, low_plane, high_plane, conv_kernel)[None]
     return (encoded, decoded)
 

time: 63.5 us -> 79.7 us (1.26)
  the two profiles are of different devices: /device:TPU:0 before, /device:TPU:16 now
where the time goes in v8:
time: 79.7 us; the launch traced here: 79.1 us
  waiting for transfers between devices  19 us (24%)
  starting transfers between devices  17.8 us (22%)
  Pallas kernels  15.1 us (19%)
  matrix products  13.2 us (17%)
  local copies, waits for them, and re-layouts  7.29 us (9%)
  other arithmetic  4.67 us (6%)
  between operations  1.96 us (2%)
    pallas_call x2, Pallas kernels, attention(): pl.pallas_call(kernel, grid=(pairs,), cost_estimate=cost, in_specs=[row_s...  15.1 us
    ppermute x4, starting transfers between devices, shifted(): return lax.ppermute(block, axis, route)  13.5 us
    ppermute x4, waiting for transfers between devices, shifted(): return lax.ppermute(block, axis, route)  13.4 us
    dot_general x3, matrix products, projected(): jnp.dot(normed, weight, preferred_element_type=jnp.float32)  7.1 us
    conv_general_dilated x3, matrix products, conv(): lax.conv_general_dilated(field[None], kernel, window_strides=(1, 1, 1), p...  4.22 us
    ppermute x7, starting transfers between devices, exchanged(): return lax.ppermute(x, 'seq', [(i, i ^ mask) for i in range(devices)])  4.16 us
    unnamed x39, local copies, waits for them, and re-layouts  3.58 us
    ppermute x7, waiting for transfers between devices, exchanged(): return lax.ppermute(x, 'seq', [(i, i ^ mask) for i in range(devices)])  3.32 us
  transfers between devices with their start and end apart: 13, of which 5 were waited for; matrix products, arithmetic and copies ran while one was open for 18% of the time, Pallas kernels for 10%

profile of v8, /device:TPU:16, one launch (start us, length us, event | category | flops | bytes accessed | tf_op | source)
XLA Modules:
  0.0 79.1 jit_solution(4787546004421391729)
XLA Ops:
  0.6 0.0 copy-start
  0.7 1.6 %collective-permute-start = (bf16[128,768]{1,0:T(8,128)(2,1)}, bf16[128,768]{1,0:T(8,128)(2,1)S(1)}, u32[]{:S(2)}, u32[]{:S(2)}) collective-permute-start(bf16[128,768]{1,0:T(8,128)(2,1)} %param.7), channel_id=1, source_target_pairs={{0,2},{1,3},{2,0},{3,1},{4,6},{5,7},{6,4},{7,5},{8,10},{9,11},{10,... | collective-permute-start | bytes 589832 | tf_op jit(solution)/shard_map/ppermute | solution.py:200
  2.3 1.6 %collective-permute-start.1 = (bf16[128,768]{1,0:T(8,128)(2,1)}, bf16[128,768]{1,0:T(8,128)(2,1)S(1)}, u32[]{:S(2)}, u32[]{:S(2)}) collective-permute-start(bf16[128,768]{1,0:T(8,128)(2,1)} %param.7), channel_id=1, source_target_pairs={{0,4},{1,5},{2,6},{3,7},{4,0},{5,1},{6,2},{7,3},{8,12},{9,13},{10,... | collective-permute-start | bytes 589832 | tf_op jit(solution)/shard_map/ppermute | solution.py:200
  3.8 0.4 collective-permute-start.2
  4.2 1.1 %convert_reduce_fusion.2 = f32[128]{0:T(128)S(1)} fusion(bf16[128,768]{1,0:T(8,128)(2,1)} %param.7), kind=kLoop, calls=%fused_computation.46 | loop fusion | flops 196480 | bytes 197120 | tf_op jit(solution)/shard_map/reduce_sum | solution.py:31
  5.3 0.7 convert_element_type.55
  6.0 1.1 %fusion.38 = f32[128]{0:T(128)S(1)} fusion(bf16[128,768]{1,0:T(8,128)(2,1)} %param.7, f32[128]{0:T(128)S(1)} %broadcast_multiply_fusion.2), kind=kLoop, calls=%fused_computation.52 | loop fusion | flops 393088 | bytes 197632 | tf_op jit(solution)/shard_map/reduce_sum | solution.py:33
  7.1 1.8 %fusion.15.refs_0_ = bf16[128,768]{1,0:T(8,128)(2,1)S(1)} fusion(bf16[768,2304]{1,0:T(8,128)(2,1)} %param.9, bf16[128,768]{1,0:T(8,128)(2,1)} %param.7, f32[768]{0:T(1024)S(1)} %convert_element_type.55, f32[128]{0:T(128)S(1)} %add_rsqrt_fusion.2, f32[128]{0:T(128)S(1)} %broadcast_multiply_fusion.2), kind=kOutput, calls=%fused_computation.27 | convolution fusion | flops 151584768 | bytes 1576960 | tf_op jit(solution)/shard_map/dot_general | solution.py:205
  8.9 0.1 collective-permute-start.4
  9.0 0.3 convolution_convert_fusion.3
  9.3 0.2 reshape_reshape.6
  9.5 0.2 copy.20
  9.7 0.1 collective-permute-start.5
  9.8 1.1 %collective-permute-done.5 = bf16[2,1,16,64]{3,2,1,0:T(8,128)(2,1)S(1)} collective-permute-done((bf16[2,1,16,64]{3,2,1,0:T(8,128)(2,1)S(1)}, bf16[2,1,16,64]{3,2,1,0:T(8,128)(2,1)S(1)}, u32[]{:S(2)}, u32[]{:S(2)}) %collective-permute-start.5) | collective-permute-done | bytes 4128 | tf_op jit(solution)/shard_map/ppermute | solution.py:26
  10.9 0.1 pad_maximum_fusion
  11.1 3.3 %collective-permute-done.2 = bf16[128,768]{1,0:T(8,128)(2,1)S(1)} collective-permute-done((bf16[128,768]{1,0:T(8,128)(2,1)}, bf16[128,768]{1,0:T(8,128)(2,1)S(1)}, u32[]{:S(2)}, u32[]{:S(2)}) %collective-permute-start.2) | collective-permute-done | bytes 196640 | tf_op jit(solution)/shard_map/ppermute | solution.py:200
  14.4 0.2 convert_reduce_fusion.1
  14.6 0.1 collective-permute-start.3
  14.7 0.4 fusion.9
  15.1 2.7 %convolution_convert_fusion.1.refs_1_.refs_3_ = bf16[512,1536]{1,0:T(8,128)(2,1)} fusion(bf16[768,2304]{1,0:T(8,128)(2,1)S(1)} %copy-done.11, bf16[512,768]{1,0:T(8,128)(2,1)S(1)} %constant_dynamic-update-slice_fusion, f32[768]{0:T(1024)S(1)} %convert_element_type.55, f32[512]{0:T(512)S(1)} %add_rsqrt_fusion.1, f32[512]{0:T(512)S(1)} %broadcast_multiply_fusion.1), kind=kOutput, calls=%fused_computation.1 | convolution fusion | flops 1210712064 | bytes 4726784 | tf_op jit(solution)/shard_map/dot_general | solution.py:205
  17.7 0.2 convert_reduce_fusion
  17.9 0.4 fusion.6
  18.3 2.6 %convolution_convert_fusion.refs_2_.refs_4_ = bf16[512,1536]{1,0:T(8,128)(2,1)} fusion(bf16[768,2304]{1,0:T(8,128)(2,1)S(1)} %copy-done.11, bf16[512,768]{1,0:T(8,128)(2,1)S(1)} %collective-permute-done.3, f32[512]{0:T(512)S(1)} %add_rsqrt_fusion, f32[512]{0:T(512)S(1)} %broadcast_multiply_fusion, f32[768]{0:T(1024)S(1)} %convert_element_type.55), kind=kOutput, calls=%fused_computation | convolution fusion | flops 1210712064 | bytes 4726784 | tf_op jit(solution)/shard_map/dot_general | solution.py:205
  21.0 0.7 copy-done.8
  21.6 7.6 %shard_map.86 = (bf16[128,768]{1,0:T(8,128)(2,1)}, f32[128,128]{1,0:T(8,128)}, f32[16,128]{1,0:T(8,128)}) custom-call(bf16[128,768]{1,0:T(8,128)(2,1)} %copy-done.8, bf16[512,1536]{1,0:T(8,128)(2,1)} %convolution_convert_fusion.1.refs_1_.refs_3_, bf16[512,1536]{1,0:T(8,128)(2,1)} %convolution_convert_fusion.refs_2_.refs_4_, ...), custom_call_target="tpu_custom_call" | custom-call | flops 805306368 | bytes 3932160 | tf_op jit(solution)/shard_map/pallas_call | solution.py:185
  29.2 0.4 collective-permute-start.9
  29.7 5.7 %collective-permute-start.6 = (bf16[1,34,16,64]{3,2,1,0:T(8,128)(2,1)S(1)}, bf16[1,34,16,64]{3,2,1,0:T(8,128)(2,1)S(1)}, u32[]{:S(2)}, u32[]{:S(2)}) collective-permute-start(bf16[1,34,16,64]{3,2,1,0:T(8,128)(2,1)S(1)} %get-tuple-element.15), channel_id=1, source_target_pairs={{0,2},{1,3},{2,4},{3,5},{4,6},{5,7},{6,8},{7,9},{8,10},{9,11},{10,... | collective-permute-start | bytes 208904 | tf_op jit(solution)/shard_map/ppermute | solution.py:22
  35.4 1.9 %collective-permute-start.7 = (bf16[1,34,16,64]{3,2,1,0:T(8,128)(2,1)S(1)}, bf16[1,34,16,64]{3,2,1,0:T(8,128)(2,1)S(1)}, u32[]{:S(2)}, u32[]{:S(2)}) collective-permute-start(bf16[1,34,16,64]{3,2,1,0:T(8,128)(2,1)S(1)} %get-tuple-element.14), channel_id=1, source_target_pairs={{2,0},{3,1},{4,2},{5,3},{6,4},{7,5},{8,6},{9,7},{10,8},{11,9},{12,... | collective-permute-start | bytes 208904 | tf_op jit(solution)/shard_map/ppermute | solution.py:22
  37.3 0.1 collective-permute-start.8
  37.4 8.7 %collective-permute-done.6.refs_6_ = bf16[1,34,16,64]{3,2,1,0:T(8,128)(2,1)S(1)} collective-permute-done((bf16[1,34,16,64]{3,2,1,0:T(8,128)(2,1)S(1)}, bf16[1,34,16,64]{3,2,1,0:T(8,128)(2,1)S(1)}, u32[]{:S(2)}, u32[]{:S(2)}) %collective-permute-start.6) | collective-permute-done | bytes 69664 | tf_op jit(solution)/shard_map/ppermute | solution.py:22
  46.1 0.7 copy-done.4
  46.8 0.7 copy-done.6
  47.4 7.5 %shard_map.87 = (f32[128,768]{1,0:T(8,128)}, f32[128,128]{1,0:T(8,128)}) custom-call(bf16[128,768]{1,0:T(8,128)(2,1)} %copy-done.10, bf16[512,1536]{1,0:T(8,128)(2,1)} %convolution_convert_fusion.1.refs_1_.refs_3_, bf16[512,1536]{1,0:T(8,128)(2,1)} %convolution_convert_fusion.refs_2_.refs_4_, bf16[512,1536]{1,0:T(8,128)(2,1)} %convolution_convert_fusion.1.refs_1_.refs_3_, ...), custom_call_target="tpu_custom_call" | custom-call | flops 805306368 | bytes 3932160 | tf_op jit(solution)/shard_map/pallas_call | solution.py:185
  55.0 1.0 %copy.21 = f32[128,128]{0,1:T(8,128)S(1)} copy(f32[128,128]{1,0:T(8,128)} %get-tuple-element.7) | data formatting | bytes 131072 | tf_op jit(solution)/shard_map/pallas_call | solution.py:185
  56.0 0.6 slice.72
  57.3 0.2 copy.22
  57.5 0.2 copy.23
  57.7 1.3 %fusion.18 = bf16[128,768]{1,0:T(8,128)(2,1)S(1)} fusion(bf16[768,768]{1,0:T(8,128)(2,1)S(1)} %copy-done, bf16[128,768]{1,0:T(8,128)(2,1)S(1)} %copy-done.1, f32[128,768]{1,0:T(8,128)S(1)} %copy.22, f32[128,768]{1,0:T(8,128)S(1)} %copy.23, bf16[128,768]{1,0:T(8,128)(2,1)} %copy-done.14, f32[128,768]{1,0:T(8,128)S(1)} %copy-done.13), kind=kOutput, calls=%fused_computation.28 | convolution fusion | flops 151977984 | bytes 2949120 | tf_op jit(solution)/shard_map/dot_general | solution.py:262
  59.1 0.3 convolution_convert_fusion.2
  59.4 0.2 reshape_reshape.7
  59.5 0.2 copy.26
  59.7 0.1 collective-permute-start.10
  59.9 1.1 %collective-permute-done.10 = bf16[2,1,16,64]{3,2,1,0:T(8,128)(2,1)S(1)} collective-permute-done((bf16[2,1,16,64]{3,2,1,0:T(8,128)(2,1)S(1)}, bf16[2,1,16,64]{3,2,1,0:T(8,128)(2,1)S(1)}, u32[]{:S(2)}, u32[]{:S(2)}) %collective-permute-start.10) | collective-permute-done | bytes 4128 | tf_op jit(solution)/shard_map/ppermute | solution.py:26
  61.0 0.2 maximum_bitcast_fusion
  61.2 0.1 pad_maximum_fusion.1
  61.3 0.2 copy.40
  61.5 0.3 pad.clone
  61.8 0.1 copy.29
  61.8 0.1 slice.75
  61.9 0.2 copy-done.12
  62.2 3.0 %convolution_select_fusion = f32[2,32,8,3,64]{4,2,3,1,0:T(8,128)S(1)} fusion(bf16[3,3,3,128,64]{3,4,2,1,0:T(8,128)(2,1)S(1)} %copy-done.12, bf16[2,34,1,7,2,128]{5,3,4,1,0,2:T(8,128)(2,1)S(1)} %slice.75, bf16[2,34,1,8,3,128]{5,3,4,1,0,2:T(8,128)(2,1)S(1)} %copy.29, pred[8,3]{0,1:T(4,128)(4,1)S(1)} %copy-done.15), kind=kOutput, calls=%fused_computation.21 | convolution fusion | flops 455172096 | bytes 1497112 | tf_op jit(solution)/shard_map/conv_general_dilated | solution.py:55
  65.2 0.2 copy.30
  65.4 1.9 %collective-permute-start.12 = (bf16[1,34,16,64]{3,2,1,0:T(8,128)(2,1)S(1)}, bf16[1,34,16,64]{3,2,1,0:T(8,128)(2,1)S(1)}, u32[]{:S(2)}, u32[]{:S(2)}) collective-permute-start(bf16[1,34,16,64]{3,2,1,0:T(8,128)(2,1)S(1)} %get-tuple-element.13), channel_id=1, source_target_pairs={{2,0},{3,1},{4,2},{5,3},{6,4},{7,5},{8,6},{9,7},{10,8},{11,9},{12,... | collective-permute-start | bytes 208904 | tf_op jit(solution)/shard_map/ppermute | solution.py:22
  67.4 3.9 %collective-permute-start.11 = (bf16[1,34,16,64]{3,2,1,0:T(8,128)(2,1)S(1)}, bf16[1,34,16,64]{3,2,1,0:T(8,128)(2,1)S(1)}, u32[]{:S(2)}, u32[]{:S(2)}) collective-permute-start(bf16[1,34,16,64]{3,2,1,0:T(8,128)(2,1)S(1)} %get-tuple-element.12), channel_id=1, source_target_pairs={{0,2},{1,3},{2,4},{3,5},{4,6},{5,7},{6,8},{7,9},{8,10},{9,11},{10,... | collective-permute-start | bytes 208904 | tf_op jit(solution)/shard_map/ppermute | solution.py:22
  71.3 4.7 %collective-permute-done.12 = bf16[1,34,16,64]{3,2,1,0:T(8,128)(2,1)S(1)} collective-permute-done((bf16[1,34,16,64]{3,2,1,0:T(8,128)(2,1)S(1)}, bf16[1,34,16,64]{3,2,1,0:T(8,128)(2,1)S(1)}, u32[]{:S(2)}, u32[]{:S(2)}) %collective-permute-start.12) | collective-permute-done | bytes 69664 | tf_op jit(solution)/shard_map/ppermute | solution.py:22
  76.0 0.1 maximum_bitcast_fusion.2
  76.3 0.6 convolution_select_fusion.1
  76.9 0.1 copy.38
  77.0 0.1 copy-done.5
  77.2 0.1 maximum_bitcast_fusion.1
  77.4 0.6 convolution_select_fusion.2
  78.0 0.1 copy.34
  78.2 0.1 fusion.54
  78.3 0.8 %copy.39 = bf16[1,2,32,16,64]{4,3,2,1,0:T(8,128)(2,1)} copy(bf16[1,2,32,16,64]{4,2,3,1,0:T(8,128)(2,1)S(1)} %fusion.54) | data formatting | bytes 262144
  (63 shorter events, 0.7 us)
Async XLA Ops:
  0.6 57.1 %copy-start = (bf16[768,768]{1,0:T(8,128)(2,1)S(1)}, bf16[768,768]{1,0:T(8,128)(2,1)}, u32[]{:S(2)}) copy-start(bf16[768,768]{1,0:T(8,128)(2,1)} %param.10) | copy-start | bytes 3538948
  0.6 8.3 %copy-start.1 = (bf16[128,768]{1,0:T(8,128)(2,1)S(1)}, bf16[128,768]{1,0:T(8,128)(2,1)}, u32[]{:S(2)}) copy-start(bf16[128,768]{1,0:T(8,128)(2,1)} %param.7) | copy-start | bytes 589828
  0.7 8.3 %copy-start.2 = (bf16[768,512]{1,0:T(8,128)(2,1)S(1)}, bf16[768,512]{1,0:T(8,128)(2,1)}, u32[]{:S(2)}) copy-start(bf16[768,512]{1,0:T(8,128)(2,1)} %param.12) | copy-start | bytes 2359300
  0.7 10.3 %collective-permute-start = (bf16[128,768]{1,0:T(8,128)(2,1)}, bf16[128,768]{1,0:T(8,128)(2,1)S(1)}, u32[]{:S(2)}, u32[]{:S(2)}) collective-permute-start(bf16[128,768]{1,0:T(8,128)(2,1)} %param.7), channel_id=1, source_target_pairs={{0,2},{1,3},{2,0},{3,1},{4,6},{5,7},{6,4},{7,5},{8,10},{9,11},{10,... | collective-permute-start | bytes 589832 | tf_op jit(solution)/shard_map/ppermute | solution.py:200
  2.3 8.8 %collective-permute-start.1 = (bf16[128,768]{1,0:T(8,128)(2,1)}, bf16[128,768]{1,0:T(8,128)(2,1)S(1)}, u32[]{:S(2)}, u32[]{:S(2)}) collective-permute-start(bf16[128,768]{1,0:T(8,128)(2,1)} %param.7), channel_id=1, source_target_pairs={{0,4},{1,5},{2,6},{3,7},{4,0},{5,1},{6,2},{7,3},{8,12},{9,13},{10,... | collective-permute-start | bytes 589832 | tf_op jit(solution)/shard_map/ppermute | solution.py:200
  3.8 10.6 %collective-permute-start.2 = (bf16[128,768]{1,0:T(8,128)(2,1)}, bf16[128,768]{1,0:T(8,128)(2,1)S(1)}, u32[]{:S(2)}, u32[]{:S(2)}) collective-permute-start(bf16[128,768]{1,0:T(8,128)(2,1)} %param.7), channel_id=1, source_target_pairs={{0,6},{1,7},{2,4},{3,5},{4,2},{5,3},{6,0},{7,1},{8,14},{9,15},{10,... | collective-permute-start | bytes 589832 | tf_op jit(solution)/shard_map/ppermute | solution.py:200
  8.9 2.2 %copy-start.10 = (bf16[128,768]{1,0:T(8,128)(2,1)}, bf16[128,768]{1,0:T(8,128)(2,1)S(1)}, u32[]{:S(2)}) copy-start(bf16[128,768]{1,0:T(8,128)(2,1)S(1)} %fusion.15.refs_0_) | copy-start | bytes 589828
  8.9 12.1 %collective-permute-start.4 = (bf16[128,768]{1,0:T(8,128)(2,1)S(1)}, bf16[128,768]{1,0:T(8,128)(2,1)S(1)}, u32[]{:S(2)}, u32[]{:S(2)}) collective-permute-start(bf16[128,768]{1,0:T(8,128)(2,1)S(1)} %fusion.15.refs_0_), channel_id=1, source_target_pairs={{0,8},{1,9},{2,10},{3,11},{4,12},{5,13},{6,14},{7,15},{8,0},{9,1},... | collective-permute-start | bytes 589832 | tf_op jit(solution)/shard_map/ppermute | solution.py:200
  9.7 1.2 %collective-permute-start.5 = (bf16[2,1,16,64]{3,2,1,0:T(8,128)(2,1)S(1)}, bf16[2,1,16,64]{3,2,1,0:T(8,128)(2,1)S(1)}, u32[]{:S(2)}, u32[]{:S(2)}) collective-permute-start(bf16[2,1,16,64]{3,2,1,0:T(8,128)(2,1)S(1)} %slice_select_fusion.1), channel_id=1, source_target_pairs={{0,1},{1,0},{2,3},{3,2},{4,5},{5,4},{6,7},{7,6},{8,9},{9,8},{10,11... | collective-permute-start | bytes 12296 | tf_op jit(solution)/shard_map/ppermute | solution.py:26
  9.8 5.3 %copy-start.11 = (bf16[768,2304]{1,0:T(8,128)(2,1)S(1)}, bf16[768,2304]{1,0:T(8,128)(2,1)}, u32[]{:S(2)}) copy-start(bf16[768,2304]{1,0:T(8,128)(2,1)} %param.9) | copy-start | bytes 10616836
  14.6 3.2 %collective-permute-start.3 = (bf16[512,768]{1,0:T(8,128)(2,1)S(1)}, bf16[512,768]{1,0:T(8,128)(2,1)S(1)}, u32[]{:S(2)}, u32[]{:S(2)}) collective-permute-start(bf16[512,768]{1,0:T(8,128)(2,1)S(1)} %constant_dynamic-update-slice_fusion), channel_id=1, source_target_pairs={{0,1},{1,0},{2,3},{3,2},{4,5},{5,4},{6,7},{7,6},{8,9},{9,8},{10,11... | collective-permute-start | bytes 2359304 | tf_op jit(solution)/shard_map/ppermute | solution.py:200
  21.0 0.7 copy-start.8
  29.2 26.7 %collective-permute-start.9 = (bf16[128,768]{1,0:T(8,128)(2,1)}, bf16[128,768]{1,0:T(8,128)(2,1)S(1)}, u32[]{:S(2)}, u32[]{:S(2)}) collective-permute-start(bf16[128,768]{1,0:T(8,128)(2,1)} %get-tuple-element.6.refs_5_), channel_id=1, source_target_pairs={{0,8},{1,9},{2,10},{3,11},{4,12},{5,13},{6,14},{7,15},{8,0},{9,1},... | collective-permute-start | bytes 589832 | tf_op jit(solution)/shard_map/ppermute | solution.py:200
  29.7 16.5 %collective-permute-start.6 = (bf16[1,34,16,64]{3,2,1,0:T(8,128)(2,1)S(1)}, bf16[1,34,16,64]{3,2,1,0:T(8,128)(2,1)S(1)}, u32[]{:S(2)}, u32[]{:S(2)}) collective-permute-start(bf16[1,34,16,64]{3,2,1,0:T(8,128)(2,1)S(1)} %get-tuple-element.15), channel_id=1, source_target_pairs={{0,2},{1,3},{2,4},{3,5},{4,6},{5,7},{6,8},{7,9},{8,10},{9,11},{10,... | collective-permute-start | bytes 208904 | tf_op jit(solution)/shard_map/ppermute | solution.py:22
  35.4 10.7 %collective-permute-start.7 = (bf16[1,34,16,64]{3,2,1,0:T(8,128)(2,1)S(1)}, bf16[1,34,16,64]{3,2,1,0:T(8,128)(2,1)S(1)}, u32[]{:S(2)}, u32[]{:S(2)}) collective-permute-start(bf16[1,34,16,64]{3,2,1,0:T(8,128)(2,1)S(1)} %get-tuple-element.14), channel_id=1, source_target_pairs={{2,0},{3,1},{4,2},{5,3},{6,4},{7,5},{8,6},{9,7},{10,8},{11,9},{12,... | collective-permute-start | bytes 208904 | tf_op jit(solution)/shard_map/ppermute | solution.py:22
  37.3 19.9 %collective-permute-start.8 = (f32[16,128]{1,0:T(8,128)}, f32[16,128]{1,0:T(8,128)S(1)}, u32[]{:S(2)}, u32[]{:S(2)}) collective-permute-start(f32[16,128]{1,0:T(8,128)} %get-tuple-element.8), channel_id=1, source_target_pairs={{0,8},{1,9},{2,10},{3,11},{4,12},{5,13},{6,14},{7,15},{8,0},{9,1},... | collective-permute-start | bytes 24584 | tf_op jit(solution)/shard_map/ppermute | solution.py:200
  46.1 0.7 copy-start.4
  46.8 0.7 copy-start.6
  55.0 2.7 %copy-start.13 = (f32[128,768]{1,0:T(8,128)S(1)}, f32[128,768]{1,0:T(8,128)}, u32[]{:S(2)}) copy-start(f32[128,768]{1,0:T(8,128)} %get-tuple-element.9) | copy-start | bytes 1179652
  56.0 1.3 %copy-start.14 = (bf16[128,768]{1,0:T(8,128)(2,1)}, bf16[128,768]{1,0:T(8,128)(2,1)S(1)}, u32[]{:S(2)}) copy-start(bf16[128,768]{1,0:T(8,128)(2,1)S(1)} %collective-permute-done.9) | copy-start | bytes 589828
  57.7 1.4 %copy-start.3 = (bf16[768,512]{1,0:T(8,128)(2,1)S(1)}, bf16[768,512]{1,0:T(8,128)(2,1)}, u32[]{:S(2)}) copy-start(bf16[768,512]{1,0:T(8,128)(2,1)} %param.11) | copy-start | bytes 2359300
  59.1 2.2 %copy-start.9 = (bf16[128,768]{1,0:T(8,128)(2,1)}, bf16[128,768]{1,0:T(8,128)(2,1)S(1)}, u32[]{:S(2)}) copy-start(bf16[128,768]{1,0:T(8,128)(2,1)S(1)} %fusion.18) | copy-start | bytes 589828
  59.7 1.2 %collective-permute-start.10 = (bf16[2,1,16,64]{3,2,1,0:T(8,128)(2,1)S(1)}, bf16[2,1,16,64]{3,2,1,0:T(8,128)(2,1)S(1)}, u32[]{:S(2)}, u32[]{:S(2)}) collective-permute-start(bf16[2,1,16,64]{3,2,1,0:T(8,128)(2,1)S(1)} %slice_select_fusion), channel_id=1, source_target_pairs={{0,1},{1,0},{2,3},{3,2},{4,5},{5,4},{6,7},{7,6},{8,9},{9,8},{10,11... | collective-permute-start | bytes 12296 | tf_op jit(solution)/shard_map/ppermute | solution.py:26
  61.2 1.0 %copy-start.12 = (bf16[3,3,3,128,64]{3,4,2,1,0:T(8,128)(2,1)S(1)}, bf16[3,3,3,128,64]{3,4,2,1,0:T(8,128)(2,1)}, u32[]{:S(2)}) copy-start(bf16[3,3,3,128,64]{3,4,2,1,0:T(8,128)(2,1)} %param.13) | copy-start | bytes 1327108
  61.2 1.0 %copy-start.15 = (pred[8,3]{0,1:T(4,128)(4,1)S(1)}, pred[8,3]{0,1:T(4,128)(4,1)}, u32[]{:S(2)}) copy-start(pred[8,3]{0,1:T(4,128)(4,1)} %constant.51) | copy-start | bytes 76
  65.2 10.8 %copy-start.7 = (bf16[1,34,16,64]{3,2,1,0:T(8,128)(2,1)S(1)}, bf16[1,34,16,64]{3,2,1,0:T(8,128)(2,1)}, u32[]{:S(2)}) copy-start(bf16[1,34,16,64]{3,2,1,0:T(8,128)(2,1)} %copy-done.6) | copy-start | bytes 208900
  65.4 10.6 %collective-permute-start.12 = (bf16[1,34,16,64]{3,2,1,0:T(8,128)(2,1)S(1)}, bf16[1,34,16,64]{3,2,1,0:T(8,128)(2,1)S(1)}, u32[]{:S(2)}, u32[]{:S(2)}) collective-permute-start(bf16[1,34,16,64]{3,2,1,0:T(8,128)(2,1)S(1)} %get-tuple-element.13), channel_id=1, source_target_pairs={{2,0},{3,1},{4,2},{5,3},{6,4},{7,5},{8,6},{9,7},{10,8},{11,9},{12,... | collective-permute-start | bytes 208904 | tf_op jit(solution)/shard_map/ppermute | solution.py:22
  67.4 9.6 %collective-permute-start.11 = (bf16[1,34,16,64]{3,2,1,0:T(8,128)(2,1)S(1)}, bf16[1,34,16,64]{3,2,1,0:T(8,128)(2,1)S(1)}, u32[]{:S(2)}, u32[]{:S(2)}) collective-permute-start(bf16[1,34,16,64]{3,2,1,0:T(8,128)(2,1)S(1)} %get-tuple-element.12), channel_id=1, source_target_pairs={{0,2},{1,3},{2,4},{3,5},{4,6},{5,7},{6,8},{7,9},{8,10},{9,11},{10,... | collective-permute-start | bytes 208904 | tf_op jit(solution)/shard_map/ppermute | solution.py:22
  76.2 0.9 %copy-start.5 = (bf16[1,34,16,64]{3,2,1,0:T(8,128)(2,1)S(1)}, bf16[1,34,16,64]{3,2,1,0:T(8,128)(2,1)}, u32[]{:S(2)}) copy-start(bf16[1,34,16,64]{3,2,1,0:T(8,128)(2,1)} %copy-done.4) | copy-start | bytes 208900

commit v9 on v7

--- a/solution.py
+++ b/solution.py
@@ -72,6 +72,12 @@
 
 def plane_send(plane, offset):
     return shifted(plane, "seq", offset)
+
+
+def corner_send(row, offset):
+    devices = range(lax.axis_size("seq"))
+    route = [(i, (i ^ 1) + offset) for i in devices if (i ^ 1) + offset in devices]
+    return lax.ppermute(row, "seq", route)
 
 
 def attention_kernel(*refs, head_size, score_scale, chunks, whole_output, ordered, rows_out):
@@ -250,13 +256,21 @@
     lower_half = position % 2 == 0
     boundary = jnp.where(lower_half, joined[:, -1:], joined[:, :1])
     partner = swapped(boundary, "seq", 0)
-    zero_plane = jnp.zeros_like(partner)
-    low_rim = jnp.where(lower_half, zero_plane, partner)
-    high_rim = jnp.where(lower_half, partner, zero_plane)
-    extended = jnp.concatenate([low_rim, joined, high_rim], axis=1)
-    low_plane = plane_send(extended[-1:], 2)
-    high_plane = plane_send(extended[:1], -2)
-    decoded = convolve(extended, low_plane, high_plane, conv_kernel)[None]
+    low_plane = plane_send(joined[-1:], 2)
+    high_plane = plane_send(joined[:1], -2)
+    low_corner = corner_send(boundary[-1:], 2)
+    high_corner = corner_send(boundary[:1], -2)
+
+    def rimmed(core, rim):
+        zero_plane = jnp.zeros_like(rim)
+        low_rim = jnp.where(lower_half, zero_plane, rim)
+        high_rim = jnp.where(lower_half, rim, zero_plane)
+        return jnp.concatenate([low_rim, core, high_rim], axis=1)
+
+    extended = rimmed(joined, partner)
+    decoded = convolve(
+        extended, rimmed(low_plane, low_corner), rimmed(high_plane, high_corner), conv_kernel
+    )[None]
     return (encoded, decoded)
 
 

time: 63.5 us -> 69.1 us (1.088)
  starting transfers between devices: 17.4 us -> 20.5 us
  waiting for transfers between devices: 5.51 us -> 7.28 us
    ppermute x0 -> x2, starting transfers between devices: none -> 5.98 us  [corner_send(): return lax.ppermute(row, 'seq', route)]
    ppermute x0 -> x2, waiting for transfers between devices: none -> 4.02 us  [corner_send(): return lax.ppermute(row, 'seq', route)]
    ppermute x2, starting transfers between devices: 6.57 us -> 3.12 us  [shifted(): return lax.ppermute(block, axis, route)]
    ppermute x1, waiting for transfers between devices: 1.16 us -> 0.01 us  [swapped(): lax.ppermute(x, axis, [(i, i ^ 1 << distance) for i in range(lax.axis_siz...]
    ppermute x2, waiting for transfers between devices: 1.09 us -> 0.01 us  [shifted(): return lax.ppermute(block, axis, route)]
  transfers between devices with their start and end apart: 10 -> 12, of which waited for: 4 -> 3; matrix products, arithmetic and copies ran while one was open for 29% -> 27% of each run, Pallas kernels for 12% -> 11%
where the time goes in v9:
time: 69.1 us; the launch traced here: 68.2 us
  starting transfers between devices  20.5 us (30%)
  Pallas kernels  15.2 us (22%)
  matrix products  12.3 us (18%)
  waiting for transfers between devices  7.28 us (11%)
  local copies, waits for them, and re-layouts  6.42 us (9%)
  other arithmetic  4.6 us (7%)
  between operations  1.88 us (3%)
    pallas_call x2, Pallas kernels, attention(): pl.pallas_call(kernel, grid=(pairs,), cost_estimate=cost, in_specs=[row_s...  15.2 us
    ppermute x7, starting transfers between devices, exchanged(): return lax.ppermute(x, 'seq', [(i, i ^ mask) for i in range(devices)])  10.8 us
    dot_general x3, matrix products, projected(): jnp.dot(normed, weight, preferred_element_type=jnp.float32)  7.2 us
    ppermute x2, starting transfers between devices, corner_send(): return lax.ppermute(row, 'seq', route)  5.98 us
    conv_general_dilated x3, matrix products, conv(): lax.conv_general_dilated(field[None], kernel, window_strides=(1, 1, 1), p...  4.23 us
    ppermute x2, waiting for transfers between devices, corner_send(): return lax.ppermute(row, 'seq', route)  4.02 us
    ppermute x7, waiting for transfers between devices, exchanged(): return lax.ppermute(x, 'seq', [(i, i ^ mask) for i in range(devices)])  3.25 us
    ppermute x2, starting transfers between devices, shifted(): return lax.ppermute(block, axis, route)  3.12 us
  transfers between devices with their start and end apart: 12, of which 3 were waited for; matrix products, arithmetic and copies ran while one was open for 27% of the time, Pallas kernels for 11%

profile of v9, /device:TPU:0, one launch (start us, length us, event | category | flops | bytes accessed | tf_op | source)
XLA Modules:
  0.0 68.2 jit_solution(11472117134965698505)
XLA Ops:
  0.6 0.0 copy-start
  0.6 0.0 copy-start.1
  0.7 3.1 %collective-permute-start = (bf16[128,768]{1,0:T(8,128)(2,1)}, bf16[128,768]{1,0:T(8,128)(2,1)S(1)}, u32[]{:S(2)}, u32[]{:S(2)}) collective-permute-start(bf16[128,768]{1,0:T(8,128)(2,1)} %param.7), channel_id=1, source_target_pairs={{0,2},{1,3},{2,0},{3,1},{4,6},{5,7},{6,4},{7,5},{8,10},{9,11},{10,... | collective-permute-start | bytes 589832 | tf_op jit(solution)/shard_map/ppermute | solution.py:206
  3.7 1.6 %collective-permute-start.1 = (bf16[128,768]{1,0:T(8,128)(2,1)}, bf16[128,768]{1,0:T(8,128)(2,1)S(1)}, u32[]{:S(2)}, u32[]{:S(2)}) collective-permute-start(bf16[128,768]{1,0:T(8,128)(2,1)} %param.7), channel_id=1, source_target_pairs={{0,4},{1,5},{2,6},{3,7},{4,0},{5,1},{6,2},{7,3},{8,12},{9,13},{10,... | collective-permute-start | bytes 589832 | tf_op jit(solution)/shard_map/ppermute | solution.py:206
  5.3 0.0 collective-permute-start.2
  5.3 1.1 %convert_reduce_fusion.2 = f32[128]{0:T(128)S(1)} fusion(bf16[128,768]{1,0:T(8,128)(2,1)} %param.7), kind=kLoop, calls=%fused_computation.46 | loop fusion | flops 196480 | bytes 197120 | tf_op jit(solution)/shard_map/reduce_sum | solution.py:31
  6.4 0.7 %convert_element_type.55 = f32[768]{0:T(1024)S(1)} convert(bf16[768]{0:T(1024)(128)(2,1)} %param.8) | non-fusion elementwise | flops 768 | bytes 4608 | tf_op jit(solution)/shard_map/convert_element_type | solution.py:34
  7.1 1.1 %fusion.38 = f32[128]{0:T(128)S(1)} fusion(bf16[128,768]{1,0:T(8,128)(2,1)} %param.7, f32[128]{0:T(128)S(1)} %broadcast_multiply_fusion.2), kind=kLoop, calls=%fused_computation.52 | loop fusion | flops 393088 | bytes 197632 | tf_op jit(solution)/shard_map/reduce_sum | solution.py:33
  8.2 0.0 copy-start.7
  8.2 1.9 %fusion.15.refs_0_ = bf16[128,768]{1,0:T(8,128)(2,1)S(1)} fusion(bf16[768,2304]{1,0:T(8,128)(2,1)} %param.9, bf16[128,768]{1,0:T(8,128)(2,1)} %param.7, f32[768]{0:T(1024)S(1)} %convert_element_type.55, f32[128]{0:T(128)S(1)} %add_rsqrt_fusion.2, f32[128]{0:T(128)S(1)} %broadcast_multiply_fusion.2), kind=kOutput, calls=%fused_computation.27 | convolution fusion | flops 151584768 | bytes 1576960 | tf_op jit(solution)/shard_map/dot_general | solution.py:211
  10.1 3.0 %collective-permute-start.4 = (bf16[128,768]{1,0:T(8,128)(2,1)S(1)}, bf16[128,768]{1,0:T(8,128)(2,1)S(1)}, u32[]{:S(2)}, u32[]{:S(2)}) collective-permute-start(bf16[128,768]{1,0:T(8,128)(2,1)S(1)} %fusion.15.refs_0_), channel_id=1, source_target_pairs={{0,8},{1,9},{2,10},{3,11},{4,12},{5,13},{6,14},{7,15},{8,0},{9,1},... | collective-permute-start | bytes 589832 | tf_op jit(solution)/shard_map/ppermute | solution.py:206
  13.2 2.3 %collective-permute-done.2 = bf16[128,768]{1,0:T(8,128)(2,1)S(1)} collective-permute-done((bf16[128,768]{1,0:T(8,128)(2,1)}, bf16[128,768]{1,0:T(8,128)(2,1)S(1)}, u32[]{:S(2)}, u32[]{:S(2)}) %collective-permute-start.2) | collective-permute-done | bytes 196640 | tf_op jit(solution)/shard_map/ppermute | solution.py:206
  15.6 0.1 collective-permute-start.3
  15.7 0.2 convert_reduce_fusion.1
  15.9 0.4 fusion.9
  16.2 2.7 %convolution_convert_fusion.1.refs_1_.refs_3_ = bf16[512,1536]{1,0:T(8,128)(2,1)} fusion(bf16[768,2304]{1,0:T(8,128)(2,1)S(1)} %copy-done.7, bf16[512,768]{1,0:T(8,128)(2,1)S(1)} %constant_dynamic-update-slice_fusion, f32[768]{0:T(1024)S(1)} %convert_element_type.55, f32[512]{0:T(512)S(1)} %add_rsqrt_fusion.1, f32[512]{0:T(512)S(1)} %broadcast_multiply_fusion.1), kind=kOutput, calls=%fused_computation.1 | convolution fusion | flops 1210712064 | bytes 4726784 | tf_op jit(solution)/shard_map/dot_general | solution.py:211
  18.9 0.0 collective-permute-done.3
  18.9 0.2 convert_reduce_fusion
  19.1 0.4 fusion.6
  19.5 2.7 %convolution_convert_fusion.refs_2_.refs_4_ = bf16[512,1536]{1,0:T(8,128)(2,1)} fusion(bf16[768,2304]{1,0:T(8,128)(2,1)S(1)} %copy-done.7, bf16[512,768]{1,0:T(8,128)(2,1)S(1)} %collective-permute-done.3, f32[512]{0:T(512)S(1)} %add_rsqrt_fusion, f32[512]{0:T(512)S(1)} %broadcast_multiply_fusion, f32[768]{0:T(1024)S(1)} %convert_element_type.55), kind=kOutput, calls=%fused_computation | convolution fusion | flops 1210712064 | bytes 4726784 | tf_op jit(solution)/shard_map/dot_general | solution.py:211
  22.1 0.7 copy-done.5
  22.8 7.6 %shard_map.86 = (bf16[128,768]{1,0:T(8,128)(2,1)}, f32[128,128]{1,0:T(8,128)}, f32[16,128]{1,0:T(8,128)}) custom-call(bf16[128,768]{1,0:T(8,128)(2,1)} %copy-done.5, bf16[512,1536]{1,0:T(8,128)(2,1)} %convolution_convert_fusion.1.refs_1_.refs_3_, bf16[512,1536]{1,0:T(8,128)(2,1)} %convolution_convert_fusion.refs_2_.refs_4_, ...), custom_call_target="tpu_custom_call" | custom-call | flops 805306368 | bytes 3932160 | tf_op jit(solution)/shard_map/pallas_call | solution.py:191
  30.4 2.9 %collective-permute-start.6 = (bf16[128,768]{1,0:T(8,128)(2,1)}, bf16[128,768]{1,0:T(8,128)(2,1)S(1)}, u32[]{:S(2)}, u32[]{:S(2)}) collective-permute-start(bf16[128,768]{1,0:T(8,128)(2,1)} %get-tuple-element.6.refs_5_), channel_id=1, source_target_pairs={{0,8},{1,9},{2,10},{3,11},{4,12},{5,13},{6,14},{7,15},{8,0},{9,1},... | collective-permute-start | bytes 589832 | tf_op jit(solution)/shard_map/ppermute | solution.py:206
  33.4 0.3 convolution_convert_fusion.2
  33.6 0.2 reshape_reshape.7
  33.8 0.2 copy.18
  34.1 0.1 collective-permute-start.5
  34.2 7.5 %shard_map.87 = (f32[128,768]{1,0:T(8,128)}, f32[128,128]{1,0:T(8,128)}) custom-call(bf16[128,768]{1,0:T(8,128)(2,1)} %copy-done.4, bf16[512,1536]{1,0:T(8,128)(2,1)} %convolution_convert_fusion.1.refs_1_.refs_3_, bf16[512,1536]{1,0:T(8,128)(2,1)} %convolution_convert_fusion.refs_2_.refs_4_, bf16[512,1536]{1,0:T(8,128)(2,1)} %convolution_convert_fusion.1.refs_1_.refs_3_, ...), custom_call_target="tpu_custom_call" | custom-call | flops 805306368 | bytes 3932160 | tf_op jit(solution)/shard_map/pallas_call | solution.py:191
  41.7 1.0 %copy.12 = f32[128,128]{0,1:T(8,128)S(1)} copy(f32[128,128]{1,0:T(8,128)} %get-tuple-element.7) | data formatting | bytes 131072 | tf_op jit(solution)/shard_map/pallas_call | solution.py:191
  42.7 0.9 %collective-permute-done.6 = bf16[128,768]{1,0:T(8,128)(2,1)S(1)} collective-permute-done((bf16[128,768]{1,0:T(8,128)(2,1)}, bf16[128,768]{1,0:T(8,128)(2,1)S(1)}, u32[]{:S(2)}, u32[]{:S(2)}) %collective-permute-start.6) | collective-permute-done | bytes 196640 | tf_op jit(solution)/shard_map/ppermute | solution.py:206
  43.6 0.5 slice.60
  44.8 0.0 collective-permute-done.5
  44.9 0.2 copy.13
  45.1 0.2 copy.14
  45.2 0.0 copy-start.3
  45.3 0.3 fusion.18
  45.6 0.8 %copy-done.3 = bf16[768,512]{1,0:T(8,128)(2,1)S(1)} copy-done((bf16[768,512]{1,0:T(8,128)(2,1)S(1)}, bf16[768,512]{1,0:T(8,128)(2,1)}, u32[]{:S(2)}) %copy-start.3) | copy-done | bytes 786456
  46.4 0.3 convolution_convert_fusion.3
  46.6 0.2 reshape_reshape.6
  46.8 0.2 copy.17
  47.0 0.1 maximum_select_fusion
  47.1 4.5 %collective-permute-start.8 = (bf16[1,1,16,128]{3,2,1,0:T(8,128)(2,1)S(1)}, bf16[1,1,16,128]{3,2,1,0:T(8,128)(2,1)S(1)}, u32[]{:S(2)}, u32[]{:S(2)}) collective-permute-start(bf16[1,1,16,128]{3,2,1,0:T(8,128)(2,1)S(1)} %get-tuple-element.16), channel_id=1, source_target_pairs={{0,3},{1,2},{2,5},{3,4},{4,7},{5,6},{6,9},{7,8},{8,11},{9,10},{10,... | collective-permute-start | bytes 12296 | tf_op jit(solution)/shard_map/ppermute | solution.py:80
  51.6 0.1 fusion.63
  51.8 0.6 collective-permute-start.7
  52.4 1.8 %collective-permute-start.9 = (bf16[1,32,16,128]{3,2,1,0:T(8,128)(2,1)S(1)}, bf16[1,32,16,128]{3,2,1,0:T(8,128)(2,1)S(1)}, u32[]{:S(2)}, u32[]{:S(2)}) collective-permute-start(bf16[1,32,16,128]{3,2,1,0:T(8,128)(2,1)S(1)} %get-tuple-element.12), channel_id=1, source_target_pairs={{0,2},{1,3},{2,4},{3,5},{4,6},{5,7},{6,8},{7,9},{8,10},{9,11},{10,... | collective-permute-start | bytes 393224 | tf_op jit(solution)/shard_map/ppermute | solution.py:22
  54.3 1.3 %collective-permute-start.11 = (bf16[1,32,16,128]{3,2,1,0:T(8,128)(2,1)S(1)}, bf16[1,32,16,128]{3,2,1,0:T(8,128)(2,1)S(1)}, u32[]{:S(2)}, u32[]{:S(2)}) collective-permute-start(bf16[1,32,16,128]{3,2,1,0:T(8,128)(2,1)S(1)} %get-tuple-element.13), channel_id=1, source_target_pairs={{2,0},{3,1},{4,2},{5,3},{6,4},{7,5},{8,6},{9,7},{10,8},{11,9},{12,... | collective-permute-start | bytes 393224 | tf_op jit(solution)/shard_map/ppermute | solution.py:22
  55.6 1.5 %collective-permute-start.10 = (bf16[1,1,16,128]{3,2,1,0:T(8,128)(2,1)S(1)}, bf16[1,1,16,128]{3,2,1,0:T(8,128)(2,1)S(1)}, u32[]{:S(2)}, u32[]{:S(2)}) collective-permute-start(bf16[1,1,16,128]{3,2,1,0:T(8,128)(2,1)S(1)} %get-tuple-element.17), channel_id=1, source_target_pairs={{2,1},{3,0},{4,3},{5,2},{6,5},{7,4},{8,7},{9,6},{10,9},{11,8},{12,... | collective-permute-start | bytes 12296 | tf_op jit(solution)/shard_map/ppermute | solution.py:80
  57.1 4.0 %collective-permute-done.10 = bf16[1,1,16,128]{3,2,1,0:T(8,128)(2,1)S(1)} collective-permute-done((bf16[1,1,16,128]{3,2,1,0:T(8,128)(2,1)S(1)}, bf16[1,1,16,128]{3,2,1,0:T(8,128)(2,1)S(1)}, u32[]{:S(2)}, u32[]{:S(2)}) %collective-permute-start.10) | collective-permute-done | bytes 4128 | tf_op jit(solution)/shard_map/ppermute | solution.py:80
  61.1 0.0 copy-start.8
  61.1 0.0 copy-start.11
  61.1 0.1 maximum_bitcast_fusion
  61.3 0.2 copy.32
  61.5 0.3 pad.clone
  61.8 0.1 copy.21
  61.9 0.1 slice.61
  62.0 0.2 copy-done.8
  62.1 3.0 %convolution_select_fusion = f32[2,32,8,3,64]{4,2,3,1,0:T(8,128)S(1)} fusion(bf16[3,3,3,128,64]{3,4,2,1,0:T(8,128)(2,1)S(1)} %copy-done.8, bf16[2,34,1,7,2,128]{5,3,4,1,0,2:T(8,128)(2,1)S(1)} %slice.61, bf16[2,34,1,8,3,128]{5,3,4,1,0,2:T(8,128)(2,1)S(1)} %copy.21, pred[8,3]{0,1:T(4,128)(4,1)S(1)} %copy-done.11), kind=kOutput, calls=%fused_computation.21 | convolution fusion | flops 455172096 | bytes 1497112 | tf_op jit(solution)/shard_map/conv_general_dilated | solution.py:55
  65.1 0.2 copy.22
  65.6 0.6 convolution_select_fusion.2
  66.2 0.1 copy.26
  66.5 0.6 convolution_select_fusion.1
  67.1 0.1 copy.30
  67.2 0.1 fusion.54
  67.4 0.8 %copy.31 = bf16[1,2,32,16,64]{4,3,2,1,0:T(8,128)(2,1)} copy(bf16[1,2,32,16,64]{4,2,3,1,0:T(8,128)(2,1)S(1)} %fusion.54) | data formatting | bytes 262144
  (51 shorter events, 0.6 us)
Async XLA Ops:
  0.6 44.6 %copy-start = (bf16[768,768]{1,0:T(8,128)(2,1)S(1)}, bf16[768,768]{1,0:T(8,128)(2,1)}, u32[]{:S(2)}) copy-start(bf16[768,768]{1,0:T(8,128)(2,1)} %param.10) | copy-start | bytes 3538948
  0.6 12.5 %copy-start.1 = (bf16[128,768]{1,0:T(8,128)(2,1)S(1)}, bf16[128,768]{1,0:T(8,128)(2,1)}, u32[]{:S(2)}) copy-start(bf16[128,768]{1,0:T(8,128)(2,1)} %param.7) | copy-start | bytes 589828
  0.7 12.5 %collective-permute-start = (bf16[128,768]{1,0:T(8,128)(2,1)}, bf16[128,768]{1,0:T(8,128)(2,1)S(1)}, u32[]{:S(2)}, u32[]{:S(2)}) collective-permute-start(bf16[128,768]{1,0:T(8,128)(2,1)} %param.7), channel_id=1, source_target_pairs={{0,2},{1,3},{2,0},{3,1},{4,6},{5,7},{6,4},{7,5},{8,10},{9,11},{10,... | collective-permute-start | bytes 589832 | tf_op jit(solution)/shard_map/ppermute | solution.py:206
  3.7 9.5 %collective-permute-start.1 = (bf16[128,768]{1,0:T(8,128)(2,1)}, bf16[128,768]{1,0:T(8,128)(2,1)S(1)}, u32[]{:S(2)}, u32[]{:S(2)}) collective-permute-start(bf16[128,768]{1,0:T(8,128)(2,1)} %param.7), channel_id=1, source_target_pairs={{0,4},{1,5},{2,6},{3,7},{4,0},{5,1},{6,2},{7,3},{8,12},{9,13},{10,... | collective-permute-start | bytes 589832 | tf_op jit(solution)/shard_map/ppermute | solution.py:206
  5.3 10.3 %collective-permute-start.2 = (bf16[128,768]{1,0:T(8,128)(2,1)}, bf16[128,768]{1,0:T(8,128)(2,1)S(1)}, u32[]{:S(2)}, u32[]{:S(2)}) collective-permute-start(bf16[128,768]{1,0:T(8,128)(2,1)} %param.7), channel_id=1, source_target_pairs={{0,6},{1,7},{2,4},{3,5},{4,2},{5,3},{6,0},{7,1},{8,14},{9,15},{10,... | collective-permute-start | bytes 589832 | tf_op jit(solution)/shard_map/ppermute | solution.py:206
  8.2 8.0 %copy-start.7 = (bf16[768,2304]{1,0:T(8,128)(2,1)S(1)}, bf16[768,2304]{1,0:T(8,128)(2,1)}, u32[]{:S(2)}) copy-start(bf16[768,2304]{1,0:T(8,128)(2,1)} %param.9) | copy-start | bytes 10616836
  10.1 6.1 %copy-start.4 = (bf16[128,768]{1,0:T(8,128)(2,1)}, bf16[128,768]{1,0:T(8,128)(2,1)S(1)}, u32[]{:S(2)}) copy-start(bf16[128,768]{1,0:T(8,128)(2,1)S(1)} %fusion.15.refs_0_) | copy-start | bytes 589828
  10.1 12.0 %collective-permute-start.4 = (bf16[128,768]{1,0:T(8,128)(2,1)S(1)}, bf16[128,768]{1,0:T(8,128)(2,1)S(1)}, u32[]{:S(2)}, u32[]{:S(2)}) collective-permute-start(bf16[128,768]{1,0:T(8,128)(2,1)S(1)} %fusion.15.refs_0_), channel_id=1, source_target_pairs={{0,8},{1,9},{2,10},{3,11},{4,12},{5,13},{6,14},{7,15},{8,0},{9,1},... | collective-permute-start | bytes 589832 | tf_op jit(solution)/shard_map/ppermute | solution.py:206
  15.6 3.3 %collective-permute-start.3 = (bf16[512,768]{1,0:T(8,128)(2,1)S(1)}, bf16[512,768]{1,0:T(8,128)(2,1)S(1)}, u32[]{:S(2)}, u32[]{:S(2)}) collective-permute-start(bf16[512,768]{1,0:T(8,128)(2,1)S(1)} %constant_dynamic-update-slice_fusion), channel_id=1, source_target_pairs={{0,1},{1,0},{2,3},{3,2},{4,5},{5,4},{6,7},{7,6},{8,9},{9,8},{10,11... | collective-permute-start | bytes 2359304 | tf_op jit(solution)/shard_map/ppermute | solution.py:206
  22.1 11.2 %copy-start.2 = (bf16[768,512]{1,0:T(8,128)(2,1)S(1)}, bf16[768,512]{1,0:T(8,128)(2,1)}, u32[]{:S(2)}) copy-start(bf16[768,512]{1,0:T(8,128)(2,1)} %param.12) | copy-start | bytes 2359300
  22.1 0.7 copy-start.5
  30.4 3.6 %copy-start.10 = (f32[16,128]{1,0:T(8,128)S(1)}, f32[16,128]{1,0:T(8,128)}, u32[]{:S(2)}) copy-start(f32[16,128]{1,0:T(8,128)} %get-tuple-element.8) | copy-start | bytes 24580
  30.4 13.2 %collective-permute-start.6 = (bf16[128,768]{1,0:T(8,128)(2,1)}, bf16[128,768]{1,0:T(8,128)(2,1)S(1)}, u32[]{:S(2)}, u32[]{:S(2)}) collective-permute-start(bf16[128,768]{1,0:T(8,128)(2,1)} %get-tuple-element.6.refs_5_), channel_id=1, source_target_pairs={{0,8},{1,9},{2,10},{3,11},{4,12},{5,13},{6,14},{7,15},{8,0},{9,1},... | collective-permute-start | bytes 589832 | tf_op jit(solution)/shard_map/ppermute | solution.py:206
  34.1 10.7 %collective-permute-start.5 = (f32[16,128]{1,0:T(8,128)S(1)}, f32[16,128]{1,0:T(8,128)S(1)}, u32[]{:S(2)}, u32[]{:S(2)}) collective-permute-start(f32[16,128]{1,0:T(8,128)S(1)} %copy-done.10), channel_id=1, source_target_pairs={{0,8},{1,9},{2,10},{3,11},{4,12},{5,13},{6,14},{7,15},{8,0},{9,1},... | collective-permute-start | bytes 24584 | tf_op jit(solution)/shard_map/ppermute | solution.py:206
  41.7 3.5 %copy-start.9 = (f32[128,768]{1,0:T(8,128)S(1)}, f32[128,768]{1,0:T(8,128)}, u32[]{:S(2)}) copy-start(f32[128,768]{1,0:T(8,128)} %get-tuple-element.9) | copy-start | bytes 1179652
  45.2 1.1 %copy-start.3 = (bf16[768,512]{1,0:T(8,128)(2,1)S(1)}, bf16[768,512]{1,0:T(8,128)(2,1)}, u32[]{:S(2)}) copy-start(bf16[768,512]{1,0:T(8,128)(2,1)} %param.11) | copy-start | bytes 2359300
  46.4 5.4 %copy-start.6 = (bf16[128,768]{1,0:T(8,128)(2,1)}, bf16[128,768]{1,0:T(8,128)(2,1)S(1)}, u32[]{:S(2)}) copy-start(bf16[128,768]{1,0:T(8,128)(2,1)S(1)} %fusion.18) | copy-start | bytes 589828
  47.1 9.9 %collective-permute-start.8 = (bf16[1,1,16,128]{3,2,1,0:T(8,128)(2,1)S(1)}, bf16[1,1,16,128]{3,2,1,0:T(8,128)(2,1)S(1)}, u32[]{:S(2)}, u32[]{:S(2)}) collective-permute-start(bf16[1,1,16,128]{3,2,1,0:T(8,128)(2,1)S(1)} %get-tuple-element.16), channel_id=1, source_target_pairs={{0,3},{1,2},{2,5},{3,4},{4,7},{5,6},{6,9},{7,8},{8,11},{9,10},{10,... | collective-permute-start | bytes 12296 | tf_op jit(solution)/shard_map/ppermute | solution.py:80
  51.8 9.3 %collective-permute-start.7 = (bf16[2,1,16,128]{3,2,1,0:T(8,128)(2,1)S(1)}, bf16[2,1,16,128]{3,2,1,0:T(8,128)(2,1)S(1)}, u32[]{:S(2)}, u32[]{:S(2)}) collective-permute-start(bf16[2,1,16,128]{3,2,1,0:T(8,128)(2,1)S(1)} %maximum_select_fusion), channel_id=1, source_target_pairs={{0,1},{1,0},{2,3},{3,2},{4,5},{5,4},{6,7},{7,6},{8,9},{9,8},{10,11... | collective-permute-start | bytes 24584 | tf_op jit(solution)/shard_map/ppermute | solution.py:26
  52.4 12.9 %collective-permute-start.9 = (bf16[1,32,16,128]{3,2,1,0:T(8,128)(2,1)S(1)}, bf16[1,32,16,128]{3,2,1,0:T(8,128)(2,1)S(1)}, u32[]{:S(2)}, u32[]{:S(2)}) collective-permute-start(bf16[1,32,16,128]{3,2,1,0:T(8,128)(2,1)S(1)} %get-tuple-element.12), channel_id=1, source_target_pairs={{0,2},{1,3},{2,4},{3,5},{4,6},{5,7},{6,8},{7,9},{8,10},{9,11},{10,... | collective-permute-start | bytes 393224 | tf_op jit(solution)/shard_map/ppermute | solution.py:22
  54.3 12.0 %collective-permute-start.11 = (bf16[1,32,16,128]{3,2,1,0:T(8,128)(2,1)S(1)}, bf16[1,32,16,128]{3,2,1,0:T(8,128)(2,1)S(1)}, u32[]{:S(2)}, u32[]{:S(2)}) collective-permute-start(bf16[1,32,16,128]{3,2,1,0:T(8,128)(2,1)S(1)} %get-tuple-element.13), channel_id=1, source_target_pairs={{2,0},{3,1},{4,2},{5,3},{6,4},{7,5},{8,6},{9,7},{10,8},{11,9},{12,... | collective-permute-start | bytes 393224 | tf_op jit(solution)/shard_map/ppermute | solution.py:22
  55.6 5.5 %collective-permute-start.10 = (bf16[1,1,16,128]{3,2,1,0:T(8,128)(2,1)S(1)}, bf16[1,1,16,128]{3,2,1,0:T(8,128)(2,1)S(1)}, u32[]{:S(2)}, u32[]{:S(2)}) collective-permute-start(bf16[1,1,16,128]{3,2,1,0:T(8,128)(2,1)S(1)} %get-tuple-element.17), channel_id=1, source_target_pairs={{2,1},{3,0},{4,3},{5,2},{6,5},{7,4},{8,7},{9,6},{10,9},{11,8},{12,... | collective-permute-start | bytes 12296 | tf_op jit(solution)/shard_map/ppermute | solution.py:80
  61.1 1.0 %copy-start.8 = (bf16[3,3,3,128,64]{3,4,2,1,0:T(8,128)(2,1)S(1)}, bf16[3,3,3,128,64]{3,4,2,1,0:T(8,128)(2,1)}, u32[]{:S(2)}) copy-start(bf16[3,3,3,128,64]{3,4,2,1,0:T(8,128)(2,1)} %param.13) | copy-start | bytes 1327108
  61.1 1.0 %copy-start.11 = (pred[8,3]{0,1:T(4,128)(4,1)S(1)}, pred[8,3]{0,1:T(4,128)(4,1)}, u32[]{:S(2)}) copy-start(pred[8,3]{0,1:T(4,128)(4,1)} %constant.52) | copy-start | bytes 76

commit v10 on v7

--- a/solution.py
+++ b/solution.py
@@ -5,7 +5,6 @@
 from jax import lax
 from jax.experimental import pallas as pl
 from jax.experimental.pallas import tpu as pltpu
-from jax.experimental.layout import Layout, with_layout_constraint
 from jax.sharding import PartitionSpec as P
 
 HEADS = 12
@@ -221,10 +220,17 @@
         mirrored_queries, kv_chunks, head_size, score_scale, jnp.bfloat16, False, rows_out=True
     )
     heads = model_width // head_size
-    other_out = exchanged(remote_out, half)
-    row_major = Layout(major_to_minor=(0, 1))
-    sent_lse = with_layout_constraint(remote_lse, row_major)
-    other_lse = with_layout_constraint(exchanged(sent_lse, half), row_major)[:heads].T
+    parts = []
+    remainder = remote_lse
+    for _ in range(3):
+        part = remainder.astype(jnp.bfloat16)
+        parts.append(part)
+        remainder = remainder - part.astype(jnp.float32)
+    packed = jnp.concatenate(parts, axis=0).reshape(-1, model_width)
+    received = exchanged(jnp.concatenate([remote_out, packed], axis=0), half)
+    other_out = received[:token_count]
+    other_parts = received[token_count:].reshape(3, -1, remote_lse.shape[-1]).astype(jnp.float32)
+    other_lse = ((other_parts[0] + other_parts[1]) + other_parts[2])[:heads].T
     own_out, own_lse = attention(
         queries, kv_chunks, head_size, score_scale, jnp.float32, False, after=remote_out
     )

time: 63.5 us -> 71.9 us (1.13)
  waiting for transfers between devices: 5.51 us -> 10.3 us
  other arithmetic: 4.54 us -> 7.13 us
  matrix products: 12.3 us -> 14 us
    ppermute x2, waiting for transfers between devices: 1.09 us -> 4.29 us  [shifted(): return lax.ppermute(block, axis, route)]
    dot_general x3, matrix products: 7.22 us -> 8.88 us  [projected(): jnp.dot(normed, weight, preferred_element_type=jnp.float32)]
    ppermute x7 -> x6, waiting for transfers between devices: 3.26 us -> 4.85 us  [exchanged(): return lax.ppermute(x, 'seq', [(i, i ^ mask) for i in range(devices)])]
    pallas_call x1 -> x0, local copies, waits for them, and re-layouts: 0.98 us -> none  [attention(): pl.pallas_call(kernel, grid=(pairs,), cost_estimate=cost, in_specs=[row_s...]
    concatenate x0 -> x2, other arithmetic: none -> 0.95 us  [the longest x1 0.94 us: body(): received = exchanged(jnp.concatenate([remote_out, packed], axis=0), half)]
    exp x1, other arithmetic: 0.01 us -> 0.87 us  [body(): other_weight = jnp.repeat(jnp.exp(other_lse - top), head_size, axis=1)]
    convert_element_type x0 -> x2, other arithmetic: none -> 0.78 us  [the longest x1 0.78 us: body(): part = remainder.astype(jnp.bfloat16)]
    unnamed x31 -> x32, local copies, waits for them, and re-layouts: 2.64 us -> 3.13 us
  transfers between devices with their start and end apart: 10 -> 9, of which waited for: 4 -> 5; matrix products, arithmetic and copies ran while one was open for 29% -> 20% of each run, Pallas kernels for 12% -> 11%
where the time goes in v10:
time: 71.9 us; the launch traced here: 71.2 us
  starting transfers between devices  16.8 us (23%)
  Pallas kernels  15.2 us (21%)
  matrix products  14 us (19%)
  waiting for transfers between devices  10.3 us (14%)
  other arithmetic  7.13 us (10%)
  local copies, waits for them, and re-layouts  5.99 us (8%)
  between operations  1.8 us (3%)
    pallas_call x2, Pallas kernels, attention(): pl.pallas_call(kernel, grid=(pairs,), cost_estimate=cost, in_specs=[row_s...  15.2 us
    ppermute x6, starting transfers between devices, exchanged(): return lax.ppermute(x, 'seq', [(i, i ^ mask) for i in range(devices)])  10.4 us
    dot_general x3, matrix products, projected(): jnp.dot(normed, weight, preferred_element_type=jnp.float32)  8.88 us
    ppermute x2, starting transfers between devices, shifted(): return lax.ppermute(block, axis, route)  6.41 us
    ppermute x6, waiting for transfers between devices, exchanged(): return lax.ppermute(x, 'seq', [(i, i ^ mask) for i in range(devices)])  4.85 us
    ppermute x2, waiting for transfers between devices, shifted(): return lax.ppermute(block, axis, route)  4.29 us
    conv_general_dilated x3, matrix products, conv(): lax.conv_general_dilated(field[None], kernel, window_strides=(1, 1, 1), p...  4.22 us
    unnamed x32, local copies, waits for them, and re-layouts  3.13 us
  transfers between devices with their start and end apart: 9, of which 5 were waited for; matrix products, arithmetic and copies ran while one was open for 20% of the time, Pallas kernels for 11%

profile of v10, /device:TPU:0, one launch (start us, length us, event | category | flops | bytes accessed | tf_op | source)
XLA Modules:
  0.0 71.2 jit_solution(13796081610704686715)
XLA Ops:
  0.6 0.0 copy-start
  0.7 3.1 %collective-permute-start = (bf16[128,768]{1,0:T(8,128)(2,1)}, bf16[128,768]{1,0:T(8,128)(2,1)S(1)}, u32[]{:S(2)}, u32[]{:S(2)}) collective-permute-start(bf16[128,768]{1,0:T(8,128)(2,1)} %param.7), channel_id=1, source_target_pairs={{0,2},{1,3},{2,0},{3,1},{4,6},{5,7},{6,4},{7,5},{8,10},{9,11},{10,... | collective-permute-start | bytes 589832 | tf_op jit(solution)/shard_map/ppermute | solution.py:199
  3.7 1.6 %collective-permute-start.1 = (bf16[128,768]{1,0:T(8,128)(2,1)}, bf16[128,768]{1,0:T(8,128)(2,1)S(1)}, u32[]{:S(2)}, u32[]{:S(2)}) collective-permute-start(bf16[128,768]{1,0:T(8,128)(2,1)} %param.7), channel_id=1, source_target_pairs={{0,4},{1,5},{2,6},{3,7},{4,0},{5,1},{6,2},{7,3},{8,12},{9,13},{10,... | collective-permute-start | bytes 589832 | tf_op jit(solution)/shard_map/ppermute | solution.py:199
  5.3 1.1 %convert_reduce_fusion.2 = f32[128]{0:T(128)S(1)} fusion(bf16[128,768]{1,0:T(8,128)(2,1)} %param.7), kind=kLoop, calls=%fused_computation.46 | loop fusion | flops 196480 | bytes 197120 | tf_op jit(solution)/shard_map/reduce_sum | solution.py:30
  6.4 0.7 convert_element_type.76
  7.1 1.1 %fusion.38 = f32[128]{0:T(128)S(1)} fusion(bf16[128,768]{1,0:T(8,128)(2,1)} %param.7, f32[128]{0:T(128)S(1)} %broadcast_multiply_fusion.2), kind=kLoop, calls=%fused_computation.52 | loop fusion | flops 393088 | bytes 197632 | tf_op jit(solution)/shard_map/reduce_sum | solution.py:32
  8.2 1.8 %fusion.15.refs_0_ = bf16[128,768]{1,0:T(8,128)(2,1)S(1)} fusion(bf16[768,2304]{1,0:T(8,128)(2,1)} %param.9, bf16[128,768]{1,0:T(8,128)(2,1)} %param.7, f32[768]{0:T(1024)S(1)} %convert_element_type.76, f32[128]{0:T(128)S(1)} %add_rsqrt_fusion.2, f32[128]{0:T(128)S(1)} %broadcast_multiply_fusion.2), kind=kOutput, calls=%fused_computation.27 | convolution fusion | flops 151584768 | bytes 1576960 | tf_op jit(solution)/shard_map/dot_general | solution.py:204
  10.0 0.0 copy-start.4
  10.0 3.0 %collective-permute-start.4 = (bf16[128,768]{1,0:T(8,128)(2,1)S(1)}, bf16[128,768]{1,0:T(8,128)(2,1)S(1)}, u32[]{:S(2)}, u32[]{:S(2)}) collective-permute-start(bf16[128,768]{1,0:T(8,128)(2,1)S(1)} %fusion.15.refs_0_), channel_id=1, source_target_pairs={{0,8},{1,9},{2,10},{3,11},{4,12},{5,13},{6,14},{7,15},{8,0},{9,1},... | collective-permute-start | bytes 589832 | tf_op jit(solution)/shard_map/ppermute | solution.py:199
  13.1 2.7 %collective-permute-done.2 = bf16[128,768]{1,0:T(8,128)(2,1)S(1)} collective-permute-done((bf16[128,768]{1,0:T(8,128)(2,1)}, bf16[128,768]{1,0:T(8,128)(2,1)S(1)}, u32[]{:S(2)}, u32[]{:S(2)}) %collective-permute-start.2) | collective-permute-done | bytes 196640 | tf_op jit(solution)/shard_map/ppermute | solution.py:199
  15.9 0.2 convert_reduce_fusion.1
  16.0 0.1 collective-permute-start.3
  16.1 0.4 fusion.9
  16.5 4.5 %convolution_convert_fusion.1.refs_1_.refs_3_ = bf16[512,1536]{1,0:T(8,128)(2,1)} fusion(bf16[768,2304]{1,0:T(8,128)(2,1)} %param.9, bf16[512,768]{1,0:T(8,128)(2,1)S(1)} %constant_dynamic-update-slice_fusion, f32[768]{0:T(1024)S(1)} %convert_element_type.76, f32[512]{0:T(512)S(1)} %add_rsqrt_fusion.1, f32[512]{0:T(512)S(1)} %broadcast_multiply_fusion.1), kind=kOutput, calls=%fused_computation.1 | convolution fusion | flops 1210712064 | bytes 4725760 | tf_op jit(solution)/shard_map/dot_general | solution.py:204
  21.0 0.2 convert_reduce_fusion
  21.2 0.4 fusion.6
  21.5 2.7 %convolution_convert_fusion.refs_2_.refs_4_ = bf16[512,1536]{1,0:T(8,128)(2,1)} fusion(bf16[768,2304]{1,0:T(8,128)(2,1)S(1)} %copy-done.7, bf16[512,768]{1,0:T(8,128)(2,1)S(1)} %collective-permute-done.3, f32[512]{0:T(512)S(1)} %add_rsqrt_fusion, f32[512]{0:T(512)S(1)} %broadcast_multiply_fusion, f32[768]{0:T(1024)S(1)} %convert_element_type.76), kind=kOutput, calls=%fused_computation | convolution fusion | flops 1210712064 | bytes 4726784 | tf_op jit(solution)/shard_map/dot_general | solution.py:204
  24.2 0.7 copy-done.5
  24.9 7.6 %shard_map.86 = (bf16[128,768]{1,0:T(8,128)(2,1)}, f32[128,128]{1,0:T(8,128)}, f32[16,128]{1,0:T(8,128)}) custom-call(bf16[128,768]{1,0:T(8,128)(2,1)} %copy-done.5, bf16[512,1536]{1,0:T(8,128)(2,1)} %convolution_convert_fusion.1.refs_1_.refs_3_, bf16[512,1536]{1,0:T(8,128)(2,1)} %convolution_convert_fusion.refs_2_.refs_4_, ...), custom_call_target="tpu_custom_call" | custom-call | flops 805306368 | bytes 3932160 | tf_op jit(solution)/shard_map/pallas_call | solution.py:184
  32.5 0.8 %fusion.81 = (bf16[16,128]{1,0:T(8,128)(2,1)S(1)}, bf16[16,128]{1,0:T(8,128)(2,1)S(1)}, bf16[16,128]{1,0:T(8,128)(2,1)S(1)}) fusion(f32[16,128]{1,0:T(8,128)} %get-tuple-element.8), kind=kLoop, calls=%fused_computation.117 | loop fusion | flops 14336 | bytes 20480 | tf_op jit(solution)/shard_map/convert_element_type | solution.py:226
  33.3 0.9 %pad_maximum_fusion.1 = bf16[136,768]{1,0:T(8,128)(2,1)S(1)} fusion(bf16[8,768]{1,0:T(8,128)(2,1)S(1)} %reshape.62, bf16[128,768]{1,0:T(8,128)(2,1)} %get-tuple-element.6.refs_5_), kind=kLoop, calls=%fused_computation.71 | loop fusion | flops 417792 | bytes 417792 | tf_op jit(solution)/shard_map/concatenate | solution.py:230
  34.3 2.7 %collective-permute-start.5 = (bf16[136,768]{1,0:T(8,128)(2,1)S(1)}, bf16[136,768]{1,0:T(8,128)(2,1)S(1)}, u32[]{:S(2)}, u32[]{:S(2)}) collective-permute-start(bf16[136,768]{1,0:T(8,128)(2,1)S(1)} %pad_maximum_fusion.1), channel_id=1, source_target_pairs={{0,8},{1,9},{2,10},{3,11},{4,12},{5,13},{6,14},{7,15},{8,0},{9,1},... | collective-permute-start | bytes 626696 | tf_op jit(solution)/shard_map/ppermute | solution.py:199
  37.0 0.3 convolution_convert_fusion.2
  37.2 0.2 reshape_reshape.7
  37.4 0.2 copy.43
  37.6 7.5 %shard_map.87 = (f32[128,768]{1,0:T(8,128)}, f32[128,128]{1,0:T(8,128)}) custom-call(bf16[128,768]{1,0:T(8,128)(2,1)} %copy-done.4, bf16[512,1536]{1,0:T(8,128)(2,1)} %convolution_convert_fusion.1.refs_1_.refs_3_, bf16[512,1536]{1,0:T(8,128)(2,1)} %convolution_convert_fusion.refs_2_.refs_4_, bf16[512,1536]{1,0:T(8,128)(2,1)} %convolution_convert_fusion.1.refs_1_.refs_3_, ...), custom_call_target="tpu_custom_call" | custom-call | flops 805306368 | bytes 3932160 | tf_op jit(solution)/shard_map/pallas_call | solution.py:184
  45.2 2.1 %collective-permute-done.5 = bf16[136,768]{1,0:T(8,128)(2,1)S(1)} collective-permute-done((bf16[136,768]{1,0:T(8,128)(2,1)S(1)}, bf16[136,768]{1,0:T(8,128)(2,1)S(1)}, u32[]{:S(2)}, u32[]{:S(2)}) %collective-permute-start.5) | collective-permute-done | bytes 208928 | tf_op jit(solution)/shard_map/ppermute | solution.py:199
  47.3 0.1 copy.65
  47.4 0.1 copy.63
  47.5 0.1 copy.64
  47.7 0.5 slice.82
  48.8 0.9 %fusion.67 = (f32[128,12]{1,0:T(8,128)S(1)}, f32[128,12]{1,0:T(8,128)S(1)}) fusion(f32[128,128]{1,0:T(8,128)} %get-tuple-element.7, f32[]{:T(128)} %bitcast.2, f32[1,12,128]{1,2,0:T(8,128)S(1)} %copy.65, f32[1,12,128]{1,2,0:T(8,128)S(1)} %copy.63, f32[1,12,128]{1,2,0:T(8,128)S(1)} %copy.64), kind=kLoop, calls=%fused_computation.85 | loop fusion | flops 9216 | bytes 36868 | tf_op jit(solution)/shard_map/exp | solution.py:240
  49.7 0.1 copy.36
  49.8 0.2 copy.37
  50.0 0.1 copy.38
  50.1 0.2 copy.39
  50.3 0.4 fusion.18
  50.7 0.8 %copy-done.3 = bf16[768,512]{1,0:T(8,128)(2,1)S(1)} copy-done((bf16[768,512]{1,0:T(8,128)(2,1)S(1)}, bf16[768,512]{1,0:T(8,128)(2,1)}, u32[]{:S(2)}) %copy-start.3) | copy-done | bytes 786456
  51.4 0.3 convolution_convert_fusion.3
  51.7 0.2 reshape_reshape.6
  51.9 0.2 copy.42
  52.1 0.1 fusion.68
  52.2 0.0 collective-permute-start.6
  52.2 1.2 %collective-permute-done.6 = bf16[2,1,16,128]{3,2,1,0:T(8,128)(2,1)S(1)} collective-permute-done((bf16[2,1,16,128]{3,2,1,0:T(8,128)(2,1)S(1)}, bf16[2,1,16,128]{3,2,1,0:T(8,128)(2,1)S(1)}, u32[]{:S(2)}, u32[]{:S(2)}) %collective-permute-start.6) | collective-permute-done | bytes 8224 | tf_op jit(solution)/shard_map/ppermute | solution.py:25
  53.4 0.1 fusion.88
  53.5 0.0 copy-start.10
  53.5 0.1 pad_maximum_fusion
  53.7 0.2 copy.60
  53.9 0.3 pad.clone
  54.2 0.1 copy.46
  54.3 0.1 slice.84
  54.4 0.2 copy-done.8
  54.5 3.0 %convolution_select_fusion = f32[2,32,8,3,64]{4,2,3,1,0:T(8,128)S(1)} fusion(bf16[3,3,3,128,64]{3,4,2,1,0:T(8,128)(2,1)S(1)} %copy-done.8, bf16[2,34,1,7,2,128]{5,3,4,1,0,2:T(8,128)(2,1)S(1)} %slice.84, bf16[2,34,1,8,3,128]{5,3,4,1,0,2:T(8,128)(2,1)S(1)} %copy.46, pred[8,3]{0,1:T(4,128)(4,1)S(1)} %copy-done.10), kind=kOutput, calls=%fused_computation.21 | convolution fusion | flops 455172096 | bytes 1497112 | tf_op jit(solution)/shard_map/conv_general_dilated | solution.py:54
  57.5 0.2 copy.47
  57.7 1.3 %collective-permute-start.8 = (bf16[1,34,16,128]{3,2,1,0:T(8,128)(2,1)S(1)}, bf16[1,34,16,128]{3,2,1,0:T(8,128)(2,1)S(1)}, u32[]{:S(2)}, u32[]{:S(2)}) collective-permute-start(bf16[1,34,16,128]{3,2,1,0:T(8,128)(2,1)S(1)} %get-tuple-element.15), channel_id=1, source_target_pairs={{2,0},{3,1},{4,2},{5,3},{6,4},{7,5},{8,6},{9,7},{10,8},{11,9},{12,... | collective-permute-start | bytes 417800 | tf_op jit(solution)/shard_map/ppermute | solution.py:21
  59.1 5.1 %collective-permute-start.7 = (bf16[1,34,16,128]{3,2,1,0:T(8,128)(2,1)S(1)}, bf16[1,34,16,128]{3,2,1,0:T(8,128)(2,1)S(1)}, u32[]{:S(2)}, u32[]{:S(2)}) collective-permute-start(bf16[1,34,16,128]{3,2,1,0:T(8,128)(2,1)S(1)} %get-tuple-element.14), channel_id=1, source_target_pairs={{0,2},{1,3},{2,4},{3,5},{4,6},{5,7},{6,8},{7,9},{8,10},{9,11},{10,... | collective-permute-start | bytes 417800 | tf_op jit(solution)/shard_map/ppermute | solution.py:21
  64.2 2.0 %collective-permute-done.8 = bf16[1,34,16,128]{3,2,1,0:T(8,128)(2,1)S(1)} collective-permute-done((bf16[1,34,16,128]{3,2,1,0:T(8,128)(2,1)S(1)}, bf16[1,34,16,128]{3,2,1,0:T(8,128)(2,1)S(1)}, u32[]{:S(2)}, u32[]{:S(2)}) %collective-permute-start.8) | collective-permute-done | bytes 139296 | tf_op jit(solution)/shard_map/ppermute | solution.py:21
  66.4 0.6 convolution_select_fusion.1
  67.0 0.1 copy.55
  67.1 2.3 %collective-permute-done.7 = bf16[1,34,16,128]{3,2,1,0:T(8,128)(2,1)S(1)} collective-permute-done((bf16[1,34,16,128]{3,2,1,0:T(8,128)(2,1)S(1)}, bf16[1,34,16,128]{3,2,1,0:T(8,128)(2,1)S(1)}, u32[]{:S(2)}, u32[]{:S(2)}) %collective-permute-start.7) | collective-permute-done | bytes 139296 | tf_op jit(solution)/shard_map/ppermute | solution.py:21
  69.5 0.6 convolution_select_fusion.2
  70.1 0.1 copy.51
  70.3 0.1 fusion.54
  70.4 0.8 %copy.56 = bf16[1,2,32,16,64]{4,3,2,1,0:T(8,128)(2,1)} copy(bf16[1,2,32,16,64]{4,2,3,1,0:T(8,128)(2,1)S(1)} %fusion.54) | data formatting | bytes 262144
  (50 shorter events, 0.7 us)
Async XLA Ops:
  0.6 49.6 %copy-start = (bf16[768,768]{1,0:T(8,128)(2,1)S(1)}, bf16[768,768]{1,0:T(8,128)(2,1)}, u32[]{:S(2)}) copy-start(bf16[768,768]{1,0:T(8,128)(2,1)} %param.10) | copy-start | bytes 3538948
  0.6 12.4 %copy-start.1 = (bf16[128,768]{1,0:T(8,128)(2,1)S(1)}, bf16[128,768]{1,0:T(8,128)(2,1)}, u32[]{:S(2)}) copy-start(bf16[128,768]{1,0:T(8,128)(2,1)} %param.7) | copy-start | bytes 589828
  0.7 12.4 %collective-permute-start = (bf16[128,768]{1,0:T(8,128)(2,1)}, bf16[128,768]{1,0:T(8,128)(2,1)S(1)}, u32[]{:S(2)}, u32[]{:S(2)}) collective-permute-start(bf16[128,768]{1,0:T(8,128)(2,1)} %param.7), channel_id=1, source_target_pairs={{0,2},{1,3},{2,0},{3,1},{4,6},{5,7},{6,4},{7,5},{8,10},{9,11},{10,... | collective-permute-start | bytes 589832 | tf_op jit(solution)/shard_map/ppermute | solution.py:199
  3.7 9.4 %collective-permute-start.1 = (bf16[128,768]{1,0:T(8,128)(2,1)}, bf16[128,768]{1,0:T(8,128)(2,1)S(1)}, u32[]{:S(2)}, u32[]{:S(2)}) collective-permute-start(bf16[128,768]{1,0:T(8,128)(2,1)} %param.7), channel_id=1, source_target_pairs={{0,4},{1,5},{2,6},{3,7},{4,0},{5,1},{6,2},{7,3},{8,12},{9,13},{10,... | collective-permute-start | bytes 589832 | tf_op jit(solution)/shard_map/ppermute | solution.py:199
  5.3 10.5 %collective-permute-start.2 = (bf16[128,768]{1,0:T(8,128)(2,1)}, bf16[128,768]{1,0:T(8,128)(2,1)S(1)}, u32[]{:S(2)}, u32[]{:S(2)}) collective-permute-start(bf16[128,768]{1,0:T(8,128)(2,1)} %param.7), channel_id=1, source_target_pairs={{0,6},{1,7},{2,4},{3,5},{4,2},{5,3},{6,0},{7,1},{8,14},{9,15},{10,... | collective-permute-start | bytes 589832 | tf_op jit(solution)/shard_map/ppermute | solution.py:199
  10.0 6.5 %copy-start.4 = (bf16[128,768]{1,0:T(8,128)(2,1)}, bf16[128,768]{1,0:T(8,128)(2,1)S(1)}, u32[]{:S(2)}) copy-start(bf16[128,768]{1,0:T(8,128)(2,1)S(1)} %fusion.15.refs_0_) | copy-start | bytes 589828
  10.0 14.2 %collective-permute-start.4 = (bf16[128,768]{1,0:T(8,128)(2,1)S(1)}, bf16[128,768]{1,0:T(8,128)(2,1)S(1)}, u32[]{:S(2)}, u32[]{:S(2)}) collective-permute-start(bf16[128,768]{1,0:T(8,128)(2,1)S(1)} %fusion.15.refs_0_), channel_id=1, source_target_pairs={{0,8},{1,9},{2,10},{3,11},{4,12},{5,13},{6,14},{7,15},{8,0},{9,1},... | collective-permute-start | bytes 589832 | tf_op jit(solution)/shard_map/ppermute | solution.py:199
  16.0 4.9 %collective-permute-start.3 = (bf16[512,768]{1,0:T(8,128)(2,1)S(1)}, bf16[512,768]{1,0:T(8,128)(2,1)S(1)}, u32[]{:S(2)}, u32[]{:S(2)}) collective-permute-start(bf16[512,768]{1,0:T(8,128)(2,1)S(1)} %constant_dynamic-update-slice_fusion), channel_id=1, source_target_pairs={{0,1},{1,0},{2,3},{3,2},{4,5},{5,4},{6,7},{7,6},{8,9},{9,8},{10,11... | collective-permute-start | bytes 2359304 | tf_op jit(solution)/shard_map/ppermute | solution.py:199
  16.5 5.0 %copy-start.7 = (bf16[768,2304]{1,0:T(8,128)(2,1)S(1)}, bf16[768,2304]{1,0:T(8,128)(2,1)}, u32[]{:S(2)}) copy-start(bf16[768,2304]{1,0:T(8,128)(2,1)} %param.9) | copy-start | bytes 10616836
  24.2 12.8 %copy-start.2 = (bf16[768,512]{1,0:T(8,128)(2,1)S(1)}, bf16[768,512]{1,0:T(8,128)(2,1)}, u32[]{:S(2)}) copy-start(bf16[768,512]{1,0:T(8,128)(2,1)} %param.12) | copy-start | bytes 2359300
  24.2 0.7 copy-start.5
  34.3 13.0 %collective-permute-start.5 = (bf16[136,768]{1,0:T(8,128)(2,1)S(1)}, bf16[136,768]{1,0:T(8,128)(2,1)S(1)}, u32[]{:S(2)}, u32[]{:S(2)}) collective-permute-start(bf16[136,768]{1,0:T(8,128)(2,1)S(1)} %pad_maximum_fusion.1), channel_id=1, source_target_pairs={{0,8},{1,9},{2,10},{3,11},{4,12},{5,13},{6,14},{7,15},{8,0},{9,1},... | collective-permute-start | bytes 626696 | tf_op jit(solution)/shard_map/ppermute | solution.py:199
  47.3 3.0 %copy-start.9 = (f32[128,768]{1,0:T(8,128)S(1)}, f32[128,768]{1,0:T(8,128)}, u32[]{:S(2)}) copy-start(f32[128,768]{1,0:T(8,128)} %get-tuple-element.9) | copy-start | bytes 1179652
  50.3 1.1 %copy-start.3 = (bf16[768,512]{1,0:T(8,128)(2,1)S(1)}, bf16[768,512]{1,0:T(8,128)(2,1)}, u32[]{:S(2)}) copy-start(bf16[768,512]{1,0:T(8,128)(2,1)} %param.11) | copy-start | bytes 2359300
  51.4 2.1 %copy-start.6 = (bf16[128,768]{1,0:T(8,128)(2,1)}, bf16[128,768]{1,0:T(8,128)(2,1)S(1)}, u32[]{:S(2)}) copy-start(bf16[128,768]{1,0:T(8,128)(2,1)S(1)} %fusion.18) | copy-start | bytes 589828
  52.2 1.2 %collective-permute-start.6 = (bf16[2,1,16,128]{3,2,1,0:T(8,128)(2,1)S(1)}, bf16[2,1,16,128]{3,2,1,0:T(8,128)(2,1)S(1)}, u32[]{:S(2)}, u32[]{:S(2)}) collective-permute-start(bf16[2,1,16,128]{3,2,1,0:T(8,128)(2,1)S(1)} %fusion.68), channel_id=1, source_target_pairs={{0,1},{1,0},{2,3},{3,2},{4,5},{5,4},{6,7},{7,6},{8,9},{9,8},{10,11... | collective-permute-start | bytes 24584 | tf_op jit(solution)/shard_map/ppermute | solution.py:25
  53.5 1.0 %copy-start.8 = (bf16[3,3,3,128,64]{3,4,2,1,0:T(8,128)(2,1)S(1)}, bf16[3,3,3,128,64]{3,4,2,1,0:T(8,128)(2,1)}, u32[]{:S(2)}) copy-start(bf16[3,3,3,128,64]{3,4,2,1,0:T(8,128)(2,1)} %param.13) | copy-start | bytes 1327108
  53.5 1.0 %copy-start.10 = (pred[8,3]{0,1:T(4,128)(4,1)S(1)}, pred[8,3]{0,1:T(4,128)(4,1)}, u32[]{:S(2)}) copy-start(pred[8,3]{0,1:T(4,128)(4,1)} %constant.51) | copy-start | bytes 76
  57.7 8.5 %collective-permute-start.8 = (bf16[1,34,16,128]{3,2,1,0:T(8,128)(2,1)S(1)}, bf16[1,34,16,128]{3,2,1,0:T(8,128)(2,1)S(1)}, u32[]{:S(2)}, u32[]{:S(2)}) collective-permute-start(bf16[1,34,16,128]{3,2,1,0:T(8,128)(2,1)S(1)} %get-tuple-element.15), channel_id=1, source_target_pairs={{2,0},{3,1},{4,2},{5,3},{6,4},{7,5},{8,6},{9,7},{10,8},{11,9},{12,... | collective-permute-start | bytes 417800 | tf_op jit(solution)/shard_map/ppermute | solution.py:21
  59.1 10.3 %collective-permute-start.7 = (bf16[1,34,16,128]{3,2,1,0:T(8,128)(2,1)S(1)}, bf16[1,34,16,128]{3,2,1,0:T(8,128)(2,1)S(1)}, u32[]{:S(2)}, u32[]{:S(2)}) collective-permute-start(bf16[1,34,16,128]{3,2,1,0:T(8,128)(2,1)S(1)} %get-tuple-element.14), channel_id=1, source_target_pairs={{0,2},{1,3},{2,4},{3,5},{4,6},{5,7},{6,8},{7,9},{8,10},{9,11},{10,... | collective-permute-start | bytes 417800 | tf_op jit(solution)/shard_map/ppermute | solution.py:21

commit v11 on v7

--- a/solution.py
+++ b/solution.py
@@ -225,10 +225,17 @@
     row_major = Layout(major_to_minor=(0, 1))
     sent_lse = with_layout_constraint(remote_lse, row_major)
     other_lse = with_layout_constraint(exchanged(sent_lse, half), row_major)[:heads].T
-    own_out, own_lse = attention(
-        queries, kv_chunks, head_size, score_scale, jnp.float32, False, after=remote_out
-    )
-    own_lse = own_lse[:, :heads]
+    own_out, own_rows = attention(
+        queries,
+        kv_chunks,
+        head_size,
+        score_scale,
+        jnp.float32,
+        False,
+        after=remote_out,
+        rows_out=True,
+    )
+    own_lse = own_rows[:heads].T
     top = jnp.maximum(own_lse, other_lse) + 0 * other_out[:1, :1].astype(jnp.float32)
     own_weight = jnp.repeat(jnp.exp(own_lse - top), head_size, axis=1)
     other_weight = jnp.repeat(jnp.exp(other_lse - top), head_size, axis=1)

time: 63.5 us -> 63.6 us (level)
  local copies, waits for them, and re-layouts: 6.26 us -> 5.29 us
  waiting for transfers between devices: 5.51 us -> 6.4 us
  other arithmetic: 4.54 us -> 5.24 us
    pallas_call x1 -> x0, local copies, waits for them, and re-layouts: 0.98 us -> none  [attention(): pl.pallas_call(kernel, grid=(pairs,), cost_estimate=cost, in_specs=[row_s...]
    ppermute x7, waiting for transfers between devices: 3.26 us -> 4.14 us  [exchanged(): return lax.ppermute(x, 'seq', [(i, i ^ mask) for i in range(devices)])]
    exp x1, other arithmetic: 0.01 us -> 0.71 us  [body(): other_weight = jnp.repeat(jnp.exp(other_lse - top), head_size, axis=1)]
  transfers between devices with their start and end apart: 10 -> 10, of which waited for: 4 -> 4; matrix products, arithmetic and copies ran while one was open for 29% -> 27% of each run, Pallas kernels for 12% -> 12%
where the time goes in v11:
time: 63.6 us; the launch traced here: 63.1 us
  starting transfers between devices  16.8 us (26%)
  Pallas kernels  15.3 us (24%)
  matrix products  12.3 us (19%)
  waiting for transfers between devices  6.4 us (10%)
  local copies, waits for them, and re-layouts  5.29 us (8%)
  other arithmetic  5.24 us (8%)
  between operations  1.82 us (3%)
    pallas_call x2, Pallas kernels, attention(): pl.pallas_call(kernel, grid=(pairs,), cost_estimate=cost, in_specs=[row_s...  15.3 us
    ppermute x7, starting transfers between devices, exchanged(): return lax.ppermute(x, 'seq', [(i, i ^ mask) for i in range(devices)])  10.8 us
    dot_general x3, matrix products, projected(): jnp.dot(normed, weight, preferred_element_type=jnp.float32)  7.22 us
    ppermute x2, starting transfers between devices, shifted(): return lax.ppermute(block, axis, route)  5.98 us
    conv_general_dilated x3, matrix products, conv(): lax.conv_general_dilated(field[None], kernel, window_strides=(1, 1, 1), p...  4.22 us
    ppermute x7, waiting for transfers between devices, exchanged(): return lax.ppermute(x, 'seq', [(i, i ^ mask) for i in range(devices)])  4.14 us
    unnamed x31, local copies, waits for them, and re-layouts  2.64 us
    reduce_sum x3, other arithmetic, layer_norm(): row_var = jnp.mean(centered * centered, axis=-1, keepdims=True)  1.84 us
  transfers between devices with their start and end apart: 10, of which 4 were waited for; matrix products, arithmetic and copies ran while one was open for 27% of the time, Pallas kernels for 12%

profile of v11, /device:TPU:0, one launch (start us, length us, event | category | flops | bytes accessed | tf_op | source)
XLA Modules:
  0.0 63.1 jit_solution(14169820683952556590)
XLA Ops:
  0.6 0.0 copy-start
  0.6 0.0 copy-start.1
  0.7 3.1 %collective-permute-start = (bf16[128,768]{1,0:T(8,128)(2,1)}, bf16[128,768]{1,0:T(8,128)(2,1)S(1)}, u32[]{:S(2)}, u32[]{:S(2)}) collective-permute-start(bf16[128,768]{1,0:T(8,128)(2,1)} %param.7), channel_id=1, source_target_pairs={{0,2},{1,3},{2,0},{3,1},{4,6},{5,7},{6,4},{7,5},{8,10},{9,11},{10,... | collective-permute-start | bytes 589832 | tf_op jit(solution)/shard_map/ppermute | solution.py:200
  3.7 1.6 %collective-permute-start.1 = (bf16[128,768]{1,0:T(8,128)(2,1)}, bf16[128,768]{1,0:T(8,128)(2,1)S(1)}, u32[]{:S(2)}, u32[]{:S(2)}) collective-permute-start(bf16[128,768]{1,0:T(8,128)(2,1)} %param.7), channel_id=1, source_target_pairs={{0,4},{1,5},{2,6},{3,7},{4,0},{5,1},{6,2},{7,3},{8,12},{9,13},{10,... | collective-permute-start | bytes 589832 | tf_op jit(solution)/shard_map/ppermute | solution.py:200
  5.3 0.0 collective-permute-start.2
  5.3 1.1 %convert_reduce_fusion.2 = f32[128]{0:T(128)S(1)} fusion(bf16[128,768]{1,0:T(8,128)(2,1)} %param.7), kind=kLoop, calls=%fused_computation.46 | loop fusion | flops 196480 | bytes 197120 | tf_op jit(solution)/shard_map/reduce_sum | solution.py:31
  6.4 0.7 %convert_element_type.55 = f32[768]{0:T(1024)S(1)} convert(bf16[768]{0:T(1024)(128)(2,1)} %param.8) | non-fusion elementwise | flops 768 | bytes 4608 | tf_op jit(solution)/shard_map/convert_element_type | solution.py:34
  7.1 1.1 %fusion.38 = f32[128]{0:T(128)S(1)} fusion(bf16[128,768]{1,0:T(8,128)(2,1)} %param.7, f32[128]{0:T(128)S(1)} %broadcast_multiply_fusion.2), kind=kLoop, calls=%fused_computation.52 | loop fusion | flops 393088 | bytes 197632 | tf_op jit(solution)/shard_map/reduce_sum | solution.py:33
  8.2 0.0 copy-start.7
  8.2 1.9 %fusion.15.refs_0_ = bf16[128,768]{1,0:T(8,128)(2,1)S(1)} fusion(bf16[768,2304]{1,0:T(8,128)(2,1)} %param.9, bf16[128,768]{1,0:T(8,128)(2,1)} %param.7, f32[768]{0:T(1024)S(1)} %convert_element_type.55, f32[128]{0:T(128)S(1)} %add_rsqrt_fusion.2, f32[128]{0:T(128)S(1)} %broadcast_multiply_fusion.2), kind=kOutput, calls=%fused_computation.27 | convolution fusion | flops 151584768 | bytes 1576960 | tf_op jit(solution)/shard_map/dot_general | solution.py:205
  10.1 3.0 %collective-permute-start.4 = (bf16[128,768]{1,0:T(8,128)(2,1)S(1)}, bf16[128,768]{1,0:T(8,128)(2,1)S(1)}, u32[]{:S(2)}, u32[]{:S(2)}) collective-permute-start(bf16[128,768]{1,0:T(8,128)(2,1)S(1)} %fusion.15.refs_0_), channel_id=1, source_target_pairs={{0,8},{1,9},{2,10},{3,11},{4,12},{5,13},{6,14},{7,15},{8,0},{9,1},... | collective-permute-start | bytes 589832 | tf_op jit(solution)/shard_map/ppermute | solution.py:200
  13.2 0.0 collective-permute-done
  13.2 0.0 collective-permute-done.1
  13.2 2.3 %collective-permute-done.2 = bf16[128,768]{1,0:T(8,128)(2,1)S(1)} collective-permute-done((bf16[128,768]{1,0:T(8,128)(2,1)}, bf16[128,768]{1,0:T(8,128)(2,1)S(1)}, u32[]{:S(2)}, u32[]{:S(2)}) %collective-permute-start.2) | collective-permute-done | bytes 196640 | tf_op jit(solution)/shard_map/ppermute | solution.py:200
  15.6 0.1 collective-permute-start.3
  15.7 0.2 convert_reduce_fusion.1
  15.9 0.4 fusion.9
  16.2 2.7 %convolution_convert_fusion.1.refs_1_.refs_3_ = bf16[512,1536]{1,0:T(8,128)(2,1)} fusion(bf16[768,2304]{1,0:T(8,128)(2,1)S(1)} %copy-done.7, bf16[512,768]{1,0:T(8,128)(2,1)S(1)} %constant_dynamic-update-slice_fusion, f32[768]{0:T(1024)S(1)} %convert_element_type.55, f32[512]{0:T(512)S(1)} %add_rsqrt_fusion.1, f32[512]{0:T(512)S(1)} %broadcast_multiply_fusion.1), kind=kOutput, calls=%fused_computation.1 | convolution fusion | flops 1210712064 | bytes 4726784 | tf_op jit(solution)/shard_map/dot_general | solution.py:205
  18.9 0.0 collective-permute-done.3
  18.9 0.2 convert_reduce_fusion
  19.1 0.4 fusion.6
  19.5 2.7 %convolution_convert_fusion.refs_2_.refs_4_ = bf16[512,1536]{1,0:T(8,128)(2,1)} fusion(bf16[768,2304]{1,0:T(8,128)(2,1)S(1)} %copy-done.7, bf16[512,768]{1,0:T(8,128)(2,1)S(1)} %collective-permute-done.3, f32[512]{0:T(512)S(1)} %add_rsqrt_fusion, f32[512]{0:T(512)S(1)} %broadcast_multiply_fusion, f32[768]{0:T(1024)S(1)} %convert_element_type.55), kind=kOutput, calls=%fused_computation | convolution fusion | flops 1210712064 | bytes 4726784 | tf_op jit(solution)/shard_map/dot_general | solution.py:205
  22.1 0.0 collective-permute-done.4.refs_0_
  22.1 0.7 %copy-done.5 = bf16[128,768]{1,0:T(8,128)(2,1)} copy-done((bf16[128,768]{1,0:T(8,128)(2,1)}, bf16[128,768]{1,0:T(8,128)(2,1)S(1)}, u32[]{:S(2)}) %copy-start.5) | copy-done | bytes 196632
  22.8 7.6 %shard_map.86 = (bf16[128,768]{1,0:T(8,128)(2,1)}, f32[128,128]{1,0:T(8,128)}, f32[16,128]{1,0:T(8,128)}) custom-call(bf16[128,768]{1,0:T(8,128)(2,1)} %copy-done.5, bf16[512,1536]{1,0:T(8,128)(2,1)} %convolution_convert_fusion.1.refs_1_.refs_3_, bf16[512,1536]{1,0:T(8,128)(2,1)} %convolution_convert_fusion.refs_2_.refs_4_, ...), custom_call_target="tpu_custom_call" | custom-call | flops 805306368 | bytes 3932160 | tf_op jit(solution)/shard_map/pallas_call | solution.py:185
  30.4 2.9 %collective-permute-start.6 = (bf16[128,768]{1,0:T(8,128)(2,1)}, bf16[128,768]{1,0:T(8,128)(2,1)S(1)}, u32[]{:S(2)}, u32[]{:S(2)}) collective-permute-start(bf16[128,768]{1,0:T(8,128)(2,1)} %get-tuple-element.6.refs_5_), channel_id=1, source_target_pairs={{0,8},{1,9},{2,10},{3,11},{4,12},{5,13},{6,14},{7,15},{8,0},{9,1},... | collective-permute-start | bytes 589832 | tf_op jit(solution)/shard_map/ppermute | solution.py:200
  33.4 0.3 convolution_convert_fusion.2
  33.7 0.2 reshape_reshape.7
  33.9 0.2 copy.16
  34.1 0.1 collective-permute-start.5
  34.2 7.6 %shard_map.87 = (f32[128,768]{1,0:T(8,128)}, f32[128,128]{1,0:T(8,128)}, f32[16,128]{1,0:T(8,128)}) custom-call(bf16[128,768]{1,0:T(8,128)(2,1)} %copy-done.4, bf16[512,1536]{1,0:T(8,128)(2,1)} %convolution_convert_fusion.1.refs_1_.refs_3_, bf16[512,1536]{1,0:T(8,128)(2,1)} %convolution_convert_fusion.refs_2_.refs_4_, ...), custom_call_target="tpu_custom_call" | custom-call | flops 805306368 | bytes 3932160 | tf_op jit(solution)/shard_map/pallas_call | solution.py:185
  41.8 1.8 %collective-permute-done.6 = bf16[128,768]{1,0:T(8,128)(2,1)S(1)} collective-permute-done((bf16[128,768]{1,0:T(8,128)(2,1)}, bf16[128,768]{1,0:T(8,128)(2,1)S(1)}, u32[]{:S(2)}, u32[]{:S(2)}) %collective-permute-start.6) | collective-permute-done | bytes 196640 | tf_op jit(solution)/shard_map/ppermute | solution.py:200
  43.6 0.5 slice.51
  44.8 0.7 %fusion.66 = (f32[128,12]{0,1:T(8,128)S(1)}, f32[128,12]{0,1:T(8,128)S(1)}) fusion(f32[16,128]{1,0:T(8,128)S(1)} %collective-permute-done.5, f32[16,128]{1,0:T(8,128)} %get-tuple-element.7, f32[]{:T(128)} %bitcast.2), kind=kLoop, calls=%fused_computation.89 | loop fusion | flops 6144 | bytes 24580 | tf_op jit(solution)/shard_map/exp | solution.py:241
  45.6 0.2 copy.11
  45.8 0.2 copy.12
  45.9 0.0 copy-start.3
  46.0 0.3 fusion.18
  46.3 0.8 %copy-done.3 = bf16[768,512]{1,0:T(8,128)(2,1)S(1)} copy-done((bf16[768,512]{1,0:T(8,128)(2,1)S(1)}, bf16[768,512]{1,0:T(8,128)(2,1)}, u32[]{:S(2)}) %copy-start.3) | copy-done | bytes 786456
  47.1 0.3 convolution_convert_fusion.3
  47.3 0.2 reshape_reshape.6
  47.5 0.2 copy.15
  47.7 0.1 fusion.63
  47.8 0.0 collective-permute-start.7
  47.8 1.2 %collective-permute-done.7 = bf16[2,1,16,128]{3,2,1,0:T(8,128)(2,1)S(1)} collective-permute-done((bf16[2,1,16,128]{3,2,1,0:T(8,128)(2,1)S(1)}, bf16[2,1,16,128]{3,2,1,0:T(8,128)(2,1)S(1)}, u32[]{:S(2)}, u32[]{:S(2)}) %collective-permute-start.7) | collective-permute-done | bytes 8224 | tf_op jit(solution)/shard_map/ppermute | solution.py:26
  49.0 0.1 pad_maximum_fusion
  49.2 0.1 fusion.84
  49.3 0.0 copy-start.8
  49.3 0.0 copy-start.11
  49.4 4.5 %collective-permute-start.8 = (bf16[1,34,16,128]{3,2,1,0:T(8,128)(2,1)S(1)}, bf16[1,34,16,128]{3,2,1,0:T(8,128)(2,1)S(1)}, u32[]{:S(2)}, u32[]{:S(2)}) collective-permute-start(bf16[1,34,16,128]{3,2,1,0:T(8,128)(2,1)S(1)} %get-tuple-element.12), channel_id=1, source_target_pairs={{0,2},{1,3},{2,4},{3,5},{4,6},{5,7},{6,8},{7,9},{8,10},{9,11},{10,... | collective-permute-start | bytes 417800 | tf_op jit(solution)/shard_map/ppermute | solution.py:22
  53.9 1.5 %collective-permute-start.9 = (bf16[1,34,16,128]{3,2,1,0:T(8,128)(2,1)S(1)}, bf16[1,34,16,128]{3,2,1,0:T(8,128)(2,1)S(1)}, u32[]{:S(2)}, u32[]{:S(2)}) collective-permute-start(bf16[1,34,16,128]{3,2,1,0:T(8,128)(2,1)S(1)} %get-tuple-element.13), channel_id=1, source_target_pairs={{2,0},{3,1},{4,2},{5,3},{6,4},{7,5},{8,6},{9,7},{10,8},{11,9},{12,... | collective-permute-start | bytes 417800 | tf_op jit(solution)/shard_map/ppermute | solution.py:22
  55.4 0.2 copy.30
  55.6 0.3 pad.clone
  55.9 0.1 copy.19
  55.9 0.1 slice.52
  56.0 3.0 %convolution_select_fusion = f32[2,32,8,3,64]{4,2,3,1,0:T(8,128)S(1)} fusion(bf16[3,3,3,128,64]{3,4,2,1,0:T(8,128)(2,1)S(1)} %copy-done.8, bf16[2,34,1,7,2,128]{5,3,4,1,0,2:T(8,128)(2,1)S(1)} %slice.52, bf16[2,34,1,8,3,128]{5,3,4,1,0,2:T(8,128)(2,1)S(1)} %copy.19, pred[8,3]{0,1:T(4,128)(4,1)S(1)} %copy-done.11), kind=kOutput, calls=%fused_computation.21 | convolution fusion | flops 455172096 | bytes 1497112 | tf_op jit(solution)/shard_map/conv_general_dilated | solution.py:55
  59.1 0.2 copy.20
  59.4 0.6 convolution_select_fusion.2
  60.1 0.1 copy.24
  60.1 1.1 %collective-permute-done.9 = bf16[1,34,16,128]{3,2,1,0:T(8,128)(2,1)S(1)} collective-permute-done((bf16[1,34,16,128]{3,2,1,0:T(8,128)(2,1)S(1)}, bf16[1,34,16,128]{3,2,1,0:T(8,128)(2,1)S(1)}, u32[]{:S(2)}, u32[]{:S(2)}) %collective-permute-start.9) | collective-permute-done | bytes 139296 | tf_op jit(solution)/shard_map/ppermute | solution.py:22
  61.4 0.6 convolution_select_fusion.1
  62.0 0.1 copy.28
  62.1 0.1 fusion.54
  62.3 0.8 %copy.29 = bf16[1,2,32,16,64]{4,3,2,1,0:T(8,128)(2,1)} copy(bf16[1,2,32,16,64]{4,2,3,1,0:T(8,128)(2,1)S(1)} %fusion.54) | data formatting | bytes 262144
  (42 shorter events, 0.6 us)
Async XLA Ops:
  0.6 45.3 %copy-start = (bf16[768,768]{1,0:T(8,128)(2,1)S(1)}, bf16[768,768]{1,0:T(8,128)(2,1)}, u32[]{:S(2)}) copy-start(bf16[768,768]{1,0:T(8,128)(2,1)} %param.10) | copy-start | bytes 3538948
  0.6 12.5 %copy-start.1 = (bf16[128,768]{1,0:T(8,128)(2,1)S(1)}, bf16[128,768]{1,0:T(8,128)(2,1)}, u32[]{:S(2)}) copy-start(bf16[128,768]{1,0:T(8,128)(2,1)} %param.7) | copy-start | bytes 589828
  0.7 12.5 %collective-permute-start = (bf16[128,768]{1,0:T(8,128)(2,1)}, bf16[128,768]{1,0:T(8,128)(2,1)S(1)}, u32[]{:S(2)}, u32[]{:S(2)}) collective-permute-start(bf16[128,768]{1,0:T(8,128)(2,1)} %param.7), channel_id=1, source_target_pairs={{0,2},{1,3},{2,0},{3,1},{4,6},{5,7},{6,4},{7,5},{8,10},{9,11},{10,... | collective-permute-start | bytes 589832 | tf_op jit(solution)/shard_map/ppermute | solution.py:200
  3.7 9.5 %collective-permute-start.1 = (bf16[128,768]{1,0:T(8,128)(2,1)}, bf16[128,768]{1,0:T(8,128)(2,1)S(1)}, u32[]{:S(2)}, u32[]{:S(2)}) collective-permute-start(bf16[128,768]{1,0:T(8,128)(2,1)} %param.7), channel_id=1, source_target_pairs={{0,4},{1,5},{2,6},{3,7},{4,0},{5,1},{6,2},{7,3},{8,12},{9,13},{10,... | collective-permute-start | bytes 589832 | tf_op jit(solution)/shard_map/ppermute | solution.py:200
  5.3 10.3 %collective-permute-start.2 = (bf16[128,768]{1,0:T(8,128)(2,1)}, bf16[128,768]{1,0:T(8,128)(2,1)S(1)}, u32[]{:S(2)}, u32[]{:S(2)}) collective-permute-start(bf16[128,768]{1,0:T(8,128)(2,1)} %param.7), channel_id=1, source_target_pairs={{0,6},{1,7},{2,4},{3,5},{4,2},{5,3},{6,0},{7,1},{8,14},{9,15},{10,... | collective-permute-start | bytes 589832 | tf_op jit(solution)/shard_map/ppermute | solution.py:200
  8.2 8.0 %copy-start.7 = (bf16[768,2304]{1,0:T(8,128)(2,1)S(1)}, bf16[768,2304]{1,0:T(8,128)(2,1)}, u32[]{:S(2)}) copy-start(bf16[768,2304]{1,0:T(8,128)(2,1)} %param.9) | copy-start | bytes 10616836
  10.1 6.1 %copy-start.4 = (bf16[128,768]{1,0:T(8,128)(2,1)}, bf16[128,768]{1,0:T(8,128)(2,1)S(1)}, u32[]{:S(2)}) copy-start(bf16[128,768]{1,0:T(8,128)(2,1)S(1)} %fusion.15.refs_0_) | copy-start | bytes 589828
  10.1 12.0 %collective-permute-start.4 = (bf16[128,768]{1,0:T(8,128)(2,1)S(1)}, bf16[128,768]{1,0:T(8,128)(2,1)S(1)}, u32[]{:S(2)}, u32[]{:S(2)}) collective-permute-start(bf16[128,768]{1,0:T(8,128)(2,1)S(1)} %fusion.15.refs_0_), channel_id=1, source_target_pairs={{0,8},{1,9},{2,10},{3,11},{4,12},{5,13},{6,14},{7,15},{8,0},{9,1},... | collective-permute-start | bytes 589832 | tf_op jit(solution)/shard_map/ppermute | solution.py:200
  15.6 3.3 %collective-permute-start.3 = (bf16[512,768]{1,0:T(8,128)(2,1)S(1)}, bf16[512,768]{1,0:T(8,128)(2,1)S(1)}, u32[]{:S(2)}, u32[]{:S(2)}) collective-permute-start(bf16[512,768]{1,0:T(8,128)(2,1)S(1)} %constant_dynamic-update-slice_fusion), channel_id=1, source_target_pairs={{0,1},{1,0},{2,3},{3,2},{4,5},{5,4},{6,7},{7,6},{8,9},{9,8},{10,11... | collective-permute-start | bytes 2359304 | tf_op jit(solution)/shard_map/ppermute | solution.py:200
  22.1 11.2 %copy-start.2 = (bf16[768,512]{1,0:T(8,128)(2,1)S(1)}, bf16[768,512]{1,0:T(8,128)(2,1)}, u32[]{:S(2)}) copy-start(bf16[768,512]{1,0:T(8,128)(2,1)} %param.12) | copy-start | bytes 2359300
  22.1 0.7 %copy-start.5 = (bf16[128,768]{1,0:T(8,128)(2,1)}, bf16[128,768]{1,0:T(8,128)(2,1)S(1)}, u32[]{:S(2)}) copy-start(bf16[128,768]{1,0:T(8,128)(2,1)S(1)} %collective-permute-done.4.refs_0_) | copy-start | bytes 589828
  30.4 3.6 %copy-start.10 = (f32[16,128]{1,0:T(8,128)S(1)}, f32[16,128]{1,0:T(8,128)}, u32[]{:S(2)}) copy-start(f32[16,128]{1,0:T(8,128)} %get-tuple-element.8) | copy-start | bytes 24580
  30.4 13.2 %collective-permute-start.6 = (bf16[128,768]{1,0:T(8,128)(2,1)}, bf16[128,768]{1,0:T(8,128)(2,1)S(1)}, u32[]{:S(2)}, u32[]{:S(2)}) collective-permute-start(bf16[128,768]{1,0:T(8,128)(2,1)} %get-tuple-element.6.refs_5_), channel_id=1, source_target_pairs={{0,8},{1,9},{2,10},{3,11},{4,12},{5,13},{6,14},{7,15},{8,0},{9,1},... | collective-permute-start | bytes 589832 | tf_op jit(solution)/shard_map/ppermute | solution.py:200
  34.1 10.7 %collective-permute-start.5 = (f32[16,128]{1,0:T(8,128)S(1)}, f32[16,128]{1,0:T(8,128)S(1)}, u32[]{:S(2)}, u32[]{:S(2)}) collective-permute-start(f32[16,128]{1,0:T(8,128)S(1)} %copy-done.10), channel_id=1, source_target_pairs={{0,8},{1,9},{2,10},{3,11},{4,12},{5,13},{6,14},{7,15},{8,0},{9,1},... | collective-permute-start | bytes 24584 | tf_op jit(solution)/shard_map/ppermute | solution.py:200
  41.8 4.1 %copy-start.9 = (f32[128,768]{1,0:T(8,128)S(1)}, f32[128,768]{1,0:T(8,128)}, u32[]{:S(2)}) copy-start(f32[128,768]{1,0:T(8,128)} %get-tuple-element.9) | copy-start | bytes 1179652
  45.9 1.1 %copy-start.3 = (bf16[768,512]{1,0:T(8,128)(2,1)S(1)}, bf16[768,512]{1,0:T(8,128)(2,1)}, u32[]{:S(2)}) copy-start(bf16[768,512]{1,0:T(8,128)(2,1)} %param.11) | copy-start | bytes 2359300
  47.1 2.1 %copy-start.6 = (bf16[128,768]{1,0:T(8,128)(2,1)}, bf16[128,768]{1,0:T(8,128)(2,1)S(1)}, u32[]{:S(2)}) copy-start(bf16[128,768]{1,0:T(8,128)(2,1)S(1)} %fusion.18) | copy-start | bytes 589828
  47.8 1.2 %collective-permute-start.7 = (bf16[2,1,16,128]{3,2,1,0:T(8,128)(2,1)S(1)}, bf16[2,1,16,128]{3,2,1,0:T(8,128)(2,1)S(1)}, u32[]{:S(2)}, u32[]{:S(2)}) collective-permute-start(bf16[2,1,16,128]{3,2,1,0:T(8,128)(2,1)S(1)} %fusion.63), channel_id=1, source_target_pairs={{0,1},{1,0},{2,3},{3,2},{4,5},{5,4},{6,7},{7,6},{8,9},{9,8},{10,11... | collective-permute-start | bytes 24584 | tf_op jit(solution)/shard_map/ppermute | solution.py:26
  49.3 6.7 %copy-start.8 = (bf16[3,3,3,128,64]{3,4,2,1,0:T(8,128)(2,1)S(1)}, bf16[3,3,3,128,64]{3,4,2,1,0:T(8,128)(2,1)}, u32[]{:S(2)}) copy-start(bf16[3,3,3,128,64]{3,4,2,1,0:T(8,128)(2,1)} %param.13) | copy-start | bytes 1327108
  49.3 6.7 %copy-start.11 = (pred[8,3]{0,1:T(4,128)(4,1)S(1)}, pred[8,3]{0,1:T(4,128)(4,1)}, u32[]{:S(2)}) copy-start(pred[8,3]{0,1:T(4,128)(4,1)} %constant.51) | copy-start | bytes 76
  49.4 9.9 %collective-permute-start.8 = (bf16[1,34,16,128]{3,2,1,0:T(8,128)(2,1)S(1)}, bf16[1,34,16,128]{3,2,1,0:T(8,128)(2,1)S(1)}, u32[]{:S(2)}, u32[]{:S(2)}) collective-permute-start(bf16[1,34,16,128]{3,2,1,0:T(8,128)(2,1)S(1)} %get-tuple-element.12), channel_id=1, source_target_pairs={{0,2},{1,3},{2,4},{3,5},{4,6},{5,7},{6,8},{7,9},{8,10},{9,11},{10,... | collective-permute-start | bytes 417800 | tf_op jit(solution)/shard_map/ppermute | solution.py:22
  53.9 7.4 %collective-permute-start.9 = (bf16[1,34,16,128]{3,2,1,0:T(8,128)(2,1)S(1)}, bf16[1,34,16,128]{3,2,1,0:T(8,128)(2,1)S(1)}, u32[]{:S(2)}, u32[]{:S(2)}) collective-permute-start(bf16[1,34,16,128]{3,2,1,0:T(8,128)(2,1)S(1)} %get-tuple-element.13), channel_id=1, source_target_pairs={{2,0},{3,1},{4,2},{5,3},{6,4},{7,5},{8,6},{9,7},{10,8},{11,9},{12,... | collective-permute-start | bytes 417800 | tf_op jit(solution)/shard_map/ppermute | solution.py:22

commit v12 on v11

--- a/solution.py
+++ b/solution.py
@@ -210,8 +210,9 @@
     head_size = model_width // HEADS
     score_scale = 1.0 / math.sqrt(head_size)
     half = lax.axis_size("seq") // 2
-    queries = projected(layer_input, norm_gain, projection[:, :model_width])
-    mirrored_queries = exchanged(queries, half)
+    query_weight = projection[:, :model_width]
+    mirrored_queries = projected(exchanged(layer_input, half), norm_gain, query_weight)
+    queries = projected(layer_input, norm_gain, query_weight)
     same_core = [layer_input] + [exchanged(layer_input, mask) for mask in range(2, half, 2)]
     mine = jnp.concatenate(same_core, axis=0)
     theirs = exchanged(mine, 1)

time: 63.6 us -> 66.4 us (1.044)
  waiting for transfers between devices: 6.4 us -> 8.68 us
  matrix products: 12.3 us -> 13.9 us
  starting transfers between devices: 16.8 us -> 15.9 us
  local copies, waits for them, and re-layouts: 5.29 us -> 4.6 us
    ppermute x7, waiting for transfers between devices: 4.14 us -> 6.42 us  [exchanged(): return lax.ppermute(x, 'seq', [(i, i ^ mask) for i in range(devices)])]
    dot_general x3 -> x4, matrix products: 7.22 us -> 8.84 us  [projected(): jnp.dot(normed, weight, preferred_element_type=jnp.float32)]
    ppermute x2, starting transfers between devices: 5.98 us -> 5.17 us  [shifted(): return lax.ppermute(block, axis, route)]
    unnamed x31 -> x27, local copies, waits for them, and re-layouts: 2.64 us -> 1.95 us
    reduce_sum x3 -> x4, other arithmetic: 1.84 us -> 2.04 us  [layer_norm(): row_var = jnp.mean(centered * centered, axis=-1, keepdims=True)]
    reduce_sum x3 -> x4, other arithmetic: 1.45 us -> 1.53 us  [layer_norm(): row_mean = jnp.mean(values32, axis=-1, keepdims=True)]
  transfers between devices with their start and end apart: 10 -> 10, of which waited for: 4 -> 5; matrix products, arithmetic and copies ran while one was open for 27% -> 24% of each run, Pallas kernels for 12% -> 12%
where the time goes in v12:
time: 66.4 us; the launch traced here: 65.8 us
  starting transfers between devices  15.9 us (24%)
  Pallas kernels  15.3 us (23%)
  matrix products  13.9 us (21%)
  waiting for transfers between devices  8.68 us (13%)
  other arithmetic  5.53 us (8%)
  local copies, waits for them, and re-layouts  4.6 us (7%)
  between operations  1.8 us (3%)
    pallas_call x2, Pallas kernels, attention(): pl.pallas_call(kernel, grid=(pairs,), cost_estimate=cost, in_specs=[row_s...  15.3 us
    ppermute x7, starting transfers between devices, exchanged(): return lax.ppermute(x, 'seq', [(i, i ^ mask) for i in range(devices)])  10.7 us
    dot_general x4, matrix products, projected(): jnp.dot(normed, weight, preferred_element_type=jnp.float32)  8.84 us
    ppermute x7, waiting for transfers between devices, exchanged(): return lax.ppermute(x, 'seq', [(i, i ^ mask) for i in range(devices)])  6.42 us
    ppermute x2, starting transfers between devices, shifted(): return lax.ppermute(block, axis, route)  5.17 us
    conv_general_dilated x3, matrix products, conv(): lax.conv_general_dilated(field[None], kernel, window_strides=(1, 1, 1), p...  4.22 us
    reduce_sum x4, other arithmetic, layer_norm(): row_var = jnp.mean(centered * centered, axis=-1, keepdims=True)  2.04 us
    unnamed x27, local copies, waits for them, and re-layouts  1.95 us
  transfers between devices with their start and end apart: 10, of which 5 were waited for; matrix products, arithmetic and copies ran while one was open for 24% of the time, Pallas kernels for 12%

profile of v12, /device:TPU:0, one launch (start us, length us, event | category | flops | bytes accessed | tf_op | source)
XLA Modules:
  0.0 65.8 jit_solution(9587162668891740021)
XLA Ops:
  0.6 0.0 copy-start
  0.6 0.0 copy-start.1
  0.7 3.1 %collective-permute-start = (bf16[128,768]{1,0:T(8,128)(2,1)}, bf16[128,768]{1,0:T(8,128)(2,1)S(1)}, u32[]{:S(2)}, u32[]{:S(2)}) collective-permute-start(bf16[128,768]{1,0:T(8,128)(2,1)} %param.7), channel_id=1, source_target_pairs={{0,2},{1,3},{2,0},{3,1},{4,6},{5,7},{6,4},{7,5},{8,10},{9,11},{10,... | collective-permute-start | bytes 589832 | tf_op jit(solution)/shard_map/ppermute | solution.py:200
  3.7 1.6 %collective-permute-start.1 = (bf16[128,768]{1,0:T(8,128)(2,1)}, bf16[128,768]{1,0:T(8,128)(2,1)S(1)}, u32[]{:S(2)}, u32[]{:S(2)}) collective-permute-start(bf16[128,768]{1,0:T(8,128)(2,1)} %param.7), channel_id=1, source_target_pairs={{0,4},{1,5},{2,6},{3,7},{4,0},{5,1},{6,2},{7,3},{8,12},{9,13},{10,... | collective-permute-start | bytes 589832 | tf_op jit(solution)/shard_map/ppermute | solution.py:200
  5.3 3.0 %collective-permute-start.4 = (bf16[128,768]{1,0:T(8,128)(2,1)}, bf16[128,768]{1,0:T(8,128)(2,1)S(1)}, u32[]{:S(2)}, u32[]{:S(2)}) collective-permute-start(bf16[128,768]{1,0:T(8,128)(2,1)} %param.7), channel_id=1, source_target_pairs={{0,8},{1,9},{2,10},{3,11},{4,12},{5,13},{6,14},{7,15},{8,0},{9,1},... | collective-permute-start | bytes 589832 | tf_op jit(solution)/shard_map/ppermute | solution.py:200
  8.3 1.1 %convert_reduce_fusion.2 = f32[128]{0:T(128)S(1)} fusion(bf16[128,768]{1,0:T(8,128)(2,1)} %param.7), kind=kLoop, calls=%fused_computation.47 | loop fusion | flops 196480 | bytes 197120 | tf_op jit(solution)/shard_map/reduce_sum | solution.py:31
  9.3 0.7 %convert_element_type.65 = f32[768]{0:T(1024)S(1)} convert(bf16[768]{0:T(1024)(128)(2,1)} %param.8) | non-fusion elementwise | flops 768 | bytes 4608 | tf_op jit(solution)/shard_map/convert_element_type | solution.py:34
  10.0 1.1 %fusion.37 = f32[128]{0:T(128)S(1)} fusion(bf16[128,768]{1,0:T(8,128)(2,1)} %param.7, f32[128]{0:T(128)S(1)} %broadcast_multiply_fusion.3), kind=kLoop, calls=%fused_computation.57 | loop fusion | flops 393088 | bytes 197632 | tf_op jit(solution)/shard_map/reduce_sum | solution.py:33
  11.2 2.4 %convolution_convert_fusion.3.refs_0_ = bf16[128,768]{1,0:T(8,128)(2,1)} fusion(bf16[768,2304]{1,0:T(8,128)(2,1)} %param.9, bf16[128,768]{1,0:T(8,128)(2,1)} %param.7, f32[768]{0:T(1024)S(1)} %convert_element_type.65, f32[128]{0:T(128)S(1)} %add_rsqrt_fusion.3, f32[128]{0:T(128)S(1)} %broadcast_multiply_fusion.3), kind=kOutput, calls=%fused_computation.27 | convolution fusion | flops 151584768 | bytes 1576960 | tf_op jit(solution)/shard_map/dot_general | solution.py:205
  13.6 0.0 collective-permute-done
  13.7 2.3 %collective-permute-done.1 = bf16[128,768]{1,0:T(8,128)(2,1)S(1)} collective-permute-done((bf16[128,768]{1,0:T(8,128)(2,1)}, bf16[128,768]{1,0:T(8,128)(2,1)S(1)}, u32[]{:S(2)}, u32[]{:S(2)}) %collective-permute-start.1) | collective-permute-done | bytes 196640 | tf_op jit(solution)/shard_map/ppermute | solution.py:200
  15.9 2.6 %collective-permute-done.2 = bf16[128,768]{1,0:T(8,128)(2,1)S(1)} collective-permute-done((bf16[128,768]{1,0:T(8,128)(2,1)}, bf16[128,768]{1,0:T(8,128)(2,1)S(1)}, u32[]{:S(2)}, u32[]{:S(2)}) %collective-permute-start.2) | collective-permute-done | bytes 196640 | tf_op jit(solution)/shard_map/ppermute | solution.py:200
  18.5 0.1 collective-permute-start.3
  18.6 0.2 convert_reduce_fusion.1
  18.8 0.4 fusion.9
  19.2 0.1 convert_reduce_fusion.3
  19.3 0.2 fusion.40
  19.5 1.1 %convolution_convert_fusion.2.refs_0_ = bf16[128,768]{1,0:T(8,128)(2,1)} fusion(bf16[768,2304]{1,0:T(8,128)(2,1)S(1)} %copy-done.5, bf16[128,768]{1,0:T(8,128)(2,1)S(1)} %collective-permute-done.4, f32[128]{0:T(128)S(1)} %add_rsqrt_fusion.2, f32[128]{0:T(128)S(1)} %broadcast_multiply_fusion.2, f32[768]{0:T(1024)S(1)} %convert_element_type.65), kind=kOutput, calls=%fused_computation.26 | convolution fusion | flops 151584768 | bytes 1577984 | tf_op jit(solution)/shard_map/dot_general | solution.py:205
  20.6 2.7 %convolution_convert_fusion.1.refs_1_.refs_3_ = bf16[512,1536]{1,0:T(8,128)(2,1)} fusion(bf16[768,2304]{1,0:T(8,128)(2,1)S(1)} %copy-done.5, bf16[512,768]{1,0:T(8,128)(2,1)S(1)} %constant_dynamic-update-slice_fusion, f32[768]{0:T(1024)S(1)} %convert_element_type.65, f32[512]{0:T(512)S(1)} %add_rsqrt_fusion.1, f32[512]{0:T(512)S(1)} %broadcast_multiply_fusion.1), kind=kOutput, calls=%fused_computation.1 | convolution fusion | flops 1210712064 | bytes 4726784 | tf_op jit(solution)/shard_map/dot_general | solution.py:205
  23.3 0.0 collective-permute-done.3
  23.3 0.2 convert_reduce_fusion
  23.5 0.4 fusion.6
  23.8 2.7 %convolution_convert_fusion.refs_2_.refs_4_ = bf16[512,1536]{1,0:T(8,128)(2,1)} fusion(bf16[768,2304]{1,0:T(8,128)(2,1)S(1)} %copy-done.5, bf16[512,768]{1,0:T(8,128)(2,1)S(1)} %collective-permute-done.3, f32[512]{0:T(512)S(1)} %add_rsqrt_fusion, f32[512]{0:T(512)S(1)} %broadcast_multiply_fusion, f32[768]{0:T(1024)S(1)} %convert_element_type.65), kind=kOutput, calls=%fused_computation | convolution fusion | flops 1210712064 | bytes 4726784 | tf_op jit(solution)/shard_map/dot_general | solution.py:205
  26.5 7.7 %shard_map.86 = (bf16[128,768]{1,0:T(8,128)(2,1)}, f32[128,128]{1,0:T(8,128)}, f32[16,128]{1,0:T(8,128)}) custom-call(bf16[128,768]{1,0:T(8,128)(2,1)} %convolution_convert_fusion.2.refs_0_, bf16[512,1536]{1,0:T(8,128)(2,1)} %convolution_convert_fusion.1.refs_1_.refs_3_, bf16[512,1536]{1,0:T(8,128)(2,1)} %convolution_convert_fusion.refs_2_.refs_4_, ...), custom_call_target="tpu_custom_call" | custom-call | flops 805306368 | bytes 3932160 | tf_op jit(solution)/shard_map/pallas_call | solution.py:185
  34.2 2.1 %collective-permute-start.6 = (bf16[128,768]{1,0:T(8,128)(2,1)}, bf16[128,768]{1,0:T(8,128)(2,1)S(1)}, u32[]{:S(2)}, u32[]{:S(2)}) collective-permute-start(bf16[128,768]{1,0:T(8,128)(2,1)} %get-tuple-element.6.refs_5_), channel_id=1, source_target_pairs={{0,8},{1,9},{2,10},{3,11},{4,12},{5,13},{6,14},{7,15},{8,0},{9,1},... | collective-permute-start | bytes 589832 | tf_op jit(solution)/shard_map/ppermute | solution.py:200
  36.3 0.3 convolution_convert_fusion.4
  36.6 0.2 reshape_reshape.7
  36.8 0.2 copy.16
  37.0 1.0 %collective-permute-start.5 = (f32[16,128]{1,0:T(8,128)S(1)}, f32[16,128]{1,0:T(8,128)S(1)}, u32[]{:S(2)}, u32[]{:S(2)}) collective-permute-start(f32[16,128]{1,0:T(8,128)S(1)} %copy-done.8), channel_id=1, source_target_pairs={{0,8},{1,9},{2,10},{3,11},{4,12},{5,13},{6,14},{7,15},{8,0},{9,1},... | collective-permute-start | bytes 24584 | tf_op jit(solution)/shard_map/ppermute | solution.py:200
  37.9 7.6 %shard_map.87 = (f32[128,768]{1,0:T(8,128)}, f32[128,128]{1,0:T(8,128)}, f32[16,128]{1,0:T(8,128)}) custom-call(bf16[128,768]{1,0:T(8,128)(2,1)} %convolution_convert_fusion.3.refs_0_, bf16[512,1536]{1,0:T(8,128)(2,1)} %convolution_convert_fusion.1.refs_1_.refs_3_, bf16[512,1536]{1,0:T(8,128)(2,1)} %convolution_convert_fusion.refs_2_.refs_4_, ...), custom_call_target="tpu_custom_call" | custom-call | flops 805306368 | bytes 3932160 | tf_op jit(solution)/shard_map/pallas_call | solution.py:185
  45.6 1.6 %collective-permute-done.6 = bf16[128,768]{1,0:T(8,128)(2,1)S(1)} collective-permute-done((bf16[128,768]{1,0:T(8,128)(2,1)}, bf16[128,768]{1,0:T(8,128)(2,1)S(1)}, u32[]{:S(2)}, u32[]{:S(2)}) %collective-permute-start.6) | collective-permute-done | bytes 196640 | tf_op jit(solution)/shard_map/ppermute | solution.py:200
  47.2 0.5 slice.51
  48.3 0.0 collective-permute-done.5
  48.3 0.7 %fusion.72 = (f32[128,12]{0,1:T(8,128)S(1)}, f32[128,12]{0,1:T(8,128)S(1)}) fusion(f32[16,128]{1,0:T(8,128)S(1)} %collective-permute-done.5, f32[16,128]{1,0:T(8,128)} %get-tuple-element.7, f32[]{:T(128)} %bitcast.2), kind=kLoop, calls=%fused_computation.100 | loop fusion | flops 6144 | bytes 24580 | tf_op jit(solution)/shard_map/exp | solution.py:242
  49.1 0.2 copy.11
  49.3 0.2 copy.12
  49.5 0.0 copy-start.3
  49.5 0.3 fusion.13
  49.8 0.8 %copy-done.3 = bf16[768,512]{1,0:T(8,128)(2,1)S(1)} copy-done((bf16[768,512]{1,0:T(8,128)(2,1)S(1)}, bf16[768,512]{1,0:T(8,128)(2,1)}, u32[]{:S(2)}) %copy-start.3) | copy-done | bytes 786456
  50.6 0.3 convolution_convert_fusion.5
  50.9 0.2 reshape_reshape.6
  51.1 0.2 copy.15
  51.2 0.1 fusion.69
  51.3 0.0 collective-permute-start.7
  51.4 1.2 %collective-permute-done.7 = bf16[2,1,16,128]{3,2,1,0:T(8,128)(2,1)S(1)} collective-permute-done((bf16[2,1,16,128]{3,2,1,0:T(8,128)(2,1)S(1)}, bf16[2,1,16,128]{3,2,1,0:T(8,128)(2,1)S(1)}, u32[]{:S(2)}, u32[]{:S(2)}) %collective-permute-start.7) | collective-permute-done | bytes 8224 | tf_op jit(solution)/shard_map/ppermute | solution.py:26
  52.5 0.1 pad_maximum_fusion
  52.7 0.1 fusion.90
  52.8 0.0 copy-start.6
  52.9 0.0 copy-start.9
  52.9 3.7 %collective-permute-start.8 = (bf16[1,34,16,128]{3,2,1,0:T(8,128)(2,1)S(1)}, bf16[1,34,16,128]{3,2,1,0:T(8,128)(2,1)S(1)}, u32[]{:S(2)}, u32[]{:S(2)}) collective-permute-start(bf16[1,34,16,128]{3,2,1,0:T(8,128)(2,1)S(1)} %get-tuple-element.12), channel_id=1, source_target_pairs={{0,2},{1,3},{2,4},{3,5},{4,6},{5,7},{6,8},{7,9},{8,10},{9,11},{10,... | collective-permute-start | bytes 417800 | tf_op jit(solution)/shard_map/ppermute | solution.py:22
  56.6 1.5 %collective-permute-start.9 = (bf16[1,34,16,128]{3,2,1,0:T(8,128)(2,1)S(1)}, bf16[1,34,16,128]{3,2,1,0:T(8,128)(2,1)S(1)}, u32[]{:S(2)}, u32[]{:S(2)}) collective-permute-start(bf16[1,34,16,128]{3,2,1,0:T(8,128)(2,1)S(1)} %get-tuple-element.13), channel_id=1, source_target_pairs={{2,0},{3,1},{4,2},{5,3},{6,4},{7,5},{8,6},{9,7},{10,8},{11,9},{12,... | collective-permute-start | bytes 417800 | tf_op jit(solution)/shard_map/ppermute | solution.py:22
  58.1 0.2 copy.30
  58.3 0.3 pad.clone
  58.6 0.1 copy.19
  58.7 0.1 slice.52
  58.8 3.0 %convolution_select_fusion = f32[2,32,8,3,64]{4,2,3,1,0:T(8,128)S(1)} fusion(bf16[3,3,3,128,64]{3,4,2,1,0:T(8,128)(2,1)S(1)} %copy-done.6, bf16[2,34,1,7,2,128]{5,3,4,1,0,2:T(8,128)(2,1)S(1)} %slice.52, bf16[2,34,1,8,3,128]{5,3,4,1,0,2:T(8,128)(2,1)S(1)} %copy.19, pred[8,3]{0,1:T(4,128)(4,1)S(1)} %copy-done.9), kind=kOutput, calls=%fused_computation.21 | convolution fusion | flops 455172096 | bytes 1497112 | tf_op jit(solution)/shard_map/conv_general_dilated | solution.py:55
  61.8 0.2 copy.20
  62.2 0.6 convolution_select_fusion.2
  62.8 0.1 copy.24
  62.9 1.1 %collective-permute-done.9 = bf16[1,34,16,128]{3,2,1,0:T(8,128)(2,1)S(1)} collective-permute-done((bf16[1,34,16,128]{3,2,1,0:T(8,128)(2,1)S(1)}, bf16[1,34,16,128]{3,2,1,0:T(8,128)(2,1)S(1)}, u32[]{:S(2)}, u32[]{:S(2)}) %collective-permute-start.9) | collective-permute-done | bytes 139296 | tf_op jit(solution)/shard_map/ppermute | solution.py:22
  64.1 0.6 convolution_select_fusion.1
  64.7 0.1 copy.28
  64.9 0.1 fusion.56
  65.0 0.8 %copy.29 = bf16[1,2,32,16,64]{4,3,2,1,0:T(8,128)(2,1)} copy(bf16[1,2,32,16,64]{4,2,3,1,0:T(8,128)(2,1)S(1)} %fusion.56) | data formatting | bytes 262144
  (43 shorter events, 0.6 us)
Async XLA Ops:
  0.6 48.8 %copy-start = (bf16[768,768]{1,0:T(8,128)(2,1)S(1)}, bf16[768,768]{1,0:T(8,128)(2,1)}, u32[]{:S(2)}) copy-start(bf16[768,768]{1,0:T(8,128)(2,1)} %param.10) | copy-start | bytes 3538948
  0.6 13.0 %copy-start.1 = (bf16[128,768]{1,0:T(8,128)(2,1)S(1)}, bf16[128,768]{1,0:T(8,128)(2,1)}, u32[]{:S(2)}) copy-start(bf16[128,768]{1,0:T(8,128)(2,1)} %param.7) | copy-start | bytes 589828
  0.7 13.0 %collective-permute-start = (bf16[128,768]{1,0:T(8,128)(2,1)}, bf16[128,768]{1,0:T(8,128)(2,1)S(1)}, u32[]{:S(2)}, u32[]{:S(2)}) collective-permute-start(bf16[128,768]{1,0:T(8,128)(2,1)} %param.7), channel_id=1, source_target_pairs={{0,2},{1,3},{2,0},{3,1},{4,6},{5,7},{6,4},{7,5},{8,10},{9,11},{10,... | collective-permute-start | bytes 589832 | tf_op jit(solution)/shard_map/ppermute | solution.py:200
  3.7 12.2 %collective-permute-start.1 = (bf16[128,768]{1,0:T(8,128)(2,1)}, bf16[128,768]{1,0:T(8,128)(2,1)S(1)}, u32[]{:S(2)}, u32[]{:S(2)}) collective-permute-start(bf16[128,768]{1,0:T(8,128)(2,1)} %param.7), channel_id=1, source_target_pairs={{0,4},{1,5},{2,6},{3,7},{4,0},{5,1},{6,2},{7,3},{8,12},{9,13},{10,... | collective-permute-start | bytes 589832 | tf_op jit(solution)/shard_map/ppermute | solution.py:200
  5.3 13.2 %collective-permute-start.2 = (bf16[128,768]{1,0:T(8,128)(2,1)}, bf16[128,768]{1,0:T(8,128)(2,1)S(1)}, u32[]{:S(2)}, u32[]{:S(2)}) collective-permute-start(bf16[128,768]{1,0:T(8,128)(2,1)} %param.7), channel_id=1, source_target_pairs={{0,6},{1,7},{2,4},{3,5},{4,2},{5,3},{6,0},{7,1},{8,14},{9,15},{10,... | collective-permute-start | bytes 589832 | tf_op jit(solution)/shard_map/ppermute | solution.py:200
  5.3 13.9 %collective-permute-start.4 = (bf16[128,768]{1,0:T(8,128)(2,1)}, bf16[128,768]{1,0:T(8,128)(2,1)S(1)}, u32[]{:S(2)}, u32[]{:S(2)}) collective-permute-start(bf16[128,768]{1,0:T(8,128)(2,1)} %param.7), channel_id=1, source_target_pairs={{0,8},{1,9},{2,10},{3,11},{4,12},{5,13},{6,14},{7,15},{8,0},{9,1},... | collective-permute-start | bytes 589832 | tf_op jit(solution)/shard_map/ppermute | solution.py:200
  13.6 5.9 %copy-start.5 = (bf16[768,2304]{1,0:T(8,128)(2,1)S(1)}, bf16[768,2304]{1,0:T(8,128)(2,1)}, u32[]{:S(2)}) copy-start(bf16[768,2304]{1,0:T(8,128)(2,1)} %param.9) | copy-start | bytes 10616836
  18.5 4.7 %collective-permute-start.3 = (bf16[512,768]{1,0:T(8,128)(2,1)S(1)}, bf16[512,768]{1,0:T(8,128)(2,1)S(1)}, u32[]{:S(2)}, u32[]{:S(2)}) collective-permute-start(bf16[512,768]{1,0:T(8,128)(2,1)S(1)} %constant_dynamic-update-slice_fusion), channel_id=1, source_target_pairs={{0,1},{1,0},{2,3},{3,2},{4,5},{5,4},{6,7},{7,6},{8,9},{9,8},{10,11... | collective-permute-start | bytes 2359304 | tf_op jit(solution)/shard_map/ppermute | solution.py:200
  26.5 9.8 %copy-start.2 = (bf16[768,512]{1,0:T(8,128)(2,1)S(1)}, bf16[768,512]{1,0:T(8,128)(2,1)}, u32[]{:S(2)}) copy-start(bf16[768,512]{1,0:T(8,128)(2,1)} %param.12) | copy-start | bytes 2359300
  34.2 2.8 %copy-start.8 = (f32[16,128]{1,0:T(8,128)S(1)}, f32[16,128]{1,0:T(8,128)}, u32[]{:S(2)}) copy-start(f32[16,128]{1,0:T(8,128)} %get-tuple-element.8) | copy-start | bytes 24580
  34.2 13.0 %collective-permute-start.6 = (bf16[128,768]{1,0:T(8,128)(2,1)}, bf16[128,768]{1,0:T(8,128)(2,1)S(1)}, u32[]{:S(2)}, u32[]{:S(2)}) collective-permute-start(bf16[128,768]{1,0:T(8,128)(2,1)} %get-tuple-element.6.refs_5_), channel_id=1, source_target_pairs={{0,8},{1,9},{2,10},{3,11},{4,12},{5,13},{6,14},{7,15},{8,0},{9,1},... | collective-permute-start | bytes 589832 | tf_op jit(solution)/shard_map/ppermute | solution.py:200
  37.0 11.4 %collective-permute-start.5 = (f32[16,128]{1,0:T(8,128)S(1)}, f32[16,128]{1,0:T(8,128)S(1)}, u32[]{:S(2)}, u32[]{:S(2)}) collective-permute-start(f32[16,128]{1,0:T(8,128)S(1)} %copy-done.8), channel_id=1, source_target_pairs={{0,8},{1,9},{2,10},{3,11},{4,12},{5,13},{6,14},{7,15},{8,0},{9,1},... | collective-permute-start | bytes 24584 | tf_op jit(solution)/shard_map/ppermute | solution.py:200
  45.6 3.9 %copy-start.7 = (f32[128,768]{1,0:T(8,128)S(1)}, f32[128,768]{1,0:T(8,128)}, u32[]{:S(2)}) copy-start(f32[128,768]{1,0:T(8,128)} %get-tuple-element.9) | copy-start | bytes 1179652
  49.5 1.1 %copy-start.3 = (bf16[768,512]{1,0:T(8,128)(2,1)S(1)}, bf16[768,512]{1,0:T(8,128)(2,1)}, u32[]{:S(2)}) copy-start(bf16[768,512]{1,0:T(8,128)(2,1)} %param.11) | copy-start | bytes 2359300
  50.6 2.1 %copy-start.4 = (bf16[128,768]{1,0:T(8,128)(2,1)}, bf16[128,768]{1,0:T(8,128)(2,1)S(1)}, u32[]{:S(2)}) copy-start(bf16[128,768]{1,0:T(8,128)(2,1)S(1)} %fusion.13) | copy-start | bytes 589828
  51.3 1.2 %collective-permute-start.7 = (bf16[2,1,16,128]{3,2,1,0:T(8,128)(2,1)S(1)}, bf16[2,1,16,128]{3,2,1,0:T(8,128)(2,1)S(1)}, u32[]{:S(2)}, u32[]{:S(2)}) collective-permute-start(bf16[2,1,16,128]{3,2,1,0:T(8,128)(2,1)S(1)} %fusion.69), channel_id=1, source_target_pairs={{0,1},{1,0},{2,3},{3,2},{4,5},{5,4},{6,7},{7,6},{8,9},{9,8},{10,11... | collective-permute-start | bytes 24584 | tf_op jit(solution)/shard_map/ppermute | solution.py:26
  52.8 5.9 %copy-start.6 = (bf16[3,3,3,128,64]{3,4,2,1,0:T(8,128)(2,1)S(1)}, bf16[3,3,3,128,64]{3,4,2,1,0:T(8,128)(2,1)}, u32[]{:S(2)}) copy-start(bf16[3,3,3,128,64]{3,4,2,1,0:T(8,128)(2,1)} %param.13) | copy-start | bytes 1327108
  52.9 5.9 %copy-start.9 = (pred[8,3]{0,1:T(4,128)(4,1)S(1)}, pred[8,3]{0,1:T(4,128)(4,1)}, u32[]{:S(2)}) copy-start(pred[8,3]{0,1:T(4,128)(4,1)} %constant.53) | copy-start | bytes 76
  52.9 9.1 %collective-permute-start.8 = (bf16[1,34,16,128]{3,2,1,0:T(8,128)(2,1)S(1)}, bf16[1,34,16,128]{3,2,1,0:T(8,128)(2,1)S(1)}, u32[]{:S(2)}, u32[]{:S(2)}) collective-permute-start(bf16[1,34,16,128]{3,2,1,0:T(8,128)(2,1)S(1)} %get-tuple-element.12), channel_id=1, source_target_pairs={{0,2},{1,3},{2,4},{3,5},{4,6},{5,7},{6,8},{7,9},{8,10},{9,11},{10,... | collective-permute-start | bytes 417800 | tf_op jit(solution)/shard_map/ppermute | solution.py:22
  56.6 7.4 %collective-permute-start.9 = (bf16[1,34,16,128]{3,2,1,0:T(8,128)(2,1)S(1)}, bf16[1,34,16,128]{3,2,1,0:T(8,128)(2,1)S(1)}, u32[]{:S(2)}, u32[]{:S(2)}) collective-permute-start(bf16[1,34,16,128]{3,2,1,0:T(8,128)(2,1)S(1)} %get-tuple-element.13), channel_id=1, source_target_pairs={{2,0},{3,1},{4,2},{5,3},{6,4},{7,5},{8,6},{9,7},{10,8},{11,9},{12,... | collective-permute-start | bytes 417800 | tf_op jit(solution)/shard_map/ppermute | solution.py:22

commit v13 on v7

--- a/solution.py
+++ b/solution.py
@@ -53,13 +53,13 @@
 def convolve(extended, low_plane, high_plane, conv_kernel):
     def conv(field, kernel, x_pad):
         return lax.conv_general_dilated(
-            field[None],
-            kernel,
+            field.transpose(0, 2, 1, 3)[None],
+            kernel.transpose(0, 2, 1, 3, 4),
             window_strides=(1, 1, 1),
-            padding=((x_pad, x_pad), (0, 0), (1, 1)),
+            padding=((x_pad, x_pad), (1, 1), (0, 0)),
             dimension_numbers=("NDHWC", "DHWIO", "NDHWC"),
             preferred_element_type=jnp.float32,
-        )[0]
+        )[0].transpose(0, 2, 1, 3)
 
     interior = lax.optimization_barrier(conv(extended, conv_kernel, 1))
     rims = jnp.concatenate(

time: 63.5 us -> 63.1 us (level)
  local copies, waits for them, and re-layouts: 6.26 us -> 4.81 us
  waiting for transfers between devices: 5.51 us -> 6.73 us
  matrix products: 12.3 us -> 11.6 us
  other arithmetic: 4.54 us -> 5.23 us
    ppermute x2, waiting for transfers between devices: 1.09 us -> 2.31 us  [shifted(): return lax.ppermute(block, axis, route)]
    unnamed x31 -> x27, local copies, waits for them, and re-layouts: 2.64 us -> 1.53 us
    conv_general_dilated x3, matrix products: 4.23 us -> 3.53 us  [conv(): lax.conv_general_dilated(field.transpose(0, 2, 1, 3)[None], kernel.transp...]
    broadcast_in_dim x1, other arithmetic: 0.12 us -> 0.81 us  [body(): decoded = convolve(extended, low_plane, high_plane, conv_kernel)[None]]
  transfers between devices with their start and end apart: 10 -> 10, of which waited for: 4 -> 4; matrix products, arithmetic and copies ran while one was open for 29% -> 27% of each run, Pallas kernels for 12% -> 12%
where the time goes in v13:
time: 63.1 us; the launch traced here: 62.6 us
  starting transfers between devices  17.2 us (27%)
  Pallas kernels  15.2 us (24%)
  matrix products  11.6 us (18%)
  waiting for transfers between devices  6.73 us (11%)
  other arithmetic  5.23 us (8%)
  local copies, waits for them, and re-layouts  4.81 us (8%)
  between operations  1.8 us (3%)
    pallas_call x2, Pallas kernels, attention(): pl.pallas_call(kernel, grid=(pairs,), cost_estimate=cost, in_specs=[row_s...  15.2 us
    ppermute x7, starting transfers between devices, exchanged(): return lax.ppermute(x, 'seq', [(i, i ^ mask) for i in range(devices)])  10.8 us
    dot_general x3, matrix products, projected(): jnp.dot(normed, weight, preferred_element_type=jnp.float32)  7.22 us
    ppermute x2, starting transfers between devices, shifted(): return lax.ppermute(block, axis, route)  6.44 us
    conv_general_dilated x3, matrix products, conv(): lax.conv_general_dilated(field.transpose(0, 2, 1, 3)[None], kernel.transp...  3.53 us
    ppermute x7, waiting for transfers between devices, exchanged(): return lax.ppermute(x, 'seq', [(i, i ^ mask) for i in range(devices)])  3.26 us
    ppermute x2, waiting for transfers between devices, shifted(): return lax.ppermute(block, axis, route)  2.31 us
    reduce_sum x3, other arithmetic, layer_norm(): row_var = jnp.mean(centered * centered, axis=-1, keepdims=True)  1.84 us
  transfers between devices with their start and end apart: 10, of which 4 were waited for; matrix products, arithmetic and copies ran while one was open for 27% of the time, Pallas kernels for 12%

profile of v13, /device:TPU:0, one launch (start us, length us, event | category | flops | bytes accessed | tf_op | source)
XLA Modules:
  0.0 62.6 jit_solution(16572703921857539733)
XLA Ops:
  0.6 0.0 copy-start
  0.6 0.0 copy-start.1
  0.7 3.1 %collective-permute-start = (bf16[128,768]{1,0:T(8,128)(2,1)}, bf16[128,768]{1,0:T(8,128)(2,1)S(1)}, u32[]{:S(2)}, u32[]{:S(2)}) collective-permute-start(bf16[128,768]{1,0:T(8,128)(2,1)} %param.7), channel_id=1, source_target_pairs={{0,2},{1,3},{2,0},{3,1},{4,6},{5,7},{6,4},{7,5},{8,10},{9,11},{10,... | collective-permute-start | bytes 589832 | tf_op jit(solution)/shard_map/ppermute | solution.py:200
  3.7 1.6 %collective-permute-start.1 = (bf16[128,768]{1,0:T(8,128)(2,1)}, bf16[128,768]{1,0:T(8,128)(2,1)S(1)}, u32[]{:S(2)}, u32[]{:S(2)}) collective-permute-start(bf16[128,768]{1,0:T(8,128)(2,1)} %param.7), channel_id=1, source_target_pairs={{0,4},{1,5},{2,6},{3,7},{4,0},{5,1},{6,2},{7,3},{8,12},{9,13},{10,... | collective-permute-start | bytes 589832 | tf_op jit(solution)/shard_map/ppermute | solution.py:200
  5.3 0.0 collective-permute-start.2
  5.3 1.1 %convert_reduce_fusion.2 = f32[128]{0:T(128)S(1)} fusion(bf16[128,768]{1,0:T(8,128)(2,1)} %param.7), kind=kLoop, calls=%fused_computation.38 | loop fusion | flops 196480 | bytes 197120 | tf_op jit(solution)/shard_map/reduce_sum | solution.py:31
  6.4 0.7 %convert_element_type.55 = f32[768]{0:T(1024)S(1)} convert(bf16[768]{0:T(1024)(128)(2,1)} %param.8) | non-fusion elementwise | flops 768 | bytes 4608 | tf_op jit(solution)/shard_map/convert_element_type | solution.py:34
  7.1 1.1 %fusion.38 = f32[128]{0:T(128)S(1)} fusion(bf16[128,768]{1,0:T(8,128)(2,1)} %param.7, f32[128]{0:T(128)S(1)} %broadcast_multiply_fusion.2), kind=kLoop, calls=%fused_computation.52 | loop fusion | flops 393088 | bytes 197632 | tf_op jit(solution)/shard_map/reduce_sum | solution.py:33
  8.2 0.0 copy-start.7
  8.2 1.9 %fusion.14.refs_0_ = bf16[128,768]{1,0:T(8,128)(2,1)S(1)} fusion(bf16[768,2304]{1,0:T(8,128)(2,1)} %param.9, bf16[128,768]{1,0:T(8,128)(2,1)} %param.7, f32[768]{0:T(1024)S(1)} %convert_element_type.55, f32[128]{0:T(128)S(1)} %add_rsqrt_fusion.2, f32[128]{0:T(128)S(1)} %broadcast_multiply_fusion.2), kind=kOutput, calls=%fused_computation.25 | convolution fusion | flops 151584768 | bytes 1576960 | tf_op jit(solution)/shard_map/dot_general | solution.py:205
  10.1 3.0 %collective-permute-start.4 = (bf16[128,768]{1,0:T(8,128)(2,1)S(1)}, bf16[128,768]{1,0:T(8,128)(2,1)S(1)}, u32[]{:S(2)}, u32[]{:S(2)}) collective-permute-start(bf16[128,768]{1,0:T(8,128)(2,1)S(1)} %fusion.14.refs_0_), channel_id=1, source_target_pairs={{0,8},{1,9},{2,10},{3,11},{4,12},{5,13},{6,14},{7,15},{8,0},{9,1},... | collective-permute-start | bytes 589832 | tf_op jit(solution)/shard_map/ppermute | solution.py:200
  13.2 0.0 collective-permute-done
  13.2 0.0 collective-permute-done.1
  13.2 2.3 %collective-permute-done.2 = bf16[128,768]{1,0:T(8,128)(2,1)S(1)} collective-permute-done((bf16[128,768]{1,0:T(8,128)(2,1)}, bf16[128,768]{1,0:T(8,128)(2,1)S(1)}, u32[]{:S(2)}, u32[]{:S(2)}) %collective-permute-start.2) | collective-permute-done | bytes 196640 | tf_op jit(solution)/shard_map/ppermute | solution.py:200
  15.6 0.1 collective-permute-start.3
  15.7 0.2 convert_reduce_fusion.1
  15.9 0.4 fusion.9
  16.2 0.0 copy-done.4
  16.2 0.0 copy-done.7
  16.2 2.7 %convolution_convert_fusion.1.refs_1_.refs_3_ = bf16[512,1536]{1,0:T(8,128)(2,1)} fusion(bf16[768,2304]{1,0:T(8,128)(2,1)S(1)} %copy-done.7, bf16[512,768]{1,0:T(8,128)(2,1)S(1)} %constant_dynamic-update-slice_fusion, f32[768]{0:T(1024)S(1)} %convert_element_type.55, f32[512]{0:T(512)S(1)} %add_rsqrt_fusion.1, f32[512]{0:T(512)S(1)} %broadcast_multiply_fusion.1), kind=kOutput, calls=%fused_computation.1 | convolution fusion | flops 1210712064 | bytes 4726784 | tf_op jit(solution)/shard_map/dot_general | solution.py:205
  18.9 0.0 collective-permute-done.3
  18.9 0.2 convert_reduce_fusion
  19.1 0.4 fusion.6
  19.5 2.7 %convolution_convert_fusion.refs_2_.refs_4_ = bf16[512,1536]{1,0:T(8,128)(2,1)} fusion(bf16[768,2304]{1,0:T(8,128)(2,1)S(1)} %copy-done.7, bf16[512,768]{1,0:T(8,128)(2,1)S(1)} %collective-permute-done.3, f32[512]{0:T(512)S(1)} %add_rsqrt_fusion, f32[512]{0:T(512)S(1)} %broadcast_multiply_fusion, f32[768]{0:T(1024)S(1)} %convert_element_type.55), kind=kOutput, calls=%fused_computation | convolution fusion | flops 1210712064 | bytes 4726784 | tf_op jit(solution)/shard_map/dot_general | solution.py:205
  22.1 0.0 collective-permute-done.4.refs_0_
  22.1 0.7 %copy-done.5 = bf16[128,768]{1,0:T(8,128)(2,1)} copy-done((bf16[128,768]{1,0:T(8,128)(2,1)}, bf16[128,768]{1,0:T(8,128)(2,1)S(1)}, u32[]{:S(2)}) %copy-start.5) | copy-done | bytes 196632
  22.8 7.6 %shard_map.86 = (bf16[128,768]{1,0:T(8,128)(2,1)}, f32[128,128]{1,0:T(8,128)}, f32[16,128]{1,0:T(8,128)}) custom-call(bf16[128,768]{1,0:T(8,128)(2,1)} %copy-done.5, bf16[512,1536]{1,0:T(8,128)(2,1)} %convolution_convert_fusion.1.refs_1_.refs_3_, bf16[512,1536]{1,0:T(8,128)(2,1)} %convolution_convert_fusion.refs_2_.refs_4_, ...), custom_call_target="tpu_custom_call" | custom-call | flops 805306368 | bytes 3932160 | tf_op jit(solution)/shard_map/pallas_call | solution.py:185
  30.4 2.9 %collective-permute-start.6 = (bf16[128,768]{1,0:T(8,128)(2,1)}, bf16[128,768]{1,0:T(8,128)(2,1)S(1)}, u32[]{:S(2)}, u32[]{:S(2)}) collective-permute-start(bf16[128,768]{1,0:T(8,128)(2,1)} %get-tuple-element.6.refs_5_), channel_id=1, source_target_pairs={{0,8},{1,9},{2,10},{3,11},{4,12},{5,13},{6,14},{7,15},{8,0},{9,1},... | collective-permute-start | bytes 589832 | tf_op jit(solution)/shard_map/ppermute | solution.py:200
  33.4 0.3 convolution_convert_fusion.2
  33.7 0.2 reshape_reshape.7
  33.9 0.2 copy.21
  34.1 0.1 collective-permute-start.5
  34.2 7.5 %shard_map.87 = (f32[128,768]{1,0:T(8,128)}, f32[128,128]{1,0:T(8,128)}) custom-call(bf16[128,768]{1,0:T(8,128)(2,1)} %copy-done.4, bf16[512,1536]{1,0:T(8,128)(2,1)} %convolution_convert_fusion.1.refs_1_.refs_3_, bf16[512,1536]{1,0:T(8,128)(2,1)} %convolution_convert_fusion.refs_2_.refs_4_, bf16[512,1536]{1,0:T(8,128)(2,1)} %convolution_convert_fusion.1.refs_1_.refs_3_, ...), custom_call_target="tpu_custom_call" | custom-call | flops 805306368 | bytes 3932160 | tf_op jit(solution)/shard_map/pallas_call | solution.py:185
  41.7 1.0 %copy.15 = f32[128,128]{0,1:T(8,128)S(1)} copy(f32[128,128]{1,0:T(8,128)} %get-tuple-element.7) | data formatting | bytes 131072 | tf_op jit(solution)/shard_map/pallas_call | solution.py:185
  42.7 0.9 %collective-permute-done.6 = bf16[128,768]{1,0:T(8,128)(2,1)S(1)} collective-permute-done((bf16[128,768]{1,0:T(8,128)(2,1)}, bf16[128,768]{1,0:T(8,128)(2,1)S(1)}, u32[]{:S(2)}, u32[]{:S(2)}) %collective-permute-start.6) | collective-permute-done | bytes 196640 | tf_op jit(solution)/shard_map/ppermute | solution.py:200
  43.6 0.5 slice.52
  44.8 0.0 collective-permute-done.5
  44.9 0.2 copy.16
  45.1 0.2 copy.17
  45.2 0.0 copy-start.3
  45.3 0.3 fusion.17
  45.6 0.8 %copy-done.3 = bf16[768,512]{1,0:T(8,128)(2,1)S(1)} copy-done((bf16[768,512]{1,0:T(8,128)(2,1)S(1)}, bf16[768,512]{1,0:T(8,128)(2,1)}, u32[]{:S(2)}) %copy-start.3) | copy-done | bytes 786456
  46.4 0.3 convolution_convert_fusion.3
  46.6 0.2 reshape_reshape.6
  46.8 0.2 copy.20
  47.0 0.1 fusion.63
  47.1 0.0 collective-permute-start.7
  47.1 1.2 %collective-permute-done.7 = bf16[2,1,16,128]{3,2,1,0:T(8,128)(2,1)S(1)} collective-permute-done((bf16[2,1,16,128]{3,2,1,0:T(8,128)(2,1)S(1)}, bf16[2,1,16,128]{3,2,1,0:T(8,128)(2,1)S(1)}, u32[]{:S(2)}, u32[]{:S(2)}) %collective-permute-start.7) | collective-permute-done | bytes 8224 | tf_op jit(solution)/shard_map/ppermute | solution.py:26
  48.3 0.1 pad_maximum_fusion
  48.5 0.0 copy-start.8
  48.5 0.0 copy-start.11
  48.5 0.1 fusion.80
  48.7 5.0 %collective-permute-start.8 = (bf16[1,34,16,128]{3,2,1,0:T(8,128)(2,1)S(1)}, bf16[1,34,16,128]{3,2,1,0:T(8,128)(2,1)S(1)}, u32[]{:S(2)}, u32[]{:S(2)}) collective-permute-start(bf16[1,34,16,128]{3,2,1,0:T(8,128)(2,1)S(1)} %get-tuple-element.10), channel_id=1, source_target_pairs={{0,2},{1,3},{2,4},{3,5},{4,6},{5,7},{6,8},{7,9},{8,10},{9,11},{10,... | collective-permute-start | bytes 417800 | tf_op jit(solution)/shard_map/ppermute | solution.py:22
  53.6 1.5 %collective-permute-start.9 = (bf16[1,34,16,128]{3,2,1,0:T(8,128)(2,1)S(1)}, bf16[1,34,16,128]{3,2,1,0:T(8,128)(2,1)S(1)}, u32[]{:S(2)}, u32[]{:S(2)}) collective-permute-start(bf16[1,34,16,128]{3,2,1,0:T(8,128)(2,1)S(1)} %get-tuple-element.11), channel_id=1, source_target_pairs={{2,0},{3,1},{4,2},{5,3},{6,4},{7,5},{8,6},{9,7},{10,8},{11,9},{12,... | collective-permute-start | bytes 417800 | tf_op jit(solution)/shard_map/ppermute | solution.py:22
  55.2 0.1 copy.23
  55.3 2.5 %convolution_select_fusion = f32[2,16,8,5,64]{4,2,3,1,0:T(8,128)S(1)} fusion(bf16[2,16,1,7,2,128]{5,3,4,1,0,2:T(8,128)(2,1)S(1)} %slice.53, bf16[2,16,1,8,5,128]{5,3,4,1,0,2:T(8,128)(2,1)S(1)} %copy.23, pred[8,5]{0,1:T(8,128)(4,1)S(1)} %copy-done.11, bf16[3,3,3,128,64]{3,4,2,1,0:T(8,128)(2,1)S(1)} %copy-done.8), kind=kOutput, calls=%fused_computation.19 | convolution fusion | flops 363216896 | bytes 1212456 | tf_op jit(solution)/shard_map/conv_general_dilated | solution.py:55
  57.8 0.1 copy.25
  58.0 0.0 collective-permute-done.8
  58.1 0.5 convolution_select_fusion.2
  58.6 0.1 copy.29
  58.7 2.3 %collective-permute-done.9 = bf16[1,34,16,128]{3,2,1,0:T(8,128)(2,1)S(1)} collective-permute-done((bf16[1,34,16,128]{3,2,1,0:T(8,128)(2,1)S(1)}, bf16[1,34,16,128]{3,2,1,0:T(8,128)(2,1)S(1)}, u32[]{:S(2)}, u32[]{:S(2)}) %collective-permute-start.9) | collective-permute-done | bytes 139296 | tf_op jit(solution)/shard_map/ppermute | solution.py:22
  61.1 0.5 convolution_select_fusion.1
  61.6 0.1 copy.33
  61.8 0.8 %fusion.41 = bf16[1,2,32,16,64]{4,3,2,1,0:T(8,128)(2,1)} fusion(f32[2,32,16,64]{3,2,1,0:T(8,128)S(1)} %slice_bitcast_fusion, f32[1,32,16,64]{3,2,1,0:T(8,128)S(1)} %get-tuple-element.16, f32[1,32,16,64]{3,2,1,0:T(8,128)S(1)} %get-tuple-element.17), kind=kLoop, calls=%fused_computation.57 | loop fusion | flops 393216 | bytes 655360 | tf_op jit(solution)/shard_map/broadcast_in_dim | solution.py:259
  (39 shorter events, 0.5 us)
Async XLA Ops:
  0.6 44.6 %copy-start = (bf16[768,768]{1,0:T(8,128)(2,1)S(1)}, bf16[768,768]{1,0:T(8,128)(2,1)}, u32[]{:S(2)}) copy-start(bf16[768,768]{1,0:T(8,128)(2,1)} %param.10) | copy-start | bytes 3538948
  0.6 12.5 %copy-start.1 = (bf16[128,768]{1,0:T(8,128)(2,1)S(1)}, bf16[128,768]{1,0:T(8,128)(2,1)}, u32[]{:S(2)}) copy-start(bf16[128,768]{1,0:T(8,128)(2,1)} %param.7) | copy-start | bytes 589828
  0.7 12.5 %collective-permute-start = (bf16[128,768]{1,0:T(8,128)(2,1)}, bf16[128,768]{1,0:T(8,128)(2,1)S(1)}, u32[]{:S(2)}, u32[]{:S(2)}) collective-permute-start(bf16[128,768]{1,0:T(8,128)(2,1)} %param.7), channel_id=1, source_target_pairs={{0,2},{1,3},{2,0},{3,1},{4,6},{5,7},{6,4},{7,5},{8,10},{9,11},{10,... | collective-permute-start | bytes 589832 | tf_op jit(solution)/shard_map/ppermute | solution.py:200
  3.7 9.5 %collective-permute-start.1 = (bf16[128,768]{1,0:T(8,128)(2,1)}, bf16[128,768]{1,0:T(8,128)(2,1)S(1)}, u32[]{:S(2)}, u32[]{:S(2)}) collective-permute-start(bf16[128,768]{1,0:T(8,128)(2,1)} %param.7), channel_id=1, source_target_pairs={{0,4},{1,5},{2,6},{3,7},{4,0},{5,1},{6,2},{7,3},{8,12},{9,13},{10,... | collective-permute-start | bytes 589832 | tf_op jit(solution)/shard_map/ppermute | solution.py:200
  5.3 10.3 %collective-permute-start.2 = (bf16[128,768]{1,0:T(8,128)(2,1)}, bf16[128,768]{1,0:T(8,128)(2,1)S(1)}, u32[]{:S(2)}, u32[]{:S(2)}) collective-permute-start(bf16[128,768]{1,0:T(8,128)(2,1)} %param.7), channel_id=1, source_target_pairs={{0,6},{1,7},{2,4},{3,5},{4,2},{5,3},{6,0},{7,1},{8,14},{9,15},{10,... | collective-permute-start | bytes 589832 | tf_op jit(solution)/shard_map/ppermute | solution.py:200
  8.2 8.0 %copy-start.7 = (bf16[768,2304]{1,0:T(8,128)(2,1)S(1)}, bf16[768,2304]{1,0:T(8,128)(2,1)}, u32[]{:S(2)}) copy-start(bf16[768,2304]{1,0:T(8,128)(2,1)} %param.9) | copy-start | bytes 10616836
  10.1 6.1 %copy-start.4 = (bf16[128,768]{1,0:T(8,128)(2,1)}, bf16[128,768]{1,0:T(8,128)(2,1)S(1)}, u32[]{:S(2)}) copy-start(bf16[128,768]{1,0:T(8,128)(2,1)S(1)} %fusion.14.refs_0_) | copy-start | bytes 589828
  10.1 12.0 %collective-permute-start.4 = (bf16[128,768]{1,0:T(8,128)(2,1)S(1)}, bf16[128,768]{1,0:T(8,128)(2,1)S(1)}, u32[]{:S(2)}, u32[]{:S(2)}) collective-permute-start(bf16[128,768]{1,0:T(8,128)(2,1)S(1)} %fusion.14.refs_0_), channel_id=1, source_target_pairs={{0,8},{1,9},{2,10},{3,11},{4,12},{5,13},{6,14},{7,15},{8,0},{9,1},... | collective-permute-start | bytes 589832 | tf_op jit(solution)/shard_map/ppermute | solution.py:200
  15.6 3.3 %collective-permute-start.3 = (bf16[512,768]{1,0:T(8,128)(2,1)S(1)}, bf16[512,768]{1,0:T(8,128)(2,1)S(1)}, u32[]{:S(2)}, u32[]{:S(2)}) collective-permute-start(bf16[512,768]{1,0:T(8,128)(2,1)S(1)} %constant_dynamic-update-slice_fusion), channel_id=1, source_target_pairs={{0,1},{1,0},{2,3},{3,2},{4,5},{5,4},{6,7},{7,6},{8,9},{9,8},{10,11... | collective-permute-start | bytes 2359304 | tf_op jit(solution)/shard_map/ppermute | solution.py:200
  22.1 11.2 %copy-start.2 = (bf16[768,512]{1,0:T(8,128)(2,1)S(1)}, bf16[768,512]{1,0:T(8,128)(2,1)}, u32[]{:S(2)}) copy-start(bf16[768,512]{1,0:T(8,128)(2,1)} %param.12) | copy-start | bytes 2359300
  22.1 0.7 %copy-start.5 = (bf16[128,768]{1,0:T(8,128)(2,1)}, bf16[128,768]{1,0:T(8,128)(2,1)S(1)}, u32[]{:S(2)}) copy-start(bf16[128,768]{1,0:T(8,128)(2,1)S(1)} %collective-permute-done.4.refs_0_) | copy-start | bytes 589828
  30.4 3.6 %copy-start.10 = (f32[16,128]{1,0:T(8,128)S(1)}, f32[16,128]{1,0:T(8,128)}, u32[]{:S(2)}) copy-start(f32[16,128]{1,0:T(8,128)} %get-tuple-element.8) | copy-start | bytes 24580
  30.4 13.2 %collective-permute-start.6 = (bf16[128,768]{1,0:T(8,128)(2,1)}, bf16[128,768]{1,0:T(8,128)(2,1)S(1)}, u32[]{:S(2)}, u32[]{:S(2)}) collective-permute-start(bf16[128,768]{1,0:T(8,128)(2,1)} %get-tuple-element.6.refs_5_), channel_id=1, source_target_pairs={{0,8},{1,9},{2,10},{3,11},{4,12},{5,13},{6,14},{7,15},{8,0},{9,1},... | collective-permute-start | bytes 589832 | tf_op jit(solution)/shard_map/ppermute | solution.py:200
  34.1 10.7 %collective-permute-start.5 = (f32[16,128]{1,0:T(8,128)S(1)}, f32[16,128]{1,0:T(8,128)S(1)}, u32[]{:S(2)}, u32[]{:S(2)}) collective-permute-start(f32[16,128]{1,0:T(8,128)S(1)} %copy-done.10), channel_id=1, source_target_pairs={{0,8},{1,9},{2,10},{3,11},{4,12},{5,13},{6,14},{7,15},{8,0},{9,1},... | collective-permute-start | bytes 24584 | tf_op jit(solution)/shard_map/ppermute | solution.py:200
  41.7 3.5 %copy-start.9 = (f32[128,768]{1,0:T(8,128)S(1)}, f32[128,768]{1,0:T(8,128)}, u32[]{:S(2)}) copy-start(f32[128,768]{1,0:T(8,128)} %get-tuple-element.9) | copy-start | bytes 1179652
  45.2 1.1 %copy-start.3 = (bf16[768,512]{1,0:T(8,128)(2,1)S(1)}, bf16[768,512]{1,0:T(8,128)(2,1)}, u32[]{:S(2)}) copy-start(bf16[768,512]{1,0:T(8,128)(2,1)} %param.11) | copy-start | bytes 2359300
  46.4 2.1 %copy-start.6 = (bf16[128,768]{1,0:T(8,128)(2,1)}, bf16[128,768]{1,0:T(8,128)(2,1)S(1)}, u32[]{:S(2)}) copy-start(bf16[128,768]{1,0:T(8,128)(2,1)S(1)} %fusion.17) | copy-start | bytes 589828
  47.1 1.2 %collective-permute-start.7 = (bf16[2,1,16,128]{3,2,1,0:T(8,128)(2,1)S(1)}, bf16[2,1,16,128]{3,2,1,0:T(8,128)(2,1)S(1)}, u32[]{:S(2)}, u32[]{:S(2)}) collective-permute-start(bf16[2,1,16,128]{3,2,1,0:T(8,128)(2,1)S(1)} %fusion.63), channel_id=1, source_target_pairs={{0,1},{1,0},{2,3},{3,2},{4,5},{5,4},{6,7},{7,6},{8,9},{9,8},{10,11... | collective-permute-start | bytes 24584 | tf_op jit(solution)/shard_map/ppermute | solution.py:26
  48.5 6.8 %copy-start.8 = (bf16[3,3,3,128,64]{3,4,2,1,0:T(8,128)(2,1)S(1)}, bf16[3,3,3,128,64]{3,4,2,1,0:T(8,128)(2,1)}, u32[]{:S(2)}) copy-start(bf16[3,3,3,128,64]{3,4,2,1,0:T(8,128)(2,1)} %param.13) | copy-start | bytes 1327108
  48.5 6.8 %copy-start.11 = (pred[8,5]{0,1:T(8,128)(4,1)S(1)}, pred[8,5]{0,1:T(8,128)(4,1)}, u32[]{:S(2)}) copy-start(pred[8,5]{0,1:T(8,128)(4,1)} %constant.51) | copy-start | bytes 124
  48.7 9.3 %collective-permute-start.8 = (bf16[1,34,16,128]{3,2,1,0:T(8,128)(2,1)S(1)}, bf16[1,34,16,128]{3,2,1,0:T(8,128)(2,1)S(1)}, u32[]{:S(2)}, u32[]{:S(2)}) collective-permute-start(bf16[1,34,16,128]{3,2,1,0:T(8,128)(2,1)S(1)} %get-tuple-element.10), channel_id=1, source_target_pairs={{0,2},{1,3},{2,4},{3,5},{4,6},{5,7},{6,8},{7,9},{8,10},{9,11},{10,... | collective-permute-start | bytes 417800 | tf_op jit(solution)/shard_map/ppermute | solution.py:22
  53.6 7.4 %collective-permute-start.9 = (bf16[1,34,16,128]{3,2,1,0:T(8,128)(2,1)S(1)}, bf16[1,34,16,128]{3,2,1,0:T(8,128)(2,1)S(1)}, u32[]{:S(2)}, u32[]{:S(2)}) collective-permute-start(bf16[1,34,16,128]{3,2,1,0:T(8,128)(2,1)S(1)} %get-tuple-element.11), channel_id=1, source_target_pairs={{2,0},{3,1},{4,2},{5,3},{6,4},{7,5},{8,6},{9,7},{10,8},{11,9},{12,... | collective-permute-start | bytes 417800 | tf_op jit(solution)/shard_map/ppermute | solution.py:22

commit v14 on v13

--- a/solution.py
+++ b/solution.py
@@ -102,9 +102,7 @@
         in_head = (lane >= h * head_size) & (lane < (h + 1) * head_size)
         q_h = jnp.where(in_head, q, jnp.zeros_like(q))
         scores = [
-            lax.dot_general(
-                q_h, k_ref[...], (((1,), (1,)), ((), ())), preferred_element_type=jnp.float32
-            )
+            jnp.dot(q_h, k_ref[...], preferred_element_type=jnp.float32)
             for k_ref in k_refs
         ]
         raw_max = scores[0].max(axis=-1, keepdims=True)
@@ -153,8 +151,8 @@
         ordered=after is not None,
         rows_out=rows_out,
     )
-    key_specs = [pl.BlockSpec((c.shape[0], pair), lambda j: (0, j)) for c in kv_chunks]
-    value_specs = [pl.BlockSpec((c.shape[0], pair), lambda j: (0, j + pairs)) for c in kv_chunks]
+    key_specs = [pl.BlockSpec((pair, c.shape[1]), lambda j: (j, 0)) for c, _ in kv_chunks]
+    value_specs = [pl.BlockSpec((c.shape[0], pair), lambda j: (0, j)) for _, c in kv_chunks]
     row_spec = pl.BlockSpec((token_count, pair), lambda j: (0, j))
     stat_width = 128
     if whole_output:
@@ -166,7 +164,7 @@
         out_specs = [row_spec, pl.BlockSpec((token_count, stat_width), lambda j: (0, 0))]
     extra = [] if after is None else [after]
     extra_specs = [pl.BlockSpec(memory_space=pl.ANY) for _ in extra]
-    keys = sum(c.shape[0] for c in kv_chunks)
+    keys = sum(c.shape[0] for _, c in kv_chunks)
     cost = pl.CostEstimate(
         flops=8 * token_count * keys * model_width,
         transcendentals=token_count * keys * (model_width // head_size),
@@ -189,7 +187,7 @@
         in_specs=[row_spec] + key_specs + value_specs + extra_specs,
         out_specs=out_specs,
         out_shape=out_shape,
-    )(queries, *kv_chunks, *kv_chunks, *extra)
+    )(queries, *[k for k, _ in kv_chunks], *[v for _, v in kv_chunks], *extra)
     if rows_out:
         return results[0], results[2]
     return results[0], results[1]
@@ -203,6 +201,15 @@
 def projected(rows, norm_gain, weight):
     normed = layer_norm(rows, norm_gain).astype(jnp.bfloat16)
     return jnp.dot(normed, weight, preferred_element_type=jnp.float32).astype(jnp.bfloat16)
+
+
+def keys_values(rows, norm_gain, key_weight, value_weight):
+    normed = layer_norm(rows, norm_gain).astype(jnp.bfloat16)
+    keys_t = lax.dot_general(
+        key_weight, normed, (((0,), (1,)), ((), ())), preferred_element_type=jnp.float32
+    ).astype(jnp.bfloat16)
+    values = jnp.dot(normed, value_weight, preferred_element_type=jnp.float32).astype(jnp.bfloat16)
+    return keys_t, values
 
 
 def body(layer_input, norm_gain, projection, output_weight, deep_weight, skip_weight, conv_kernel):
@@ -215,8 +222,9 @@
     same_core = [layer_input] + [exchanged(layer_input, mask) for mask in range(2, half, 2)]
     mine = jnp.concatenate(same_core, axis=0)
     theirs = exchanged(mine, 1)
-    kv_weight = projection[:, model_width:]
-    kv_chunks = [projected(mine, norm_gain, kv_weight), projected(theirs, norm_gain, kv_weight)]
+    key_weight = projection[:, model_width : 2 * model_width]
+    value_weight = projection[:, 2 * model_width :]
+    kv_chunks = [keys_values(rows, norm_gain, key_weight, value_weight) for rows in (mine, theirs)]
     remote_out, remote_lse = attention(
         mirrored_queries, kv_chunks, head_size, score_scale, jnp.bfloat16, False, rows_out=True
     )

time: 63.1 us -> 64.8 us (1.027)
  matrix products: 11.6 us -> 13.6 us
    dot_general x0 -> x4, matrix products: none -> 7.3 us  [the longest x2 3.8 us: keys_values(): lax.dot_general(key_weight, normed, (((0,), (1,)), ((), ())), preferred_e...]
    dot_general x3 -> x1, matrix products: 7.22 us -> 1.89 us  [projected(): jnp.dot(normed, weight, preferred_element_type=jnp.float32)]
  transfers between devices with their start and end apart: 10 -> 10, of which waited for: 4 -> 4; matrix products, arithmetic and copies ran while one was open for 27% -> 29% of each run, Pallas kernels for 12% -> 12%
where the time goes in v14:
time: 64.8 us; the launch traced here: 64.3 us
  starting transfers between devices  17.1 us (26%)
  Pallas kernels  14.9 us (23%)
  matrix products  13.6 us (21%)
  waiting for transfers between devices  6.85 us (11%)
  other arithmetic  5.23 us (8%)
  local copies, waits for them, and re-layouts  4.81 us (7%)
  between operations  1.8 us (3%)
    pallas_call x2, Pallas kernels, attention(): pl.pallas_call(kernel, grid=(pairs,), cost_estimate=cost, in_specs=[row_s...  14.9 us
    ppermute x7, starting transfers between devices, exchanged(): return lax.ppermute(x, 'seq', [(i, i ^ mask) for i in range(devices)])  10.8 us
    ppermute x2, starting transfers between devices, shifted(): return lax.ppermute(block, axis, route)  6.32 us
    dot_general x2, matrix products, keys_values(): lax.dot_general(key_weight, normed, (((0,), (1,)), ((), ())), preferred_e...  3.8 us
    conv_general_dilated x3, matrix products, conv(): lax.conv_general_dilated(field.transpose(0, 2, 1, 3)[None], kernel.transp...  3.54 us
    dot_general x2, matrix products, keys_values(): jnp.dot(normed, value_weight, preferred_element_type=jnp.float32)  3.5 us
    ppermute x7, waiting for transfers between devices, exchanged(): return lax.ppermute(x, 'seq', [(i, i ^ mask) for i in range(devices)])  3.38 us
    ppermute x2, waiting for transfers between devices, shifted(): return lax.ppermute(block, axis, route)  2.31 us
  transfers between devices with their start and end apart: 10, of which 4 were waited for; matrix products, arithmetic and copies ran while one was open for 29% of the time, Pallas kernels for 12%

profile of v14, /device:TPU:0, one launch (start us, length us, event | category | flops | bytes accessed | tf_op | source)
XLA Modules:
  0.0 64.3 jit_solution(8415451524788089036)
XLA Ops:
  0.6 0.0 copy-start
  0.6 0.0 copy-start.1
  0.7 3.1 %collective-permute-start = (bf16[128,768]{1,0:T(8,128)(2,1)}, bf16[128,768]{1,0:T(8,128)(2,1)S(1)}, u32[]{:S(2)}, u32[]{:S(2)}) collective-permute-start(bf16[128,768]{1,0:T(8,128)(2,1)} %param.7), channel_id=1, source_target_pairs={{0,2},{1,3},{2,0},{3,1},{4,6},{5,7},{6,4},{7,5},{8,10},{9,11},{10,... | collective-permute-start | bytes 589832 | tf_op jit(solution)/shard_map/ppermute | solution.py:198
  3.7 1.6 %collective-permute-start.1 = (bf16[128,768]{1,0:T(8,128)(2,1)}, bf16[128,768]{1,0:T(8,128)(2,1)S(1)}, u32[]{:S(2)}, u32[]{:S(2)}) collective-permute-start(bf16[128,768]{1,0:T(8,128)(2,1)} %param.7), channel_id=1, source_target_pairs={{0,4},{1,5},{2,6},{3,7},{4,0},{5,1},{6,2},{7,3},{8,12},{9,13},{10,... | collective-permute-start | bytes 589832 | tf_op jit(solution)/shard_map/ppermute | solution.py:198
  5.3 0.0 collective-permute-start.2
  5.3 1.1 %convert_reduce_fusion.2 = f32[128]{0:T(128)S(1)} fusion(bf16[128,768]{1,0:T(8,128)(2,1)} %param.7), kind=kLoop, calls=%fused_computation.38 | loop fusion | flops 196480 | bytes 197120 | tf_op jit(solution)/shard_map/reduce_sum | solution.py:31
  6.4 0.7 %convert_element_type.65 = f32[768]{0:T(1024)S(1)} convert(bf16[768]{0:T(1024)(128)(2,1)} %param.8) | non-fusion elementwise | flops 768 | bytes 4608 | tf_op jit(solution)/shard_map/convert_element_type | solution.py:34
  7.1 1.1 %fusion.34 = f32[128]{0:T(128)S(1)} fusion(bf16[128,768]{1,0:T(8,128)(2,1)} %param.7, f32[128]{0:T(128)S(1)} %broadcast_multiply_fusion.2), kind=kLoop, calls=%fused_computation.52 | loop fusion | flops 393088 | bytes 197632 | tf_op jit(solution)/shard_map/reduce_sum | solution.py:33
  8.2 0.0 copy-start.7
  8.2 1.9 %fusion.14.refs_0_ = bf16[128,768]{1,0:T(8,128)(2,1)S(1)} fusion(bf16[768,2304]{1,0:T(8,128)(2,1)} %param.9, bf16[128,768]{1,0:T(8,128)(2,1)} %param.7, f32[768]{0:T(1024)S(1)} %convert_element_type.65, f32[128]{0:T(128)S(1)} %add_rsqrt_fusion.2, f32[128]{0:T(128)S(1)} %broadcast_multiply_fusion.2), kind=kOutput, calls=%fused_computation.27 | convolution fusion | flops 151584768 | bytes 1576960 | tf_op jit(solution)/shard_map/dot_general | solution.py:203
  10.1 3.0 %collective-permute-start.4 = (bf16[128,768]{1,0:T(8,128)(2,1)S(1)}, bf16[128,768]{1,0:T(8,128)(2,1)S(1)}, u32[]{:S(2)}, u32[]{:S(2)}) collective-permute-start(bf16[128,768]{1,0:T(8,128)(2,1)S(1)} %fusion.14.refs_0_), channel_id=1, source_target_pairs={{0,8},{1,9},{2,10},{3,11},{4,12},{5,13},{6,14},{7,15},{8,0},{9,1},... | collective-permute-start | bytes 589832 | tf_op jit(solution)/shard_map/ppermute | solution.py:198
  13.2 0.0 collective-permute-done
  13.2 0.0 collective-permute-done.1
  13.2 2.3 %collective-permute-done.2 = bf16[128,768]{1,0:T(8,128)(2,1)S(1)} collective-permute-done((bf16[128,768]{1,0:T(8,128)(2,1)}, bf16[128,768]{1,0:T(8,128)(2,1)S(1)}, u32[]{:S(2)}, u32[]{:S(2)}) %collective-permute-start.2) | collective-permute-done | bytes 196640 | tf_op jit(solution)/shard_map/ppermute | solution.py:198
  15.6 0.1 collective-permute-start.3
  15.7 0.2 convert_reduce_fusion.1
  15.9 0.4 fusion.7
  16.2 1.7 %convolution_convert_fusion.1.refs_3_ = bf16[512,768]{1,0:T(8,128)(2,1)} fusion(bf16[768,2304]{1,0:T(8,128)(2,1)S(1)} %copy-done.7, bf16[512,768]{1,0:T(8,128)(2,1)S(1)} %constant_dynamic-update-slice_fusion, f32[768]{0:T(1024)S(1)} %convert_element_type.65, f32[512]{0:T(512)S(1)} %add_rsqrt_fusion.1, f32[512]{0:T(512)S(1)} %broadcast_multiply_fusion.1), kind=kOutput, calls=%fused_computation.16 | convolution fusion | flops 606339072 | bytes 2760704 | tf_op jit(solution)/shard_map/dot_general | solution.py:211
  18.0 1.9 %fusion.10.refs_1_ = bf16[768,512]{1,0:T(8,128)(2,1)} fusion(bf16[768,2304]{1,0:T(8,128)(2,1)S(1)} %copy-done.7, bf16[512,768]{1,0:T(8,128)(2,1)S(1)} %constant_dynamic-update-slice_fusion, f32[768]{0:T(1024)S(1)} %convert_element_type.65, f32[512]{0:T(512)S(1)} %add_rsqrt_fusion.1, f32[512]{0:T(512)S(1)} %broadcast_multiply_fusion.1), kind=kOutput, calls=%fused_computation.19 | convolution fusion | flops 606339072 | bytes 2760704 | tf_op jit(solution)/shard_map/dot_general | solution.py:208
  19.9 0.0 collective-permute-done.3
  19.9 0.2 convert_reduce_fusion
  20.1 0.4 fusion.4
  20.4 1.8 %convolution_convert_fusion.refs_4_ = bf16[512,768]{1,0:T(8,128)(2,1)} fusion(bf16[768,2304]{1,0:T(8,128)(2,1)S(1)} %copy-done.7, bf16[512,768]{1,0:T(8,128)(2,1)S(1)} %collective-permute-done.3, f32[512]{0:T(512)S(1)} %add_rsqrt_fusion, f32[512]{0:T(512)S(1)} %broadcast_multiply_fusion, f32[768]{0:T(1024)S(1)} %convert_element_type.65), kind=kOutput, calls=%fused_computation.15 | convolution fusion | flops 606339072 | bytes 2760704 | tf_op jit(solution)/shard_map/dot_general | solution.py:211
  22.2 1.9 %fusion.11.refs_2_ = bf16[768,512]{1,0:T(8,128)(2,1)} fusion(bf16[768,2304]{1,0:T(8,128)(2,1)S(1)} %copy-done.7, bf16[512,768]{1,0:T(8,128)(2,1)S(1)} %collective-permute-done.3, f32[512]{0:T(512)S(1)} %add_rsqrt_fusion, f32[512]{0:T(512)S(1)} %broadcast_multiply_fusion, f32[768]{0:T(1024)S(1)} %convert_element_type.65), kind=kOutput, calls=%fused_computation.20 | convolution fusion | flops 606339072 | bytes 2760704 | tf_op jit(solution)/shard_map/dot_general | solution.py:208
  24.1 0.0 collective-permute-done.4.refs_0_
  24.1 0.7 %copy-done.5 = bf16[128,768]{1,0:T(8,128)(2,1)} copy-done((bf16[128,768]{1,0:T(8,128)(2,1)}, bf16[128,768]{1,0:T(8,128)(2,1)S(1)}, u32[]{:S(2)}) %copy-start.5) | copy-done | bytes 196632
  24.8 7.5 %shard_map.86 = (bf16[128,768]{1,0:T(8,128)(2,1)}, f32[128,128]{1,0:T(8,128)}, f32[16,128]{1,0:T(8,128)}) custom-call(bf16[128,768]{1,0:T(8,128)(2,1)} %copy-done.5, bf16[768,512]{1,0:T(8,128)(2,1)} %fusion.10.refs_1_, bf16[768,512]{1,0:T(8,128)(2,1)} %fusion.11.refs_2_, bf16[512,768]{1,0:T(8,128)(2,1)} %convolution_convert_fusion.1.refs_3_, ...), custom_call_target="tpu_custom_call" | custom-call | flops 805306368 | bytes 3932160 | tf_op jit(solution)/shard_map/pallas_call | solution.py:183
  32.3 2.9 %collective-permute-start.6 = (bf16[128,768]{1,0:T(8,128)(2,1)}, bf16[128,768]{1,0:T(8,128)(2,1)S(1)}, u32[]{:S(2)}, u32[]{:S(2)}) collective-permute-start(bf16[128,768]{1,0:T(8,128)(2,1)} %get-tuple-element.6.refs_5_), channel_id=1, source_target_pairs={{0,8},{1,9},{2,10},{3,11},{4,12},{5,13},{6,14},{7,15},{8,0},{9,1},... | collective-permute-start | bytes 589832 | tf_op jit(solution)/shard_map/ppermute | solution.py:198
  35.2 0.3 convolution_convert_fusion.4
  35.5 0.2 reshape_reshape.7
  35.7 0.2 copy.25
  35.9 0.1 collective-permute-start.5
  36.0 7.4 %shard_map.87 = (f32[128,768]{1,0:T(8,128)}, f32[128,128]{1,0:T(8,128)}) custom-call(bf16[128,768]{1,0:T(8,128)(2,1)} %copy-done.4, bf16[768,512]{1,0:T(8,128)(2,1)} %fusion.10.refs_1_, bf16[768,512]{1,0:T(8,128)(2,1)} %fusion.11.refs_2_, bf16[512,768]{1,0:T(8,128)(2,1)} %convolution_convert_fusion.1.refs_3_, ...), custom_call_target="tpu_custom_call" | custom-call | flops 805306368 | bytes 3932160 | tf_op jit(solution)/shard_map/pallas_call | solution.py:183
  43.4 1.0 %copy.19 = f32[128,128]{0,1:T(8,128)S(1)} copy(f32[128,128]{1,0:T(8,128)} %get-tuple-element.7) | data formatting | bytes 131072 | tf_op jit(solution)/shard_map/pallas_call | solution.py:183
  44.4 1.0 %collective-permute-done.6 = bf16[128,768]{1,0:T(8,128)(2,1)S(1)} collective-permute-done((bf16[128,768]{1,0:T(8,128)(2,1)}, bf16[128,768]{1,0:T(8,128)(2,1)S(1)}, u32[]{:S(2)}, u32[]{:S(2)}) %collective-permute-start.6) | collective-permute-done | bytes 196640 | tf_op jit(solution)/shard_map/ppermute | solution.py:198
  45.5 0.5 slice.56
  46.6 0.0 collective-permute-done.5
  46.7 0.2 copy.20
  46.9 0.2 copy.21
  47.1 0.0 copy-start.3
  47.1 0.3 fusion.17
  47.5 0.8 %copy-done.3 = bf16[768,512]{1,0:T(8,128)(2,1)S(1)} copy-done((bf16[768,512]{1,0:T(8,128)(2,1)S(1)}, bf16[768,512]{1,0:T(8,128)(2,1)}, u32[]{:S(2)}) %copy-start.3) | copy-done | bytes 786456
  48.2 0.3 convolution_convert_fusion.5
  48.5 0.2 reshape_reshape.6
  48.7 0.2 copy.24
  48.9 0.1 fusion.59
  49.0 0.0 collective-permute-start.7
  49.0 1.2 %collective-permute-done.7 = bf16[2,1,16,128]{3,2,1,0:T(8,128)(2,1)S(1)} collective-permute-done((bf16[2,1,16,128]{3,2,1,0:T(8,128)(2,1)S(1)}, bf16[2,1,16,128]{3,2,1,0:T(8,128)(2,1)S(1)}, u32[]{:S(2)}, u32[]{:S(2)}) %collective-permute-start.7) | collective-permute-done | bytes 8224 | tf_op jit(solution)/shard_map/ppermute | solution.py:26
  50.1 0.1 pad_maximum_fusion
  50.3 0.0 copy-start.8
  50.3 0.0 copy-start.11
  50.3 0.1 fusion.80
  50.5 4.8 %collective-permute-start.8 = (bf16[1,34,16,128]{3,2,1,0:T(8,128)(2,1)S(1)}, bf16[1,34,16,128]{3,2,1,0:T(8,128)(2,1)S(1)}, u32[]{:S(2)}, u32[]{:S(2)}) collective-permute-start(bf16[1,34,16,128]{3,2,1,0:T(8,128)(2,1)S(1)} %get-tuple-element.10), channel_id=1, source_target_pairs={{0,2},{1,3},{2,4},{3,5},{4,6},{5,7},{6,8},{7,9},{8,10},{9,11},{10,... | collective-permute-start | bytes 417800 | tf_op jit(solution)/shard_map/ppermute | solution.py:22
  55.4 1.5 %collective-permute-start.9 = (bf16[1,34,16,128]{3,2,1,0:T(8,128)(2,1)S(1)}, bf16[1,34,16,128]{3,2,1,0:T(8,128)(2,1)S(1)}, u32[]{:S(2)}, u32[]{:S(2)}) collective-permute-start(bf16[1,34,16,128]{3,2,1,0:T(8,128)(2,1)S(1)} %get-tuple-element.11), channel_id=1, source_target_pairs={{2,0},{3,1},{4,2},{5,3},{6,4},{7,5},{8,6},{9,7},{10,8},{11,9},{12,... | collective-permute-start | bytes 417800 | tf_op jit(solution)/shard_map/ppermute | solution.py:22
  56.9 0.1 copy.27
  57.0 2.5 %convolution_select_fusion = f32[2,16,8,5,64]{4,2,3,1,0:T(8,128)S(1)} fusion(bf16[2,16,1,7,2,128]{5,3,4,1,0,2:T(8,128)(2,1)S(1)} %slice.57, bf16[2,16,1,8,5,128]{5,3,4,1,0,2:T(8,128)(2,1)S(1)} %copy.27, pred[8,5]{0,1:T(8,128)(4,1)S(1)} %copy-done.11, bf16[3,3,3,128,64]{3,4,2,1,0:T(8,128)(2,1)S(1)} %copy-done.8), kind=kOutput, calls=%fused_computation.21 | convolution fusion | flops 363216896 | bytes 1212456 | tf_op jit(solution)/shard_map/conv_general_dilated | solution.py:55
  59.5 0.1 copy.29
  59.7 0.0 collective-permute-done.8
  59.8 0.5 convolution_select_fusion.2
  60.3 0.1 copy.33
  60.4 2.3 %collective-permute-done.9 = bf16[1,34,16,128]{3,2,1,0:T(8,128)(2,1)S(1)} collective-permute-done((bf16[1,34,16,128]{3,2,1,0:T(8,128)(2,1)S(1)}, bf16[1,34,16,128]{3,2,1,0:T(8,128)(2,1)S(1)}, u32[]{:S(2)}, u32[]{:S(2)}) %collective-permute-start.9) | collective-permute-done | bytes 139296 | tf_op jit(solution)/shard_map/ppermute | solution.py:22
  62.8 0.5 convolution_select_fusion.1
  63.4 0.1 copy.37
  63.5 0.8 %fusion.37 = bf16[1,2,32,16,64]{4,3,2,1,0:T(8,128)(2,1)} fusion(f32[2,32,16,64]{3,2,1,0:T(8,128)S(1)} %slice_bitcast_fusion, f32[1,32,16,64]{3,2,1,0:T(8,128)S(1)} %get-tuple-element.16, f32[1,32,16,64]{3,2,1,0:T(8,128)S(1)} %get-tuple-element.17), kind=kLoop, calls=%fused_computation.57 | loop fusion | flops 393216 | bytes 655360 | tf_op jit(solution)/shard_map/broadcast_in_dim | solution.py:267
  (41 shorter events, 0.5 us)
Async XLA Ops:
  0.6 46.5 %copy-start = (bf16[768,768]{1,0:T(8,128)(2,1)S(1)}, bf16[768,768]{1,0:T(8,128)(2,1)}, u32[]{:S(2)}) copy-start(bf16[768,768]{1,0:T(8,128)(2,1)} %param.10) | copy-start | bytes 3538948
  0.6 12.5 %copy-start.1 = (bf16[128,768]{1,0:T(8,128)(2,1)S(1)}, bf16[128,768]{1,0:T(8,128)(2,1)}, u32[]{:S(2)}) copy-start(bf16[128,768]{1,0:T(8,128)(2,1)} %param.7) | copy-start | bytes 589828
  0.7 12.5 %collective-permute-start = (bf16[128,768]{1,0:T(8,128)(2,1)}, bf16[128,768]{1,0:T(8,128)(2,1)S(1)}, u32[]{:S(2)}, u32[]{:S(2)}) collective-permute-start(bf16[128,768]{1,0:T(8,128)(2,1)} %param.7), channel_id=1, source_target_pairs={{0,2},{1,3},{2,0},{3,1},{4,6},{5,7},{6,4},{7,5},{8,10},{9,11},{10,... | collective-permute-start | bytes 589832 | tf_op jit(solution)/shard_map/ppermute | solution.py:198
  3.7 9.5 %collective-permute-start.1 = (bf16[128,768]{1,0:T(8,128)(2,1)}, bf16[128,768]{1,0:T(8,128)(2,1)S(1)}, u32[]{:S(2)}, u32[]{:S(2)}) collective-permute-start(bf16[128,768]{1,0:T(8,128)(2,1)} %param.7), channel_id=1, source_target_pairs={{0,4},{1,5},{2,6},{3,7},{4,0},{5,1},{6,2},{7,3},{8,12},{9,13},{10,... | collective-permute-start | bytes 589832 | tf_op jit(solution)/shard_map/ppermute | solution.py:198
  5.3 10.3 %collective-permute-start.2 = (bf16[128,768]{1,0:T(8,128)(2,1)}, bf16[128,768]{1,0:T(8,128)(2,1)S(1)}, u32[]{:S(2)}, u32[]{:S(2)}) collective-permute-start(bf16[128,768]{1,0:T(8,128)(2,1)} %param.7), channel_id=1, source_target_pairs={{0,6},{1,7},{2,4},{3,5},{4,2},{5,3},{6,0},{7,1},{8,14},{9,15},{10,... | collective-permute-start | bytes 589832 | tf_op jit(solution)/shard_map/ppermute | solution.py:198
  8.2 8.0 %copy-start.7 = (bf16[768,2304]{1,0:T(8,128)(2,1)S(1)}, bf16[768,2304]{1,0:T(8,128)(2,1)}, u32[]{:S(2)}) copy-start(bf16[768,2304]{1,0:T(8,128)(2,1)} %param.9) | copy-start | bytes 10616836
  10.1 6.1 %copy-start.4 = (bf16[128,768]{1,0:T(8,128)(2,1)}, bf16[128,768]{1,0:T(8,128)(2,1)S(1)}, u32[]{:S(2)}) copy-start(bf16[128,768]{1,0:T(8,128)(2,1)S(1)} %fusion.14.refs_0_) | copy-start | bytes 589828
  10.1 14.0 %collective-permute-start.4 = (bf16[128,768]{1,0:T(8,128)(2,1)S(1)}, bf16[128,768]{1,0:T(8,128)(2,1)S(1)}, u32[]{:S(2)}, u32[]{:S(2)}) collective-permute-start(bf16[128,768]{1,0:T(8,128)(2,1)S(1)} %fusion.14.refs_0_), channel_id=1, source_target_pairs={{0,8},{1,9},{2,10},{3,11},{4,12},{5,13},{6,14},{7,15},{8,0},{9,1},... | collective-permute-start | bytes 589832 | tf_op jit(solution)/shard_map/ppermute | solution.py:198
  15.6 4.3 %collective-permute-start.3 = (bf16[512,768]{1,0:T(8,128)(2,1)S(1)}, bf16[512,768]{1,0:T(8,128)(2,1)S(1)}, u32[]{:S(2)}, u32[]{:S(2)}) collective-permute-start(bf16[512,768]{1,0:T(8,128)(2,1)S(1)} %constant_dynamic-update-slice_fusion), channel_id=1, source_target_pairs={{0,1},{1,0},{2,3},{3,2},{4,5},{5,4},{6,7},{7,6},{8,9},{9,8},{10,11... | collective-permute-start | bytes 2359304 | tf_op jit(solution)/shard_map/ppermute | solution.py:198
  24.1 11.1 %copy-start.2 = (bf16[768,512]{1,0:T(8,128)(2,1)S(1)}, bf16[768,512]{1,0:T(8,128)(2,1)}, u32[]{:S(2)}) copy-start(bf16[768,512]{1,0:T(8,128)(2,1)} %param.12) | copy-start | bytes 2359300
  24.1 0.7 %copy-start.5 = (bf16[128,768]{1,0:T(8,128)(2,1)}, bf16[128,768]{1,0:T(8,128)(2,1)S(1)}, u32[]{:S(2)}) copy-start(bf16[128,768]{1,0:T(8,128)(2,1)S(1)} %collective-permute-done.4.refs_0_) | copy-start | bytes 589828
  32.3 3.6 %copy-start.10 = (f32[16,128]{1,0:T(8,128)S(1)}, f32[16,128]{1,0:T(8,128)}, u32[]{:S(2)}) copy-start(f32[16,128]{1,0:T(8,128)} %get-tuple-element.8) | copy-start | bytes 24580
  32.3 13.2 %collective-permute-start.6 = (bf16[128,768]{1,0:T(8,128)(2,1)}, bf16[128,768]{1,0:T(8,128)(2,1)S(1)}, u32[]{:S(2)}, u32[]{:S(2)}) collective-permute-start(bf16[128,768]{1,0:T(8,128)(2,1)} %get-tuple-element.6.refs_5_), channel_id=1, source_target_pairs={{0,8},{1,9},{2,10},{3,11},{4,12},{5,13},{6,14},{7,15},{8,0},{9,1},... | collective-permute-start | bytes 589832 | tf_op jit(solution)/shard_map/ppermute | solution.py:198
  35.9 10.7 %collective-permute-start.5 = (f32[16,128]{1,0:T(8,128)S(1)}, f32[16,128]{1,0:T(8,128)S(1)}, u32[]{:S(2)}, u32[]{:S(2)}) collective-permute-start(f32[16,128]{1,0:T(8,128)S(1)} %copy-done.10), channel_id=1, source_target_pairs={{0,8},{1,9},{2,10},{3,11},{4,12},{5,13},{6,14},{7,15},{8,0},{9,1},... | collective-permute-start | bytes 24584 | tf_op jit(solution)/shard_map/ppermute | solution.py:198
  43.4 3.7 %copy-start.9 = (f32[128,768]{1,0:T(8,128)S(1)}, f32[128,768]{1,0:T(8,128)}, u32[]{:S(2)}) copy-start(f32[128,768]{1,0:T(8,128)} %get-tuple-element.9) | copy-start | bytes 1179652
  47.1 1.1 %copy-start.3 = (bf16[768,512]{1,0:T(8,128)(2,1)S(1)}, bf16[768,512]{1,0:T(8,128)(2,1)}, u32[]{:S(2)}) copy-start(bf16[768,512]{1,0:T(8,128)(2,1)} %param.11) | copy-start | bytes 2359300
  48.2 2.1 %copy-start.6 = (bf16[128,768]{1,0:T(8,128)(2,1)}, bf16[128,768]{1,0:T(8,128)(2,1)S(1)}, u32[]{:S(2)}) copy-start(bf16[128,768]{1,0:T(8,128)(2,1)S(1)} %fusion.17) | copy-start | bytes 589828
  49.0 1.2 %collective-permute-start.7 = (bf16[2,1,16,128]{3,2,1,0:T(8,128)(2,1)S(1)}, bf16[2,1,16,128]{3,2,1,0:T(8,128)(2,1)S(1)}, u32[]{:S(2)}, u32[]{:S(2)}) collective-permute-start(bf16[2,1,16,128]{3,2,1,0:T(8,128)(2,1)S(1)} %fusion.59), channel_id=1, source_target_pairs={{0,1},{1,0},{2,3},{3,2},{4,5},{5,4},{6,7},{7,6},{8,9},{9,8},{10,11... | collective-permute-start | bytes 24584 | tf_op jit(solution)/shard_map/ppermute | solution.py:26
  50.3 6.7 %copy-start.8 = (bf16[3,3,3,128,64]{3,4,2,1,0:T(8,128)(2,1)S(1)}, bf16[3,3,3,128,64]{3,4,2,1,0:T(8,128)(2,1)}, u32[]{:S(2)}) copy-start(bf16[3,3,3,128,64]{3,4,2,1,0:T(8,128)(2,1)} %param.13) | copy-start | bytes 1327108
  50.3 6.7 %copy-start.11 = (pred[8,5]{0,1:T(8,128)(4,1)S(1)}, pred[8,5]{0,1:T(8,128)(4,1)}, u32[]{:S(2)}) copy-start(pred[8,5]{0,1:T(8,128)(4,1)} %constant.51) | copy-start | bytes 124
  50.5 9.2 %collective-permute-start.8 = (bf16[1,34,16,128]{3,2,1,0:T(8,128)(2,1)S(1)}, bf16[1,34,16,128]{3,2,1,0:T(8,128)(2,1)S(1)}, u32[]{:S(2)}, u32[]{:S(2)}) collective-permute-start(bf16[1,34,16,128]{3,2,1,0:T(8,128)(2,1)S(1)} %get-tuple-element.10), channel_id=1, source_target_pairs={{0,2},{1,3},{2,4},{3,5},{4,6},{5,7},{6,8},{7,9},{8,10},{9,11},{10,... | collective-permute-start | bytes 417800 | tf_op jit(solution)/shard_map/ppermute | solution.py:22
  55.4 7.4 %collective-permute-start.9 = (bf16[1,34,16,128]{3,2,1,0:T(8,128)(2,1)S(1)}, bf16[1,34,16,128]{3,2,1,0:T(8,128)(2,1)S(1)}, u32[]{:S(2)}, u32[]{:S(2)}) collective-permute-start(bf16[1,34,16,128]{3,2,1,0:T(8,128)(2,1)S(1)} %get-tuple-element.11), channel_id=1, source_target_pairs={{2,0},{3,1},{4,2},{5,3},{6,4},{7,5},{8,6},{9,7},{10,8},{11,9},{12,... | collective-permute-start | bytes 417800 | tf_op jit(solution)/shard_map/ppermute | solution.py:22

commit v15 on v11

--- a/solution.py
+++ b/solution.py
@@ -53,13 +53,13 @@
 def convolve(extended, low_plane, high_plane, conv_kernel):
     def conv(field, kernel, x_pad):
         return lax.conv_general_dilated(
-            field[None],
-            kernel,
+            field.transpose(0, 2, 1, 3)[None],
+            kernel.transpose(0, 2, 1, 3, 4),
             window_strides=(1, 1, 1),
-            padding=((x_pad, x_pad), (0, 0), (1, 1)),
+            padding=((x_pad, x_pad), (1, 1), (0, 0)),
             dimension_numbers=("NDHWC", "DHWIO", "NDHWC"),
             preferred_element_type=jnp.float32,
-        )[0]
+        )[0].transpose(0, 2, 1, 3)
 
     interior = lax.optimization_barrier(conv(extended, conv_kernel, 1))
     rims = jnp.concatenate(

time: 63.6 us -> 63.2 us (level)
  local copies, waits for them, and re-layouts: 5.29 us -> 3.83 us
  waiting for transfers between devices: 6.4 us -> 7.61 us
  matrix products: 12.3 us -> 11.6 us
  other arithmetic: 5.24 us -> 5.93 us
    ppermute x2, waiting for transfers between devices: 1.1 us -> 2.31 us  [shifted(): return lax.ppermute(block, axis, route)]
    unnamed x31 -> x27, local copies, waits for them, and re-layouts: 2.64 us -> 1.53 us
    conv_general_dilated x3, matrix products: 4.22 us -> 3.53 us  [conv(): lax.conv_general_dilated(field.transpose(0, 2, 1, 3)[None], kernel.transp...]
    broadcast_in_dim x1, other arithmetic: 0.12 us -> 0.81 us  [body(): decoded = convolve(extended, low_plane, high_plane, conv_kernel)[None]]
  transfers between devices with their start and end apart: 10 -> 10, of which waited for: 4 -> 4; matrix products, arithmetic and copies ran while one was open for 27% -> 25% of each run, Pallas kernels for 12% -> 12%
where the time goes in v15:
time: 63.2 us; the launch traced here: 62.7 us
  starting transfers between devices  16.6 us (26%)
  Pallas kernels  15.3 us (24%)
  matrix products  11.6 us (18%)
  waiting for transfers between devices  7.61 us (12%)
  other arithmetic  5.93 us (9%)
  local copies, waits for them, and re-layouts  3.83 us (6%)
  between operations  1.79 us (3%)
    pallas_call x2, Pallas kernels, attention(): pl.pallas_call(kernel, grid=(pairs,), cost_estimate=cost, in_specs=[row_s...  15.3 us
    ppermute x7, starting transfers between devices, exchanged(): return lax.ppermute(x, 'seq', [(i, i ^ mask) for i in range(devices)])  10.8 us
    dot_general x3, matrix products, projected(): jnp.dot(normed, weight, preferred_element_type=jnp.float32)  7.22 us
    ppermute x2, starting transfers between devices, shifted(): return lax.ppermute(block, axis, route)  5.84 us
    ppermute x7, waiting for transfers between devices, exchanged(): return lax.ppermute(x, 'seq', [(i, i ^ mask) for i in range(devices)])  4.14 us
    conv_general_dilated x3, matrix products, conv(): lax.conv_general_dilated(field.transpose(0, 2, 1, 3)[None], kernel.transp...  3.53 us
    ppermute x2, waiting for transfers between devices, shifted(): return lax.ppermute(block, axis, route)  2.31 us
    reduce_sum x3, other arithmetic, layer_norm(): row_var = jnp.mean(centered * centered, axis=-1, keepdims=True)  1.84 us
  transfers between devices with their start and end apart: 10, of which 4 were waited for; matrix products, arithmetic and copies ran while one was open for 25% of the time, Pallas kernels for 12%

profile of v15, /device:TPU:0, one launch (start us, length us, event | category | flops | bytes accessed | tf_op | source)
XLA Modules:
  0.0 62.7 jit_solution(2411062740272779845)
XLA Ops:
  0.6 0.0 copy-start
  0.6 0.0 copy-start.1
  0.7 3.1 %collective-permute-start = (bf16[128,768]{1,0:T(8,128)(2,1)}, bf16[128,768]{1,0:T(8,128)(2,1)S(1)}, u32[]{:S(2)}, u32[]{:S(2)}) collective-permute-start(bf16[128,768]{1,0:T(8,128)(2,1)} %param.7), channel_id=1, source_target_pairs={{0,2},{1,3},{2,0},{3,1},{4,6},{5,7},{6,4},{7,5},{8,10},{9,11},{10,... | collective-permute-start | bytes 589832 | tf_op jit(solution)/shard_map/ppermute | solution.py:200
  3.7 1.6 %collective-permute-start.1 = (bf16[128,768]{1,0:T(8,128)(2,1)}, bf16[128,768]{1,0:T(8,128)(2,1)S(1)}, u32[]{:S(2)}, u32[]{:S(2)}) collective-permute-start(bf16[128,768]{1,0:T(8,128)(2,1)} %param.7), channel_id=1, source_target_pairs={{0,4},{1,5},{2,6},{3,7},{4,0},{5,1},{6,2},{7,3},{8,12},{9,13},{10,... | collective-permute-start | bytes 589832 | tf_op jit(solution)/shard_map/ppermute | solution.py:200
  5.3 0.0 collective-permute-start.2
  5.3 1.1 %convert_reduce_fusion.2 = f32[128]{0:T(128)S(1)} fusion(bf16[128,768]{1,0:T(8,128)(2,1)} %param.7), kind=kLoop, calls=%fused_computation.38 | loop fusion | flops 196480 | bytes 197120 | tf_op jit(solution)/shard_map/reduce_sum | solution.py:31
  6.4 0.7 %convert_element_type.55 = f32[768]{0:T(1024)S(1)} convert(bf16[768]{0:T(1024)(128)(2,1)} %param.8) | non-fusion elementwise | flops 768 | bytes 4608 | tf_op jit(solution)/shard_map/convert_element_type | solution.py:34
  7.1 1.1 %fusion.38 = f32[128]{0:T(128)S(1)} fusion(bf16[128,768]{1,0:T(8,128)(2,1)} %param.7, f32[128]{0:T(128)S(1)} %broadcast_multiply_fusion.2), kind=kLoop, calls=%fused_computation.52 | loop fusion | flops 393088 | bytes 197632 | tf_op jit(solution)/shard_map/reduce_sum | solution.py:33
  8.2 0.0 copy-start.7
  8.2 1.9 %fusion.14.refs_0_ = bf16[128,768]{1,0:T(8,128)(2,1)S(1)} fusion(bf16[768,2304]{1,0:T(8,128)(2,1)} %param.9, bf16[128,768]{1,0:T(8,128)(2,1)} %param.7, f32[768]{0:T(1024)S(1)} %convert_element_type.55, f32[128]{0:T(128)S(1)} %add_rsqrt_fusion.2, f32[128]{0:T(128)S(1)} %broadcast_multiply_fusion.2), kind=kOutput, calls=%fused_computation.25 | convolution fusion | flops 151584768 | bytes 1576960 | tf_op jit(solution)/shard_map/dot_general | solution.py:205
  10.1 3.0 %collective-permute-start.4 = (bf16[128,768]{1,0:T(8,128)(2,1)S(1)}, bf16[128,768]{1,0:T(8,128)(2,1)S(1)}, u32[]{:S(2)}, u32[]{:S(2)}) collective-permute-start(bf16[128,768]{1,0:T(8,128)(2,1)S(1)} %fusion.14.refs_0_), channel_id=1, source_target_pairs={{0,8},{1,9},{2,10},{3,11},{4,12},{5,13},{6,14},{7,15},{8,0},{9,1},... | collective-permute-start | bytes 589832 | tf_op jit(solution)/shard_map/ppermute | solution.py:200
  13.2 0.0 collective-permute-done
  13.2 0.0 collective-permute-done.1
  13.2 2.3 %collective-permute-done.2 = bf16[128,768]{1,0:T(8,128)(2,1)S(1)} collective-permute-done((bf16[128,768]{1,0:T(8,128)(2,1)}, bf16[128,768]{1,0:T(8,128)(2,1)S(1)}, u32[]{:S(2)}, u32[]{:S(2)}) %collective-permute-start.2) | collective-permute-done | bytes 196640 | tf_op jit(solution)/shard_map/ppermute | solution.py:200
  15.6 0.1 collective-permute-start.3
  15.7 0.2 convert_reduce_fusion.1
  15.9 0.4 fusion.9
  16.2 2.7 %convolution_convert_fusion.1.refs_1_.refs_3_ = bf16[512,1536]{1,0:T(8,128)(2,1)} fusion(bf16[768,2304]{1,0:T(8,128)(2,1)S(1)} %copy-done.7, bf16[512,768]{1,0:T(8,128)(2,1)S(1)} %constant_dynamic-update-slice_fusion, f32[768]{0:T(1024)S(1)} %convert_element_type.55, f32[512]{0:T(512)S(1)} %add_rsqrt_fusion.1, f32[512]{0:T(512)S(1)} %broadcast_multiply_fusion.1), kind=kOutput, calls=%fused_computation.1 | convolution fusion | flops 1210712064 | bytes 4726784 | tf_op jit(solution)/shard_map/dot_general | solution.py:205
  18.9 0.0 collective-permute-done.3
  18.9 0.2 convert_reduce_fusion
  19.1 0.4 fusion.6
  19.5 2.7 %convolution_convert_fusion.refs_2_.refs_4_ = bf16[512,1536]{1,0:T(8,128)(2,1)} fusion(bf16[768,2304]{1,0:T(8,128)(2,1)S(1)} %copy-done.7, bf16[512,768]{1,0:T(8,128)(2,1)S(1)} %collective-permute-done.3, f32[512]{0:T(512)S(1)} %add_rsqrt_fusion, f32[512]{0:T(512)S(1)} %broadcast_multiply_fusion, f32[768]{0:T(1024)S(1)} %convert_element_type.55), kind=kOutput, calls=%fused_computation | convolution fusion | flops 1210712064 | bytes 4726784 | tf_op jit(solution)/shard_map/dot_general | solution.py:205
  22.1 0.0 collective-permute-done.4.refs_0_
  22.1 0.7 %copy-done.5 = bf16[128,768]{1,0:T(8,128)(2,1)} copy-done((bf16[128,768]{1,0:T(8,128)(2,1)}, bf16[128,768]{1,0:T(8,128)(2,1)S(1)}, u32[]{:S(2)}) %copy-start.5) | copy-done | bytes 196632
  22.8 7.6 %shard_map.86 = (bf16[128,768]{1,0:T(8,128)(2,1)}, f32[128,128]{1,0:T(8,128)}, f32[16,128]{1,0:T(8,128)}) custom-call(bf16[128,768]{1,0:T(8,128)(2,1)} %copy-done.5, bf16[512,1536]{1,0:T(8,128)(2,1)} %convolution_convert_fusion.1.refs_1_.refs_3_, bf16[512,1536]{1,0:T(8,128)(2,1)} %convolution_convert_fusion.refs_2_.refs_4_, ...), custom_call_target="tpu_custom_call" | custom-call | flops 805306368 | bytes 3932160 | tf_op jit(solution)/shard_map/pallas_call | solution.py:185
  30.4 2.9 %collective-permute-start.6 = (bf16[128,768]{1,0:T(8,128)(2,1)}, bf16[128,768]{1,0:T(8,128)(2,1)S(1)}, u32[]{:S(2)}, u32[]{:S(2)}) collective-permute-start(bf16[128,768]{1,0:T(8,128)(2,1)} %get-tuple-element.6.refs_5_), channel_id=1, source_target_pairs={{0,8},{1,9},{2,10},{3,11},{4,12},{5,13},{6,14},{7,15},{8,0},{9,1},... | collective-permute-start | bytes 589832 | tf_op jit(solution)/shard_map/ppermute | solution.py:200
  33.4 0.0 copy-done.2
  33.4 0.3 convolution_convert_fusion.2
  33.7 0.2 reshape_reshape.7
  33.9 0.2 copy.19
  34.1 0.1 collective-permute-start.5
  34.2 7.6 %shard_map.87 = (f32[128,768]{1,0:T(8,128)}, f32[128,128]{1,0:T(8,128)}, f32[16,128]{1,0:T(8,128)}) custom-call(bf16[128,768]{1,0:T(8,128)(2,1)} %copy-done.4, bf16[512,1536]{1,0:T(8,128)(2,1)} %convolution_convert_fusion.1.refs_1_.refs_3_, bf16[512,1536]{1,0:T(8,128)(2,1)} %convolution_convert_fusion.refs_2_.refs_4_, ...), custom_call_target="tpu_custom_call" | custom-call | flops 805306368 | bytes 3932160 | tf_op jit(solution)/shard_map/pallas_call | solution.py:185
  41.8 1.8 %collective-permute-done.6 = bf16[128,768]{1,0:T(8,128)(2,1)S(1)} collective-permute-done((bf16[128,768]{1,0:T(8,128)(2,1)}, bf16[128,768]{1,0:T(8,128)(2,1)S(1)}, u32[]{:S(2)}, u32[]{:S(2)}) %collective-permute-start.6) | collective-permute-done | bytes 196640 | tf_op jit(solution)/shard_map/ppermute | solution.py:200
  43.6 0.5 slice.51
  44.8 0.0 collective-permute-done.5
  44.8 0.7 %fusion.66 = (f32[128,12]{0,1:T(8,128)S(1)}, f32[128,12]{0,1:T(8,128)S(1)}) fusion(f32[16,128]{1,0:T(8,128)S(1)} %collective-permute-done.5, f32[16,128]{1,0:T(8,128)} %get-tuple-element.7, f32[]{:T(128)} %bitcast.2), kind=kLoop, calls=%fused_computation.89 | loop fusion | flops 6144 | bytes 24580 | tf_op jit(solution)/shard_map/exp | solution.py:241
  45.6 0.2 copy.14
  45.8 0.2 copy.15
  45.9 0.0 copy-start.3
  46.0 0.3 fusion.17
  46.3 0.8 %copy-done.3 = bf16[768,512]{1,0:T(8,128)(2,1)S(1)} copy-done((bf16[768,512]{1,0:T(8,128)(2,1)S(1)}, bf16[768,512]{1,0:T(8,128)(2,1)}, u32[]{:S(2)}) %copy-start.3) | copy-done | bytes 786456
  47.1 0.3 convolution_convert_fusion.3
  47.3 0.2 reshape_reshape.6
  47.5 0.2 copy.18
  47.7 0.1 fusion.63
  47.8 0.0 collective-permute-start.7
  47.8 1.2 %collective-permute-done.7 = bf16[2,1,16,128]{3,2,1,0:T(8,128)(2,1)S(1)} collective-permute-done((bf16[2,1,16,128]{3,2,1,0:T(8,128)(2,1)S(1)}, bf16[2,1,16,128]{3,2,1,0:T(8,128)(2,1)S(1)}, u32[]{:S(2)}, u32[]{:S(2)}) %collective-permute-start.7) | collective-permute-done | bytes 8224 | tf_op jit(solution)/shard_map/ppermute | solution.py:26
  49.0 0.1 pad_maximum_fusion
  49.2 0.0 copy-start.8
  49.2 0.0 copy-start.11
  49.2 0.1 fusion.84
  49.4 4.4 %collective-permute-start.8 = (bf16[1,34,16,128]{3,2,1,0:T(8,128)(2,1)S(1)}, bf16[1,34,16,128]{3,2,1,0:T(8,128)(2,1)S(1)}, u32[]{:S(2)}, u32[]{:S(2)}) collective-permute-start(bf16[1,34,16,128]{3,2,1,0:T(8,128)(2,1)S(1)} %get-tuple-element.10), channel_id=1, source_target_pairs={{0,2},{1,3},{2,4},{3,5},{4,6},{5,7},{6,8},{7,9},{8,10},{9,11},{10,... | collective-permute-start | bytes 417800 | tf_op jit(solution)/shard_map/ppermute | solution.py:22
  53.7 1.5 %collective-permute-start.9 = (bf16[1,34,16,128]{3,2,1,0:T(8,128)(2,1)S(1)}, bf16[1,34,16,128]{3,2,1,0:T(8,128)(2,1)S(1)}, u32[]{:S(2)}, u32[]{:S(2)}) collective-permute-start(bf16[1,34,16,128]{3,2,1,0:T(8,128)(2,1)S(1)} %get-tuple-element.11), channel_id=1, source_target_pairs={{2,0},{3,1},{4,2},{5,3},{6,4},{7,5},{8,6},{9,7},{10,8},{11,9},{12,... | collective-permute-start | bytes 417800 | tf_op jit(solution)/shard_map/ppermute | solution.py:22
  55.3 0.1 copy.21
  55.4 0.0 copy-done.8
  55.4 2.5 %convolution_select_fusion = f32[2,16,8,5,64]{4,2,3,1,0:T(8,128)S(1)} fusion(bf16[2,16,1,7,2,128]{5,3,4,1,0,2:T(8,128)(2,1)S(1)} %slice.52, bf16[2,16,1,8,5,128]{5,3,4,1,0,2:T(8,128)(2,1)S(1)} %copy.21, pred[8,5]{0,1:T(8,128)(4,1)S(1)} %copy-done.11, bf16[3,3,3,128,64]{3,4,2,1,0:T(8,128)(2,1)S(1)} %copy-done.8), kind=kOutput, calls=%fused_computation.19 | convolution fusion | flops 363216896 | bytes 1212456 | tf_op jit(solution)/shard_map/conv_general_dilated | solution.py:55
  57.9 0.1 copy.23
  58.1 0.0 collective-permute-done.8
  58.2 0.5 convolution_select_fusion.2
  58.7 0.1 copy.27
  58.8 2.3 %collective-permute-done.9 = bf16[1,34,16,128]{3,2,1,0:T(8,128)(2,1)S(1)} collective-permute-done((bf16[1,34,16,128]{3,2,1,0:T(8,128)(2,1)S(1)}, bf16[1,34,16,128]{3,2,1,0:T(8,128)(2,1)S(1)}, u32[]{:S(2)}, u32[]{:S(2)}) %collective-permute-start.9) | collective-permute-done | bytes 139296 | tf_op jit(solution)/shard_map/ppermute | solution.py:22
  61.2 0.5 convolution_select_fusion.1
  61.7 0.1 copy.31
  61.9 0.8 %fusion.41 = bf16[1,2,32,16,64]{4,3,2,1,0:T(8,128)(2,1)} fusion(f32[2,32,16,64]{3,2,1,0:T(8,128)S(1)} %slice_bitcast_fusion, f32[1,32,16,64]{3,2,1,0:T(8,128)S(1)} %get-tuple-element.16, f32[1,32,16,64]{3,2,1,0:T(8,128)S(1)} %get-tuple-element.17), kind=kLoop, calls=%fused_computation.57 | loop fusion | flops 393216 | bytes 655360 | tf_op jit(solution)/shard_map/broadcast_in_dim | solution.py:266
  (38 shorter events, 0.5 us)
Async XLA Ops:
  0.6 45.3 %copy-start = (bf16[768,768]{1,0:T(8,128)(2,1)S(1)}, bf16[768,768]{1,0:T(8,128)(2,1)}, u32[]{:S(2)}) copy-start(bf16[768,768]{1,0:T(8,128)(2,1)} %param.10) | copy-start | bytes 3538948
  0.6 12.5 %copy-start.1 = (bf16[128,768]{1,0:T(8,128)(2,1)S(1)}, bf16[128,768]{1,0:T(8,128)(2,1)}, u32[]{:S(2)}) copy-start(bf16[128,768]{1,0:T(8,128)(2,1)} %param.7) | copy-start | bytes 589828
  0.7 12.5 %collective-permute-start = (bf16[128,768]{1,0:T(8,128)(2,1)}, bf16[128,768]{1,0:T(8,128)(2,1)S(1)}, u32[]{:S(2)}, u32[]{:S(2)}) collective-permute-start(bf16[128,768]{1,0:T(8,128)(2,1)} %param.7), channel_id=1, source_target_pairs={{0,2},{1,3},{2,0},{3,1},{4,6},{5,7},{6,4},{7,5},{8,10},{9,11},{10,... | collective-permute-start | bytes 589832 | tf_op jit(solution)/shard_map/ppermute | solution.py:200
  3.7 9.5 %collective-permute-start.1 = (bf16[128,768]{1,0:T(8,128)(2,1)}, bf16[128,768]{1,0:T(8,128)(2,1)S(1)}, u32[]{:S(2)}, u32[]{:S(2)}) collective-permute-start(bf16[128,768]{1,0:T(8,128)(2,1)} %param.7), channel_id=1, source_target_pairs={{0,4},{1,5},{2,6},{3,7},{4,0},{5,1},{6,2},{7,3},{8,12},{9,13},{10,... | collective-permute-start | bytes 589832 | tf_op jit(solution)/shard_map/ppermute | solution.py:200
  5.3 10.3 %collective-permute-start.2 = (bf16[128,768]{1,0:T(8,128)(2,1)}, bf16[128,768]{1,0:T(8,128)(2,1)S(1)}, u32[]{:S(2)}, u32[]{:S(2)}) collective-permute-start(bf16[128,768]{1,0:T(8,128)(2,1)} %param.7), channel_id=1, source_target_pairs={{0,6},{1,7},{2,4},{3,5},{4,2},{5,3},{6,0},{7,1},{8,14},{9,15},{10,... | collective-permute-start | bytes 589832 | tf_op jit(solution)/shard_map/ppermute | solution.py:200
  8.2 8.0 %copy-start.7 = (bf16[768,2304]{1,0:T(8,128)(2,1)S(1)}, bf16[768,2304]{1,0:T(8,128)(2,1)}, u32[]{:S(2)}) copy-start(bf16[768,2304]{1,0:T(8,128)(2,1)} %param.9) | copy-start | bytes 10616836
  10.1 6.1 %copy-start.4 = (bf16[128,768]{1,0:T(8,128)(2,1)}, bf16[128,768]{1,0:T(8,128)(2,1)S(1)}, u32[]{:S(2)}) copy-start(bf16[128,768]{1,0:T(8,128)(2,1)S(1)} %fusion.14.refs_0_) | copy-start | bytes 589828
  10.1 12.0 %collective-permute-start.4 = (bf16[128,768]{1,0:T(8,128)(2,1)S(1)}, bf16[128,768]{1,0:T(8,128)(2,1)S(1)}, u32[]{:S(2)}, u32[]{:S(2)}) collective-permute-start(bf16[128,768]{1,0:T(8,128)(2,1)S(1)} %fusion.14.refs_0_), channel_id=1, source_target_pairs={{0,8},{1,9},{2,10},{3,11},{4,12},{5,13},{6,14},{7,15},{8,0},{9,1},... | collective-permute-start | bytes 589832 | tf_op jit(solution)/shard_map/ppermute | solution.py:200
  15.6 3.3 %collective-permute-start.3 = (bf16[512,768]{1,0:T(8,128)(2,1)S(1)}, bf16[512,768]{1,0:T(8,128)(2,1)S(1)}, u32[]{:S(2)}, u32[]{:S(2)}) collective-permute-start(bf16[512,768]{1,0:T(8,128)(2,1)S(1)} %constant_dynamic-update-slice_fusion), channel_id=1, source_target_pairs={{0,1},{1,0},{2,3},{3,2},{4,5},{5,4},{6,7},{7,6},{8,9},{9,8},{10,11... | collective-permute-start | bytes 2359304 | tf_op jit(solution)/shard_map/ppermute | solution.py:200
  22.1 11.2 %copy-start.2 = (bf16[768,512]{1,0:T(8,128)(2,1)S(1)}, bf16[768,512]{1,0:T(8,128)(2,1)}, u32[]{:S(2)}) copy-start(bf16[768,512]{1,0:T(8,128)(2,1)} %param.12) | copy-start | bytes 2359300
  22.1 0.7 %copy-start.5 = (bf16[128,768]{1,0:T(8,128)(2,1)}, bf16[128,768]{1,0:T(8,128)(2,1)S(1)}, u32[]{:S(2)}) copy-start(bf16[128,768]{1,0:T(8,128)(2,1)S(1)} %collective-permute-done.4.refs_0_) | copy-start | bytes 589828
  30.4 3.6 %copy-start.10 = (f32[16,128]{1,0:T(8,128)S(1)}, f32[16,128]{1,0:T(8,128)}, u32[]{:S(2)}) copy-start(f32[16,128]{1,0:T(8,128)} %get-tuple-element.8) | copy-start | bytes 24580
  30.4 13.2 %collective-permute-start.6 = (bf16[128,768]{1,0:T(8,128)(2,1)}, bf16[128,768]{1,0:T(8,128)(2,1)S(1)}, u32[]{:S(2)}, u32[]{:S(2)}) collective-permute-start(bf16[128,768]{1,0:T(8,128)(2,1)} %get-tuple-element.6.refs_5_), channel_id=1, source_target_pairs={{0,8},{1,9},{2,10},{3,11},{4,12},{5,13},{6,14},{7,15},{8,0},{9,1},... | collective-permute-start | bytes 589832 | tf_op jit(solution)/shard_map/ppermute | solution.py:200
  34.1 10.7 %collective-permute-start.5 = (f32[16,128]{1,0:T(8,128)S(1)}, f32[16,128]{1,0:T(8,128)S(1)}, u32[]{:S(2)}, u32[]{:S(2)}) collective-permute-start(f32[16,128]{1,0:T(8,128)S(1)} %copy-done.10), channel_id=1, source_target_pairs={{0,8},{1,9},{2,10},{3,11},{4,12},{5,13},{6,14},{7,15},{8,0},{9,1},... | collective-permute-start | bytes 24584 | tf_op jit(solution)/shard_map/ppermute | solution.py:200
  41.8 4.1 %copy-start.9 = (f32[128,768]{1,0:T(8,128)S(1)}, f32[128,768]{1,0:T(8,128)}, u32[]{:S(2)}) copy-start(f32[128,768]{1,0:T(8,128)} %get-tuple-element.9) | copy-start | bytes 1179652
  45.9 1.1 %copy-start.3 = (bf16[768,512]{1,0:T(8,128)(2,1)S(1)}, bf16[768,512]{1,0:T(8,128)(2,1)}, u32[]{:S(2)}) copy-start(bf16[768,512]{1,0:T(8,128)(2,1)} %param.11) | copy-start | bytes 2359300
  47.1 2.1 %copy-start.6 = (bf16[128,768]{1,0:T(8,128)(2,1)}, bf16[128,768]{1,0:T(8,128)(2,1)S(1)}, u32[]{:S(2)}) copy-start(bf16[128,768]{1,0:T(8,128)(2,1)S(1)} %fusion.17) | copy-start | bytes 589828
  47.8 1.2 %collective-permute-start.7 = (bf16[2,1,16,128]{3,2,1,0:T(8,128)(2,1)S(1)}, bf16[2,1,16,128]{3,2,1,0:T(8,128)(2,1)S(1)}, u32[]{:S(2)}, u32[]{:S(2)}) collective-permute-start(bf16[2,1,16,128]{3,2,1,0:T(8,128)(2,1)S(1)} %fusion.63), channel_id=1, source_target_pairs={{0,1},{1,0},{2,3},{3,2},{4,5},{5,4},{6,7},{7,6},{8,9},{9,8},{10,11... | collective-permute-start | bytes 24584 | tf_op jit(solution)/shard_map/ppermute | solution.py:26
  49.2 6.2 %copy-start.8 = (bf16[3,3,3,128,64]{3,4,2,1,0:T(8,128)(2,1)S(1)}, bf16[3,3,3,128,64]{3,4,2,1,0:T(8,128)(2,1)}, u32[]{:S(2)}) copy-start(bf16[3,3,3,128,64]{3,4,2,1,0:T(8,128)(2,1)} %param.13) | copy-start | bytes 1327108
  49.2 6.2 %copy-start.11 = (pred[8,5]{0,1:T(8,128)(4,1)S(1)}, pred[8,5]{0,1:T(8,128)(4,1)}, u32[]{:S(2)}) copy-start(pred[8,5]{0,1:T(8,128)(4,1)} %constant.51) | copy-start | bytes 124
  49.4 8.7 %collective-permute-start.8 = (bf16[1,34,16,128]{3,2,1,0:T(8,128)(2,1)S(1)}, bf16[1,34,16,128]{3,2,1,0:T(8,128)(2,1)S(1)}, u32[]{:S(2)}, u32[]{:S(2)}) collective-permute-start(bf16[1,34,16,128]{3,2,1,0:T(8,128)(2,1)S(1)} %get-tuple-element.10), channel_id=1, source_target_pairs={{0,2},{1,3},{2,4},{3,5},{4,6},{5,7},{6,8},{7,9},{8,10},{9,11},{10,... | collective-permute-start | bytes 417800 | tf_op jit(solution)/shard_map/ppermute | solution.py:22
  53.7 7.4 %collective-permute-start.9 = (bf16[1,34,16,128]{3,2,1,0:T(8,128)(2,1)S(1)}, bf16[1,34,16,128]{3,2,1,0:T(8,128)(2,1)S(1)}, u32[]{:S(2)}, u32[]{:S(2)}) collective-permute-start(bf16[1,34,16,128]{3,2,1,0:T(8,128)(2,1)S(1)} %get-tuple-element.11), channel_id=1, source_target_pairs={{2,0},{3,1},{4,2},{5,3},{6,4},{7,5},{8,6},{9,7},{10,8},{11,9},{12,... | collective-permute-start | bytes 417800 | tf_op jit(solution)/shard_map/ppermute | solution.py:22

commit v16 on v13

--- a/solution.py
+++ b/solution.py
@@ -226,7 +226,7 @@
     sent_lse = with_layout_constraint(remote_lse, row_major)
     other_lse = with_layout_constraint(exchanged(sent_lse, half), row_major)[:heads].T
     own_out, own_lse = attention(
-        queries, kv_chunks, head_size, score_scale, jnp.float32, False, after=remote_out
+        queries, kv_chunks, head_size, score_scale, jnp.float32, False
     )
     own_lse = own_lse[:, :heads]
     top = jnp.maximum(own_lse, other_lse) + 0 * other_out[:1, :1].astype(jnp.float32)

time: 63.1 us -> 63.1 us (level)
  no operation moved by 1% of the time
where the time goes in v16:
time: 63.1 us; the launch traced here: 62.6 us
  starting transfers between devices  17.2 us (27%)
  Pallas kernels  15.2 us (24%)
  matrix products  11.6 us (18%)
  waiting for transfers between devices  6.73 us (11%)
  other arithmetic  5.23 us (8%)
  local copies, waits for them, and re-layouts  4.81 us (8%)
  between operations  1.8 us (3%)
    pallas_call x2, Pallas kernels, attention(): pl.pallas_call(kernel, grid=(pairs,), cost_estimate=cost, in_specs=[row_s...  15.2 us
    ppermute x7, starting transfers between devices, exchanged(): return lax.ppermute(x, 'seq', [(i, i ^ mask) for i in range(devices)])  10.8 us
    dot_general x3, matrix products, projected(): jnp.dot(normed, weight, preferred_element_type=jnp.float32)  7.22 us
    ppermute x2, starting transfers between devices, shifted(): return lax.ppermute(block, axis, route)  6.44 us
    conv_general_dilated x3, matrix products, conv(): lax.conv_general_dilated(field.transpose(0, 2, 1, 3)[None], kernel.transp...  3.53 us
    ppermute x7, waiting for transfers between devices, exchanged(): return lax.ppermute(x, 'seq', [(i, i ^ mask) for i in range(devices)])  3.26 us
    ppermute x2, waiting for transfers between devices, shifted(): return lax.ppermute(block, axis, route)  2.31 us
    reduce_sum x3, other arithmetic, layer_norm(): row_var = jnp.mean(centered * centered, axis=-1, keepdims=True)  1.84 us
  transfers between devices with their start and end apart: 10, of which 4 were waited for; matrix products, arithmetic and copies ran while one was open for 27% of the time, Pallas kernels for 12%

profile of v16, /device:TPU:0, one launch (start us, length us, event | category | flops | bytes accessed | tf_op | source)
XLA Modules:
  0.0 62.6 jit_solution(10130027121394425370)
XLA Ops:
  0.6 0.0 copy-start
  0.6 0.0 copy-start.1
  0.7 3.1 %collective-permute-start = (bf16[128,768]{1,0:T(8,128)(2,1)}, bf16[128,768]{1,0:T(8,128)(2,1)S(1)}, u32[]{:S(2)}, u32[]{:S(2)}) collective-permute-start(bf16[128,768]{1,0:T(8,128)(2,1)} %param.7), channel_id=1, source_target_pairs={{0,2},{1,3},{2,0},{3,1},{4,6},{5,7},{6,4},{7,5},{8,10},{9,11},{10,... | collective-permute-start | bytes 589832 | tf_op jit(solution)/shard_map/ppermute | solution.py:200
  3.7 1.6 %collective-permute-start.1 = (bf16[128,768]{1,0:T(8,128)(2,1)}, bf16[128,768]{1,0:T(8,128)(2,1)S(1)}, u32[]{:S(2)}, u32[]{:S(2)}) collective-permute-start(bf16[128,768]{1,0:T(8,128)(2,1)} %param.7), channel_id=1, source_target_pairs={{0,4},{1,5},{2,6},{3,7},{4,0},{5,1},{6,2},{7,3},{8,12},{9,13},{10,... | collective-permute-start | bytes 589832 | tf_op jit(solution)/shard_map/ppermute | solution.py:200
  5.3 0.0 collective-permute-start.2
  5.3 1.1 %convert_reduce_fusion.2 = f32[128]{0:T(128)S(1)} fusion(bf16[128,768]{1,0:T(8,128)(2,1)} %param.7), kind=kLoop, calls=%fused_computation.38 | loop fusion | flops 196480 | bytes 197120 | tf_op jit(solution)/shard_map/reduce_sum | solution.py:31
  6.4 0.7 %convert_element_type.55 = f32[768]{0:T(1024)S(1)} convert(bf16[768]{0:T(1024)(128)(2,1)} %param.8) | non-fusion elementwise | flops 768 | bytes 4608 | tf_op jit(solution)/shard_map/convert_element_type | solution.py:34
  7.1 1.1 %fusion.38 = f32[128]{0:T(128)S(1)} fusion(bf16[128,768]{1,0:T(8,128)(2,1)} %param.7, f32[128]{0:T(128)S(1)} %broadcast_multiply_fusion.2), kind=kLoop, calls=%fused_computation.52 | loop fusion | flops 393088 | bytes 197632 | tf_op jit(solution)/shard_map/reduce_sum | solution.py:33
  8.2 0.0 copy-start.7
  8.2 1.9 %fusion.14.refs_0_ = bf16[128,768]{1,0:T(8,128)(2,1)S(1)} fusion(bf16[768,2304]{1,0:T(8,128)(2,1)} %param.9, bf16[128,768]{1,0:T(8,128)(2,1)} %param.7, f32[768]{0:T(1024)S(1)} %convert_element_type.55, f32[128]{0:T(128)S(1)} %add_rsqrt_fusion.2, f32[128]{0:T(128)S(1)} %broadcast_multiply_fusion.2), kind=kOutput, calls=%fused_computation.25 | convolution fusion | flops 151584768 | bytes 1576960 | tf_op jit(solution)/shard_map/dot_general | solution.py:205
  10.1 3.0 %collective-permute-start.4 = (bf16[128,768]{1,0:T(8,128)(2,1)S(1)}, bf16[128,768]{1,0:T(8,128)(2,1)S(1)}, u32[]{:S(2)}, u32[]{:S(2)}) collective-permute-start(bf16[128,768]{1,0:T(8,128)(2,1)S(1)} %fusion.14.refs_0_), channel_id=1, source_target_pairs={{0,8},{1,9},{2,10},{3,11},{4,12},{5,13},{6,14},{7,15},{8,0},{9,1},... | collective-permute-start | bytes 589832 | tf_op jit(solution)/shard_map/ppermute | solution.py:200
  13.2 0.0 collective-permute-done
  13.2 0.0 collective-permute-done.1
  13.2 2.3 %collective-permute-done.2 = bf16[128,768]{1,0:T(8,128)(2,1)S(1)} collective-permute-done((bf16[128,768]{1,0:T(8,128)(2,1)}, bf16[128,768]{1,0:T(8,128)(2,1)S(1)}, u32[]{:S(2)}, u32[]{:S(2)}) %collective-permute-start.2) | collective-permute-done | bytes 196640 | tf_op jit(solution)/shard_map/ppermute | solution.py:200
  15.6 0.1 collective-permute-start.3
  15.7 0.2 convert_reduce_fusion.1
  15.9 0.4 fusion.9
  16.2 0.0 copy-done.4
  16.2 0.0 copy-done.7
  16.2 2.7 %convolution_convert_fusion.1.refs_1_.refs_3_ = bf16[512,1536]{1,0:T(8,128)(2,1)} fusion(bf16[768,2304]{1,0:T(8,128)(2,1)S(1)} %copy-done.7, bf16[512,768]{1,0:T(8,128)(2,1)S(1)} %constant_dynamic-update-slice_fusion, f32[768]{0:T(1024)S(1)} %convert_element_type.55, f32[512]{0:T(512)S(1)} %add_rsqrt_fusion.1, f32[512]{0:T(512)S(1)} %broadcast_multiply_fusion.1), kind=kOutput, calls=%fused_computation.1 | convolution fusion | flops 1210712064 | bytes 4726784 | tf_op jit(solution)/shard_map/dot_general | solution.py:205
  18.9 0.0 collective-permute-done.3
  18.9 0.2 convert_reduce_fusion
  19.1 0.4 fusion.6
  19.5 2.7 %convolution_convert_fusion.refs_2_.refs_4_ = bf16[512,1536]{1,0:T(8,128)(2,1)} fusion(bf16[768,2304]{1,0:T(8,128)(2,1)S(1)} %copy-done.7, bf16[512,768]{1,0:T(8,128)(2,1)S(1)} %collective-permute-done.3, f32[512]{0:T(512)S(1)} %add_rsqrt_fusion, f32[512]{0:T(512)S(1)} %broadcast_multiply_fusion, f32[768]{0:T(1024)S(1)} %convert_element_type.55), kind=kOutput, calls=%fused_computation | convolution fusion | flops 1210712064 | bytes 4726784 | tf_op jit(solution)/shard_map/dot_general | solution.py:205
  22.1 0.0 collective-permute-done.4.refs_0_
  22.1 0.7 %copy-done.5 = bf16[128,768]{1,0:T(8,128)(2,1)} copy-done((bf16[128,768]{1,0:T(8,128)(2,1)}, bf16[128,768]{1,0:T(8,128)(2,1)S(1)}, u32[]{:S(2)}) %copy-start.5) | copy-done | bytes 196632
  22.8 7.6 %shard_map.87 = (bf16[128,768]{1,0:T(8,128)(2,1)}, f32[128,128]{1,0:T(8,128)}, f32[16,128]{1,0:T(8,128)}) custom-call(bf16[128,768]{1,0:T(8,128)(2,1)} %copy-done.5, bf16[512,1536]{1,0:T(8,128)(2,1)} %convolution_convert_fusion.1.refs_1_.refs_3_, bf16[512,1536]{1,0:T(8,128)(2,1)} %convolution_convert_fusion.refs_2_.refs_4_, ...), custom_call_target="tpu_custom_call" | custom-call | flops 805306368 | bytes 3932160 | tf_op jit(solution)/shard_map/pallas_call | solution.py:185
  30.4 2.9 %collective-permute-start.6 = (bf16[128,768]{1,0:T(8,128)(2,1)}, bf16[128,768]{1,0:T(8,128)(2,1)S(1)}, u32[]{:S(2)}, u32[]{:S(2)}) collective-permute-start(bf16[128,768]{1,0:T(8,128)(2,1)} %get-tuple-element.8), channel_id=1, source_target_pairs={{0,8},{1,9},{2,10},{3,11},{4,12},{5,13},{6,14},{7,15},{8,0},{9,1},... | collective-permute-start | bytes 589832 | tf_op jit(solution)/shard_map/ppermute | solution.py:200
  33.4 0.3 convolution_convert_fusion.2
  33.7 0.2 reshape_reshape.7
  33.9 0.2 copy.21
  34.1 0.1 collective-permute-start.5
  34.2 7.5 %shard_map.86 = (f32[128,768]{1,0:T(8,128)}, f32[128,128]{1,0:T(8,128)}) custom-call(bf16[128,768]{1,0:T(8,128)(2,1)} %copy-done.4, bf16[512,1536]{1,0:T(8,128)(2,1)} %convolution_convert_fusion.1.refs_1_.refs_3_, bf16[512,1536]{1,0:T(8,128)(2,1)} %convolution_convert_fusion.refs_2_.refs_4_, bf16[512,1536]{1,0:T(8,128)(2,1)} %convolution_convert_fusion.1.refs_1_.refs_3_, ...), custom_call_target="tpu_custom_call" | custom-call | flops 805306368 | bytes 3932160 | tf_op jit(solution)/shard_map/pallas_call | solution.py:185
  41.7 1.0 %copy.15 = f32[128,128]{0,1:T(8,128)S(1)} copy(f32[128,128]{1,0:T(8,128)} %get-tuple-element.6) | data formatting | bytes 131072 | tf_op jit(solution)/shard_map/pallas_call | solution.py:185
  42.7 0.9 %collective-permute-done.6 = bf16[128,768]{1,0:T(8,128)(2,1)S(1)} collective-permute-done((bf16[128,768]{1,0:T(8,128)(2,1)}, bf16[128,768]{1,0:T(8,128)(2,1)S(1)}, u32[]{:S(2)}, u32[]{:S(2)}) %collective-permute-start.6) | collective-permute-done | bytes 196640 | tf_op jit(solution)/shard_map/ppermute | solution.py:200
  43.6 0.5 slice.52
  44.8 0.0 collective-permute-done.5
  44.9 0.2 copy.16
  45.1 0.2 copy.17
  45.2 0.0 copy-start.3
  45.3 0.3 fusion.17
  45.6 0.8 %copy-done.3 = bf16[768,512]{1,0:T(8,128)(2,1)S(1)} copy-done((bf16[768,512]{1,0:T(8,128)(2,1)S(1)}, bf16[768,512]{1,0:T(8,128)(2,1)}, u32[]{:S(2)}) %copy-start.3) | copy-done | bytes 786456
  46.4 0.3 convolution_convert_fusion.3
  46.6 0.2 reshape_reshape.6
  46.8 0.2 copy.20
  47.0 0.1 fusion.63
  47.1 0.0 collective-permute-start.7
  47.1 1.2 %collective-permute-done.7 = bf16[2,1,16,128]{3,2,1,0:T(8,128)(2,1)S(1)} collective-permute-done((bf16[2,1,16,128]{3,2,1,0:T(8,128)(2,1)S(1)}, bf16[2,1,16,128]{3,2,1,0:T(8,128)(2,1)S(1)}, u32[]{:S(2)}, u32[]{:S(2)}) %collective-permute-start.7) | collective-permute-done | bytes 8224 | tf_op jit(solution)/shard_map/ppermute | solution.py:26
  48.3 0.1 pad_maximum_fusion
  48.5 0.0 copy-start.8
  48.5 0.0 copy-start.11
  48.5 0.1 fusion.80
  48.7 5.0 %collective-permute-start.8 = (bf16[1,34,16,128]{3,2,1,0:T(8,128)(2,1)S(1)}, bf16[1,34,16,128]{3,2,1,0:T(8,128)(2,1)S(1)}, u32[]{:S(2)}, u32[]{:S(2)}) collective-permute-start(bf16[1,34,16,128]{3,2,1,0:T(8,128)(2,1)S(1)} %get-tuple-element.10), channel_id=1, source_target_pairs={{0,2},{1,3},{2,4},{3,5},{4,6},{5,7},{6,8},{7,9},{8,10},{9,11},{10,... | collective-permute-start | bytes 417800 | tf_op jit(solution)/shard_map/ppermute | solution.py:22
  53.6 1.5 %collective-permute-start.9 = (bf16[1,34,16,128]{3,2,1,0:T(8,128)(2,1)S(1)}, bf16[1,34,16,128]{3,2,1,0:T(8,128)(2,1)S(1)}, u32[]{:S(2)}, u32[]{:S(2)}) collective-permute-start(bf16[1,34,16,128]{3,2,1,0:T(8,128)(2,1)S(1)} %get-tuple-element.11), channel_id=1, source_target_pairs={{2,0},{3,1},{4,2},{5,3},{6,4},{7,5},{8,6},{9,7},{10,8},{11,9},{12,... | collective-permute-start | bytes 417800 | tf_op jit(solution)/shard_map/ppermute | solution.py:22
  55.2 0.1 copy.23
  55.3 2.5 %convolution_select_fusion = f32[2,16,8,5,64]{4,2,3,1,0:T(8,128)S(1)} fusion(bf16[2,16,1,7,2,128]{5,3,4,1,0,2:T(8,128)(2,1)S(1)} %slice.53, bf16[2,16,1,8,5,128]{5,3,4,1,0,2:T(8,128)(2,1)S(1)} %copy.23, pred[8,5]{0,1:T(8,128)(4,1)S(1)} %copy-done.11, bf16[3,3,3,128,64]{3,4,2,1,0:T(8,128)(2,1)S(1)} %copy-done.8), kind=kOutput, calls=%fused_computation.19 | convolution fusion | flops 363216896 | bytes 1212456 | tf_op jit(solution)/shard_map/conv_general_dilated | solution.py:55
  57.8 0.1 copy.25
  58.0 0.0 collective-permute-done.8
  58.1 0.5 convolution_select_fusion.2
  58.6 0.1 copy.29
  58.7 2.3 %collective-permute-done.9 = bf16[1,34,16,128]{3,2,1,0:T(8,128)(2,1)S(1)} collective-permute-done((bf16[1,34,16,128]{3,2,1,0:T(8,128)(2,1)S(1)}, bf16[1,34,16,128]{3,2,1,0:T(8,128)(2,1)S(1)}, u32[]{:S(2)}, u32[]{:S(2)}) %collective-permute-start.9) | collective-permute-done | bytes 139296 | tf_op jit(solution)/shard_map/ppermute | solution.py:22
  61.1 0.5 convolution_select_fusion.1
  61.6 0.1 copy.33
  61.8 0.8 %fusion.41 = bf16[1,2,32,16,64]{4,3,2,1,0:T(8,128)(2,1)} fusion(f32[2,32,16,64]{3,2,1,0:T(8,128)S(1)} %slice_bitcast_fusion, f32[1,32,16,64]{3,2,1,0:T(8,128)S(1)} %get-tuple-element.16, f32[1,32,16,64]{3,2,1,0:T(8,128)S(1)} %get-tuple-element.17), kind=kLoop, calls=%fused_computation.57 | loop fusion | flops 393216 | bytes 655360 | tf_op jit(solution)/shard_map/broadcast_in_dim | solution.py:259
  (39 shorter events, 0.5 us)
Async XLA Ops:
  0.6 44.6 %copy-start = (bf16[768,768]{1,0:T(8,128)(2,1)S(1)}, bf16[768,768]{1,0:T(8,128)(2,1)}, u32[]{:S(2)}) copy-start(bf16[768,768]{1,0:T(8,128)(2,1)} %param.10) | copy-start | bytes 3538948
  0.6 12.5 %copy-start.1 = (bf16[128,768]{1,0:T(8,128)(2,1)S(1)}, bf16[128,768]{1,0:T(8,128)(2,1)}, u32[]{:S(2)}) copy-start(bf16[128,768]{1,0:T(8,128)(2,1)} %param.7) | copy-start | bytes 589828
  0.7 12.5 %collective-permute-start = (bf16[128,768]{1,0:T(8,128)(2,1)}, bf16[128,768]{1,0:T(8,128)(2,1)S(1)}, u32[]{:S(2)}, u32[]{:S(2)}) collective-permute-start(bf16[128,768]{1,0:T(8,128)(2,1)} %param.7), channel_id=1, source_target_pairs={{0,2},{1,3},{2,0},{3,1},{4,6},{5,7},{6,4},{7,5},{8,10},{9,11},{10,... | collective-permute-start | bytes 589832 | tf_op jit(solution)/shard_map/ppermute | solution.py:200
  3.7 9.5 %collective-permute-start.1 = (bf16[128,768]{1,0:T(8,128)(2,1)}, bf16[128,768]{1,0:T(8,128)(2,1)S(1)}, u32[]{:S(2)}, u32[]{:S(2)}) collective-permute-start(bf16[128,768]{1,0:T(8,128)(2,1)} %param.7), channel_id=1, source_target_pairs={{0,4},{1,5},{2,6},{3,7},{4,0},{5,1},{6,2},{7,3},{8,12},{9,13},{10,... | collective-permute-start | bytes 589832 | tf_op jit(solution)/shard_map/ppermute | solution.py:200
  5.3 10.3 %collective-permute-start.2 = (bf16[128,768]{1,0:T(8,128)(2,1)}, bf16[128,768]{1,0:T(8,128)(2,1)S(1)}, u32[]{:S(2)}, u32[]{:S(2)}) collective-permute-start(bf16[128,768]{1,0:T(8,128)(2,1)} %param.7), channel_id=1, source_target_pairs={{0,6},{1,7},{2,4},{3,5},{4,2},{5,3},{6,0},{7,1},{8,14},{9,15},{10,... | collective-permute-start | bytes 589832 | tf_op jit(solution)/shard_map/ppermute | solution.py:200
  8.2 8.0 %copy-start.7 = (bf16[768,2304]{1,0:T(8,128)(2,1)S(1)}, bf16[768,2304]{1,0:T(8,128)(2,1)}, u32[]{:S(2)}) copy-start(bf16[768,2304]{1,0:T(8,128)(2,1)} %param.9) | copy-start | bytes 10616836
  10.1 6.1 %copy-start.4 = (bf16[128,768]{1,0:T(8,128)(2,1)}, bf16[128,768]{1,0:T(8,128)(2,1)S(1)}, u32[]{:S(2)}) copy-start(bf16[128,768]{1,0:T(8,128)(2,1)S(1)} %fusion.14.refs_0_) | copy-start | bytes 589828
  10.1 12.0 %collective-permute-start.4 = (bf16[128,768]{1,0:T(8,128)(2,1)S(1)}, bf16[128,768]{1,0:T(8,128)(2,1)S(1)}, u32[]{:S(2)}, u32[]{:S(2)}) collective-permute-start(bf16[128,768]{1,0:T(8,128)(2,1)S(1)} %fusion.14.refs_0_), channel_id=1, source_target_pairs={{0,8},{1,9},{2,10},{3,11},{4,12},{5,13},{6,14},{7,15},{8,0},{9,1},... | collective-permute-start | bytes 589832 | tf_op jit(solution)/shard_map/ppermute | solution.py:200
  15.6 3.3 %collective-permute-start.3 = (bf16[512,768]{1,0:T(8,128)(2,1)S(1)}, bf16[512,768]{1,0:T(8,128)(2,1)S(1)}, u32[]{:S(2)}, u32[]{:S(2)}) collective-permute-start(bf16[512,768]{1,0:T(8,128)(2,1)S(1)} %constant_dynamic-update-slice_fusion), channel_id=1, source_target_pairs={{0,1},{1,0},{2,3},{3,2},{4,5},{5,4},{6,7},{7,6},{8,9},{9,8},{10,11... | collective-permute-start | bytes 2359304 | tf_op jit(solution)/shard_map/ppermute | solution.py:200
  22.1 11.2 %copy-start.2 = (bf16[768,512]{1,0:T(8,128)(2,1)S(1)}, bf16[768,512]{1,0:T(8,128)(2,1)}, u32[]{:S(2)}) copy-start(bf16[768,512]{1,0:T(8,128)(2,1)} %param.12) | copy-start | bytes 2359300
  22.1 0.7 %copy-start.5 = (bf16[128,768]{1,0:T(8,128)(2,1)}, bf16[128,768]{1,0:T(8,128)(2,1)S(1)}, u32[]{:S(2)}) copy-start(bf16[128,768]{1,0:T(8,128)(2,1)S(1)} %collective-permute-done.4.refs_0_) | copy-start | bytes 589828
  30.4 3.6 %copy-start.10 = (f32[16,128]{1,0:T(8,128)S(1)}, f32[16,128]{1,0:T(8,128)}, u32[]{:S(2)}) copy-start(f32[16,128]{1,0:T(8,128)} %get-tuple-element.7) | copy-start | bytes 24580
  30.4 13.2 %collective-permute-start.6 = (bf16[128,768]{1,0:T(8,128)(2,1)}, bf16[128,768]{1,0:T(8,128)(2,1)S(1)}, u32[]{:S(2)}, u32[]{:S(2)}) collective-permute-start(bf16[128,768]{1,0:T(8,128)(2,1)} %get-tuple-element.8), channel_id=1, source_target_pairs={{0,8},{1,9},{2,10},{3,11},{4,12},{5,13},{6,14},{7,15},{8,0},{9,1},... | collective-permute-start | bytes 589832 | tf_op jit(solution)/shard_map/ppermute | solution.py:200
  34.1 10.7 %collective-permute-start.5 = (f32[16,128]{1,0:T(8,128)S(1)}, f32[16,128]{1,0:T(8,128)S(1)}, u32[]{:S(2)}, u32[]{:S(2)}) collective-permute-start(f32[16,128]{1,0:T(8,128)S(1)} %copy-done.10), channel_id=1, source_target_pairs={{0,8},{1,9},{2,10},{3,11},{4,12},{5,13},{6,14},{7,15},{8,0},{9,1},... | collective-permute-start | bytes 24584 | tf_op jit(solution)/shard_map/ppermute | solution.py:200
  41.7 3.5 %copy-start.9 = (f32[128,768]{1,0:T(8,128)S(1)}, f32[128,768]{1,0:T(8,128)}, u32[]{:S(2)}) copy-start(f32[128,768]{1,0:T(8,128)} %get-tuple-element.9) | copy-start | bytes 1179652
  45.2 1.1 %copy-start.3 = (bf16[768,512]{1,0:T(8,128)(2,1)S(1)}, bf16[768,512]{1,0:T(8,128)(2,1)}, u32[]{:S(2)}) copy-start(bf16[768,512]{1,0:T(8,128)(2,1)} %param.11) | copy-start | bytes 2359300
  46.4 2.1 %copy-start.6 = (bf16[128,768]{1,0:T(8,128)(2,1)}, bf16[128,768]{1,0:T(8,128)(2,1)S(1)}, u32[]{:S(2)}) copy-start(bf16[128,768]{1,0:T(8,128)(2,1)S(1)} %fusion.17) | copy-start | bytes 589828
  47.1 1.2 %collective-permute-start.7 = (bf16[2,1,16,128]{3,2,1,0:T(8,128)(2,1)S(1)}, bf16[2,1,16,128]{3,2,1,0:T(8,128)(2,1)S(1)}, u32[]{:S(2)}, u32[]{:S(2)}) collective-permute-start(bf16[2,1,16,128]{3,2,1,0:T(8,128)(2,1)S(1)} %fusion.63), channel_id=1, source_target_pairs={{0,1},{1,0},{2,3},{3,2},{4,5},{5,4},{6,7},{7,6},{8,9},{9,8},{10,11... | collective-permute-start | bytes 24584 | tf_op jit(solution)/shard_map/ppermute | solution.py:26
  48.5 6.8 %copy-start.8 = (bf16[3,3,3,128,64]{3,4,2,1,0:T(8,128)(2,1)S(1)}, bf16[3,3,3,128,64]{3,4,2,1,0:T(8,128)(2,1)}, u32[]{:S(2)}) copy-start(bf16[3,3,3,128,64]{3,4,2,1,0:T(8,128)(2,1)} %param.13) | copy-start | bytes 1327108
  48.5 6.8 %copy-start.11 = (pred[8,5]{0,1:T(8,128)(4,1)S(1)}, pred[8,5]{0,1:T(8,128)(4,1)}, u32[]{:S(2)}) copy-start(pred[8,5]{0,1:T(8,128)(4,1)} %constant.51) | copy-start | bytes 124
  48.7 9.3 %collective-permute-start.8 = (bf16[1,34,16,128]{3,2,1,0:T(8,128)(2,1)S(1)}, bf16[1,34,16,128]{3,2,1,0:T(8,128)(2,1)S(1)}, u32[]{:S(2)}, u32[]{:S(2)}) collective-permute-start(bf16[1,34,16,128]{3,2,1,0:T(8,128)(2,1)S(1)} %get-tuple-element.10), channel_id=1, source_target_pairs={{0,2},{1,3},{2,4},{3,5},{4,6},{5,7},{6,8},{7,9},{8,10},{9,11},{10,... | collective-permute-start | bytes 417800 | tf_op jit(solution)/shard_map/ppermute | solution.py:22
  53.6 7.4 %collective-permute-start.9 = (bf16[1,34,16,128]{3,2,1,0:T(8,128)(2,1)S(1)}, bf16[1,34,16,128]{3,2,1,0:T(8,128)(2,1)S(1)}, u32[]{:S(2)}, u32[]{:S(2)}) collective-permute-start(bf16[1,34,16,128]{3,2,1,0:T(8,128)(2,1)S(1)} %get-tuple-element.11), channel_id=1, source_target_pairs={{2,0},{3,1},{4,2},{5,3},{6,4},{7,5},{8,6},{9,7},{10,8},{11,9},{12,... | collective-permute-start | bytes 417800 | tf_op jit(solution)/shard_map/ppermute | solution.py:22

commit v17 on v16

--- a/solution.py
+++ b/solution.py
@@ -215,6 +215,7 @@
     same_core = [layer_input] + [exchanged(layer_input, mask) for mask in range(2, half, 2)]
     mine = jnp.concatenate(same_core, axis=0)
     theirs = exchanged(mine, 1)
+    mirrored_queries, theirs = lax.optimization_barrier((mirrored_queries, theirs))
     kv_weight = projection[:, model_width:]
     kv_chunks = [projected(mine, norm_gain, kv_weight), projected(theirs, norm_gain, kv_weight)]
     remote_out, remote_lse = attention(

time: 63.1 us -> 66.3 us (1.051)
  waiting for transfers between devices: 6.73 us -> 10.5 us
    ppermute x2, waiting for transfers between devices: 2.31 us -> 4.45 us  [shifted(): return lax.ppermute(block, axis, route)]
    ppermute x7, waiting for transfers between devices: 3.26 us -> 4.91 us  [exchanged(): return lax.ppermute(x, 'seq', [(i, i ^ mask) for i in range(devices)])]
  transfers between devices with their start and end apart: 10 -> 10, of which waited for: 4 -> 5; matrix products, arithmetic and copies ran while one was open for 27% -> 17% of each run, Pallas kernels for 12% -> 11%
where the time goes in v17:
time: 66.3 us; the launch traced here: 65.7 us
  starting transfers between devices  16.7 us (25%)
  Pallas kernels  15.2 us (23%)
  matrix products  11.6 us (17%)
  waiting for transfers between devices  10.5 us (16%)
  other arithmetic  5.23 us (8%)
  local copies, waits for them, and re-layouts  4.63 us (7%)
  between operations  1.78 us (3%)
    pallas_call x2, Pallas kernels, attention(): pl.pallas_call(kernel, grid=(pairs,), cost_estimate=cost, in_specs=[row_s...  15.2 us
    ppermute x7, starting transfers between devices, exchanged(): return lax.ppermute(x, 'seq', [(i, i ^ mask) for i in range(devices)])  10.8 us
    dot_general x3, matrix products, projected(): jnp.dot(normed, weight, preferred_element_type=jnp.float32)  7.22 us
    ppermute x2, starting transfers between devices, shifted(): return lax.ppermute(block, axis, route)  5.91 us
    ppermute x7, waiting for transfers between devices, exchanged(): return lax.ppermute(x, 'seq', [(i, i ^ mask) for i in range(devices)])  4.91 us
    ppermute x2, waiting for transfers between devices, shifted(): return lax.ppermute(block, axis, route)  4.45 us
    conv_general_dilated x3, matrix products, conv(): lax.conv_general_dilated(field.transpose(0, 2, 1, 3)[None], kernel.transp...  3.53 us
    reduce_sum x3, other arithmetic, layer_norm(): row_var = jnp.mean(centered * centered, axis=-1, keepdims=True)  1.84 us
  transfers between devices with their start and end apart: 10, of which 5 were waited for; matrix products, arithmetic and copies ran while one was open for 17% of the time, Pallas kernels for 11%

profile of v17, /device:TPU:0, one launch (start us, length us, event | category | flops | bytes accessed | tf_op | source)
XLA Modules:
  0.0 65.7 jit_solution(4813582940765509184)
XLA Ops:
  0.6 0.0 copy-start
  0.6 0.0 copy-start.1
  0.7 3.1 %collective-permute-start = (bf16[128,768]{1,0:T(8,128)(2,1)}, bf16[128,768]{1,0:T(8,128)(2,1)S(1)}, u32[]{:S(2)}, u32[]{:S(2)}) collective-permute-start(bf16[128,768]{1,0:T(8,128)(2,1)} %param.7), channel_id=1, source_target_pairs={{0,2},{1,3},{2,0},{3,1},{4,6},{5,7},{6,4},{7,5},{8,10},{9,11},{10,... | collective-permute-start | bytes 589832 | tf_op jit(solution)/shard_map/ppermute | solution.py:200
  3.7 1.6 %collective-permute-start.1 = (bf16[128,768]{1,0:T(8,128)(2,1)}, bf16[128,768]{1,0:T(8,128)(2,1)S(1)}, u32[]{:S(2)}, u32[]{:S(2)}) collective-permute-start(bf16[128,768]{1,0:T(8,128)(2,1)} %param.7), channel_id=1, source_target_pairs={{0,4},{1,5},{2,6},{3,7},{4,0},{5,1},{6,2},{7,3},{8,12},{9,13},{10,... | collective-permute-start | bytes 589832 | tf_op jit(solution)/shard_map/ppermute | solution.py:200
  5.3 0.0 collective-permute-start.2
  5.3 1.1 %convert_reduce_fusion.2 = f32[128]{0:T(128)S(1)} fusion(bf16[128,768]{1,0:T(8,128)(2,1)} %param.7), kind=kLoop, calls=%fused_computation.38 | loop fusion | flops 196480 | bytes 197120 | tf_op jit(solution)/shard_map/reduce_sum | solution.py:31
  6.4 0.7 %convert_element_type.55 = f32[768]{0:T(1024)S(1)} convert(bf16[768]{0:T(1024)(128)(2,1)} %param.8) | non-fusion elementwise | flops 768 | bytes 4608 | tf_op jit(solution)/shard_map/convert_element_type | solution.py:34
  7.1 1.1 %fusion.38 = f32[128]{0:T(128)S(1)} fusion(bf16[128,768]{1,0:T(8,128)(2,1)} %param.7, f32[128]{0:T(128)S(1)} %broadcast_multiply_fusion.2), kind=kLoop, calls=%fused_computation.52 | loop fusion | flops 393088 | bytes 197632 | tf_op jit(solution)/shard_map/reduce_sum | solution.py:33
  8.2 0.0 copy-start.7
  8.2 1.9 %fusion.14.refs_0_ = bf16[128,768]{1,0:T(8,128)(2,1)S(1)} fusion(bf16[768,2304]{1,0:T(8,128)(2,1)} %param.9, bf16[128,768]{1,0:T(8,128)(2,1)} %param.7, f32[768]{0:T(1024)S(1)} %convert_element_type.55, f32[128]{0:T(128)S(1)} %add_rsqrt_fusion.2, f32[128]{0:T(128)S(1)} %broadcast_multiply_fusion.2), kind=kOutput, calls=%fused_computation.25 | convolution fusion | flops 151584768 | bytes 1576960 | tf_op jit(solution)/shard_map/dot_general | solution.py:205
  10.1 0.0 copy-start.4
  10.1 3.0 %collective-permute-start.3 = (bf16[128,768]{1,0:T(8,128)(2,1)S(1)}, bf16[128,768]{1,0:T(8,128)(2,1)S(1)}, u32[]{:S(2)}, u32[]{:S(2)}) collective-permute-start(bf16[128,768]{1,0:T(8,128)(2,1)S(1)} %fusion.14.refs_0_), channel_id=1, source_target_pairs={{0,8},{1,9},{2,10},{3,11},{4,12},{5,13},{6,14},{7,15},{8,0},{9,1},... | collective-permute-start | bytes 589832 | tf_op jit(solution)/shard_map/ppermute | solution.py:200
  13.2 0.0 copy-done.1
  13.2 0.0 collective-permute-done
  13.2 0.0 collective-permute-done.1
  13.2 2.3 %collective-permute-done.2 = bf16[128,768]{1,0:T(8,128)(2,1)S(1)} collective-permute-done((bf16[128,768]{1,0:T(8,128)(2,1)}, bf16[128,768]{1,0:T(8,128)(2,1)S(1)}, u32[]{:S(2)}, u32[]{:S(2)}) %collective-permute-start.2) | collective-permute-done | bytes 196640 | tf_op jit(solution)/shard_map/ppermute | solution.py:200
  15.6 0.1 collective-permute-start.4
  15.7 0.2 convert_reduce_fusion.1
  15.9 0.4 fusion.9
  16.2 0.0 copy-done.4
  16.2 2.7 %convolution_convert_fusion.1.refs_1_.refs_3_ = bf16[512,1536]{1,0:T(8,128)(2,1)} fusion(bf16[768,2304]{1,0:T(8,128)(2,1)S(1)} %copy-done.7, bf16[512,768]{1,0:T(8,128)(2,1)S(1)} %constant_dynamic-update-slice_fusion, f32[768]{0:T(1024)S(1)} %convert_element_type.55, f32[512]{0:T(512)S(1)} %add_rsqrt_fusion.1, f32[512]{0:T(512)S(1)} %broadcast_multiply_fusion.1), kind=kOutput, calls=%fused_computation.1 | convolution fusion | flops 1210712064 | bytes 4726784 | tf_op jit(solution)/shard_map/dot_general | solution.py:205
  18.9 2.6 %collective-permute-done.3.refs_0_ = bf16[128,768]{1,0:T(8,128)(2,1)S(1)} collective-permute-done((bf16[128,768]{1,0:T(8,128)(2,1)S(1)}, bf16[128,768]{1,0:T(8,128)(2,1)S(1)}, u32[]{:S(2)}, u32[]{:S(2)}) %collective-permute-start.3) | collective-permute-done | bytes 196640 | tf_op jit(solution)/shard_map/ppermute | solution.py:200
  21.5 0.0 collective-permute-done.4
  21.5 0.2 convert_reduce_fusion
  21.7 0.4 fusion.6
  22.0 2.7 %convolution_convert_fusion.refs_2_.refs_4_ = bf16[512,1536]{1,0:T(8,128)(2,1)} fusion(bf16[768,2304]{1,0:T(8,128)(2,1)S(1)} %copy-done.7, bf16[512,768]{1,0:T(8,128)(2,1)S(1)} %collective-permute-done.4, f32[512]{0:T(512)S(1)} %add_rsqrt_fusion, f32[512]{0:T(512)S(1)} %broadcast_multiply_fusion, f32[768]{0:T(1024)S(1)} %convert_element_type.55), kind=kOutput, calls=%fused_computation | convolution fusion | flops 1210712064 | bytes 4726784 | tf_op jit(solution)/shard_map/dot_general | solution.py:205
  24.7 7.7 %shard_map.87 = (bf16[128,768]{1,0:T(8,128)(2,1)}, f32[128,128]{1,0:T(8,128)}, f32[16,128]{1,0:T(8,128)}) custom-call(bf16[128,768]{1,0:T(8,128)(2,1)} %copy-done.5, bf16[512,1536]{1,0:T(8,128)(2,1)} %convolution_convert_fusion.1.refs_1_.refs_3_, bf16[512,1536]{1,0:T(8,128)(2,1)} %convolution_convert_fusion.refs_2_.refs_4_, ...), custom_call_target="tpu_custom_call" | custom-call | flops 805306368 | bytes 3932160 | tf_op jit(solution)/shard_map/pallas_call | solution.py:185
  32.4 0.4 collective-permute-start.6
  32.8 0.0 copy-done.2
  32.8 0.3 convolution_convert_fusion.2
  33.1 0.2 reshape_reshape.7
  33.3 0.2 copy.21
  33.5 2.7 %collective-permute-start.5 = (f32[16,128]{1,0:T(8,128)S(1)}, f32[16,128]{1,0:T(8,128)S(1)}, u32[]{:S(2)}, u32[]{:S(2)}) collective-permute-start(f32[16,128]{1,0:T(8,128)S(1)} %copy-done.10), channel_id=1, source_target_pairs={{0,8},{1,9},{2,10},{3,11},{4,12},{5,13},{6,14},{7,15},{8,0},{9,1},... | collective-permute-start | bytes 24584 | tf_op jit(solution)/shard_map/ppermute | solution.py:200
  36.2 7.5 %shard_map.86 = (f32[128,768]{1,0:T(8,128)}, f32[128,128]{1,0:T(8,128)}) custom-call(bf16[128,768]{1,0:T(8,128)(2,1)} %copy-done.4, bf16[512,1536]{1,0:T(8,128)(2,1)} %convolution_convert_fusion.1.refs_1_.refs_3_, bf16[512,1536]{1,0:T(8,128)(2,1)} %convolution_convert_fusion.refs_2_.refs_4_, bf16[512,1536]{1,0:T(8,128)(2,1)} %convolution_convert_fusion.1.refs_1_.refs_3_, ...), custom_call_target="tpu_custom_call" | custom-call | flops 805306368 | bytes 3932160 | tf_op jit(solution)/shard_map/pallas_call | solution.py:185
  43.7 1.0 %copy.15 = f32[128,128]{0,1:T(8,128)S(1)} copy(f32[128,128]{1,0:T(8,128)} %get-tuple-element.9) | data formatting | bytes 131072 | tf_op jit(solution)/shard_map/pallas_call | solution.py:185
  44.7 0.0 collective-permute-done.6
  44.7 0.5 slice.52
  45.9 0.0 collective-permute-done.5
  45.9 0.2 copy.16
  46.1 0.2 copy.17
  46.3 0.0 copy-start.3
  46.3 0.3 fusion.17
  46.7 0.8 %copy-done.3 = bf16[768,512]{1,0:T(8,128)(2,1)S(1)} copy-done((bf16[768,512]{1,0:T(8,128)(2,1)S(1)}, bf16[768,512]{1,0:T(8,128)(2,1)}, u32[]{:S(2)}) %copy-start.3) | copy-done | bytes 786456
  47.5 0.3 convolution_convert_fusion.3
  47.7 0.2 reshape_reshape.6
  47.9 0.2 copy.20
  48.1 0.1 fusion.63
  48.2 0.0 collective-permute-start.7
  48.2 1.2 %collective-permute-done.7 = bf16[2,1,16,128]{3,2,1,0:T(8,128)(2,1)S(1)} collective-permute-done((bf16[2,1,16,128]{3,2,1,0:T(8,128)(2,1)S(1)}, bf16[2,1,16,128]{3,2,1,0:T(8,128)(2,1)S(1)}, u32[]{:S(2)}, u32[]{:S(2)}) %collective-permute-start.7) | collective-permute-done | bytes 8224 | tf_op jit(solution)/shard_map/ppermute | solution.py:26
  49.4 0.1 fusion.80
  49.6 0.1 pad_maximum_fusion
  49.7 0.1 copy.23
  49.9 0.5 copy-done.8
  50.4 2.5 %convolution_select_fusion = f32[2,16,8,5,64]{4,2,3,1,0:T(8,128)S(1)} fusion(bf16[2,16,1,7,2,128]{5,3,4,1,0,2:T(8,128)(2,1)S(1)} %slice.53, bf16[2,16,1,8,5,128]{5,3,4,1,0,2:T(8,128)(2,1)S(1)} %copy.23, pred[8,5]{0,1:T(8,128)(4,1)S(1)} %copy-done.11, bf16[3,3,3,128,64]{3,4,2,1,0:T(8,128)(2,1)S(1)} %copy-done.8), kind=kOutput, calls=%fused_computation.19 | convolution fusion | flops 363216896 | bytes 1212456 | tf_op jit(solution)/shard_map/conv_general_dilated | solution.py:55
  52.9 0.1 copy.25
  53.0 1.3 %collective-permute-start.9 = (bf16[1,34,16,128]{3,2,1,0:T(8,128)(2,1)S(1)}, bf16[1,34,16,128]{3,2,1,0:T(8,128)(2,1)S(1)}, u32[]{:S(2)}, u32[]{:S(2)}) collective-permute-start(bf16[1,34,16,128]{3,2,1,0:T(8,128)(2,1)S(1)} %get-tuple-element.15), channel_id=1, source_target_pairs={{2,0},{3,1},{4,2},{5,3},{6,4},{7,5},{8,6},{9,7},{10,8},{11,9},{12,... | collective-permute-start | bytes 417800 | tf_op jit(solution)/shard_map/ppermute | solution.py:22
  54.4 4.6 %collective-permute-start.8 = (bf16[1,34,16,128]{3,2,1,0:T(8,128)(2,1)S(1)}, bf16[1,34,16,128]{3,2,1,0:T(8,128)(2,1)S(1)}, u32[]{:S(2)}, u32[]{:S(2)}) collective-permute-start(bf16[1,34,16,128]{3,2,1,0:T(8,128)(2,1)S(1)} %get-tuple-element.14), channel_id=1, source_target_pairs={{0,2},{1,3},{2,4},{3,5},{4,6},{5,7},{6,8},{7,9},{8,10},{9,11},{10,... | collective-permute-start | bytes 417800 | tf_op jit(solution)/shard_map/ppermute | solution.py:22
  59.0 2.0 %collective-permute-done.9 = bf16[1,34,16,128]{3,2,1,0:T(8,128)(2,1)S(1)} collective-permute-done((bf16[1,34,16,128]{3,2,1,0:T(8,128)(2,1)S(1)}, bf16[1,34,16,128]{3,2,1,0:T(8,128)(2,1)S(1)}, u32[]{:S(2)}, u32[]{:S(2)}) %collective-permute-start.9) | collective-permute-done | bytes 139296 | tf_op jit(solution)/shard_map/ppermute | solution.py:22
  61.1 0.5 convolution_select_fusion.1
  61.6 0.1 copy.33
  61.7 2.4 %collective-permute-done.8 = bf16[1,34,16,128]{3,2,1,0:T(8,128)(2,1)S(1)} collective-permute-done((bf16[1,34,16,128]{3,2,1,0:T(8,128)(2,1)S(1)}, bf16[1,34,16,128]{3,2,1,0:T(8,128)(2,1)S(1)}, u32[]{:S(2)}, u32[]{:S(2)}) %collective-permute-start.8) | collective-permute-done | bytes 139296 | tf_op jit(solution)/shard_map/ppermute | solution.py:22
  64.3 0.5 convolution_select_fusion.2
  64.8 0.1 copy.29
  64.9 0.8 %fusion.41 = bf16[1,2,32,16,64]{4,3,2,1,0:T(8,128)(2,1)} fusion(f32[2,32,16,64]{3,2,1,0:T(8,128)S(1)} %slice_bitcast_fusion, f32[1,32,16,64]{3,2,1,0:T(8,128)S(1)} %get-tuple-element.20, f32[1,32,16,64]{3,2,1,0:T(8,128)S(1)} %get-tuple-element.21), kind=kLoop, calls=%fused_computation.57 | loop fusion | flops 393216 | bytes 655360 | tf_op jit(solution)/shard_map/broadcast_in_dim | solution.py:260
  (39 shorter events, 0.5 us)
Async XLA Ops:
  0.6 45.7 %copy-start = (bf16[768,768]{1,0:T(8,128)(2,1)S(1)}, bf16[768,768]{1,0:T(8,128)(2,1)}, u32[]{:S(2)}) copy-start(bf16[768,768]{1,0:T(8,128)(2,1)} %param.10) | copy-start | bytes 3538948
  0.6 12.5 %copy-start.1 = (bf16[128,768]{1,0:T(8,128)(2,1)S(1)}, bf16[128,768]{1,0:T(8,128)(2,1)}, u32[]{:S(2)}) copy-start(bf16[128,768]{1,0:T(8,128)(2,1)} %param.7) | copy-start | bytes 589828
  0.7 12.5 %collective-permute-start = (bf16[128,768]{1,0:T(8,128)(2,1)}, bf16[128,768]{1,0:T(8,128)(2,1)S(1)}, u32[]{:S(2)}, u32[]{:S(2)}) collective-permute-start(bf16[128,768]{1,0:T(8,128)(2,1)} %param.7), channel_id=1, source_target_pairs={{0,2},{1,3},{2,0},{3,1},{4,6},{5,7},{6,4},{7,5},{8,10},{9,11},{10,... | collective-permute-start | bytes 589832 | tf_op jit(solution)/shard_map/ppermute | solution.py:200
  3.7 9.5 %collective-permute-start.1 = (bf16[128,768]{1,0:T(8,128)(2,1)}, bf16[128,768]{1,0:T(8,128)(2,1)S(1)}, u32[]{:S(2)}, u32[]{:S(2)}) collective-permute-start(bf16[128,768]{1,0:T(8,128)(2,1)} %param.7), channel_id=1, source_target_pairs={{0,4},{1,5},{2,6},{3,7},{4,0},{5,1},{6,2},{7,3},{8,12},{9,13},{10,... | collective-permute-start | bytes 589832 | tf_op jit(solution)/shard_map/ppermute | solution.py:200
  5.3 10.3 %collective-permute-start.2 = (bf16[128,768]{1,0:T(8,128)(2,1)}, bf16[128,768]{1,0:T(8,128)(2,1)S(1)}, u32[]{:S(2)}, u32[]{:S(2)}) collective-permute-start(bf16[128,768]{1,0:T(8,128)(2,1)} %param.7), channel_id=1, source_target_pairs={{0,6},{1,7},{2,4},{3,5},{4,2},{5,3},{6,0},{7,1},{8,14},{9,15},{10,... | collective-permute-start | bytes 589832 | tf_op jit(solution)/shard_map/ppermute | solution.py:200
  8.2 8.0 %copy-start.7 = (bf16[768,2304]{1,0:T(8,128)(2,1)S(1)}, bf16[768,2304]{1,0:T(8,128)(2,1)}, u32[]{:S(2)}) copy-start(bf16[768,2304]{1,0:T(8,128)(2,1)} %param.9) | copy-start | bytes 10616836
  10.1 6.1 %copy-start.4 = (bf16[128,768]{1,0:T(8,128)(2,1)}, bf16[128,768]{1,0:T(8,128)(2,1)S(1)}, u32[]{:S(2)}) copy-start(bf16[128,768]{1,0:T(8,128)(2,1)S(1)} %fusion.14.refs_0_) | copy-start | bytes 589828
  10.1 11.3 %collective-permute-start.3 = (bf16[128,768]{1,0:T(8,128)(2,1)S(1)}, bf16[128,768]{1,0:T(8,128)(2,1)S(1)}, u32[]{:S(2)}, u32[]{:S(2)}) collective-permute-start(bf16[128,768]{1,0:T(8,128)(2,1)S(1)} %fusion.14.refs_0_), channel_id=1, source_target_pairs={{0,8},{1,9},{2,10},{3,11},{4,12},{5,13},{6,14},{7,15},{8,0},{9,1},... | collective-permute-start | bytes 589832 | tf_op jit(solution)/shard_map/ppermute | solution.py:200
  15.6 5.9 %collective-permute-start.4 = (bf16[512,768]{1,0:T(8,128)(2,1)S(1)}, bf16[512,768]{1,0:T(8,128)(2,1)S(1)}, u32[]{:S(2)}, u32[]{:S(2)}) collective-permute-start(bf16[512,768]{1,0:T(8,128)(2,1)S(1)} %constant_dynamic-update-slice_fusion), channel_id=1, source_target_pairs={{0,1},{1,0},{2,3},{3,2},{4,5},{5,4},{6,7},{7,6},{8,9},{9,8},{10,11... | collective-permute-start | bytes 2359304 | tf_op jit(solution)/shard_map/ppermute | solution.py:200
  21.5 3.2 %copy-start.5 = (bf16[128,768]{1,0:T(8,128)(2,1)}, bf16[128,768]{1,0:T(8,128)(2,1)S(1)}, u32[]{:S(2)}) copy-start(bf16[128,768]{1,0:T(8,128)(2,1)S(1)} %collective-permute-done.3.refs_0_) | copy-start | bytes 589828
  24.7 8.1 %copy-start.2 = (bf16[768,512]{1,0:T(8,128)(2,1)S(1)}, bf16[768,512]{1,0:T(8,128)(2,1)}, u32[]{:S(2)}) copy-start(bf16[768,512]{1,0:T(8,128)(2,1)} %param.12) | copy-start | bytes 2359300
  32.4 1.1 %copy-start.10 = (f32[16,128]{1,0:T(8,128)S(1)}, f32[16,128]{1,0:T(8,128)}, u32[]{:S(2)}) copy-start(f32[16,128]{1,0:T(8,128)} %get-tuple-element.11) | copy-start | bytes 24580
  32.4 12.3 %collective-permute-start.6 = (bf16[128,768]{1,0:T(8,128)(2,1)}, bf16[128,768]{1,0:T(8,128)(2,1)S(1)}, u32[]{:S(2)}, u32[]{:S(2)}) collective-permute-start(bf16[128,768]{1,0:T(8,128)(2,1)} %get-tuple-element.12), channel_id=1, source_target_pairs={{0,8},{1,9},{2,10},{3,11},{4,12},{5,13},{6,14},{7,15},{8,0},{9,1},... | collective-permute-start | bytes 589832 | tf_op jit(solution)/shard_map/ppermute | solution.py:200
  33.5 12.4 %collective-permute-start.5 = (f32[16,128]{1,0:T(8,128)S(1)}, f32[16,128]{1,0:T(8,128)S(1)}, u32[]{:S(2)}, u32[]{:S(2)}) collective-permute-start(f32[16,128]{1,0:T(8,128)S(1)} %copy-done.10), channel_id=1, source_target_pairs={{0,8},{1,9},{2,10},{3,11},{4,12},{5,13},{6,14},{7,15},{8,0},{9,1},... | collective-permute-start | bytes 24584 | tf_op jit(solution)/shard_map/ppermute | solution.py:200
  43.7 2.6 %copy-start.9 = (f32[128,768]{1,0:T(8,128)S(1)}, f32[128,768]{1,0:T(8,128)}, u32[]{:S(2)}) copy-start(f32[128,768]{1,0:T(8,128)} %get-tuple-element.13) | copy-start | bytes 1179652
  46.3 1.1 %copy-start.3 = (bf16[768,512]{1,0:T(8,128)(2,1)S(1)}, bf16[768,512]{1,0:T(8,128)(2,1)}, u32[]{:S(2)}) copy-start(bf16[768,512]{1,0:T(8,128)(2,1)} %param.11) | copy-start | bytes 2359300
  47.4 2.1 %copy-start.6 = (bf16[128,768]{1,0:T(8,128)(2,1)}, bf16[128,768]{1,0:T(8,128)(2,1)S(1)}, u32[]{:S(2)}) copy-start(bf16[128,768]{1,0:T(8,128)(2,1)S(1)} %fusion.17) | copy-start | bytes 589828
  48.2 1.2 %collective-permute-start.7 = (bf16[2,1,16,128]{3,2,1,0:T(8,128)(2,1)S(1)}, bf16[2,1,16,128]{3,2,1,0:T(8,128)(2,1)S(1)}, u32[]{:S(2)}, u32[]{:S(2)}) collective-permute-start(bf16[2,1,16,128]{3,2,1,0:T(8,128)(2,1)S(1)} %fusion.63), channel_id=1, source_target_pairs={{0,1},{1,0},{2,3},{3,2},{4,5},{5,4},{6,7},{7,6},{8,9},{9,8},{10,11... | collective-permute-start | bytes 24584 | tf_op jit(solution)/shard_map/ppermute | solution.py:26
  49.4 1.0 %copy-start.8 = (bf16[3,3,3,128,64]{3,4,2,1,0:T(8,128)(2,1)S(1)}, bf16[3,3,3,128,64]{3,4,2,1,0:T(8,128)(2,1)}, u32[]{:S(2)}) copy-start(bf16[3,3,3,128,64]{3,4,2,1,0:T(8,128)(2,1)} %param.13) | copy-start | bytes 1327108
  49.4 1.0 %copy-start.11 = (pred[8,5]{0,1:T(8,128)(4,1)S(1)}, pred[8,5]{0,1:T(8,128)(4,1)}, u32[]{:S(2)}) copy-start(pred[8,5]{0,1:T(8,128)(4,1)} %constant.51) | copy-start | bytes 124
  53.0 8.0 %collective-permute-start.9 = (bf16[1,34,16,128]{3,2,1,0:T(8,128)(2,1)S(1)}, bf16[1,34,16,128]{3,2,1,0:T(8,128)(2,1)S(1)}, u32[]{:S(2)}, u32[]{:S(2)}) collective-permute-start(bf16[1,34,16,128]{3,2,1,0:T(8,128)(2,1)S(1)} %get-tuple-element.15), channel_id=1, source_target_pairs={{2,0},{3,1},{4,2},{5,3},{6,4},{7,5},{8,6},{9,7},{10,8},{11,9},{12,... | collective-permute-start | bytes 417800 | tf_op jit(solution)/shard_map/ppermute | solution.py:22
  54.4 9.8 %collective-permute-start.8 = (bf16[1,34,16,128]{3,2,1,0:T(8,128)(2,1)S(1)}, bf16[1,34,16,128]{3,2,1,0:T(8,128)(2,1)S(1)}, u32[]{:S(2)}, u32[]{:S(2)}) collective-permute-start(bf16[1,34,16,128]{3,2,1,0:T(8,128)(2,1)S(1)} %get-tuple-element.14), channel_id=1, source_target_pairs={{0,2},{1,3},{2,4},{3,5},{4,6},{5,7},{6,8},{7,9},{8,10},{9,11},{10,... | collective-permute-start | bytes 417800 | tf_op jit(solution)/shard_map/ppermute | solution.py:22
